TPU v7x, 512 devices: a whole 4x8x8 slice. The times are simulated.
512 devices in a mesh: row: 32 (over z, x), col: 16 (over y, core).
Axes of the slice: x: 4, y: 8, z: 8, core: 2. Of those that a mesh axis runs over, the one named last changes fastest.
Arguments:
- coeffs: float32 [4096, 128], P(('row', 'col')), may hold values from -6 to 6
- basis: float32 [256, 128, 4096], P('row', 'col'), may hold values from -0.1875 to 0.1875
- observed: float32 [256, 128, 128], P('row', 'col'), may hold values from -6 to 6
- lift_w: float32 [32], replicated, may hold values from -3 to 3
- lift_b: float32 [32], replicated, may hold values from -3 to 3
- w_one: bfloat16 [3, 3, 32, 32], replicated, may hold values from -0.375 to 0.375
- b_one: float32 [32], replicated, may hold values from -3 to 3
- w_two: bfloat16 [3, 3, 32, 32], replicated, may hold values from -0.375 to 0.375
- b_two: float32 [32], replicated, may hold values from -3 to 3
- read_w: float32 [32], replicated, may hold values from -1 to 1
Outputs:
- pressure: float32 [256, 128, 128], P('row', 'col')
- grad_coeffs: float32 [4096, 128], P(('row', 'col'))
All inputs are finite; a program needn't handle non-finite values.
Results may differ from a plain program's by a relative error of at most 0.015.
Values may be sent and summed in bfloat16 or wider, within the bound.
No kernel may reach another device: no remote copies, remote signals or barrier semaphores. Data moves between devices by JAX's collectives and lax.ppermute only.
A program may use at most 64 MiB of HBM per device.

v0:
```python
import jax
import jax.numpy as jnp
from jax import lax
from jax.sharding import PartitionSpec as P

prior_weight = 0.1


def with_halo(block, sides, width):
    for axis, dim in sides:
        count = lax.axis_size(axis)
        forward = [(i, i + 1) for i in range(count - 1)]
        backward = [(target, source) for source, target in forward]
        low = lax.ppermute(
            lax.slice_in_dim(block, block.shape[dim] - width, None, axis=dim), axis, forward
        )
        high = lax.ppermute(lax.slice_in_dim(block, 0, width, axis=dim), axis, backward)
        block = jnp.concatenate([low, block, high], axis=dim)
    return block


def extend_tile(values):
    return with_halo(values, (("row", 0), ("col", 1)), 1)


def conv_fwd(values, weights, extend):
    padded = extend(values)
    nrow = values.shape[0]
    ncol = values.shape[1]
    running = jnp.zeros(values.shape[:3] + (weights.shape[3],), jnp.float32)
    for shift_x in range(3):
        for shift_y in range(3):
            window = padded[shift_x : shift_x + nrow, shift_y : shift_y + ncol]
            running = running + jnp.einsum(
                "xybi,io->xybo",
                window,
                weights[shift_x, shift_y],
                preferred_element_type=jnp.float32,
            )
    return running


def conv_back(grads, weights, extend):
    padded = extend(grads)
    nrow = grads.shape[0]
    ncol = grads.shape[1]
    running = jnp.zeros(grads.shape[:3] + (weights.shape[2],), jnp.float32)
    for shift_x in range(3):
        for shift_y in range(3):
            window = padded[2 - shift_x : 2 - shift_x + nrow, 2 - shift_y : 2 - shift_y + ncol]
            running = running + jnp.einsum(
                "xybo,io->xybi",
                window,
                weights[shift_x, shift_y],
                preferred_element_type=jnp.float32,
            )
    return running


def surrogate(logperm, observed, lift_w, lift_b, w_one, b_one, w_two, b_two, read_w, extend):
    lifted = (logperm[..., None] * lift_w + lift_b).astype(jnp.bfloat16)
    hidden_one = jnp.tanh(conv_fwd(lifted, w_one, extend) + b_one).astype(jnp.bfloat16)
    hidden_two = jnp.tanh(conv_fwd(hidden_one, w_two, extend) + b_two)
    pressure = jnp.sum(hidden_two * read_w, axis=-1)
    misfit = pressure - observed
    grad_two = (misfit[..., None] * read_w * (1.0 - hidden_two * hidden_two)).astype(jnp.bfloat16)
    h_one = hidden_one.astype(jnp.float32)
    grad_one = (conv_back(grad_two, w_two, extend) * (1.0 - h_one * h_one)).astype(jnp.bfloat16)
    grad_field = jnp.sum(conv_back(grad_one, w_one, extend) * lift_w, axis=-1)
    return (pressure, grad_field)


def shards(coeffs, basis, observed, lift_w, lift_b, w_one, b_one, w_two, b_two, read_w):
    tile_rows, tile_cols, mode_count = basis.shape
    batch_size = coeffs.shape[1]
    flat_basis = basis.reshape(tile_rows * tile_cols, mode_count)
    basis_part = flat_basis
    logperm = jnp.dot(
        basis_part,
        lax.all_gather(coeffs, ("row", "col"), axis=0, tiled=True),
        precision=lax.Precision.HIGHEST,
        preferred_element_type=jnp.float32,
    )
    logperm = logperm.reshape(tile_rows, tile_cols, batch_size)
    pressure, grad_field = surrogate(
        logperm, observed, lift_w, lift_b, w_one, b_one, w_two, b_two, read_w, extend_tile
    )
    grad_flat = grad_field.reshape(tile_rows * tile_cols, batch_size)
    basis_part = flat_basis
    summed = lax.psum_scatter(
        lax.dot_general(
            basis_part,
            grad_flat,
            (((0,), (0,)), ((), ())),
            precision=lax.Precision.HIGHEST,
            preferred_element_type=jnp.float32,
        ),
        ("row", "col"),
        scatter_dimension=0,
        tiled=True,
    )
    grad_coeffs = summed + prior_weight * coeffs
    return (pressure, grad_coeffs)


def solution(mesh):
    return jax.shard_map(
        shards,
        mesh=mesh,
        in_specs=(
            P(("row", "col"), None),
            P("row", "col", None),
            P("row", "col", None),
            P(),
            P(),
            P(),
            P(),
            P(),
            P(),
            P(),
        ),
        out_specs=(P("row", "col", None), P(("row", "col"), None)),
        check_vma=False,
    )
```

profile of v0, /device:TPU:1, one launch (start us, length us, event | category | flops | bytes accessed | tf_op | source)
XLA Modules:
  0.0 521.0 jit_solution(12413397913941933140)
XLA Ops:
  7.2 0.7 all-gather.2.cloned.1.call-update
  8.0 126.0 %all-gather.2.cloned.1.call-done = f32[4096,128]{1,0:T(8,128)} async-done(((f32[8,128]{1,0:T(8,128)}), f32[4096,128]{1,0:T(8,128)}) %all-gather.2.cloned.1.call-update) | async-done | bytes 2097168 | tf_op jit(solution)/shard_map/all_gather | solution.py:80
  134.0 3.0 fusion
  137.2 3.0 collective-permute-start
  140.3 1.3 collective-permute-start.1
  142.0 3.3 collective-permute-done.1
  145.3 4.7 collective-permute-start.2
  150.0 1.9 collective-permute-start.3
  152.6 3.2 collective-permute-done.3
  158.3 3.1 collective-permute-start.4
  161.4 1.3 collective-permute-start.5
  163.1 3.4 collective-permute-done.5
  166.5 3.9 collective-permute-start.6
  170.4 1.9 collective-permute-start.7
  172.9 3.2 collective-permute-done.7
  178.2 0.5 multiply_reduce_fusion
  179.3 1.3 collective-permute-start.9
  180.6 4.0 collective-permute-start.8
  184.9 1.0 collective-permute-done.8
  185.9 3.0 collective-permute-start.11
  188.9 1.9 collective-permute-start.10
  191.4 3.3 collective-permute-done.10
  196.6 1.3 collective-permute-start.13
  197.9 4.7 collective-permute-start.12
  202.9 1.0 collective-permute-done.12
  204.0 2.7 collective-permute-start.15
  206.6 2.1 collective-permute-start.14
  209.3 3.1 collective-permute-done.14
  214.3 3.2 convolution_bitcast_fusion
  217.5 295.0 %all-reduce.3.cloned.1.call-done = f32[4096,128]{0,1:T(8,128)} async-done(((f32[4096,128]{0,1:T(8,128)}), f32[4096,128]{0,1:T(8,128)}) %all-reduce.3.cloned.1.call-update) | async-done | bytes 2097168
  512.5 0.9 constant_dynamic-slice_fusion
  513.5 0.6 multiply_add_fusion
  (82 shorter events, 12.9 us)
Async XLA Ops:
  7.2 126.9 %copy-start = (f32[8,8,4096]{2,1,0:T(8,128)S(1)}, f32[8,8,4096]{2,1,0:T(8,128)}, u32[]{:S(2)}) copy-start(f32[8,8,4096]{2,1,0:T(8,128)} %param.11) | copy-start | bytes 3145732
  7.2 126.8 %all-gather.2.cloned.1.call-start = ((), (), s32[]{:S(2)}) async-start(), calls=%async_computation | async-start | bytes 2101248 | tf_op jit(solution)/shard_map/all_gather | solution.py:80
  7.9 129.1 %copy-start.6 = (f32[32]{0:T(128)S(1)}, f32[32]{0:T(128)}, u32[]{:S(2)}) copy-start(f32[32]{0:T(128)} %param.13) | copy-start | bytes 388
  7.9 129.1 %copy-start.7 = (f32[32]{0:T(128)S(1)}, f32[32]{0:T(128)}, u32[]{:S(2)}) copy-start(f32[32]{0:T(128)} %param.14) | copy-start | bytes 388
  7.9 133.6 %copy-start.2 = (bf16[3,3,32,32]{3,2,1,0:T(8,128)(2,1)S(1)}, bf16[3,3,32,32]{3,2,1,0:T(8,128)(2,1)}, u32[]{:S(2)}) copy-start(bf16[3,3,32,32]{3,2,1,0:T(8,128)(2,1)} %param.15) | copy-start | bytes 55300
  7.9 504.6 %all-reduce.3.cloned.1.call-start = ((), (), s32[]{:S(2)}) async-start(), calls=%async_computation.1 | async-start | bytes 4194304
  137.2 4.7 collective-permute-start
  140.3 5.0 collective-permute-start.1
  145.3 7.2 %collective-permute-start.2 = (bf16[10,1,128,32]{2,3,1,0:T(8,128)(2,1)S(1)}, bf16[10,1,128,32]{2,3,1,0:T(8,128)(2,1)S(1)}, u32[]{:S(2)}, u32[]{:S(2)}) collective-permute-start(bf16[10,1,128,32]{2,3,1,0:T(8,128)(2,1)S(1)} %get-tuple-element.16), channel_id=1, source_target_pairs={{0,1},{1,2},{2,3},{3,4},{4,5},{5,6},{6,7},{7,8},{8,9},{9,10},{10,1... | collective-permute-start | bytes 245768 | tf_op jit(solution)/shard_map/ppermute | solution.py:14
  150.0 5.8 %collective-permute-start.3 = (bf16[10,1,128,32]{2,3,1,0:T(8,128)(2,1)S(1)}, bf16[10,1,128,32]{2,3,1,0:T(8,128)(2,1)S(1)}, u32[]{:S(2)}, u32[]{:S(2)}) collective-permute-start(bf16[10,1,128,32]{2,3,1,0:T(8,128)(2,1)S(1)} %get-tuple-element.17), channel_id=1, source_target_pairs={{1,0},{2,1},{3,2},{4,3},{5,4},{6,5},{7,6},{8,7},{9,8},{10,9},{11,1... | collective-permute-start | bytes 245768 | tf_op jit(solution)/shard_map/ppermute | solution.py:17
  157.2 0.7 copy-start.10
  157.8 4.9 copy-start.1
  158.3 4.7 collective-permute-start.4
  161.4 5.0 collective-permute-start.5
  166.5 6.5 %collective-permute-start.6 = (bf16[10,1,128,32]{2,3,1,0:T(8,128)(2,1)S(1)}, bf16[10,1,128,32]{2,3,1,0:T(8,128)(2,1)S(1)}, u32[]{:S(2)}, u32[]{:S(2)}) collective-permute-start(bf16[10,1,128,32]{2,3,1,0:T(8,128)(2,1)S(1)} %get-tuple-element.12), channel_id=1, source_target_pairs={{0,1},{1,2},{2,3},{3,4},{4,5},{5,6},{6,7},{7,8},{8,9},{9,10},{10,1... | collective-permute-start | bytes 245768 | tf_op jit(solution)/shard_map/ppermute | solution.py:14
  170.4 5.8 %collective-permute-start.7 = (bf16[10,1,128,32]{2,3,1,0:T(8,128)(2,1)S(1)}, bf16[10,1,128,32]{2,3,1,0:T(8,128)(2,1)S(1)}, u32[]{:S(2)}, u32[]{:S(2)}) collective-permute-start(bf16[10,1,128,32]{2,3,1,0:T(8,128)(2,1)S(1)} %get-tuple-element.13), channel_id=1, source_target_pairs={{1,0},{2,1},{3,2},{4,3},{5,4},{6,5},{7,6},{8,7},{9,8},{10,9},{11,1... | collective-permute-start | bytes 245768 | tf_op jit(solution)/shard_map/ppermute | solution.py:17
  177.6 0.7 copy-start.8
  177.6 0.7 copy-start.9
  178.2 0.8 copy-start.4
  178.8 6.1 %copy-start.3 = (f32[8,8,128]{2,1,0:T(8,128)}, f32[8,8,128]{2,1,0:T(8,128)S(1)}, u32[]{:S(2)}) copy-start(f32[8,8,128]{2,1,0:T(8,128)S(1)} %get-tuple-element.26) | copy-start | bytes 98308
  179.3 5.6 %collective-permute-start.9 = (bf16[1,8,128,32]{2,3,1,0:T(8,128)(2,1)S(1)}, bf16[1,8,128,32]{2,3,1,0:T(8,128)(2,1)S(1)}, u32[]{:S(2)}, u32[]{:S(2)}) collective-permute-start(bf16[1,8,128,32]{2,3,1,0:T(8,128)(2,1)S(1)} %get-tuple-element.21), channel_id=1, source_target_pairs={{16,0},{32,16},{48,32},{64,48},{80,64},{96,80},{112,96},{128,112},... | collective-permute-start | bytes 196616 | tf_op jit(solution)/shard_map/ppermute | solution.py:17
  180.6 5.3 %collective-permute-start.8 = (bf16[1,8,128,32]{2,3,1,0:T(8,128)(2,1)S(1)}, bf16[1,8,128,32]{2,3,1,0:T(8,128)(2,1)S(1)}, u32[]{:S(2)}, u32[]{:S(2)}) collective-permute-start(bf16[1,8,128,32]{2,3,1,0:T(8,128)(2,1)S(1)} %get-tuple-element.20), channel_id=1, source_target_pairs={{0,16},{16,32},{32,48},{48,64},{64,80},{80,96},{96,112},{112,128},... | collective-permute-start | bytes 196616 | tf_op jit(solution)/shard_map/ppermute | solution.py:14
  185.9 9.3 %collective-permute-start.11 = (bf16[10,1,128,32]{2,3,1,0:T(8,128)(2,1)S(1)}, bf16[10,1,128,32]{2,3,1,0:T(8,128)(2,1)S(1)}, u32[]{:S(2)}, u32[]{:S(2)}) collective-permute-start(bf16[10,1,128,32]{2,3,1,0:T(8,128)(2,1)S(1)} %get-tuple-element.9), channel_id=1, source_target_pairs={{0,1},{1,2},{2,3},{3,4},{4,5},{5,6},{6,7},{7,8},{8,9},{9,10},{10,1... | collective-permute-start | bytes 245768 | tf_op jit(solution)/shard_map/ppermute | solution.py:14
  188.9 5.8 %collective-permute-start.10 = (bf16[10,1,128,32]{2,3,1,0:T(8,128)(2,1)S(1)}, bf16[10,1,128,32]{2,3,1,0:T(8,128)(2,1)S(1)}, u32[]{:S(2)}, u32[]{:S(2)}) collective-permute-start(bf16[10,1,128,32]{2,3,1,0:T(8,128)(2,1)S(1)} %get-tuple-element.8), channel_id=1, source_target_pairs={{1,0},{2,1},{3,2},{4,3},{5,4},{6,5},{7,6},{8,7},{9,8},{10,9},{11,1... | collective-permute-start | bytes 245768 | tf_op jit(solution)/shard_map/ppermute | solution.py:17
  196.6 6.3 %collective-permute-start.13 = (bf16[1,8,128,32]{2,3,1,0:T(8,128)(2,1)S(1)}, bf16[1,8,128,32]{2,3,1,0:T(8,128)(2,1)S(1)}, u32[]{:S(2)}, u32[]{:S(2)}) collective-permute-start(bf16[1,8,128,32]{2,3,1,0:T(8,128)(2,1)S(1)} %get-tuple-element.19), channel_id=1, source_target_pairs={{16,0},{32,16},{48,32},{64,48},{80,64},{96,80},{112,96},{128,112},... | collective-permute-start | bytes 196616 | tf_op jit(solution)/shard_map/ppermute | solution.py:17
  197.9 6.0 %collective-permute-start.12 = (bf16[1,8,128,32]{2,3,1,0:T(8,128)(2,1)S(1)}, bf16[1,8,128,32]{2,3,1,0:T(8,128)(2,1)S(1)}, u32[]{:S(2)}, u32[]{:S(2)}) collective-permute-start(bf16[1,8,128,32]{2,3,1,0:T(8,128)(2,1)S(1)} %get-tuple-element.18), channel_id=1, source_target_pairs={{0,16},{16,32},{32,48},{48,64},{64,80},{80,96},{96,112},{112,128},... | collective-permute-start | bytes 196616 | tf_op jit(solution)/shard_map/ppermute | solution.py:14
  204.0 9.0 %collective-permute-start.15 = (bf16[10,1,128,32]{2,3,1,0:T(8,128)(2,1)S(1)}, bf16[10,1,128,32]{2,3,1,0:T(8,128)(2,1)S(1)}, u32[]{:S(2)}, u32[]{:S(2)}) collective-permute-start(bf16[10,1,128,32]{2,3,1,0:T(8,128)(2,1)S(1)} %get-tuple-element.7), channel_id=1, source_target_pairs={{0,1},{1,2},{2,3},{3,4},{4,5},{5,6},{6,7},{7,8},{8,9},{9,10},{10,1... | collective-permute-start | bytes 245768 | tf_op jit(solution)/shard_map/ppermute | solution.py:14
  206.6 5.8 %collective-permute-start.14 = (bf16[10,1,128,32]{2,3,1,0:T(8,128)(2,1)S(1)}, bf16[10,1,128,32]{2,3,1,0:T(8,128)(2,1)S(1)}, u32[]{:S(2)}, u32[]{:S(2)}) collective-permute-start(bf16[10,1,128,32]{2,3,1,0:T(8,128)(2,1)S(1)} %get-tuple-element.6), channel_id=1, source_target_pairs={{1,0},{2,1},{3,2},{4,3},{5,4},{6,5},{7,6},{8,7},{9,8},{10,9},{11,1... | collective-permute-start | bytes 245768 | tf_op jit(solution)/shard_map/ppermute | solution.py:17
  217.5 296.0 %copy-start.5 = (f32[8,128]{1,0:T(8,128)S(1)}, f32[8,128]{1,0:T(8,128)}, u32[]{:S(2)}) copy-start(f32[8,128]{1,0:T(8,128)} %param.10) | copy-start | bytes 12292
Sparse Core Ops, SparseCore 0:
  12.2 121.8 all-gather.1
  217.6 294.8 all-reduce.2
where the time goes:
time: 522 us; the launch traced here: 521 us
  waiting for transfers between devices  443 us (85%)
  starting transfers between devices  42.1 us (8%)
  matrix products  18 us (3%)
  between operations  14.6 us (3%)
    unnamed x3, waiting for transfers between devices  296 us
    all_gather x1, waiting for transfers between devices, shards(): lax.all_gather(coeffs, ('row', 'col'), axis=0, tiled=True)  126 us
    ppermute x8, starting transfers between devices, with_halo(): lax.ppermute(lax.slice_in_dim(block, block.shape[dim] - width, None, axis...  29 us
    ppermute x8, waiting for transfers between devices, with_halo(): lax.ppermute(lax.slice_in_dim(block, 0, width, axis=dim), axis, backward)  19.4 us
    ppermute x8, starting transfers between devices, with_halo(): lax.ppermute(lax.slice_in_dim(block, 0, width, axis=dim), axis, backward)  13 us
  transfers between devices with their start and end apart: 18, of which 10 were waited for; matrix products, arithmetic and copies ran while one was open for 1% of the time, Pallas kernels for 0%

commit v1 on v0

--- a/solution.py
+++ b/solution.py
@@ -1,9 +1,15 @@
 import jax
 import jax.numpy as jnp
 from jax import lax
-from jax.sharding import PartitionSpec as P
+from jax.sharding import Mesh, PartitionSpec as P
+import numpy as np
 
 prior_weight = 0.1
+
+
+ROW_AXES = ("z", "x")
+COL_AXES = ("y", "core")
+ALL_AXES = ROW_AXES + COL_AXES
 
 
 def with_halo(block, sides, width):
@@ -20,7 +26,7 @@
 
 
 def extend_tile(values):
-    return with_halo(values, (("row", 0), ("col", 1)), 1)
+    return with_halo(values, ((ROW_AXES, 0), (COL_AXES, 1)), 1)
 
 
 def conv_fwd(values, weights, extend):
@@ -75,9 +81,13 @@
     batch_size = coeffs.shape[1]
     flat_basis = basis.reshape(tile_rows * tile_cols, mode_count)
     basis_part = flat_basis
+    gathered = coeffs
+    for position, axis in enumerate(ALL_AXES):
+        gathered = lax.all_gather(gathered, axis, axis=position, tiled=False)
+    gathered = gathered.reshape(-1, batch_size)
     logperm = jnp.dot(
         basis_part,
-        lax.all_gather(coeffs, ("row", "col"), axis=0, tiled=True),
+        gathered,
         precision=lax.Precision.HIGHEST,
         preferred_element_type=jnp.float32,
     )
@@ -87,30 +97,31 @@
     )
     grad_flat = grad_field.reshape(tile_rows * tile_cols, batch_size)
     basis_part = flat_basis
-    summed = lax.psum_scatter(
-        lax.dot_general(
-            basis_part,
-            grad_flat,
-            (((0,), (0,)), ((), ())),
-            precision=lax.Precision.HIGHEST,
-            preferred_element_type=jnp.float32,
-        ),
-        ("row", "col"),
-        scatter_dimension=0,
-        tiled=True,
+    projected = lax.dot_general(
+        basis_part,
+        grad_flat,
+        (((0,), (0,)), ((), ())),
+        precision=lax.Precision.HIGHEST,
+        preferred_element_type=jnp.float32,
     )
+    sizes = tuple(lax.axis_size(axis) for axis in ALL_AXES)
+    summed = projected.reshape(sizes + (coeffs.shape[0], batch_size))
+    for position in reversed(range(len(ALL_AXES))):
+        summed = lax.psum_scatter(summed, ALL_AXES[position], scatter_dimension=position, tiled=False)
     grad_coeffs = summed + prior_weight * coeffs
     return (pressure, grad_coeffs)
 
 
 def solution(mesh):
+    row_size, col_size = mesh.devices.shape
+    fine = Mesh(mesh.devices.reshape(row_size // 8, 8, col_size // 2, 2), ALL_AXES)
     return jax.shard_map(
         shards,
-        mesh=mesh,
+        mesh=fine,
         in_specs=(
-            P(("row", "col"), None),
-            P("row", "col", None),
-            P("row", "col", None),
+            P(ALL_AXES, None),
+            P(ROW_AXES, COL_AXES, None),
+            P(ROW_AXES, COL_AXES, None),
             P(),
             P(),
             P(),
@@ -119,6 +130,6 @@
             P(),
             P(),
         ),
-        out_specs=(P("row", "col", None), P(("row", "col"), None)),
+        out_specs=(P(ROW_AXES, COL_AXES, None), P(ALL_AXES, None)),
         check_vma=False,
     )

time: 522 us -> 459 us (0.88); the launches traced: 521 us -> 451 us
  waiting for transfers between devices: 443 us -> 304 us
  blocking collectives: 0 us -> 57.6 us
  local copies, waits for them, and re-layouts: 1.66 us -> 14.1 us
    unnamed x3 -> x8, waiting for transfers between devices: 296 us -> 212 us
    all_gather x1 -> x2, waiting for transfers between devices: 126 us -> 70.8 us  [shards(): gathered = lax.all_gather(gathered, axis, axis=position, tiled=False)]
    all_gather x0 -> x2, blocking collectives: none -> 41.6 us  [shards(): gathered = lax.all_gather(gathered, axis, axis=position, tiled=False)]
    unnamed x0 -> x1, blocking collectives: none -> 15.9 us
    reduce_scatter x1 -> x3, local copies, waits for them, and re-layouts: 0.05 us -> 6.56 us  [shards(): lax.psum_scatter(summed, ALL_AXES[position], scatter_dimension=position,...]
  transfers between devices with their start and end apart: 18 -> 21, of which waited for: 10 -> 13; matrix products, arithmetic and copies ran while one was open for 1% -> 2% of each run, Pallas kernels for 0% -> 0%
where the time goes in v1:
time: 459 us; the launch traced here: 451 us
  waiting for transfers between devices  304 us (66%)
  blocking collectives  57.6 us (13%)
  starting transfers between devices  41.6 us (9%)
  matrix products  16.8 us (4%)
  between operations  14.3 us (3%)
  local copies, waits for them, and re-layouts  14.1 us (3%)
    unnamed x8, waiting for transfers between devices  212 us
    all_gather x2, waiting for transfers between devices, shards(): gathered = lax.all_gather(gathered, axis, axis=position, tiled=False)  70.8 us
    all_gather x2, blocking collectives, shards(): gathered = lax.all_gather(gathered, axis, axis=position, tiled=False)  41.6 us
    ppermute x8, starting transfers between devices, with_halo(): lax.ppermute(lax.slice_in_dim(block, block.shape[dim] - width, None, axis...  28.3 us
    ppermute x8, waiting for transfers between devices, with_halo(): lax.ppermute(lax.slice_in_dim(block, 0, width, axis=dim), axis, backward)  19.4 us
    unnamed x1, blocking collectives  15.9 us
    ppermute x8, starting transfers between devices, with_halo(): lax.ppermute(lax.slice_in_dim(block, 0, width, axis=dim), axis, backward)  13 us
  transfers between devices with their start and end apart: 21, of which 13 were waited for; matrix products, arithmetic and copies ran while one was open for 2% of the time, Pallas kernels for 0%

profile of v1, /device:TPU:1, one launch (start us, length us, event | category | flops | bytes accessed | tf_op | source)
XLA Modules:
  0.0 450.8 jit_solution(15876714315967454040)
XLA Ops:
  7.2 17.4 %all-gather = f32[32,128]{1,0:T(8,128)S(1)} all-gather(f32[8,128]{1,0:T(8,128)} %param.10), channel_id=2, replica_groups=mesh['z'=4,'x'=8,'y'=8,'core'=2] {'z'}, dimensions={0}, use_global_device_ids=true | all-gather | bytes 20480 | tf_op jit(solution)/shard_map/all_gather | solution.py:86
  24.7 24.2 %all-gather.1 = f32[4,64,128]{2,1,0:T(8,128)} all-gather(f32[4,8,128]{2,1,0:T(8,128)S(1)} %bitcast.278), channel_id=3, replica_groups=mesh['z'=4,'x'=8,'y'=8,'core'=2] {'x'}, dimensions={1}, use_global_device_ids=true | all-gather | bytes 147456 | tf_op jit(solution)/shard_map/all_gather | solution.py:86
  48.9 44.5 %all-gather.7.cloned.1.call-done = f32[4,8,64,128]{3,2,1,0:T(8,128)} async-done(((f32[4,8,8,128]{3,2,1,0:T(8,128)}), f32[4,8,64,128]{3,2,1,0:T(8,128)}) %all-gather.7.cloned.1.call-update) | async-done | bytes 1048592 | tf_op jit(solution)/shard_map/all_gather | solution.py:86
  93.6 26.3 %all-gather.9.cloned.1.call-done = f32[4,8,8,16,128]{4,3,2,1,0:T(8,128)} async-done(((f32[4,8,8,8,128]{4,3,2,1,0:T(8,128)}), f32[4,8,8,16,128]{4,3,2,1,0:T(8,128)}) %all-gather.9.cloned.1.call-update) | async-done | bytes 2097168 | tf_op jit(solution)/shard_map/all_gather | solution.py:86
  119.8 3.0 fusion.174
  123.1 2.1 collective-permute-start
  126.9 3.3 collective-permute-done.1
  130.2 4.7 %collective-permute-start.2 = (bf16[10,1,128,32]{2,3,1,0:T(8,128)(2,1)S(1)}, bf16[10,1,128,32]{2,3,1,0:T(8,128)(2,1)S(1)}, u32[]{:S(2)}, u32[]{:S(2)}) collective-permute-start(bf16[10,1,128,32]{2,3,1,0:T(8,128)(2,1)S(1)} %get-tuple-element.12), channel_id=1, source_target_pairs={{0,1},{1,2},{2,3},{3,4},{4,5},{5,6},{6,7},{7,8},{8,9},{9,10},{10,1... | collective-permute-start | bytes 245768 | tf_op jit(solution)/shard_map/ppermute | solution.py:20
  134.9 1.9 collective-permute-start.3
  137.5 3.2 collective-permute-done.3
  143.3 3.1 collective-permute-start.4
  148.0 3.4 collective-permute-done.5
  151.4 3.6 collective-permute-start.6
  155.0 1.9 collective-permute-start.7
  157.6 3.2 collective-permute-done.7
  165.2 4.8 %collective-permute-start.8 = (bf16[1,8,128,32]{2,3,1,0:T(8,128)(2,1)S(1)}, bf16[1,8,128,32]{2,3,1,0:T(8,128)(2,1)S(1)}, u32[]{:S(2)}, u32[]{:S(2)}) collective-permute-start(bf16[1,8,128,32]{2,3,1,0:T(8,128)(2,1)S(1)} %get-tuple-element.16), channel_id=1, source_target_pairs={{0,16},{16,32},{32,48},{48,64},{64,80},{80,96},{96,112},{112,128},... | collective-permute-start | bytes 196616 | tf_op jit(solution)/shard_map/ppermute | solution.py:20
  171.4 2.7 collective-permute-start.11
  174.1 1.9 collective-permute-start.10
  176.6 3.3 collective-permute-done.10
  183.2 4.6 %collective-permute-start.12 = (bf16[1,8,128,32]{2,3,1,0:T(8,128)(2,1)S(1)}, bf16[1,8,128,32]{2,3,1,0:T(8,128)(2,1)S(1)}, u32[]{:S(2)}, u32[]{:S(2)}) collective-permute-start(bf16[1,8,128,32]{2,3,1,0:T(8,128)(2,1)S(1)} %get-tuple-element.14), channel_id=1, source_target_pairs={{0,16},{16,32},{32,48},{48,64},{64,80},{80,96},{96,112},{112,128},... | collective-permute-start | bytes 196616 | tf_op jit(solution)/shard_map/ppermute | solution.py:20
  189.1 2.7 collective-permute-start.15
  191.8 2.1 collective-permute-start.14
  194.5 3.1 collective-permute-done.14
  199.5 1.8 convolution_bitcast_fusion
  201.4 1.8 copy.104
  204.6 55.4 %all-reduce.8.cloned.1.call-done = f32[4,8,8,2,8,128]{5,4,3,2,1,0:T(8,128)} async-done(((f32[4,8,8,2,8,128]{5,4,3,2,1,0:T(8,128)}), f32[4,8,8,2,8,128]{5,4,3,2,1,0:T(8,128)}) %all-reduce.8.cloned.1.call-update) | async-done | bytes 2097168
  260.0 3.0 dynamic-slice_bitcast_fusion
  264.3 75.2 %all-reduce.10.cloned.1.call-done = f32[4,8,8,8,128]{4,3,2,1,0:T(8,128)} async-done(((f32[4,8,8,8,128]{4,3,2,1,0:T(8,128)}), f32[4,8,8,8,128]{4,3,2,1,0:T(8,128)}) %all-reduce.10.cloned.1.call-update) | async-done | bytes 1048592
  339.5 2.2 dynamic-slice_bitcast_fusion.1
  344.3 81.5 %all-reduce.12.cloned.1.call-done = f32[4,8,8,128]{3,2,1,0:T(8,128)} async-done(((f32[4,8,8,128]{3,2,1,0:T(8,128)}), f32[4,8,8,128]{3,2,1,0:T(8,128)}) %all-reduce.12.cloned.1.call-update) | async-done | bytes 131088
  425.8 1.4 dynamic-slice_bitcast_fusion.2
  427.1 15.9 %all-reduce.3 = f32[4,8,128]{2,1,0:T(8,128)S(1)} all-reduce(f32[4,8,128]{2,1,0:T(8,128)S(1)} %dynamic-slice_bitcast_fusion.2), channel_id=9, replica_groups=mesh['z'=4,'x'=8,'y'=8,'core'=2] {'z'}, use_global_device_ids=true, to_apply=%region_5.0.clone | all-reduce | flops 4096 | bytes 32768
  (100 shorter events, 27.2 us)
Async XLA Ops:
  7.2 112.7 %copy-start = (f32[8,8,4096]{2,1,0:T(8,128)S(1)}, f32[8,8,4096]{2,1,0:T(8,128)}, u32[]{:S(2)}) copy-start(f32[8,8,4096]{2,1,0:T(8,128)} %param.11) | copy-start | bytes 3145732
  7.2 86.3 %all-gather.7.cloned.1.call-start = ((), (), s32[]{:S(2)}) async-start(), calls=%async_computation | async-start | bytes 1179648 | tf_op jit(solution)/shard_map/all_gather | solution.py:86
  48.9 70.9 %all-gather.9.cloned.1.call-start = ((), (), s32[]{:S(2)}) async-start(), calls=%async_computation.1 | async-start | bytes 3145728 | tf_op jit(solution)/shard_map/all_gather | solution.py:86
  93.5 166.5 %all-reduce.8.cloned.1.call-start = ((), (), s32[]{:S(2)}) async-start(), calls=%async_computation.2 | async-start | bytes 4194304
  119.8 3.0 copy-start.6
  119.8 3.0 copy-start.7
  119.8 6.7 %copy-start.2 = (bf16[3,3,32,32]{3,2,1,0:T(8,128)(2,1)S(1)}, bf16[3,3,32,32]{3,2,1,0:T(8,128)(2,1)}, u32[]{:S(2)}) copy-start(bf16[3,3,32,32]{3,2,1,0:T(8,128)(2,1)} %param.15) | copy-start | bytes 55300
  123.1 3.8 collective-permute-start
  125.2 5.0 %collective-permute-start.1 = (bf16[1,8,128,32]{2,3,1,0:T(8,128)(2,1)S(1)}, bf16[1,8,128,32]{2,3,1,0:T(8,128)(2,1)S(1)}, u32[]{:S(2)}, u32[]{:S(2)}) collective-permute-start(bf16[1,8,128,32]{2,3,1,0:T(8,128)(2,1)S(1)} %get-tuple-element.21), channel_id=1, source_target_pairs={{16,0},{32,16},{48,32},{64,48},{80,64},{96,80},{112,96},{128,112},... | collective-permute-start | bytes 196616 | tf_op jit(solution)/shard_map/ppermute | solution.py:23
  130.2 7.3 %collective-permute-start.2 = (bf16[10,1,128,32]{2,3,1,0:T(8,128)(2,1)S(1)}, bf16[10,1,128,32]{2,3,1,0:T(8,128)(2,1)S(1)}, u32[]{:S(2)}, u32[]{:S(2)}) collective-permute-start(bf16[10,1,128,32]{2,3,1,0:T(8,128)(2,1)S(1)} %get-tuple-element.12), channel_id=1, source_target_pairs={{0,1},{1,2},{2,3},{3,4},{4,5},{5,6},{6,7},{7,8},{8,9},{9,10},{10,1... | collective-permute-start | bytes 245768 | tf_op jit(solution)/shard_map/ppermute | solution.py:20
  134.9 5.8 %collective-permute-start.3 = (bf16[10,1,128,32]{2,3,1,0:T(8,128)(2,1)S(1)}, bf16[10,1,128,32]{2,3,1,0:T(8,128)(2,1)S(1)}, u32[]{:S(2)}, u32[]{:S(2)}) collective-permute-start(bf16[10,1,128,32]{2,3,1,0:T(8,128)(2,1)S(1)} %get-tuple-element.13), channel_id=1, source_target_pairs={{1,0},{2,1},{3,2},{4,3},{5,4},{6,5},{7,6},{8,7},{9,8},{10,9},{11,1... | collective-permute-start | bytes 245768 | tf_op jit(solution)/shard_map/ppermute | solution.py:23
  142.1 0.7 copy-start.10
  142.8 4.9 %copy-start.1 = (bf16[3,3,32,32]{3,2,1,0:T(8,128)(2,1)S(1)}, bf16[3,3,32,32]{3,2,1,0:T(8,128)(2,1)}, u32[]{:S(2)}) copy-start(bf16[3,3,32,32]{3,2,1,0:T(8,128)(2,1)} %param.17) | copy-start | bytes 55300
  143.3 4.7 %collective-permute-start.4 = (bf16[1,8,128,32]{2,3,1,0:T(8,128)(2,1)S(1)}, bf16[1,8,128,32]{2,3,1,0:T(8,128)(2,1)S(1)}, u32[]{:S(2)}, u32[]{:S(2)}) collective-permute-start(bf16[1,8,128,32]{2,3,1,0:T(8,128)(2,1)S(1)} %get-tuple-element.18), channel_id=1, source_target_pairs={{0,16},{16,32},{32,48},{48,64},{64,80},{80,96},{96,112},{112,128},... | collective-permute-start | bytes 196616 | tf_op jit(solution)/shard_map/ppermute | solution.py:20
  146.4 5.0 %collective-permute-start.5 = (bf16[1,8,128,32]{2,3,1,0:T(8,128)(2,1)S(1)}, bf16[1,8,128,32]{2,3,1,0:T(8,128)(2,1)S(1)}, u32[]{:S(2)}, u32[]{:S(2)}) collective-permute-start(bf16[1,8,128,32]{2,3,1,0:T(8,128)(2,1)S(1)} %get-tuple-element.19), channel_id=1, source_target_pairs={{16,0},{32,16},{48,32},{64,48},{80,64},{96,80},{112,96},{128,112},... | collective-permute-start | bytes 196616 | tf_op jit(solution)/shard_map/ppermute | solution.py:23
  151.4 6.2 %collective-permute-start.6 = (bf16[10,1,128,32]{2,3,1,0:T(8,128)(2,1)S(1)}, bf16[10,1,128,32]{2,3,1,0:T(8,128)(2,1)S(1)}, u32[]{:S(2)}, u32[]{:S(2)}) collective-permute-start(bf16[10,1,128,32]{2,3,1,0:T(8,128)(2,1)S(1)} %get-tuple-element.8), channel_id=1, source_target_pairs={{0,1},{1,2},{2,3},{3,4},{4,5},{5,6},{6,7},{7,8},{8,9},{9,10},{10,1... | collective-permute-start | bytes 245768 | tf_op jit(solution)/shard_map/ppermute | solution.py:20
  155.0 5.8 %collective-permute-start.7 = (bf16[10,1,128,32]{2,3,1,0:T(8,128)(2,1)S(1)}, bf16[10,1,128,32]{2,3,1,0:T(8,128)(2,1)S(1)}, u32[]{:S(2)}, u32[]{:S(2)}) collective-permute-start(bf16[10,1,128,32]{2,3,1,0:T(8,128)(2,1)S(1)} %get-tuple-element.9), channel_id=1, source_target_pairs={{1,0},{2,1},{3,2},{4,3},{5,4},{6,5},{7,6},{8,7},{9,8},{10,9},{11,1... | collective-permute-start | bytes 245768 | tf_op jit(solution)/shard_map/ppermute | solution.py:23
  162.2 0.7 copy-start.8
  162.2 0.7 copy-start.9
  162.9 0.8 copy-start.4
  163.4 6.9 %copy-start.3 = (f32[8,8,128]{2,1,0:T(8,128)}, f32[8,8,128]{2,1,0:T(8,128)S(1)}, u32[]{:S(2)}) copy-start(f32[8,8,128]{2,1,0:T(8,128)S(1)} %get-tuple-element.22) | copy-start | bytes 98308
  163.9 6.4 %collective-permute-start.9 = (bf16[1,8,128,32]{2,3,1,0:T(8,128)(2,1)S(1)}, bf16[1,8,128,32]{2,3,1,0:T(8,128)(2,1)S(1)}, u32[]{:S(2)}, u32[]{:S(2)}) collective-permute-start(bf16[1,8,128,32]{2,3,1,0:T(8,128)(2,1)S(1)} %get-tuple-element.17), channel_id=1, source_target_pairs={{16,0},{32,16},{48,32},{64,48},{80,64},{96,80},{112,96},{128,112},... | collective-permute-start | bytes 196616 | tf_op jit(solution)/shard_map/ppermute | solution.py:23
  165.2 6.2 %collective-permute-start.8 = (bf16[1,8,128,32]{2,3,1,0:T(8,128)(2,1)S(1)}, bf16[1,8,128,32]{2,3,1,0:T(8,128)(2,1)S(1)}, u32[]{:S(2)}, u32[]{:S(2)}) collective-permute-start(bf16[1,8,128,32]{2,3,1,0:T(8,128)(2,1)S(1)} %get-tuple-element.16), channel_id=1, source_target_pairs={{0,16},{16,32},{32,48},{48,64},{64,80},{80,96},{96,112},{112,128},... | collective-permute-start | bytes 196616 | tf_op jit(solution)/shard_map/ppermute | solution.py:20
  171.4 9.0 %collective-permute-start.11 = (bf16[10,1,128,32]{2,3,1,0:T(8,128)(2,1)S(1)}, bf16[10,1,128,32]{2,3,1,0:T(8,128)(2,1)S(1)}, u32[]{:S(2)}, u32[]{:S(2)}) collective-permute-start(bf16[10,1,128,32]{2,3,1,0:T(8,128)(2,1)S(1)} %get-tuple-element.5), channel_id=1, source_target_pairs={{0,1},{1,2},{2,3},{3,4},{4,5},{5,6},{6,7},{7,8},{8,9},{9,10},{10,1... | collective-permute-start | bytes 245768 | tf_op jit(solution)/shard_map/ppermute | solution.py:20
  174.1 5.8 %collective-permute-start.10 = (bf16[10,1,128,32]{2,3,1,0:T(8,128)(2,1)S(1)}, bf16[10,1,128,32]{2,3,1,0:T(8,128)(2,1)S(1)}, u32[]{:S(2)}, u32[]{:S(2)}) collective-permute-start(bf16[10,1,128,32]{2,3,1,0:T(8,128)(2,1)S(1)} %get-tuple-element.4), channel_id=1, source_target_pairs={{1,0},{2,1},{3,2},{4,3},{5,4},{6,5},{7,6},{8,7},{9,8},{10,9},{11,1... | collective-permute-start | bytes 245768 | tf_op jit(solution)/shard_map/ppermute | solution.py:23
  181.9 6.2 %collective-permute-start.13 = (bf16[1,8,128,32]{2,3,1,0:T(8,128)(2,1)S(1)}, bf16[1,8,128,32]{2,3,1,0:T(8,128)(2,1)S(1)}, u32[]{:S(2)}, u32[]{:S(2)}) collective-permute-start(bf16[1,8,128,32]{2,3,1,0:T(8,128)(2,1)S(1)} %get-tuple-element.15), channel_id=1, source_target_pairs={{16,0},{32,16},{48,32},{64,48},{80,64},{96,80},{112,96},{128,112},... | collective-permute-start | bytes 196616 | tf_op jit(solution)/shard_map/ppermute | solution.py:23
  183.2 5.9 %collective-permute-start.12 = (bf16[1,8,128,32]{2,3,1,0:T(8,128)(2,1)S(1)}, bf16[1,8,128,32]{2,3,1,0:T(8,128)(2,1)S(1)}, u32[]{:S(2)}, u32[]{:S(2)}) collective-permute-start(bf16[1,8,128,32]{2,3,1,0:T(8,128)(2,1)S(1)} %get-tuple-element.14), channel_id=1, source_target_pairs={{0,16},{16,32},{32,48},{48,64},{64,80},{80,96},{96,112},{112,128},... | collective-permute-start | bytes 196616 | tf_op jit(solution)/shard_map/ppermute | solution.py:20
  189.1 9.0 %collective-permute-start.15 = (bf16[10,1,128,32]{2,3,1,0:T(8,128)(2,1)S(1)}, bf16[10,1,128,32]{2,3,1,0:T(8,128)(2,1)S(1)}, u32[]{:S(2)}, u32[]{:S(2)}) collective-permute-start(bf16[10,1,128,32]{2,3,1,0:T(8,128)(2,1)S(1)} %get-tuple-element.3), channel_id=1, source_target_pairs={{0,1},{1,2},{2,3},{3,4},{4,5},{5,6},{6,7},{7,8},{8,9},{9,10},{10,1... | collective-permute-start | bytes 245768 | tf_op jit(solution)/shard_map/ppermute | solution.py:20
  191.8 5.8 %collective-permute-start.14 = (bf16[10,1,128,32]{2,3,1,0:T(8,128)(2,1)S(1)}, bf16[10,1,128,32]{2,3,1,0:T(8,128)(2,1)S(1)}, u32[]{:S(2)}, u32[]{:S(2)}) collective-permute-start(bf16[10,1,128,32]{2,3,1,0:T(8,128)(2,1)S(1)} %get-tuple-element.2), channel_id=1, source_target_pairs={{1,0},{2,1},{3,2},{4,3},{5,4},{6,5},{7,6},{8,7},{9,8},{10,9},{11,1... | collective-permute-start | bytes 245768 | tf_op jit(solution)/shard_map/ppermute | solution.py:23
  203.2 136.2 %all-reduce.10.cloned.1.call-start = ((), (), s32[]{:S(2)}) async-start(), calls=%async_computation.3 | async-start | bytes 2097152
  260.0 183.1 %copy-start.5 = (f32[8,128]{1,0:T(8,128)S(1)}, f32[8,128]{1,0:T(8,128)}, u32[]{:S(2)}) copy-start(f32[8,128]{1,0:T(8,128)} %param.10) | copy-start | bytes 12292
  263.0 162.8 %all-reduce.12.cloned.1.call-start = ((), (), s32[]{:S(2)}) async-start(), calls=%async_computation.4 | async-start | bytes 262144
Sparse Core Ops, SparseCore 0:
  49.0 44.4 all-gather.6
  95.6 24.2 all-gather.8
  203.4 56.5 all-reduce.7
  263.1 76.3 all-reduce.9
  342.2 83.4 all-reduce.11

commit v2 on v1

--- a/solution.py
+++ b/solution.py
@@ -76,18 +76,70 @@
     return (pressure, grad_field)
 
 
+def bit_order(sizes):
+    groups = []
+    low = 0
+    for size in reversed(sizes):
+        width = size.bit_length() - 1
+        groups.append(list(range(low, low + width)))
+        low += width
+    core_bits, rest = groups[0], groups[1:]
+    order = list(core_bits)
+    depth = 0
+    while any(depth < len(group) for group in rest):
+        for group in rest:
+            if depth < len(group):
+                order.append(group[depth])
+        depth += 1
+    return order, low
+
+
+def exchange(values, bit, count):
+    pairs = [(i, i ^ (1 << bit)) for i in range(count)]
+    return lax.ppermute(values, ALL_AXES, pairs)
+
+
+def scatter_sum(projected, mode_block, sizes):
+    order, nbits = bit_order(sizes)
+    count = 1 << nbits
+    me = lax.axis_index(ALL_AXES)
+    data = projected.reshape((2,) * nbits + (mode_block, projected.shape[1]))
+    present = list(range(nbits - 1, -1, -1))
+    for bit in order:
+        dim = present.index(bit)
+        mine = (me >> bit) & 1
+        keep = lax.dynamic_index_in_dim(data, mine, axis=dim, keepdims=False)
+        send = lax.dynamic_index_in_dim(data, 1 - mine, axis=dim, keepdims=False)
+        data = keep + exchange(send, bit, count)
+        present.pop(dim)
+    return data
+
+
+def gather_all(block, sizes):
+    order, nbits = bit_order(sizes)
+    count = 1 << nbits
+    me = lax.axis_index(ALL_AXES)
+    data = block
+    present = []
+    for bit in reversed(order):
+        mine = (me >> bit) & 1
+        other = exchange(data, bit, count)
+        low = jnp.where(mine == 0, data, other)
+        high = jnp.where(mine == 0, other, data)
+        dim = sum(1 for b in present if b > bit)
+        data = jnp.stack([low, high], axis=dim)
+        present.insert(dim, bit)
+    return data.reshape(count * block.shape[0], block.shape[1])
+
+
 def shards(coeffs, basis, observed, lift_w, lift_b, w_one, b_one, w_two, b_two, read_w):
     tile_rows, tile_cols, mode_count = basis.shape
     batch_size = coeffs.shape[1]
+    sizes = tuple(lax.axis_size(axis) for axis in ALL_AXES)
     flat_basis = basis.reshape(tile_rows * tile_cols, mode_count)
-    basis_part = flat_basis
-    gathered = coeffs
-    for position, axis in enumerate(ALL_AXES):
-        gathered = lax.all_gather(gathered, axis, axis=position, tiled=False)
-    gathered = gathered.reshape(-1, batch_size)
     logperm = jnp.dot(
-        basis_part,
-        gathered,
+        flat_basis,
+        gather_all(coeffs, sizes),
         precision=lax.Precision.HIGHEST,
         preferred_element_type=jnp.float32,
     )
@@ -96,18 +148,14 @@
         logperm, observed, lift_w, lift_b, w_one, b_one, w_two, b_two, read_w, extend_tile
     )
     grad_flat = grad_field.reshape(tile_rows * tile_cols, batch_size)
-    basis_part = flat_basis
     projected = lax.dot_general(
-        basis_part,
+        flat_basis,
         grad_flat,
         (((0,), (0,)), ((), ())),
         precision=lax.Precision.HIGHEST,
         preferred_element_type=jnp.float32,
     )
-    sizes = tuple(lax.axis_size(axis) for axis in ALL_AXES)
-    summed = projected.reshape(sizes + (coeffs.shape[0], batch_size))
-    for position in reversed(range(len(ALL_AXES))):
-        summed = lax.psum_scatter(summed, ALL_AXES[position], scatter_dimension=position, tiled=False)
+    summed = scatter_sum(projected, coeffs.shape[0], sizes)
     grad_coeffs = summed + prior_weight * coeffs
     return (pressure, grad_coeffs)
 

time: 459 us -> 270 us (0.59)
  the two profiles are of different devices: /device:TPU:1 before, /device:TPU:24 now
where the time goes in v2:
time: 270 us; the launch traced here: 269 us
  starting transfers between devices  131 us (49%)
  waiting for transfers between devices  108 us (40%)
  matrix products  16.7 us (6%)
  other arithmetic  6.65 us (2%)
  local copies, waits for them, and re-layouts  4.85 us (2%)
    ppermute x18, waiting for transfers between devices, exchange(): return lax.ppermute(values, ALL_AXES, pairs)  89.7 us
    ppermute x18, starting transfers between devices, exchange(): return lax.ppermute(values, ALL_AXES, pairs)  83.6 us
    ppermute x8, starting transfers between devices, with_halo(): lax.ppermute(lax.slice_in_dim(block, block.shape[dim] - width, None, axis...  33.1 us
    ppermute x8, starting transfers between devices, with_halo(): lax.ppermute(lax.slice_in_dim(block, 0, width, axis=dim), axis, backward)  14.8 us
    ppermute x8, waiting for transfers between devices, with_halo(): lax.ppermute(lax.slice_in_dim(block, 0, width, axis=dim), axis, backward)  14.2 us
    dot_general x18, matrix products, conv_fwd(): jnp.einsum('xybi,io->xybo', window, weights[shift_x, shift_y], preferred_...  6.47 us
    dot_general x18, matrix products, conv_back(): jnp.einsum('xybo,io->xybi', window, weights[shift_x, shift_y], preferred_...  5.5 us
  transfers between devices with their start and end apart: 34, of which 28 were waited for; matrix products, arithmetic and copies ran while one was open for 2% of the time, Pallas kernels for 0%

profile of v2, /device:TPU:24, one launch (start us, length us, event | category | flops | bytes accessed | tf_op | source)
XLA Modules:
  0.0 268.7 jit_solution(5214314804322613010)
XLA Ops:
  0.6 4.4 %collective-permute-start = (f32[8,128]{1,0:T(8,128)}, f32[8,128]{1,0:T(8,128)S(1)}, u32[]{:S(2)}, u32[]{:S(2)}) collective-permute-start(f32[8,128]{1,0:T(8,128)} %param.10), channel_id=1, source_target_pairs={{0,64},{1,65},{2,66},{3,67},{4,68},{5,69},{6,70},{7,71},{8,72},{9,... | collective-permute-start | bytes 12296 | tf_op jit(solution)/shard_map/ppermute | solution.py:99
  7.5 5.0 %collective-permute-start.1 = (f32[2,8,128]{2,1,0:T(8,128)S(1)}, f32[2,8,128]{2,1,0:T(8,128)S(1)}, u32[]{:S(2)}, u32[]{:S(2)}) collective-permute-start(f32[2,8,128]{2,1,0:T(8,128)S(1)} %pad_maximum_fusion.32), channel_id=1, source_target_pairs={{0,8},{1,9},{2,10},{3,11},{4,12},{5,13},{6,14},{7,15},{8,0},{9,1},... | collective-permute-start | bytes 24584 | tf_op jit(solution)/shard_map/ppermute | solution.py:99
  12.6 4.4 %collective-permute-done.1 = f32[2,8,128]{2,1,0:T(8,128)S(1)} collective-permute-done((f32[2,8,128]{2,1,0:T(8,128)S(1)}, f32[2,8,128]{2,1,0:T(8,128)S(1)}, u32[]{:S(2)}, u32[]{:S(2)}) %collective-permute-start.1) | collective-permute-done | bytes 8224 | tf_op jit(solution)/shard_map/ppermute | solution.py:99
  17.0 10.6 %collective-permute-start.2 = (f32[2,2,8,128]{3,2,1,0:T(8,128)S(1)}, f32[2,2,8,128]{3,2,1,0:T(8,128)S(1)}, u32[]{:S(2)}, u32[]{:S(2)}) collective-permute-start(f32[2,2,8,128]{3,2,1,0:T(8,128)S(1)} %pad_maximum_fusion.31), channel_id=1, source_target_pairs={{0,256},{1,257},{2,258},{3,259},{4,260},{5,261},{6,262},{7,263},{8... | collective-permute-start | bytes 49160 | tf_op jit(solution)/shard_map/ppermute | solution.py:99
  29.3 4.9 %collective-permute-start.3 = (f32[2,2,2,8,128]{4,3,2,1,0:T(8,128)S(1)}, f32[2,2,2,8,128]{4,3,2,1,0:T(8,128)S(1)}, u32[]{:S(2)}, u32[]{:S(2)}) collective-permute-start(f32[2,2,2,8,128]{4,3,2,1,0:T(8,128)S(1)} %pad_maximum_fusion.30), channel_id=1, source_target_pairs={{0,32},{1,33},{2,34},{3,35},{4,36},{5,37},{6,38},{7,39},{8,40},{9,... | collective-permute-start | bytes 98312 | tf_op jit(solution)/shard_map/ppermute | solution.py:99
  38.9 5.4 %collective-permute-done.4 = f32[2,2,2,2,8,128]{5,4,3,2,1,0:T(8,128)S(1)} collective-permute-done((f32[2,2,2,2,8,128]{5,4,3,2,1,0:T(8,128)S(1)}, f32[2,2,2,2,8,128]{5,4,3,2,1,0:T(8,128)S(1)}, u32[]{:S(2)}, u32[]{:S(2)}) %collective-permute-start.4) | collective-permute-done | bytes 65568 | tf_op jit(solution)/shard_map/ppermute | solution.py:99
  44.3 4.4 %collective-permute-start.5 = (f32[2,2,2,2,2,8,128]{6,5,4,3,2,1,0:T(8,128)S(1)}, f32[2,2,2,2,2,8,128]{6,5,4,3,2,1,0:T(8,128)S(1)}, u32[]{:S(2)}, u32[]{:S(2)}) collective-permute-start(f32[2,2,2,2,2,8,128]{6,5,4,3,2,1,0:T(8,128)S(1)} %pad_maximum_fusion.16), channel_id=1, source_target_pairs={{0,128},{1,129},{2,130},{3,131},{4,132},{5,133},{6,134},{7,135},{8... | collective-permute-start | bytes 393224 | tf_op jit(solution)/shard_map/ppermute | solution.py:99
  48.8 4.7 %collective-permute-done.5 = f32[2,2,2,2,2,8,128]{6,5,4,3,2,1,0:T(8,128)S(1)} collective-permute-done((f32[2,2,2,2,2,8,128]{6,5,4,3,2,1,0:T(8,128)S(1)}, f32[2,2,2,2,2,8,128]{6,5,4,3,2,1,0:T(8,128)S(1)}, u32[]{:S(2)}, u32[]{:S(2)}) %collective-permute-start.5) | collective-permute-done | bytes 131104 | tf_op jit(solution)/shard_map/ppermute | solution.py:99
  53.5 3.4 %collective-permute-start.6 = (f32[2,2,2,2,2,2,8,128]{7,6,5,4,3,2,1,0:T(8,128)S(1)}, f32[2,2,2,2,2,2,8,128]{7,6,5,4,3,2,1,0:T(8,128)S(1)}, u32[]{:S(2)}, u32[]{:S(2)}) collective-permute-start(f32[2,2,2,2,2,2,8,128]{7,6,5,4,3,2,1,0:T(8,128)S(1)} %pad_maximum_fusion.15), channel_id=1, source_target_pairs={{0,16},{1,17},{2,18},{3,19},{4,20},{5,21},{6,22},{7,23},{8,24},{9,... | collective-permute-start | bytes 786440 | tf_op jit(solution)/shard_map/ppermute | solution.py:99
  56.9 4.9 %collective-permute-done.6 = f32[2,2,2,2,2,2,8,128]{7,6,5,4,3,2,1,0:T(8,128)S(1)} collective-permute-done((f32[2,2,2,2,2,2,8,128]{7,6,5,4,3,2,1,0:T(8,128)S(1)}, f32[2,2,2,2,2,2,8,128]{7,6,5,4,3,2,1,0:T(8,128)S(1)}, u32[]{:S(2)}, u32[]{:S(2)}) %collective-permute-start.6) | collective-permute-done | bytes 262176 | tf_op jit(solution)/shard_map/ppermute | solution.py:99
  63.8 9.1 %collective-permute-done.7 = f32[2,2,2,2,2,2,2,8,128]{8,7,6,5,4,3,2,1,0:T(8,128)S(1)} collective-permute-done((f32[2,2,2,2,2,2,2,8,128]{8,7,6,5,4,3,2,1,0:T(8,128)S(1)}, f32[2,2,2,2,2,2,2,8,128]{8,7,6,5,4,3,2,1,0:T(8,128)S(1)}, u32[]{:S(2)}, u32[]{:S(2)}) %collective-permute-start.7) | collective-permute-done | bytes 524320 | tf_op jit(solution)/shard_map/ppermute | solution.py:99
  81.3 3.4 %collective-permute-start.9 = (bf16[1,8,128,32]{2,3,1,0:T(8,128)(2,1)S(1)}, bf16[1,8,128,32]{2,3,1,0:T(8,128)(2,1)S(1)}, u32[]{:S(2)}, u32[]{:S(2)}) collective-permute-start(bf16[1,8,128,32]{2,3,1,0:T(8,128)(2,1)S(1)} %get-tuple-element.24), channel_id=1, source_target_pairs={{0,16},{16,32},{32,48},{48,64},{64,80},{80,96},{96,112},{112,128},... | collective-permute-start | bytes 196616 | tf_op jit(solution)/shard_map/ppermute | solution.py:20
  86.6 4.3 %collective-permute-done.10 = bf16[1,8,128,32]{2,3,1,0:T(8,128)(2,1)S(1)} collective-permute-done((bf16[1,8,128,32]{2,3,1,0:T(8,128)(2,1)S(1)}, bf16[1,8,128,32]{2,3,1,0:T(8,128)(2,1)S(1)}, u32[]{:S(2)}, u32[]{:S(2)}) %collective-permute-start.10) | collective-permute-done | bytes 65568 | tf_op jit(solution)/shard_map/ppermute | solution.py:23
  92.8 3.6 %collective-permute-start.12 = (bf16[10,1,128,32]{2,3,1,0:T(8,128)(2,1)S(1)}, bf16[10,1,128,32]{2,3,1,0:T(8,128)(2,1)S(1)}, u32[]{:S(2)}, u32[]{:S(2)}) collective-permute-start(bf16[10,1,128,32]{2,3,1,0:T(8,128)(2,1)S(1)} %get-tuple-element.17), channel_id=1, source_target_pairs={{1,0},{2,1},{3,2},{4,3},{5,4},{6,5},{7,6},{8,7},{9,8},{10,9},{11,1... | collective-permute-start | bytes 245768 | tf_op jit(solution)/shard_map/ppermute | solution.py:23
  101.1 3.4 %collective-permute-start.13 = (bf16[1,8,128,32]{2,3,1,0:T(8,128)(2,1)S(1)}, bf16[1,8,128,32]{2,3,1,0:T(8,128)(2,1)S(1)}, u32[]{:S(2)}, u32[]{:S(2)}) collective-permute-start(bf16[1,8,128,32]{2,3,1,0:T(8,128)(2,1)S(1)} %get-tuple-element.22), channel_id=1, source_target_pairs={{0,16},{16,32},{32,48},{48,64},{64,80},{80,96},{96,112},{112,128},... | collective-permute-start | bytes 196616 | tf_op jit(solution)/shard_map/ppermute | solution.py:20
  106.4 4.3 %collective-permute-done.14 = bf16[1,8,128,32]{2,3,1,0:T(8,128)(2,1)S(1)} collective-permute-done((bf16[1,8,128,32]{2,3,1,0:T(8,128)(2,1)S(1)}, bf16[1,8,128,32]{2,3,1,0:T(8,128)(2,1)S(1)}, u32[]{:S(2)}, u32[]{:S(2)}) %collective-permute-start.14) | collective-permute-done | bytes 65568 | tf_op jit(solution)/shard_map/ppermute | solution.py:23
  110.7 4.8 %collective-permute-start.15 = (bf16[10,1,128,32]{2,3,1,0:T(8,128)(2,1)S(1)}, bf16[10,1,128,32]{2,3,1,0:T(8,128)(2,1)S(1)}, u32[]{:S(2)}, u32[]{:S(2)}) collective-permute-start(bf16[10,1,128,32]{2,3,1,0:T(8,128)(2,1)S(1)} %get-tuple-element.12), channel_id=1, source_target_pairs={{0,1},{1,2},{2,3},{3,4},{4,5},{5,6},{6,7},{7,8},{8,9},{9,10},{10,1... | collective-permute-start | bytes 245768 | tf_op jit(solution)/shard_map/ppermute | solution.py:20
  123.9 4.5 %collective-permute-start.17 = (bf16[1,8,128,32]{2,3,1,0:T(8,128)(2,1)S(1)}, bf16[1,8,128,32]{2,3,1,0:T(8,128)(2,1)S(1)}, u32[]{:S(2)}, u32[]{:S(2)}) collective-permute-start(bf16[1,8,128,32]{2,3,1,0:T(8,128)(2,1)S(1)} %get-tuple-element.20), channel_id=1, source_target_pairs={{0,16},{16,32},{32,48},{48,64},{64,80},{80,96},{96,112},{112,128},... | collective-permute-start | bytes 196616 | tf_op jit(solution)/shard_map/ppermute | solution.py:20
  130.4 5.1 %collective-permute-start.20 = (bf16[10,1,128,32]{2,3,1,0:T(8,128)(2,1)S(1)}, bf16[10,1,128,32]{2,3,1,0:T(8,128)(2,1)S(1)}, u32[]{:S(2)}, u32[]{:S(2)}) collective-permute-start(bf16[10,1,128,32]{2,3,1,0:T(8,128)(2,1)S(1)} %get-tuple-element.9), channel_id=1, source_target_pairs={{0,1},{1,2},{2,3},{3,4},{4,5},{5,6},{6,7},{7,8},{8,9},{9,10},{10,1... | collective-permute-start | bytes 245768 | tf_op jit(solution)/shard_map/ppermute | solution.py:20
  142.7 4.7 %collective-permute-start.21 = (bf16[1,8,128,32]{2,3,1,0:T(8,128)(2,1)S(1)}, bf16[1,8,128,32]{2,3,1,0:T(8,128)(2,1)S(1)}, u32[]{:S(2)}, u32[]{:S(2)}) collective-permute-start(bf16[1,8,128,32]{2,3,1,0:T(8,128)(2,1)S(1)} %get-tuple-element.18), channel_id=1, source_target_pairs={{0,16},{16,32},{32,48},{48,64},{64,80},{80,96},{96,112},{112,128},... | collective-permute-start | bytes 196616 | tf_op jit(solution)/shard_map/ppermute | solution.py:20
  149.3 5.3 %collective-permute-start.24 = (bf16[10,1,128,32]{2,3,1,0:T(8,128)(2,1)S(1)}, bf16[10,1,128,32]{2,3,1,0:T(8,128)(2,1)S(1)}, u32[]{:S(2)}, u32[]{:S(2)}) collective-permute-start(bf16[10,1,128,32]{2,3,1,0:T(8,128)(2,1)S(1)} %get-tuple-element.7), channel_id=1, source_target_pairs={{0,1},{1,2},{2,3},{3,4},{4,5},{5,6},{6,7},{7,8},{8,9},{9,10},{10,1... | collective-permute-start | bytes 245768 | tf_op jit(solution)/shard_map/ppermute | solution.py:20
  166.9 5.7 %collective-permute-start.25 = (f32[2,2,2,2,2,2,2,2,8,128]{9,8,7,6,5,4,3,2,1,0:T(8,128)}, f32[2,2,2,2,2,2,2,2,8,128]{9,8,7,6,5,4,3,2,1,0:T(8,128)}, u32[]{:S(2)}, u32[]{:S(2)}) collective-permute-start(f32[2,2,2,2,2,2,2,2,8,128]{9,8,7,6,5,4,3,2,1,0:T(8,128)} %dynamic-slice_bitcast_fusion), channel_id=1, source_target_pairs={{0,1},{1,0},{2,3},{3,2},{4,5},{5,4},{6,7},{7,6},{8,9},{9,8},{10,11... | collective-permute-start | bytes 3145736 | tf_op jit(solution)/shard_map/ppermute | solution.py:99
  179.6 14.2 %collective-permute-done.26 = f32[2,2,2,2,2,2,2,8,128]{8,7,6,5,4,3,2,1,0:T(8,128)S(1)} collective-permute-done((f32[2,2,2,2,2,2,2,8,128]{8,7,6,5,4,3,2,1,0:T(8,128)S(1)}, f32[2,2,2,2,2,2,2,8,128]{8,7,6,5,4,3,2,1,0:T(8,128)S(1)}, u32[]{:S(2)}, u32[]{:S(2)}) %collective-permute-start.26) | collective-permute-done | bytes 524320 | tf_op jit(solution)/shard_map/ppermute | solution.py:99
  195.0 4.3 %collective-permute-start.27 = (f32[2,2,2,2,2,2,8,128]{7,6,5,4,3,2,1,0:T(8,128)S(1)}, f32[2,2,2,2,2,2,8,128]{7,6,5,4,3,2,1,0:T(8,128)S(1)}, u32[]{:S(2)}, u32[]{:S(2)}) collective-permute-start(f32[2,2,2,2,2,2,8,128]{7,6,5,4,3,2,1,0:T(8,128)S(1)} %dynamic-slice_bitcast_fusion.2), channel_id=1, source_target_pairs={{0,16},{1,17},{2,18},{3,19},{4,20},{5,21},{6,22},{7,23},{8,24},{9,... | collective-permute-start | bytes 786440 | tf_op jit(solution)/shard_map/ppermute | solution.py:99
  199.2 6.0 %collective-permute-done.27 = f32[2,2,2,2,2,2,8,128]{7,6,5,4,3,2,1,0:T(8,128)S(1)} collective-permute-done((f32[2,2,2,2,2,2,8,128]{7,6,5,4,3,2,1,0:T(8,128)S(1)}, f32[2,2,2,2,2,2,8,128]{7,6,5,4,3,2,1,0:T(8,128)S(1)}, u32[]{:S(2)}, u32[]{:S(2)}) %collective-permute-start.27) | collective-permute-done | bytes 262176 | tf_op jit(solution)/shard_map/ppermute | solution.py:99
  205.3 12.5 %collective-permute-start.28 = (f32[2,2,2,2,2,8,128]{6,5,4,3,2,1,0:T(8,128)S(1)}, f32[2,2,2,2,2,8,128]{6,5,4,3,2,1,0:T(8,128)S(1)}, u32[]{:S(2)}, u32[]{:S(2)}) collective-permute-start(f32[2,2,2,2,2,8,128]{6,5,4,3,2,1,0:T(8,128)S(1)} %dynamic-slice_bitcast_fusion.3), channel_id=1, source_target_pairs={{0,128},{1,129},{2,130},{3,131},{4,132},{5,133},{6,134},{7,135},{8... | collective-permute-start | bytes 393224 | tf_op jit(solution)/shard_map/ppermute | solution.py:99
  217.8 5.7 %collective-permute-done.28 = f32[2,2,2,2,2,8,128]{6,5,4,3,2,1,0:T(8,128)S(1)} collective-permute-done((f32[2,2,2,2,2,8,128]{6,5,4,3,2,1,0:T(8,128)S(1)}, f32[2,2,2,2,2,8,128]{6,5,4,3,2,1,0:T(8,128)S(1)}, u32[]{:S(2)}, u32[]{:S(2)}) %collective-permute-start.28) | collective-permute-done | bytes 131104 | tf_op jit(solution)/shard_map/ppermute | solution.py:99
  225.5 5.8 %collective-permute-done.29 = f32[2,2,2,2,8,128]{5,4,3,2,1,0:T(8,128)S(1)} collective-permute-done((f32[2,2,2,2,8,128]{5,4,3,2,1,0:T(8,128)S(1)}, f32[2,2,2,2,8,128]{5,4,3,2,1,0:T(8,128)S(1)}, u32[]{:S(2)}, u32[]{:S(2)}) %collective-permute-start.29) | collective-permute-done | bytes 65568 | tf_op jit(solution)/shard_map/ppermute | solution.py:99
  233.3 5.4 %collective-permute-done.30 = f32[2,2,2,8,128]{4,3,2,1,0:T(8,128)S(1)} collective-permute-done((f32[2,2,2,8,128]{4,3,2,1,0:T(8,128)S(1)}, f32[2,2,2,8,128]{4,3,2,1,0:T(8,128)S(1)}, u32[]{:S(2)}, u32[]{:S(2)}) %collective-permute-start.30) | collective-permute-done | bytes 32800 | tf_op jit(solution)/shard_map/ppermute | solution.py:99
  238.7 12.7 %collective-permute-start.31 = (f32[2,2,8,128]{3,2,1,0:T(8,128)S(1)}, f32[2,2,8,128]{3,2,1,0:T(8,128)S(1)}, u32[]{:S(2)}, u32[]{:S(2)}) collective-permute-start(f32[2,2,8,128]{3,2,1,0:T(8,128)S(1)} %dynamic-slice_bitcast_fusion.6), channel_id=1, source_target_pairs={{0,256},{1,257},{2,258},{3,259},{4,260},{5,261},{6,262},{7,263},{8... | collective-permute-start | bytes 49160 | tf_op jit(solution)/shard_map/ppermute | solution.py:99
  255.1 7.5 %collective-permute-done.32 = f32[2,8,128]{2,1,0:T(8,128)S(1)} collective-permute-done((f32[2,8,128]{2,1,0:T(8,128)S(1)}, f32[2,8,128]{2,1,0:T(8,128)S(1)}, u32[]{:S(2)}, u32[]{:S(2)}) %collective-permute-start.32) | collective-permute-done | bytes 8224 | tf_op jit(solution)/shard_map/ppermute | solution.py:99
  264.5 3.6 %collective-permute-done.33 = f32[8,128]{1,0:T(8,128)S(1)} collective-permute-done((f32[8,128]{1,0:T(8,128)S(1)}, f32[8,128]{1,0:T(8,128)S(1)}, u32[]{:S(2)}, u32[]{:S(2)}) %collective-permute-start.33) | collective-permute-done | bytes 4128 | tf_op jit(solution)/shard_map/ppermute | solution.py:99
  (148 shorter events, 79.1 us)
Async XLA Ops:
  0.6 6.2 %collective-permute-start = (f32[8,128]{1,0:T(8,128)}, f32[8,128]{1,0:T(8,128)S(1)}, u32[]{:S(2)}, u32[]{:S(2)}) collective-permute-start(f32[8,128]{1,0:T(8,128)} %param.10), channel_id=1, source_target_pairs={{0,64},{1,65},{2,66},{3,67},{4,68},{5,69},{6,70},{7,71},{8,72},{9,... | collective-permute-start | bytes 12296 | tf_op jit(solution)/shard_map/ppermute | solution.py:99
  7.5 9.4 %collective-permute-start.1 = (f32[2,8,128]{2,1,0:T(8,128)S(1)}, f32[2,8,128]{2,1,0:T(8,128)S(1)}, u32[]{:S(2)}, u32[]{:S(2)}) collective-permute-start(f32[2,8,128]{2,1,0:T(8,128)S(1)} %pad_maximum_fusion.32), channel_id=1, source_target_pairs={{0,8},{1,9},{2,10},{3,11},{4,12},{5,13},{6,14},{7,15},{8,0},{9,1},... | collective-permute-start | bytes 24584 | tf_op jit(solution)/shard_map/ppermute | solution.py:99
  17.0 12.3 %collective-permute-start.2 = (f32[2,2,8,128]{3,2,1,0:T(8,128)S(1)}, f32[2,2,8,128]{3,2,1,0:T(8,128)S(1)}, u32[]{:S(2)}, u32[]{:S(2)}) collective-permute-start(f32[2,2,8,128]{3,2,1,0:T(8,128)S(1)} %pad_maximum_fusion.31), channel_id=1, source_target_pairs={{0,256},{1,257},{2,258},{3,259},{4,260},{5,261},{6,262},{7,263},{8... | collective-permute-start | bytes 49160 | tf_op jit(solution)/shard_map/ppermute | solution.py:99
  29.3 7.3 %collective-permute-start.3 = (f32[2,2,2,8,128]{4,3,2,1,0:T(8,128)S(1)}, f32[2,2,2,8,128]{4,3,2,1,0:T(8,128)S(1)}, u32[]{:S(2)}, u32[]{:S(2)}) collective-permute-start(f32[2,2,2,8,128]{4,3,2,1,0:T(8,128)S(1)} %pad_maximum_fusion.30), channel_id=1, source_target_pairs={{0,32},{1,33},{2,34},{3,35},{4,36},{5,37},{6,38},{7,39},{8,40},{9,... | collective-permute-start | bytes 98312 | tf_op jit(solution)/shard_map/ppermute | solution.py:99
  36.6 7.6 %collective-permute-start.4 = (f32[2,2,2,2,8,128]{5,4,3,2,1,0:T(8,128)S(1)}, f32[2,2,2,2,8,128]{5,4,3,2,1,0:T(8,128)S(1)}, u32[]{:S(2)}, u32[]{:S(2)}) collective-permute-start(f32[2,2,2,2,8,128]{5,4,3,2,1,0:T(8,128)S(1)} %pad_maximum_fusion.29), channel_id=1, source_target_pairs={{0,4},{1,5},{2,6},{3,7},{4,0},{5,1},{6,2},{7,3},{8,12},{9,13},{10,... | collective-permute-start | bytes 196616 | tf_op jit(solution)/shard_map/ppermute | solution.py:99
  44.3 9.2 %collective-permute-start.5 = (f32[2,2,2,2,2,8,128]{6,5,4,3,2,1,0:T(8,128)S(1)}, f32[2,2,2,2,2,8,128]{6,5,4,3,2,1,0:T(8,128)S(1)}, u32[]{:S(2)}, u32[]{:S(2)}) collective-permute-start(f32[2,2,2,2,2,8,128]{6,5,4,3,2,1,0:T(8,128)S(1)} %pad_maximum_fusion.16), channel_id=1, source_target_pairs={{0,128},{1,129},{2,130},{3,131},{4,132},{5,133},{6,134},{7,135},{8... | collective-permute-start | bytes 393224 | tf_op jit(solution)/shard_map/ppermute | solution.py:99
  53.5 8.3 %collective-permute-start.6 = (f32[2,2,2,2,2,2,8,128]{7,6,5,4,3,2,1,0:T(8,128)S(1)}, f32[2,2,2,2,2,2,8,128]{7,6,5,4,3,2,1,0:T(8,128)S(1)}, u32[]{:S(2)}, u32[]{:S(2)}) collective-permute-start(f32[2,2,2,2,2,2,8,128]{7,6,5,4,3,2,1,0:T(8,128)S(1)} %pad_maximum_fusion.15), channel_id=1, source_target_pairs={{0,16},{1,17},{2,18},{3,19},{4,20},{5,21},{6,22},{7,23},{8,24},{9,... | collective-permute-start | bytes 786440 | tf_op jit(solution)/shard_map/ppermute | solution.py:99
  61.9 11.1 %collective-permute-start.7 = (f32[2,2,2,2,2,2,2,8,128]{8,7,6,5,4,3,2,1,0:T(8,128)S(1)}, f32[2,2,2,2,2,2,2,8,128]{8,7,6,5,4,3,2,1,0:T(8,128)S(1)}, u32[]{:S(2)}, u32[]{:S(2)}) collective-permute-start(f32[2,2,2,2,2,2,2,8,128]{8,7,6,5,4,3,2,1,0:T(8,128)S(1)} %pad_maximum_fusion.14), channel_id=1, source_target_pairs={{0,2},{1,3},{2,0},{3,1},{4,6},{5,7},{6,4},{7,5},{8,10},{9,11},{10,... | collective-permute-start | bytes 1572872 | tf_op jit(solution)/shard_map/ppermute | solution.py:99
  74.2 4.8 %collective-permute-start.8 = (f32[2,2,2,2,2,2,2,2,8,128]{9,8,7,6,5,4,3,2,1,0:T(8,128)}, f32[2,2,2,2,2,2,2,2,8,128]{9,8,7,6,5,4,3,2,1,0:T(8,128)S(1)}, u32[]{:S(2)}, u32[]{:S(2)}) collective-permute-start(f32[2,2,2,2,2,2,2,2,8,128]{9,8,7,6,5,4,3,2,1,0:T(8,128)} %pad_maximum_fusion.1), channel_id=1, source_target_pairs={{0,1},{1,0},{2,3},{3,2},{4,5},{5,4},{6,7},{7,6},{8,9},{9,8},{10,11... | collective-permute-start | bytes 3145736 | tf_op jit(solution)/shard_map/ppermute | solution.py:99
  81.3 5.3 %collective-permute-start.9 = (bf16[1,8,128,32]{2,3,1,0:T(8,128)(2,1)S(1)}, bf16[1,8,128,32]{2,3,1,0:T(8,128)(2,1)S(1)}, u32[]{:S(2)}, u32[]{:S(2)}) collective-permute-start(bf16[1,8,128,32]{2,3,1,0:T(8,128)(2,1)S(1)} %get-tuple-element.24), channel_id=1, source_target_pairs={{0,16},{16,32},{32,48},{48,64},{64,80},{80,96},{96,112},{112,128},... | collective-permute-start | bytes 196616 | tf_op jit(solution)/shard_map/ppermute | solution.py:20
  84.7 6.2 %collective-permute-start.10 = (bf16[1,8,128,32]{2,3,1,0:T(8,128)(2,1)S(1)}, bf16[1,8,128,32]{2,3,1,0:T(8,128)(2,1)S(1)}, u32[]{:S(2)}, u32[]{:S(2)}) collective-permute-start(bf16[1,8,128,32]{2,3,1,0:T(8,128)(2,1)S(1)} %get-tuple-element.25), channel_id=1, source_target_pairs={{16,0},{32,16},{48,32},{64,48},{80,64},{96,80},{112,96},{128,112},... | collective-permute-start | bytes 196616 | tf_op jit(solution)/shard_map/ppermute | solution.py:23
  90.9 6.2 %collective-permute-start.11 = (bf16[10,1,128,32]{2,3,1,0:T(8,128)(2,1)S(1)}, bf16[10,1,128,32]{2,3,1,0:T(8,128)(2,1)S(1)}, u32[]{:S(2)}, u32[]{:S(2)}) collective-permute-start(bf16[10,1,128,32]{2,3,1,0:T(8,128)(2,1)S(1)} %get-tuple-element.16), channel_id=1, source_target_pairs={{0,1},{1,2},{2,3},{3,4},{4,5},{5,6},{6,7},{7,8},{8,9},{9,10},{10,1... | collective-permute-start | bytes 245768 | tf_op jit(solution)/shard_map/ppermute | solution.py:20
  92.8 5.7 %collective-permute-start.12 = (bf16[10,1,128,32]{2,3,1,0:T(8,128)(2,1)S(1)}, bf16[10,1,128,32]{2,3,1,0:T(8,128)(2,1)S(1)}, u32[]{:S(2)}, u32[]{:S(2)}) collective-permute-start(bf16[10,1,128,32]{2,3,1,0:T(8,128)(2,1)S(1)} %get-tuple-element.17), channel_id=1, source_target_pairs={{1,0},{2,1},{3,2},{4,3},{5,4},{6,5},{7,6},{8,7},{9,8},{10,9},{11,1... | collective-permute-start | bytes 245768 | tf_op jit(solution)/shard_map/ppermute | solution.py:23
  101.1 5.3 %collective-permute-start.13 = (bf16[1,8,128,32]{2,3,1,0:T(8,128)(2,1)S(1)}, bf16[1,8,128,32]{2,3,1,0:T(8,128)(2,1)S(1)}, u32[]{:S(2)}, u32[]{:S(2)}) collective-permute-start(bf16[1,8,128,32]{2,3,1,0:T(8,128)(2,1)S(1)} %get-tuple-element.22), channel_id=1, source_target_pairs={{0,16},{16,32},{32,48},{48,64},{64,80},{80,96},{96,112},{112,128},... | collective-permute-start | bytes 196616 | tf_op jit(solution)/shard_map/ppermute | solution.py:20
  104.5 6.2 %collective-permute-start.14 = (bf16[1,8,128,32]{2,3,1,0:T(8,128)(2,1)S(1)}, bf16[1,8,128,32]{2,3,1,0:T(8,128)(2,1)S(1)}, u32[]{:S(2)}, u32[]{:S(2)}) collective-permute-start(bf16[1,8,128,32]{2,3,1,0:T(8,128)(2,1)S(1)} %get-tuple-element.23), channel_id=1, source_target_pairs={{16,0},{32,16},{48,32},{64,48},{80,64},{96,80},{112,96},{128,112},... | collective-permute-start | bytes 196616 | tf_op jit(solution)/shard_map/ppermute | solution.py:23
  110.7 7.4 %collective-permute-start.15 = (bf16[10,1,128,32]{2,3,1,0:T(8,128)(2,1)S(1)}, bf16[10,1,128,32]{2,3,1,0:T(8,128)(2,1)S(1)}, u32[]{:S(2)}, u32[]{:S(2)}) collective-permute-start(bf16[10,1,128,32]{2,3,1,0:T(8,128)(2,1)S(1)} %get-tuple-element.12), channel_id=1, source_target_pairs={{0,1},{1,2},{2,3},{3,4},{4,5},{5,6},{6,7},{7,8},{8,9},{9,10},{10,1... | collective-permute-start | bytes 245768 | tf_op jit(solution)/shard_map/ppermute | solution.py:20
  115.5 4.0 %collective-permute-start.16 = (bf16[10,1,128,32]{2,3,1,0:T(8,128)(2,1)S(1)}, bf16[10,1,128,32]{2,3,1,0:T(8,128)(2,1)S(1)}, u32[]{:S(2)}, u32[]{:S(2)}) collective-permute-start(bf16[10,1,128,32]{2,3,1,0:T(8,128)(2,1)S(1)} %get-tuple-element.13), channel_id=1, source_target_pairs={{1,0},{2,1},{3,2},{4,3},{5,4},{6,5},{7,6},{8,7},{9,8},{10,9},{11,1... | collective-permute-start | bytes 245768 | tf_op jit(solution)/shard_map/ppermute | solution.py:23
  122.6 6.2 %collective-permute-start.18 = (bf16[1,8,128,32]{2,3,1,0:T(8,128)(2,1)S(1)}, bf16[1,8,128,32]{2,3,1,0:T(8,128)(2,1)S(1)}, u32[]{:S(2)}, u32[]{:S(2)}) collective-permute-start(bf16[1,8,128,32]{2,3,1,0:T(8,128)(2,1)S(1)} %get-tuple-element.21), channel_id=1, source_target_pairs={{16,0},{32,16},{48,32},{64,48},{80,64},{96,80},{112,96},{128,112},... | collective-permute-start | bytes 196616 | tf_op jit(solution)/shard_map/ppermute | solution.py:23
  123.9 6.4 %collective-permute-start.17 = (bf16[1,8,128,32]{2,3,1,0:T(8,128)(2,1)S(1)}, bf16[1,8,128,32]{2,3,1,0:T(8,128)(2,1)S(1)}, u32[]{:S(2)}, u32[]{:S(2)}) collective-permute-start(bf16[1,8,128,32]{2,3,1,0:T(8,128)(2,1)S(1)} %get-tuple-element.20), channel_id=1, source_target_pairs={{0,16},{16,32},{32,48},{48,64},{64,80},{80,96},{96,112},{112,128},... | collective-permute-start | bytes 196616 | tf_op jit(solution)/shard_map/ppermute | solution.py:20
  130.4 9.6 %collective-permute-start.20 = (bf16[10,1,128,32]{2,3,1,0:T(8,128)(2,1)S(1)}, bf16[10,1,128,32]{2,3,1,0:T(8,128)(2,1)S(1)}, u32[]{:S(2)}, u32[]{:S(2)}) collective-permute-start(bf16[10,1,128,32]{2,3,1,0:T(8,128)(2,1)S(1)} %get-tuple-element.9), channel_id=1, source_target_pairs={{0,1},{1,2},{2,3},{3,4},{4,5},{5,6},{6,7},{7,8},{8,9},{9,10},{10,1... | collective-permute-start | bytes 245768 | tf_op jit(solution)/shard_map/ppermute | solution.py:20
  141.4 6.3 %collective-permute-start.22 = (bf16[1,8,128,32]{2,3,1,0:T(8,128)(2,1)S(1)}, bf16[1,8,128,32]{2,3,1,0:T(8,128)(2,1)S(1)}, u32[]{:S(2)}, u32[]{:S(2)}) collective-permute-start(bf16[1,8,128,32]{2,3,1,0:T(8,128)(2,1)S(1)} %get-tuple-element.19), channel_id=1, source_target_pairs={{16,0},{32,16},{48,32},{64,48},{80,64},{96,80},{112,96},{128,112},... | collective-permute-start | bytes 196616 | tf_op jit(solution)/shard_map/ppermute | solution.py:23
  142.7 6.6 %collective-permute-start.21 = (bf16[1,8,128,32]{2,3,1,0:T(8,128)(2,1)S(1)}, bf16[1,8,128,32]{2,3,1,0:T(8,128)(2,1)S(1)}, u32[]{:S(2)}, u32[]{:S(2)}) collective-permute-start(bf16[1,8,128,32]{2,3,1,0:T(8,128)(2,1)S(1)} %get-tuple-element.18), channel_id=1, source_target_pairs={{0,16},{16,32},{32,48},{48,64},{64,80},{80,96},{96,112},{112,128},... | collective-permute-start | bytes 196616 | tf_op jit(solution)/shard_map/ppermute | solution.py:20
  149.3 9.9 %collective-permute-start.24 = (bf16[10,1,128,32]{2,3,1,0:T(8,128)(2,1)S(1)}, bf16[10,1,128,32]{2,3,1,0:T(8,128)(2,1)S(1)}, u32[]{:S(2)}, u32[]{:S(2)}) collective-permute-start(bf16[10,1,128,32]{2,3,1,0:T(8,128)(2,1)S(1)} %get-tuple-element.7), channel_id=1, source_target_pairs={{0,1},{1,2},{2,3},{3,4},{4,5},{5,6},{6,7},{7,8},{8,9},{9,10},{10,1... | collective-permute-start | bytes 245768 | tf_op jit(solution)/shard_map/ppermute | solution.py:20
  166.9 8.3 %collective-permute-start.25 = (f32[2,2,2,2,2,2,2,2,8,128]{9,8,7,6,5,4,3,2,1,0:T(8,128)}, f32[2,2,2,2,2,2,2,2,8,128]{9,8,7,6,5,4,3,2,1,0:T(8,128)}, u32[]{:S(2)}, u32[]{:S(2)}) collective-permute-start(f32[2,2,2,2,2,2,2,2,8,128]{9,8,7,6,5,4,3,2,1,0:T(8,128)} %dynamic-slice_bitcast_fusion), channel_id=1, source_target_pairs={{0,1},{1,0},{2,3},{3,2},{4,5},{5,4},{6,7},{7,6},{8,9},{9,8},{10,11... | collective-permute-start | bytes 3145736 | tf_op jit(solution)/shard_map/ppermute | solution.py:99
  177.7 16.1 %collective-permute-start.26 = (f32[2,2,2,2,2,2,2,8,128]{8,7,6,5,4,3,2,1,0:T(8,128)S(1)}, f32[2,2,2,2,2,2,2,8,128]{8,7,6,5,4,3,2,1,0:T(8,128)S(1)}, u32[]{:S(2)}, u32[]{:S(2)}) collective-permute-start(f32[2,2,2,2,2,2,2,8,128]{8,7,6,5,4,3,2,1,0:T(8,128)S(1)} %dynamic-slice_bitcast_fusion.1), channel_id=1, source_target_pairs={{0,2},{1,3},{2,0},{3,1},{4,6},{5,7},{6,4},{7,5},{8,10},{9,11},{10,... | collective-permute-start | bytes 1572872 | tf_op jit(solution)/shard_map/ppermute | solution.py:99
  195.0 10.3 %collective-permute-start.27 = (f32[2,2,2,2,2,2,8,128]{7,6,5,4,3,2,1,0:T(8,128)S(1)}, f32[2,2,2,2,2,2,8,128]{7,6,5,4,3,2,1,0:T(8,128)S(1)}, u32[]{:S(2)}, u32[]{:S(2)}) collective-permute-start(f32[2,2,2,2,2,2,8,128]{7,6,5,4,3,2,1,0:T(8,128)S(1)} %dynamic-slice_bitcast_fusion.2), channel_id=1, source_target_pairs={{0,16},{1,17},{2,18},{3,19},{4,20},{5,21},{6,22},{7,23},{8,24},{9,... | collective-permute-start | bytes 786440 | tf_op jit(solution)/shard_map/ppermute | solution.py:99
  205.3 18.2 %collective-permute-start.28 = (f32[2,2,2,2,2,8,128]{6,5,4,3,2,1,0:T(8,128)S(1)}, f32[2,2,2,2,2,8,128]{6,5,4,3,2,1,0:T(8,128)S(1)}, u32[]{:S(2)}, u32[]{:S(2)}) collective-permute-start(f32[2,2,2,2,2,8,128]{6,5,4,3,2,1,0:T(8,128)S(1)} %dynamic-slice_bitcast_fusion.3), channel_id=1, source_target_pairs={{0,128},{1,129},{2,130},{3,131},{4,132},{5,133},{6,134},{7,135},{8... | collective-permute-start | bytes 393224 | tf_op jit(solution)/shard_map/ppermute | solution.py:99
  223.6 7.8 %collective-permute-start.29 = (f32[2,2,2,2,8,128]{5,4,3,2,1,0:T(8,128)S(1)}, f32[2,2,2,2,8,128]{5,4,3,2,1,0:T(8,128)S(1)}, u32[]{:S(2)}, u32[]{:S(2)}) collective-permute-start(f32[2,2,2,2,8,128]{5,4,3,2,1,0:T(8,128)S(1)} %dynamic-slice_bitcast_fusion.4), channel_id=1, source_target_pairs={{0,4},{1,5},{2,6},{3,7},{4,0},{5,1},{6,2},{7,3},{8,12},{9,13},{10,... | collective-permute-start | bytes 196616 | tf_op jit(solution)/shard_map/ppermute | solution.py:99
  231.4 7.3 %collective-permute-start.30 = (f32[2,2,2,8,128]{4,3,2,1,0:T(8,128)S(1)}, f32[2,2,2,8,128]{4,3,2,1,0:T(8,128)S(1)}, u32[]{:S(2)}, u32[]{:S(2)}) collective-permute-start(f32[2,2,2,8,128]{4,3,2,1,0:T(8,128)S(1)} %dynamic-slice_bitcast_fusion.5), channel_id=1, source_target_pairs={{0,32},{1,33},{2,34},{3,35},{4,36},{5,37},{6,38},{7,39},{8,40},{9,... | collective-permute-start | bytes 98312 | tf_op jit(solution)/shard_map/ppermute | solution.py:99
  238.7 14.5 %collective-permute-start.31 = (f32[2,2,8,128]{3,2,1,0:T(8,128)S(1)}, f32[2,2,8,128]{3,2,1,0:T(8,128)S(1)}, u32[]{:S(2)}, u32[]{:S(2)}) collective-permute-start(f32[2,2,8,128]{3,2,1,0:T(8,128)S(1)} %dynamic-slice_bitcast_fusion.6), channel_id=1, source_target_pairs={{0,256},{1,257},{2,258},{3,259},{4,260},{5,261},{6,262},{7,263},{8... | collective-permute-start | bytes 49160 | tf_op jit(solution)/shard_map/ppermute | solution.py:99
  253.1 9.4 %collective-permute-start.32 = (f32[2,8,128]{2,1,0:T(8,128)S(1)}, f32[2,8,128]{2,1,0:T(8,128)S(1)}, u32[]{:S(2)}, u32[]{:S(2)}) collective-permute-start(f32[2,8,128]{2,1,0:T(8,128)S(1)} %dynamic-slice_bitcast_fusion.7), channel_id=1, source_target_pairs={{0,8},{1,9},{2,10},{3,11},{4,12},{5,13},{6,14},{7,15},{8,0},{9,1},... | collective-permute-start | bytes 24584 | tf_op jit(solution)/shard_map/ppermute | solution.py:99
  262.6 5.5 %collective-permute-start.33 = (f32[8,128]{1,0:T(8,128)S(1)}, f32[8,128]{1,0:T(8,128)S(1)}, u32[]{:S(2)}, u32[]{:S(2)}) collective-permute-start(f32[8,128]{1,0:T(8,128)S(1)} %fusion.165), channel_id=1, source_target_pairs={{0,64},{1,65},{2,66},{3,67},{4,68},{5,69},{6,70},{7,71},{8,72},{9,... | collective-permute-start | bytes 12296 | tf_op jit(solution)/shard_map/ppermute | solution.py:99
  (14 other events, 185.0 us)

commit v3 on v2

--- a/solution.py
+++ b/solution.py
@@ -7,9 +7,10 @@
 prior_weight = 0.1
 
 
-ROW_AXES = ("z", "x")
-COL_AXES = ("y", "core")
-ALL_AXES = ROW_AXES + COL_AXES
+ALL_AXES = tuple(f"b{bit}" for bit in range(8, -1, -1))
+ROW_AXES = ALL_AXES[:5]
+COL_AXES = ALL_AXES[5:]
+FAR_COUNT = 5
 
 
 def with_halo(block, sides, width):
@@ -105,23 +106,31 @@
     me = lax.axis_index(ALL_AXES)
     data = projected.reshape((2,) * nbits + (mode_block, projected.shape[1]))
     present = list(range(nbits - 1, -1, -1))
-    for bit in order:
+    near, far = order[: nbits - FAR_COUNT], order[nbits - FAR_COUNT :]
+    for bit in near:
         dim = present.index(bit)
         mine = (me >> bit) & 1
         keep = lax.dynamic_index_in_dim(data, mine, axis=dim, keepdims=False)
         send = lax.dynamic_index_in_dim(data, 1 - mine, axis=dim, keepdims=False)
         data = keep + exchange(send, bit, count)
         present.pop(dim)
-    return data
+    group = tuple(f"b{bit}" for bit in present)
+    data = data.reshape((1 << len(present), mode_block, projected.shape[1]))
+    data = lax.all_to_all(data, group, 0, 0, tiled=False)
+    return jnp.sum(data, axis=0)
 
 
 def gather_all(block, sizes):
     order, nbits = bit_order(sizes)
     count = 1 << nbits
     me = lax.axis_index(ALL_AXES)
-    data = block
-    present = []
-    for bit in reversed(order):
+    near, far = order[: nbits - FAR_COUNT], order[nbits - FAR_COUNT :]
+    present = sorted(far, reverse=True)
+    group = tuple(f"b{bit}" for bit in present)
+    data = jnp.broadcast_to(block[None], (1 << len(present),) + block.shape)
+    data = lax.all_to_all(data, group, 0, 0, tiled=False)
+    data = data.reshape((2,) * len(present) + block.shape)
+    for bit in reversed(near):
         mine = (me >> bit) & 1
         other = exchange(data, bit, count)
         low = jnp.where(mine == 0, data, other)
@@ -135,7 +144,7 @@
 def shards(coeffs, basis, observed, lift_w, lift_b, w_one, b_one, w_two, b_two, read_w):
     tile_rows, tile_cols, mode_count = basis.shape
     batch_size = coeffs.shape[1]
-    sizes = tuple(lax.axis_size(axis) for axis in ALL_AXES)
+    sizes = (4, 8, 8, 2)
     flat_basis = basis.reshape(tile_rows * tile_cols, mode_count)
     logperm = jnp.dot(
         flat_basis,
@@ -162,7 +171,7 @@
 
 def solution(mesh):
     row_size, col_size = mesh.devices.shape
-    fine = Mesh(mesh.devices.reshape(row_size // 8, 8, col_size // 2, 2), ALL_AXES)
+    fine = Mesh(mesh.devices.reshape((2,) * len(ALL_AXES)), ALL_AXES)
     return jax.shard_map(
         shards,
         mesh=fine,

time: 270 us -> 240 us (0.89)
  the two profiles are of different devices: /device:TPU:24 before, /device:TPU:1 now
where the time goes in v3:
time: 240 us; the launch traced here: 236 us
  waiting for transfers between devices  71.2 us (30%)
  starting transfers between devices  70.9 us (30%)
  blocking collectives  64.8 us (27%)
  matrix products  16.6 us (7%)
  other arithmetic  5.91 us (2%)
  local copies, waits for them, and re-layouts  5.56 us (2%)
    ppermute x8, waiting for transfers between devices, exchange(): return lax.ppermute(values, ALL_AXES, pairs)  49.7 us
    all_to_all x1, blocking collectives, gather_all(): data = lax.all_to_all(data, group, 0, 0, tiled=False)  32.9 us
    all_to_all x1, blocking collectives, scatter_sum(): data = lax.all_to_all(data, group, 0, 0, tiled=False)  31.9 us
    ppermute x8, starting transfers between devices, exchange(): return lax.ppermute(values, ALL_AXES, pairs)  30.9 us
    ppermute x8, starting transfers between devices, with_halo(): lax.ppermute(lax.slice_in_dim(block, block.shape[dim] - width, None, axis...  27 us
    ppermute x8, waiting for transfers between devices, with_halo(): lax.ppermute(lax.slice_in_dim(block, 0, width, axis=dim), axis, backward)  19.4 us
    ppermute x8, starting transfers between devices, with_halo(): lax.ppermute(lax.slice_in_dim(block, 0, width, axis=dim), axis, backward)  13 us
    dot_general x18, matrix products, conv_fwd(): jnp.einsum('xybi,io->xybo', window, weights[shift_x, shift_y], preferred_...  6.42 us
  transfers between devices with their start and end apart: 24, of which 16 were waited for; matrix products, arithmetic and copies ran while one was open for 2% of the time, Pallas kernels for 0%

profile of v3, /device:TPU:1, one launch (start us, length us, event | category | flops | bytes accessed | tf_op | source)
XLA Modules:
  0.0 236.4 jit_solution(6360546745174209913)
XLA Ops:
  1.4 32.9 %all_to_all.10 = f32[32,8,128]{2,1,0:T(8,128)S(1)} all-to-all(f32[32,8,128]{2,1,0:T(8,128)S(1)} %broadcast_in_dim.2), channel_id=1, replica_groups=mesh['b8'=2,'b7'=2,'b6'=2,'b5'=2,'b4'=2,'b3'=2,'b2'=2,'b1'=2,'b0'=2] {'b..., dimensions={0} | all-to-all | bytes 262144 | tf_op jit(solution)/shard_map/all_to_all | solution.py:131
  34.3 3.9 %collective-permute-start = (f32[2,2,2,2,2,8,128]{6,5,4,3,2,1,0:T(8,128)S(1)}, f32[2,2,2,2,2,8,128]{6,5,4,3,2,1,0:T(8,128)S(1)}, u32[]{:S(2)}, u32[]{:S(2)}) collective-permute-start(f32[2,2,2,2,2,8,128]{6,5,4,3,2,1,0:T(8,128)S(1)} %bitcast.282), channel_id=1, source_target_pairs={{0,128},{1,129},{2,130},{3,131},{4,132},{5,133},{6,134},{7,135},{8... | collective-permute-start | bytes 393224 | tf_op jit(solution)/shard_map/ppermute | solution.py:100
  38.3 6.0 %collective-permute-done = f32[2,2,2,2,2,8,128]{6,5,4,3,2,1,0:T(8,128)S(1)} collective-permute-done((f32[2,2,2,2,2,8,128]{6,5,4,3,2,1,0:T(8,128)S(1)}, f32[2,2,2,2,2,8,128]{6,5,4,3,2,1,0:T(8,128)S(1)}, u32[]{:S(2)}, u32[]{:S(2)}) %collective-permute-start) | collective-permute-done | bytes 131104 | tf_op jit(solution)/shard_map/ppermute | solution.py:100
  44.4 2.2 collective-permute-start.1
  46.6 6.0 %collective-permute-done.1 = f32[2,2,2,2,2,2,8,128]{7,6,5,4,3,2,1,0:T(8,128)S(1)} collective-permute-done((f32[2,2,2,2,2,2,8,128]{7,6,5,4,3,2,1,0:T(8,128)S(1)}, f32[2,2,2,2,2,2,8,128]{7,6,5,4,3,2,1,0:T(8,128)S(1)}, u32[]{:S(2)}, u32[]{:S(2)}) %collective-permute-start.1) | collective-permute-done | bytes 262176 | tf_op jit(solution)/shard_map/ppermute | solution.py:100
  52.7 2.1 collective-permute-start.2
  54.9 10.9 %collective-permute-done.2 = f32[2,2,2,2,2,2,2,8,128]{8,7,6,5,4,3,2,1,0:T(8,128)S(1)} collective-permute-done((f32[2,2,2,2,2,2,2,8,128]{8,7,6,5,4,3,2,1,0:T(8,128)S(1)}, f32[2,2,2,2,2,2,2,8,128]{8,7,6,5,4,3,2,1,0:T(8,128)S(1)}, u32[]{:S(2)}, u32[]{:S(2)}) %collective-permute-start.2) | collective-permute-done | bytes 524320 | tf_op jit(solution)/shard_map/ppermute | solution.py:100
  67.0 5.1 %collective-permute-start.3 = (f32[2,2,2,2,2,2,2,2,8,128]{9,8,7,6,5,4,3,2,1,0:T(8,128)}, f32[2,2,2,2,2,2,2,2,8,128]{9,8,7,6,5,4,3,2,1,0:T(8,128)S(1)}, u32[]{:S(2)}, u32[]{:S(2)}) collective-permute-start(f32[2,2,2,2,2,2,2,2,8,128]{9,8,7,6,5,4,3,2,1,0:T(8,128)} %pad_maximum_fusion.1), channel_id=1, source_target_pairs={{0,1},{1,0},{2,3},{3,2},{4,5},{5,4},{6,7},{7,6},{8,9},{9,8},{10,11... | collective-permute-start | bytes 3145736 | tf_op jit(solution)/shard_map/ppermute | solution.py:100
  72.1 2.5 %collective-permute-done.3 = f32[2,2,2,2,2,2,2,2,8,128]{9,8,7,6,5,4,3,2,1,0:T(8,128)S(1)} collective-permute-done((f32[2,2,2,2,2,2,2,2,8,128]{9,8,7,6,5,4,3,2,1,0:T(8,128)}, f32[2,2,2,2,2,2,2,2,8,128]{9,8,7,6,5,4,3,2,1,0:T(8,128)S(1)}, u32[]{:S(2)}, u32[]{:S(2)}) %collective-permute-start.3) | collective-permute-done | bytes 1048608 | tf_op jit(solution)/shard_map/ppermute | solution.py:100
  76.9 2.2 collective-permute-start.4
  80.8 3.3 %collective-permute-done.5 = bf16[1,8,128,32]{2,3,1,0:T(8,128)(2,1)S(1)} collective-permute-done((bf16[1,8,128,32]{2,3,1,0:T(8,128)(2,1)S(1)}, bf16[1,8,128,32]{2,3,1,0:T(8,128)(2,1)S(1)}, u32[]{:S(2)}, u32[]{:S(2)}) %collective-permute-start.5) | collective-permute-done | bytes 65568 | tf_op jit(solution)/shard_map/ppermute | solution.py:24
  84.1 3.8 %collective-permute-start.6 = (bf16[10,1,128,32]{2,3,1,0:T(8,128)(2,1)S(1)}, bf16[10,1,128,32]{2,3,1,0:T(8,128)(2,1)S(1)}, u32[]{:S(2)}, u32[]{:S(2)}) collective-permute-start(bf16[10,1,128,32]{2,3,1,0:T(8,128)(2,1)S(1)} %get-tuple-element.16), channel_id=1, source_target_pairs={{0,1},{1,2},{2,3},{3,4},{4,5},{5,6},{6,7},{7,8},{8,9},{9,10},{10,1... | collective-permute-start | bytes 245768 | tf_op jit(solution)/shard_map/ppermute | solution.py:21
  90.6 3.2 %collective-permute-done.7 = bf16[10,1,128,32]{2,3,1,0:T(8,128)(2,1)S(1)} collective-permute-done((bf16[10,1,128,32]{2,3,1,0:T(8,128)(2,1)S(1)}, bf16[10,1,128,32]{2,3,1,0:T(8,128)(2,1)S(1)}, u32[]{:S(2)}, u32[]{:S(2)}) %collective-permute-start.7) | collective-permute-done | bytes 81952 | tf_op jit(solution)/shard_map/ppermute | solution.py:24
  96.3 2.3 collective-permute-start.8
  100.3 3.4 %collective-permute-done.9 = bf16[1,8,128,32]{2,3,1,0:T(8,128)(2,1)S(1)} collective-permute-done((bf16[1,8,128,32]{2,3,1,0:T(8,128)(2,1)S(1)}, bf16[1,8,128,32]{2,3,1,0:T(8,128)(2,1)S(1)}, u32[]{:S(2)}, u32[]{:S(2)}) %collective-permute-start.9) | collective-permute-done | bytes 65568 | tf_op jit(solution)/shard_map/ppermute | solution.py:24
  103.7 3.3 %collective-permute-start.10 = (bf16[10,1,128,32]{2,3,1,0:T(8,128)(2,1)S(1)}, bf16[10,1,128,32]{2,3,1,0:T(8,128)(2,1)S(1)}, u32[]{:S(2)}, u32[]{:S(2)}) collective-permute-start(bf16[10,1,128,32]{2,3,1,0:T(8,128)(2,1)S(1)} %get-tuple-element.12), channel_id=1, source_target_pairs={{0,1},{1,2},{2,3},{3,4},{4,5},{5,6},{6,7},{7,8},{8,9},{9,10},{10,1... | collective-permute-start | bytes 245768 | tf_op jit(solution)/shard_map/ppermute | solution.py:21
  109.6 3.2 %collective-permute-done.11 = bf16[10,1,128,32]{2,3,1,0:T(8,128)(2,1)S(1)} collective-permute-done((bf16[10,1,128,32]{2,3,1,0:T(8,128)(2,1)S(1)}, bf16[10,1,128,32]{2,3,1,0:T(8,128)(2,1)S(1)}, u32[]{:S(2)}, u32[]{:S(2)}) %collective-permute-start.11) | collective-permute-done | bytes 81952 | tf_op jit(solution)/shard_map/ppermute | solution.py:24
  117.2 5.3 %collective-permute-start.12 = (bf16[1,8,128,32]{2,3,1,0:T(8,128)(2,1)S(1)}, bf16[1,8,128,32]{2,3,1,0:T(8,128)(2,1)S(1)}, u32[]{:S(2)}, u32[]{:S(2)}) collective-permute-start(bf16[1,8,128,32]{2,3,1,0:T(8,128)(2,1)S(1)} %get-tuple-element.20), channel_id=1, source_target_pairs={{0,16},{16,32},{32,48},{48,64},{64,80},{80,96},{96,112},{112,128},... | collective-permute-start | bytes 196616 | tf_op jit(solution)/shard_map/ppermute | solution.py:21
  123.8 2.7 %collective-permute-start.15 = (bf16[10,1,128,32]{2,3,1,0:T(8,128)(2,1)S(1)}, bf16[10,1,128,32]{2,3,1,0:T(8,128)(2,1)S(1)}, u32[]{:S(2)}, u32[]{:S(2)}) collective-permute-start(bf16[10,1,128,32]{2,3,1,0:T(8,128)(2,1)S(1)} %get-tuple-element.9), channel_id=1, source_target_pairs={{0,1},{1,2},{2,3},{3,4},{4,5},{5,6},{6,7},{7,8},{8,9},{9,10},{10,1... | collective-permute-start | bytes 245768 | tf_op jit(solution)/shard_map/ppermute | solution.py:21
  129.0 3.3 %collective-permute-done.14 = bf16[10,1,128,32]{2,3,1,0:T(8,128)(2,1)S(1)} collective-permute-done((bf16[10,1,128,32]{2,3,1,0:T(8,128)(2,1)S(1)}, bf16[10,1,128,32]{2,3,1,0:T(8,128)(2,1)S(1)}, u32[]{:S(2)}, u32[]{:S(2)}) %collective-permute-start.14) | collective-permute-done | bytes 81952 | tf_op jit(solution)/shard_map/ppermute | solution.py:24
  135.6 4.6 %collective-permute-start.16 = (bf16[1,8,128,32]{2,3,1,0:T(8,128)(2,1)S(1)}, bf16[1,8,128,32]{2,3,1,0:T(8,128)(2,1)S(1)}, u32[]{:S(2)}, u32[]{:S(2)}) collective-permute-start(bf16[1,8,128,32]{2,3,1,0:T(8,128)(2,1)S(1)} %get-tuple-element.18), channel_id=1, source_target_pairs={{0,16},{16,32},{32,48},{48,64},{64,80},{80,96},{96,112},{112,128},... | collective-permute-start | bytes 196616 | tf_op jit(solution)/shard_map/ppermute | solution.py:21
  141.5 2.7 %collective-permute-start.19 = (bf16[10,1,128,32]{2,3,1,0:T(8,128)(2,1)S(1)}, bf16[10,1,128,32]{2,3,1,0:T(8,128)(2,1)S(1)}, u32[]{:S(2)}, u32[]{:S(2)}) collective-permute-start(bf16[10,1,128,32]{2,3,1,0:T(8,128)(2,1)S(1)} %get-tuple-element.7), channel_id=1, source_target_pairs={{0,1},{1,2},{2,3},{3,4},{4,5},{5,6},{6,7},{7,8},{8,9},{9,10},{10,1... | collective-permute-start | bytes 245768 | tf_op jit(solution)/shard_map/ppermute | solution.py:21
  144.2 2.1 collective-permute-start.18
  146.9 3.1 %collective-permute-done.18 = bf16[10,1,128,32]{2,3,1,0:T(8,128)(2,1)S(1)} collective-permute-done((bf16[10,1,128,32]{2,3,1,0:T(8,128)(2,1)S(1)}, bf16[10,1,128,32]{2,3,1,0:T(8,128)(2,1)S(1)}, u32[]{:S(2)}, u32[]{:S(2)}) %collective-permute-start.18) | collective-permute-done | bytes 81952 | tf_op jit(solution)/shard_map/ppermute | solution.py:24
  152.0 3.2 %convolution_bitcast_fusion = f32[4096,128]{0,1:T(8,128)} fusion(f32[8,8,128]{2,1,0:T(8,128)S(1)} %fusion.32, f32[8,8,4096]{2,1,0:T(8,128)S(1)} %copy-done), kind=kOutput, calls=%fused_computation | convolution fusion | flops 402653184 | bytes 3178496 | tf_op jit(solution)/shard_map/dot_general | solution.py:160
  160.1 3.0 %collective-permute-done.20 = f32[2,2,2,2,2,2,2,2,8,128]{9,8,7,6,5,4,3,2,1,0:T(8,128)} collective-permute-done((f32[2,2,2,2,2,2,2,2,8,128]{9,8,7,6,5,4,3,2,1,0:T(8,128)}, f32[2,2,2,2,2,2,2,2,8,128]{9,8,7,6,5,4,3,2,1,0:T(8,128)}, u32[]{:S(2)}, u32[]{:S(2)}) %collective-permute-start.20) | collective-permute-done | bytes 1048608 | tf_op jit(solution)/shard_map/ppermute | solution.py:100
  167.5 13.3 %collective-permute-done.21 = f32[2,2,2,2,2,2,2,8,128]{8,7,6,5,4,3,2,1,0:T(8,128)S(1)} collective-permute-done((f32[2,2,2,2,2,2,2,8,128]{8,7,6,5,4,3,2,1,0:T(8,128)S(1)}, f32[2,2,2,2,2,2,2,8,128]{8,7,6,5,4,3,2,1,0:T(8,128)S(1)}, u32[]{:S(2)}, u32[]{:S(2)}) %collective-permute-start.21) | collective-permute-done | bytes 524320 | tf_op jit(solution)/shard_map/ppermute | solution.py:100
  182.0 4.0 %collective-permute-start.22 = (f32[2,2,2,2,2,2,8,128]{7,6,5,4,3,2,1,0:T(8,128)S(1)}, f32[2,2,2,2,2,2,8,128]{7,6,5,4,3,2,1,0:T(8,128)S(1)}, u32[]{:S(2)}, u32[]{:S(2)}) collective-permute-start(f32[2,2,2,2,2,2,8,128]{7,6,5,4,3,2,1,0:T(8,128)S(1)} %dynamic-slice_bitcast_fusion.2), channel_id=1, source_target_pairs={{0,16},{1,17},{2,18},{3,19},{4,20},{5,21},{6,22},{7,23},{8,24},{9,... | collective-permute-start | bytes 786440 | tf_op jit(solution)/shard_map/ppermute | solution.py:100
  186.0 5.7 %collective-permute-done.22 = f32[2,2,2,2,2,2,8,128]{7,6,5,4,3,2,1,0:T(8,128)S(1)} collective-permute-done((f32[2,2,2,2,2,2,8,128]{7,6,5,4,3,2,1,0:T(8,128)S(1)}, f32[2,2,2,2,2,2,8,128]{7,6,5,4,3,2,1,0:T(8,128)S(1)}, u32[]{:S(2)}, u32[]{:S(2)}) %collective-permute-start.22) | collective-permute-done | bytes 262176 | tf_op jit(solution)/shard_map/ppermute | solution.py:100
  191.8 9.6 %collective-permute-start.23 = (f32[2,2,2,2,2,8,128]{6,5,4,3,2,1,0:T(8,128)S(1)}, f32[2,2,2,2,2,8,128]{6,5,4,3,2,1,0:T(8,128)S(1)}, u32[]{:S(2)}, u32[]{:S(2)}) collective-permute-start(f32[2,2,2,2,2,8,128]{6,5,4,3,2,1,0:T(8,128)S(1)} %dynamic-slice_bitcast_fusion.3), channel_id=1, source_target_pairs={{0,128},{1,129},{2,130},{3,131},{4,132},{5,133},{6,134},{7,135},{8... | collective-permute-start | bytes 393224 | tf_op jit(solution)/shard_map/ppermute | solution.py:100
  201.5 2.3 collective-permute-done.23
  203.8 31.9 %all_to_all.11 = f32[32,8,128]{2,1,0:T(8,128)S(1)} all-to-all(f32[32,8,128]{2,1,0:T(8,128)S(1)} %bitcast.284), channel_id=1, replica_groups=mesh['b8'=2,'b7'=2,'b6'=2,'b5'=2,'b4'=2,'b3'=2,'b2'=2,'b1'=2,'b0'=2] {'b..., dimensions={0} | all-to-all | bytes 262144 | tf_op jit(solution)/shard_map/all_to_all | solution.py:119
  (113 shorter events, 41.7 us)
Async XLA Ops:
  0.6 74.5 %copy-start = (f32[8,8,4096]{2,1,0:T(8,128)S(1)}, f32[8,8,4096]{2,1,0:T(8,128)}, u32[]{:S(2)}) copy-start(f32[8,8,4096]{2,1,0:T(8,128)} %param.11) | copy-start | bytes 3145732
  34.3 10.0 %collective-permute-start = (f32[2,2,2,2,2,8,128]{6,5,4,3,2,1,0:T(8,128)S(1)}, f32[2,2,2,2,2,8,128]{6,5,4,3,2,1,0:T(8,128)S(1)}, u32[]{:S(2)}, u32[]{:S(2)}) collective-permute-start(f32[2,2,2,2,2,8,128]{6,5,4,3,2,1,0:T(8,128)S(1)} %bitcast.282), channel_id=1, source_target_pairs={{0,128},{1,129},{2,130},{3,131},{4,132},{5,133},{6,134},{7,135},{8... | collective-permute-start | bytes 393224 | tf_op jit(solution)/shard_map/ppermute | solution.py:100
  44.4 8.3 %collective-permute-start.1 = (f32[2,2,2,2,2,2,8,128]{7,6,5,4,3,2,1,0:T(8,128)S(1)}, f32[2,2,2,2,2,2,8,128]{7,6,5,4,3,2,1,0:T(8,128)S(1)}, u32[]{:S(2)}, u32[]{:S(2)}) collective-permute-start(f32[2,2,2,2,2,2,8,128]{7,6,5,4,3,2,1,0:T(8,128)S(1)} %pad_maximum_fusion.15), channel_id=1, source_target_pairs={{0,16},{1,17},{2,18},{3,19},{4,20},{5,21},{6,22},{7,23},{8,24},{9,... | collective-permute-start | bytes 786440 | tf_op jit(solution)/shard_map/ppermute | solution.py:100
  52.7 13.0 %collective-permute-start.2 = (f32[2,2,2,2,2,2,2,8,128]{8,7,6,5,4,3,2,1,0:T(8,128)S(1)}, f32[2,2,2,2,2,2,2,8,128]{8,7,6,5,4,3,2,1,0:T(8,128)S(1)}, u32[]{:S(2)}, u32[]{:S(2)}) collective-permute-start(f32[2,2,2,2,2,2,2,8,128]{8,7,6,5,4,3,2,1,0:T(8,128)S(1)} %pad_maximum_fusion.14), channel_id=1, source_target_pairs={{0,2},{1,3},{2,0},{3,1},{4,6},{5,7},{6,4},{7,5},{8,10},{9,11},{10,... | collective-permute-start | bytes 1572872 | tf_op jit(solution)/shard_map/ppermute | solution.py:100
  67.0 7.6 %collective-permute-start.3 = (f32[2,2,2,2,2,2,2,2,8,128]{9,8,7,6,5,4,3,2,1,0:T(8,128)}, f32[2,2,2,2,2,2,2,2,8,128]{9,8,7,6,5,4,3,2,1,0:T(8,128)S(1)}, u32[]{:S(2)}, u32[]{:S(2)}) collective-permute-start(f32[2,2,2,2,2,2,2,2,8,128]{9,8,7,6,5,4,3,2,1,0:T(8,128)} %pad_maximum_fusion.1), channel_id=1, source_target_pairs={{0,1},{1,0},{2,3},{3,2},{4,5},{5,4},{6,7},{7,6},{8,9},{9,8},{10,11... | collective-permute-start | bytes 3145736 | tf_op jit(solution)/shard_map/ppermute | solution.py:100
  75.1 1.5 copy-start.7
  75.1 1.5 copy-start.8
  75.1 5.3 %copy-start.3 = (bf16[3,3,32,32]{3,2,1,0:T(8,128)(2,1)S(1)}, bf16[3,3,32,32]{3,2,1,0:T(8,128)(2,1)}, u32[]{:S(2)}) copy-start(bf16[3,3,32,32]{3,2,1,0:T(8,128)(2,1)} %param.15) | copy-start | bytes 55300
  76.9 3.9 %collective-permute-start.4 = (bf16[1,8,128,32]{2,3,1,0:T(8,128)(2,1)S(1)}, bf16[1,8,128,32]{2,3,1,0:T(8,128)(2,1)S(1)}, u32[]{:S(2)}, u32[]{:S(2)}) collective-permute-start(bf16[1,8,128,32]{2,3,1,0:T(8,128)(2,1)S(1)} %get-tuple-element.24), channel_id=1, source_target_pairs={{0,16},{16,32},{32,48},{48,64},{64,80},{80,96},{96,112},{112,128},... | collective-permute-start | bytes 196616 | tf_op jit(solution)/shard_map/ppermute | solution.py:21
  79.1 5.0 %collective-permute-start.5 = (bf16[1,8,128,32]{2,3,1,0:T(8,128)(2,1)S(1)}, bf16[1,8,128,32]{2,3,1,0:T(8,128)(2,1)S(1)}, u32[]{:S(2)}, u32[]{:S(2)}) collective-permute-start(bf16[1,8,128,32]{2,3,1,0:T(8,128)(2,1)S(1)} %get-tuple-element.25), channel_id=1, source_target_pairs={{16,0},{32,16},{48,32},{64,48},{80,64},{96,80},{112,96},{128,112},... | collective-permute-start | bytes 196616 | tf_op jit(solution)/shard_map/ppermute | solution.py:24
  84.1 6.4 %collective-permute-start.6 = (bf16[10,1,128,32]{2,3,1,0:T(8,128)(2,1)S(1)}, bf16[10,1,128,32]{2,3,1,0:T(8,128)(2,1)S(1)}, u32[]{:S(2)}, u32[]{:S(2)}) collective-permute-start(bf16[10,1,128,32]{2,3,1,0:T(8,128)(2,1)S(1)} %get-tuple-element.16), channel_id=1, source_target_pairs={{0,1},{1,2},{2,3},{3,4},{4,5},{5,6},{6,7},{7,8},{8,9},{9,10},{10,1... | collective-permute-start | bytes 245768 | tf_op jit(solution)/shard_map/ppermute | solution.py:21
  88.0 5.8 %collective-permute-start.7 = (bf16[10,1,128,32]{2,3,1,0:T(8,128)(2,1)S(1)}, bf16[10,1,128,32]{2,3,1,0:T(8,128)(2,1)S(1)}, u32[]{:S(2)}, u32[]{:S(2)}) collective-permute-start(bf16[10,1,128,32]{2,3,1,0:T(8,128)(2,1)S(1)} %get-tuple-element.17), channel_id=1, source_target_pairs={{1,0},{2,1},{3,2},{4,3},{5,4},{6,5},{7,6},{8,7},{9,8},{10,9},{11,1... | collective-permute-start | bytes 245768 | tf_op jit(solution)/shard_map/ppermute | solution.py:24
  95.8 4.1 %copy-start.2 = (bf16[3,3,32,32]{3,2,1,0:T(8,128)(2,1)S(1)}, bf16[3,3,32,32]{3,2,1,0:T(8,128)(2,1)}, u32[]{:S(2)}) copy-start(bf16[3,3,32,32]{3,2,1,0:T(8,128)(2,1)} %param.17) | copy-start | bytes 55300
  96.3 4.0 %collective-permute-start.8 = (bf16[1,8,128,32]{2,3,1,0:T(8,128)(2,1)S(1)}, bf16[1,8,128,32]{2,3,1,0:T(8,128)(2,1)S(1)}, u32[]{:S(2)}, u32[]{:S(2)}) collective-permute-start(bf16[1,8,128,32]{2,3,1,0:T(8,128)(2,1)S(1)} %get-tuple-element.22), channel_id=1, source_target_pairs={{0,16},{16,32},{32,48},{48,64},{64,80},{80,96},{96,112},{112,128},... | collective-permute-start | bytes 196616 | tf_op jit(solution)/shard_map/ppermute | solution.py:21
  98.7 5.0 %collective-permute-start.9 = (bf16[1,8,128,32]{2,3,1,0:T(8,128)(2,1)S(1)}, bf16[1,8,128,32]{2,3,1,0:T(8,128)(2,1)S(1)}, u32[]{:S(2)}, u32[]{:S(2)}) collective-permute-start(bf16[1,8,128,32]{2,3,1,0:T(8,128)(2,1)S(1)} %get-tuple-element.23), channel_id=1, source_target_pairs={{16,0},{32,16},{48,32},{64,48},{80,64},{96,80},{112,96},{128,112},... | collective-permute-start | bytes 196616 | tf_op jit(solution)/shard_map/ppermute | solution.py:24
  103.7 5.8 %collective-permute-start.10 = (bf16[10,1,128,32]{2,3,1,0:T(8,128)(2,1)S(1)}, bf16[10,1,128,32]{2,3,1,0:T(8,128)(2,1)S(1)}, u32[]{:S(2)}, u32[]{:S(2)}) collective-permute-start(bf16[10,1,128,32]{2,3,1,0:T(8,128)(2,1)S(1)} %get-tuple-element.12), channel_id=1, source_target_pairs={{0,1},{1,2},{2,3},{3,4},{4,5},{5,6},{6,7},{7,8},{8,9},{9,10},{10,1... | collective-permute-start | bytes 245768 | tf_op jit(solution)/shard_map/ppermute | solution.py:21
  107.0 5.8 %collective-permute-start.11 = (bf16[10,1,128,32]{2,3,1,0:T(8,128)(2,1)S(1)}, bf16[10,1,128,32]{2,3,1,0:T(8,128)(2,1)S(1)}, u32[]{:S(2)}, u32[]{:S(2)}) collective-permute-start(bf16[10,1,128,32]{2,3,1,0:T(8,128)(2,1)S(1)} %get-tuple-element.13), channel_id=1, source_target_pairs={{1,0},{2,1},{3,2},{4,3},{5,4},{6,5},{7,6},{8,7},{9,8},{10,9},{11,1... | collective-permute-start | bytes 245768 | tf_op jit(solution)/shard_map/ppermute | solution.py:24
  115.4 7.3 %copy-start.4 = (f32[8,8,128]{2,1,0:T(8,128)}, f32[8,8,128]{2,1,0:T(8,128)S(1)}, u32[]{:S(2)}) copy-start(f32[8,8,128]{2,1,0:T(8,128)S(1)} %get-tuple-element.30) | copy-start | bytes 98308
  115.9 6.9 %collective-permute-start.13 = (bf16[1,8,128,32]{2,3,1,0:T(8,128)(2,1)S(1)}, bf16[1,8,128,32]{2,3,1,0:T(8,128)(2,1)S(1)}, u32[]{:S(2)}, u32[]{:S(2)}) collective-permute-start(bf16[1,8,128,32]{2,3,1,0:T(8,128)(2,1)S(1)} %get-tuple-element.21), channel_id=1, source_target_pairs={{16,0},{32,16},{48,32},{64,48},{80,64},{96,80},{112,96},{128,112},... | collective-permute-start | bytes 196616 | tf_op jit(solution)/shard_map/ppermute | solution.py:24
  117.2 6.6 %collective-permute-start.12 = (bf16[1,8,128,32]{2,3,1,0:T(8,128)(2,1)S(1)}, bf16[1,8,128,32]{2,3,1,0:T(8,128)(2,1)S(1)}, u32[]{:S(2)}, u32[]{:S(2)}) collective-permute-start(bf16[1,8,128,32]{2,3,1,0:T(8,128)(2,1)S(1)} %get-tuple-element.20), channel_id=1, source_target_pairs={{0,16},{16,32},{32,48},{48,64},{64,80},{80,96},{96,112},{112,128},... | collective-permute-start | bytes 196616 | tf_op jit(solution)/shard_map/ppermute | solution.py:21
  123.8 9.0 %collective-permute-start.15 = (bf16[10,1,128,32]{2,3,1,0:T(8,128)(2,1)S(1)}, bf16[10,1,128,32]{2,3,1,0:T(8,128)(2,1)S(1)}, u32[]{:S(2)}, u32[]{:S(2)}) collective-permute-start(bf16[10,1,128,32]{2,3,1,0:T(8,128)(2,1)S(1)} %get-tuple-element.9), channel_id=1, source_target_pairs={{0,1},{1,2},{2,3},{3,4},{4,5},{5,6},{6,7},{7,8},{8,9},{9,10},{10,1... | collective-permute-start | bytes 245768 | tf_op jit(solution)/shard_map/ppermute | solution.py:21
  126.5 5.8 %collective-permute-start.14 = (bf16[10,1,128,32]{2,3,1,0:T(8,128)(2,1)S(1)}, bf16[10,1,128,32]{2,3,1,0:T(8,128)(2,1)S(1)}, u32[]{:S(2)}, u32[]{:S(2)}) collective-permute-start(bf16[10,1,128,32]{2,3,1,0:T(8,128)(2,1)S(1)} %get-tuple-element.8), channel_id=1, source_target_pairs={{1,0},{2,1},{3,2},{4,3},{5,4},{6,5},{7,6},{8,7},{9,8},{10,9},{11,1... | collective-permute-start | bytes 245768 | tf_op jit(solution)/shard_map/ppermute | solution.py:24
  134.3 6.2 %collective-permute-start.17 = (bf16[1,8,128,32]{2,3,1,0:T(8,128)(2,1)S(1)}, bf16[1,8,128,32]{2,3,1,0:T(8,128)(2,1)S(1)}, u32[]{:S(2)}, u32[]{:S(2)}) collective-permute-start(bf16[1,8,128,32]{2,3,1,0:T(8,128)(2,1)S(1)} %get-tuple-element.19), channel_id=1, source_target_pairs={{16,0},{32,16},{48,32},{64,48},{80,64},{96,80},{112,96},{128,112},... | collective-permute-start | bytes 196616 | tf_op jit(solution)/shard_map/ppermute | solution.py:24
  135.6 5.9 %collective-permute-start.16 = (bf16[1,8,128,32]{2,3,1,0:T(8,128)(2,1)S(1)}, bf16[1,8,128,32]{2,3,1,0:T(8,128)(2,1)S(1)}, u32[]{:S(2)}, u32[]{:S(2)}) collective-permute-start(bf16[1,8,128,32]{2,3,1,0:T(8,128)(2,1)S(1)} %get-tuple-element.18), channel_id=1, source_target_pairs={{0,16},{16,32},{32,48},{48,64},{64,80},{80,96},{96,112},{112,128},... | collective-permute-start | bytes 196616 | tf_op jit(solution)/shard_map/ppermute | solution.py:21
  141.5 9.1 %collective-permute-start.19 = (bf16[10,1,128,32]{2,3,1,0:T(8,128)(2,1)S(1)}, bf16[10,1,128,32]{2,3,1,0:T(8,128)(2,1)S(1)}, u32[]{:S(2)}, u32[]{:S(2)}) collective-permute-start(bf16[10,1,128,32]{2,3,1,0:T(8,128)(2,1)S(1)} %get-tuple-element.7), channel_id=1, source_target_pairs={{0,1},{1,2},{2,3},{3,4},{4,5},{5,6},{6,7},{7,8},{8,9},{9,10},{10,1... | collective-permute-start | bytes 245768 | tf_op jit(solution)/shard_map/ppermute | solution.py:21
  144.2 5.8 %collective-permute-start.18 = (bf16[10,1,128,32]{2,3,1,0:T(8,128)(2,1)S(1)}, bf16[10,1,128,32]{2,3,1,0:T(8,128)(2,1)S(1)}, u32[]{:S(2)}, u32[]{:S(2)}) collective-permute-start(bf16[10,1,128,32]{2,3,1,0:T(8,128)(2,1)S(1)} %get-tuple-element.6), channel_id=1, source_target_pairs={{1,0},{2,1},{3,2},{4,3},{5,4},{6,5},{7,6},{8,7},{9,8},{10,9},{11,1... | collective-permute-start | bytes 245768 | tf_op jit(solution)/shard_map/ppermute | solution.py:24
  158.2 4.9 %collective-permute-start.20 = (f32[2,2,2,2,2,2,2,2,8,128]{9,8,7,6,5,4,3,2,1,0:T(8,128)}, f32[2,2,2,2,2,2,2,2,8,128]{9,8,7,6,5,4,3,2,1,0:T(8,128)}, u32[]{:S(2)}, u32[]{:S(2)}) collective-permute-start(f32[2,2,2,2,2,2,2,2,8,128]{9,8,7,6,5,4,3,2,1,0:T(8,128)} %dynamic-slice_bitcast_fusion), channel_id=1, source_target_pairs={{0,1},{1,0},{2,3},{3,2},{4,5},{5,4},{6,7},{7,6},{8,9},{9,8},{10,11... | collective-permute-start | bytes 3145736 | tf_op jit(solution)/shard_map/ppermute | solution.py:100
  164.6 1.0 copy-start.1
  165.6 15.3 %collective-permute-start.21 = (f32[2,2,2,2,2,2,2,8,128]{8,7,6,5,4,3,2,1,0:T(8,128)S(1)}, f32[2,2,2,2,2,2,2,8,128]{8,7,6,5,4,3,2,1,0:T(8,128)S(1)}, u32[]{:S(2)}, u32[]{:S(2)}) collective-permute-start(f32[2,2,2,2,2,2,2,8,128]{8,7,6,5,4,3,2,1,0:T(8,128)S(1)} %dynamic-slice_bitcast_fusion.1), channel_id=1, source_target_pairs={{0,2},{1,3},{2,0},{3,1},{4,6},{5,7},{6,4},{7,5},{8,10},{9,11},{10,... | collective-permute-start | bytes 1572872 | tf_op jit(solution)/shard_map/ppermute | solution.py:100
  182.0 53.8 %copy-start.6 = (f32[8,128]{1,0:T(8,128)S(1)}, f32[8,128]{1,0:T(8,128)}, u32[]{:S(2)}) copy-start(f32[8,128]{1,0:T(8,128)} %param.10) | copy-start | bytes 12292
  182.0 9.7 %collective-permute-start.22 = (f32[2,2,2,2,2,2,8,128]{7,6,5,4,3,2,1,0:T(8,128)S(1)}, f32[2,2,2,2,2,2,8,128]{7,6,5,4,3,2,1,0:T(8,128)S(1)}, u32[]{:S(2)}, u32[]{:S(2)}) collective-permute-start(f32[2,2,2,2,2,2,8,128]{7,6,5,4,3,2,1,0:T(8,128)S(1)} %dynamic-slice_bitcast_fusion.2), channel_id=1, source_target_pairs={{0,16},{1,17},{2,18},{3,19},{4,20},{5,21},{6,22},{7,23},{8,24},{9,... | collective-permute-start | bytes 786440 | tf_op jit(solution)/shard_map/ppermute | solution.py:100
  191.8 12.0 %collective-permute-start.23 = (f32[2,2,2,2,2,8,128]{6,5,4,3,2,1,0:T(8,128)S(1)}, f32[2,2,2,2,2,8,128]{6,5,4,3,2,1,0:T(8,128)S(1)}, u32[]{:S(2)}, u32[]{:S(2)}) collective-permute-start(f32[2,2,2,2,2,8,128]{6,5,4,3,2,1,0:T(8,128)S(1)} %dynamic-slice_bitcast_fusion.3), channel_id=1, source_target_pairs={{0,128},{1,129},{2,130},{3,131},{4,132},{5,133},{6,134},{7,135},{8... | collective-permute-start | bytes 393224 | tf_op jit(solution)/shard_map/ppermute | solution.py:100
  (4 other events, 2.7 us)

commit v4 on v3

--- a/solution.py
+++ b/solution.py
@@ -26,18 +26,26 @@
     return block
 
 
-def extend_tile(values):
-    return with_halo(values, ((ROW_AXES, 0), (COL_AXES, 1)), 1)
-
-
-def conv_fwd(values, weights, extend):
-    padded = extend(values)
-    nrow = values.shape[0]
-    ncol = values.shape[1]
-    running = jnp.zeros(values.shape[:3] + (weights.shape[3],), jnp.float32)
+HALO = 4
+
+
+def inside_grid(tile_rows, tile_cols, halo):
+    row_count = lax.axis_size(ROW_AXES)
+    col_count = lax.axis_size(COL_AXES)
+    rows = lax.axis_index(ROW_AXES) * tile_rows - halo + jnp.arange(tile_rows + 2 * halo)
+    cols = lax.axis_index(COL_AXES) * tile_cols - halo + jnp.arange(tile_cols + 2 * halo)
+    row_ok = (rows >= 0) & (rows < row_count * tile_rows)
+    col_ok = (cols >= 0) & (cols < col_count * tile_cols)
+    return (row_ok[:, None] & col_ok[None, :])[:, :, None, None]
+
+
+def conv_valid(values, weights):
+    nrow = values.shape[0] - 2
+    ncol = values.shape[1] - 2
+    running = jnp.zeros((nrow, ncol) + values.shape[2:3] + (weights.shape[3],), jnp.float32)
     for shift_x in range(3):
         for shift_y in range(3):
-            window = padded[shift_x : shift_x + nrow, shift_y : shift_y + ncol]
+            window = values[shift_x : shift_x + nrow, shift_y : shift_y + ncol]
             running = running + jnp.einsum(
                 "xybi,io->xybo",
                 window,
@@ -47,14 +55,13 @@
     return running
 
 
-def conv_back(grads, weights, extend):
-    padded = extend(grads)
-    nrow = grads.shape[0]
-    ncol = grads.shape[1]
-    running = jnp.zeros(grads.shape[:3] + (weights.shape[2],), jnp.float32)
+def convt_valid(grads, weights):
+    nrow = grads.shape[0] - 2
+    ncol = grads.shape[1] - 2
+    running = jnp.zeros((nrow, ncol) + grads.shape[2:3] + (weights.shape[2],), jnp.float32)
     for shift_x in range(3):
         for shift_y in range(3):
-            window = padded[2 - shift_x : 2 - shift_x + nrow, 2 - shift_y : 2 - shift_y + ncol]
+            window = grads[2 - shift_x : 2 - shift_x + nrow, 2 - shift_y : 2 - shift_y + ncol]
             running = running + jnp.einsum(
                 "xybo,io->xybi",
                 window,
@@ -64,17 +71,34 @@
     return running
 
 
-def surrogate(logperm, observed, lift_w, lift_b, w_one, b_one, w_two, b_two, read_w, extend):
-    lifted = (logperm[..., None] * lift_w + lift_b).astype(jnp.bfloat16)
-    hidden_one = jnp.tanh(conv_fwd(lifted, w_one, extend) + b_one).astype(jnp.bfloat16)
-    hidden_two = jnp.tanh(conv_fwd(hidden_one, w_two, extend) + b_two)
+def trim(values, width):
+    return values[width : values.shape[0] - width, width : values.shape[1] - width]
+
+
+def surrogate(logperm, observed, lift_w, lift_b, w_one, b_one, w_two, b_two, read_w):
+    tile_rows, tile_cols, batch_size = logperm.shape
+    both = jnp.concatenate([logperm, observed], axis=-1)
+    wide = with_halo(both, ((ROW_AXES, 0), (COL_AXES, 1)), HALO)
+    field = wide[..., :batch_size]
+    measured = trim(wide[..., batch_size:], 2)
+    mask = inside_grid(tile_rows, tile_cols, HALO)
+    zero = jnp.float32(0.0)
+    lifted = jnp.where(mask, field[..., None] * lift_w + lift_b, zero).astype(jnp.bfloat16)
+    hidden_one = jnp.where(
+        trim(mask, 1), jnp.tanh(conv_valid(lifted, w_one) + b_one), zero
+    ).astype(jnp.bfloat16)
+    hidden_two = jnp.tanh(conv_valid(hidden_one, w_two) + b_two)
     pressure = jnp.sum(hidden_two * read_w, axis=-1)
-    misfit = pressure - observed
-    grad_two = (misfit[..., None] * read_w * (1.0 - hidden_two * hidden_two)).astype(jnp.bfloat16)
-    h_one = hidden_one.astype(jnp.float32)
-    grad_one = (conv_back(grad_two, w_two, extend) * (1.0 - h_one * h_one)).astype(jnp.bfloat16)
-    grad_field = jnp.sum(conv_back(grad_one, w_one, extend) * lift_w, axis=-1)
-    return (pressure, grad_field)
+    misfit = pressure - measured
+    grad_two = jnp.where(
+        trim(mask, 2), misfit[..., None] * read_w * (1.0 - hidden_two * hidden_two), zero
+    ).astype(jnp.bfloat16)
+    h_one = trim(hidden_one, 2).astype(jnp.float32)
+    grad_one = jnp.where(
+        trim(mask, 3), convt_valid(grad_two, w_two) * (1.0 - h_one * h_one), zero
+    ).astype(jnp.bfloat16)
+    grad_field = jnp.sum(convt_valid(grad_one, w_one) * lift_w, axis=-1)
+    return (trim(pressure, 2), grad_field)
 
 
 def bit_order(sizes):
@@ -154,7 +178,7 @@
     )
     logperm = logperm.reshape(tile_rows, tile_cols, batch_size)
     pressure, grad_field = surrogate(
-        logperm, observed, lift_w, lift_b, w_one, b_one, w_two, b_two, read_w, extend_tile
+        logperm, observed, lift_w, lift_b, w_one, b_one, w_two, b_two, read_w
     )
     grad_flat = grad_field.reshape(tile_rows * tile_cols, batch_size)
     projected = lax.dot_general(

time: 240 us -> 200 us (0.83)
  blocking collectives: 64.8 us -> 32.9 us
  starting transfers between devices: 70.9 us -> 42.7 us
  matrix products: 16.6 us -> 32.4 us
  other arithmetic: 5.91 us -> 10.3 us
    all_to_all x1 -> x0, blocking collectives: 31.9 us -> none  [scatter_sum(): data = lax.all_to_all(data, group, 0, 0, tiled=False)]
    ppermute x8 -> x2, starting transfers between devices: 27 us -> 6.05 us  [with_halo(): lax.ppermute(lax.slice_in_dim(block, block.shape[dim] - width, None, axis...]
    dot_general x36, matrix products: 11.9 us -> 27.5 us  [the longest x18 21 us: conv_valid(): jnp.einsum('xybi,io->xybo', window, weights[shift_x, shift_y], preferred_...]
    all_to_all x0 -> x1, waiting for transfers between devices: none -> 13.5 us  [scatter_sum(): data = lax.all_to_all(data, group, 0, 0, tiled=False)]
    ppermute x8 -> x2, waiting for transfers between devices: 19.4 us -> 6.86 us  [with_halo(): lax.ppermute(lax.slice_in_dim(block, 0, width, axis=dim), axis, backward)]
    all_to_all x0 -> x1, starting transfers between devices: none -> 11.8 us  [scatter_sum(): data = lax.all_to_all(data, group, 0, 0, tiled=False)]
    ppermute x8 -> x2, starting transfers between devices: 13 us -> 3.21 us  [with_halo(): lax.ppermute(lax.slice_in_dim(block, 0, width, axis=dim), axis, backward)]
    ppermute x8, starting transfers between devices: 30.9 us -> 21.7 us  [exchange(): return lax.ppermute(values, ALL_AXES, pairs)]
  transfers between devices with their start and end apart: 24 -> 13, of which waited for: 16 -> 11; matrix products, arithmetic and copies ran while one was open for 2% -> 1% of each run, Pallas kernels for 0% -> 0%
where the time goes in v4:
time: 200 us; the launch traced here: 198 us
  waiting for transfers between devices  72.7 us (36%)
  starting transfers between devices  42.7 us (21%)
  blocking collectives  32.9 us (16%)
  matrix products  32.4 us (16%)
  other arithmetic  10.3 us (5%)
  local copies, waits for them, and re-layouts  5.99 us (3%)
    ppermute x8, waiting for transfers between devices, exchange(): return lax.ppermute(values, ALL_AXES, pairs)  52.3 us
    all_to_all x1, blocking collectives, gather_all(): data = lax.all_to_all(data, group, 0, 0, tiled=False)  32.9 us
    ppermute x8, starting transfers between devices, exchange(): return lax.ppermute(values, ALL_AXES, pairs)  21.7 us
    dot_general x18, matrix products, conv_valid(): jnp.einsum('xybi,io->xybo', window, weights[shift_x, shift_y], preferred_...  21 us
    all_to_all x1, waiting for transfers between devices, scatter_sum(): data = lax.all_to_all(data, group, 0, 0, tiled=False)  13.5 us
    all_to_all x1, starting transfers between devices, scatter_sum(): data = lax.all_to_all(data, group, 0, 0, tiled=False)  11.8 us
    ppermute x2, waiting for transfers between devices, with_halo(): lax.ppermute(lax.slice_in_dim(block, 0, width, axis=dim), axis, backward)  6.86 us
    dot_general x18, matrix products, convt_valid(): jnp.einsum('xybo,io->xybi', window, weights[shift_x, shift_y], preferred_...  6.51 us
  transfers between devices with their start and end apart: 13, of which 11 were waited for; matrix products, arithmetic and copies ran while one was open for 1% of the time, Pallas kernels for 0%

profile of v4, /device:TPU:1, one launch (start us, length us, event | category | flops | bytes accessed | tf_op | source)
XLA Modules:
  0.0 198.2 jit_solution(9054319414982488567)
XLA Ops:
  1.4 32.9 %all_to_all.10 = f32[32,8,128]{2,1,0:T(8,128)S(1)} all-to-all(f32[32,8,128]{2,1,0:T(8,128)S(1)} %broadcast_in_dim.75), channel_id=1, replica_groups=mesh['b8'=2,'b7'=2,'b6'=2,'b5'=2,'b4'=2,'b3'=2,'b2'=2,'b1'=2,'b0'=2] {'b..., dimensions={0} | all-to-all | bytes 262144 | tf_op jit(solution)/shard_map/all_to_all | solution.py:155
  34.3 3.9 %collective-permute-start = (f32[2,2,2,2,2,8,128]{6,5,4,3,2,1,0:T(8,128)S(1)}, f32[2,2,2,2,2,8,128]{6,5,4,3,2,1,0:T(8,128)S(1)}, u32[]{:S(2)}, u32[]{:S(2)}) collective-permute-start(f32[2,2,2,2,2,8,128]{6,5,4,3,2,1,0:T(8,128)S(1)} %bitcast.321), channel_id=1, source_target_pairs={{0,128},{1,129},{2,130},{3,131},{4,132},{5,133},{6,134},{7,135},{8... | collective-permute-start | bytes 393224 | tf_op jit(solution)/shard_map/ppermute | solution.py:124
  38.3 6.0 %collective-permute-done = f32[2,2,2,2,2,8,128]{6,5,4,3,2,1,0:T(8,128)S(1)} collective-permute-done((f32[2,2,2,2,2,8,128]{6,5,4,3,2,1,0:T(8,128)S(1)}, f32[2,2,2,2,2,8,128]{6,5,4,3,2,1,0:T(8,128)S(1)}, u32[]{:S(2)}, u32[]{:S(2)}) %collective-permute-start) | collective-permute-done | bytes 131104 | tf_op jit(solution)/shard_map/ppermute | solution.py:124
  44.4 2.2 %collective-permute-start.1 = (f32[2,2,2,2,2,2,8,128]{7,6,5,4,3,2,1,0:T(8,128)S(1)}, f32[2,2,2,2,2,2,8,128]{7,6,5,4,3,2,1,0:T(8,128)S(1)}, u32[]{:S(2)}, u32[]{:S(2)}) collective-permute-start(f32[2,2,2,2,2,2,8,128]{7,6,5,4,3,2,1,0:T(8,128)S(1)} %pad_maximum_fusion.3), channel_id=1, source_target_pairs={{0,16},{1,17},{2,18},{3,19},{4,20},{5,21},{6,22},{7,23},{8,24},{9,... | collective-permute-start | bytes 786440 | tf_op jit(solution)/shard_map/ppermute | solution.py:124
  46.6 6.0 %collective-permute-done.1 = f32[2,2,2,2,2,2,8,128]{7,6,5,4,3,2,1,0:T(8,128)S(1)} collective-permute-done((f32[2,2,2,2,2,2,8,128]{7,6,5,4,3,2,1,0:T(8,128)S(1)}, f32[2,2,2,2,2,2,8,128]{7,6,5,4,3,2,1,0:T(8,128)S(1)}, u32[]{:S(2)}, u32[]{:S(2)}) %collective-permute-start.1) | collective-permute-done | bytes 262176 | tf_op jit(solution)/shard_map/ppermute | solution.py:124
  52.7 2.1 %collective-permute-start.2 = (f32[2,2,2,2,2,2,2,8,128]{8,7,6,5,4,3,2,1,0:T(8,128)S(1)}, f32[2,2,2,2,2,2,2,8,128]{8,7,6,5,4,3,2,1,0:T(8,128)S(1)}, u32[]{:S(2)}, u32[]{:S(2)}) collective-permute-start(f32[2,2,2,2,2,2,2,8,128]{8,7,6,5,4,3,2,1,0:T(8,128)S(1)} %pad_maximum_fusion.2), channel_id=1, source_target_pairs={{0,2},{1,3},{2,0},{3,1},{4,6},{5,7},{6,4},{7,5},{8,10},{9,11},{10,... | collective-permute-start | bytes 1572872 | tf_op jit(solution)/shard_map/ppermute | solution.py:124
  54.9 10.9 %collective-permute-done.2 = f32[2,2,2,2,2,2,2,8,128]{8,7,6,5,4,3,2,1,0:T(8,128)S(1)} collective-permute-done((f32[2,2,2,2,2,2,2,8,128]{8,7,6,5,4,3,2,1,0:T(8,128)S(1)}, f32[2,2,2,2,2,2,2,8,128]{8,7,6,5,4,3,2,1,0:T(8,128)S(1)}, u32[]{:S(2)}, u32[]{:S(2)}) %collective-permute-start.2) | collective-permute-done | bytes 524320 | tf_op jit(solution)/shard_map/ppermute | solution.py:124
  67.0 5.1 %collective-permute-start.3 = (f32[2,2,2,2,2,2,2,2,8,128]{9,8,7,6,5,4,3,2,1,0:T(8,128)}, f32[2,2,2,2,2,2,2,2,8,128]{9,8,7,6,5,4,3,2,1,0:T(8,128)S(1)}, u32[]{:S(2)}, u32[]{:S(2)}) collective-permute-start(f32[2,2,2,2,2,2,2,2,8,128]{9,8,7,6,5,4,3,2,1,0:T(8,128)} %pad_maximum_fusion.1), channel_id=1, source_target_pairs={{0,1},{1,0},{2,3},{3,2},{4,5},{5,4},{6,7},{7,6},{8,9},{9,8},{10,11... | collective-permute-start | bytes 3145736 | tf_op jit(solution)/shard_map/ppermute | solution.py:124
  72.4 2.2 %collective-permute-done.3 = f32[2,2,2,2,2,2,2,2,8,128]{9,8,7,6,5,4,3,2,1,0:T(8,128)S(1)} collective-permute-done((f32[2,2,2,2,2,2,2,2,8,128]{9,8,7,6,5,4,3,2,1,0:T(8,128)}, f32[2,2,2,2,2,2,2,2,8,128]{9,8,7,6,5,4,3,2,1,0:T(8,128)S(1)}, u32[]{:S(2)}, u32[]{:S(2)}) %collective-permute-start.3) | collective-permute-done | bytes 1048608 | tf_op jit(solution)/shard_map/ppermute | solution.py:124
  76.7 2.2 %collective-permute-start.4 = (f32[4,8,256]{2,1,0:T(8,128)S(1)}, f32[4,8,256]{2,1,0:T(8,128)S(1)}, u32[]{:S(2)}, u32[]{:S(2)}) collective-permute-start(f32[4,8,256]{2,1,0:T(8,128)S(1)} %get-tuple-element.12), channel_id=1, source_target_pairs={{0,16},{16,32},{32,48},{48,64},{64,80},{80,96},{96,112},{112,128},... | collective-permute-start | bytes 98312 | tf_op jit(solution)/shard_map/ppermute | solution.py:21
  80.3 3.3 %collective-permute-done.5 = f32[4,8,256]{2,1,0:T(8,128)S(1)} collective-permute-done((f32[4,8,256]{2,1,0:T(8,128)S(1)}, f32[4,8,256]{2,1,0:T(8,128)S(1)}, u32[]{:S(2)}, u32[]{:S(2)}) %collective-permute-start.5) | collective-permute-done | bytes 32800 | tf_op jit(solution)/shard_map/ppermute | solution.py:24
  83.6 3.8 %collective-permute-start.6 = (f32[16,4,256]{2,1,0:T(4,128)S(1)}, f32[16,4,256]{2,1,0:T(4,128)S(1)}, u32[]{:S(2)}, u32[]{:S(2)}) collective-permute-start(f32[16,4,256]{2,1,0:T(4,128)S(1)} %get-tuple-element.10), channel_id=1, source_target_pairs={{0,1},{1,2},{2,3},{3,4},{4,5},{5,6},{6,7},{7,8},{8,9},{9,10},{10,1... | collective-permute-start | bytes 196616 | tf_op jit(solution)/shard_map/ppermute | solution.py:21
  87.4 1.9 collective-permute-start.7
  89.4 3.6 %collective-permute-done.7 = f32[16,4,256]{2,1,0:T(4,128)S(1)} collective-permute-done((f32[16,4,256]{2,1,0:T(4,128)S(1)}, f32[16,4,256]{2,1,0:T(4,128)S(1)}, u32[]{:S(2)}, u32[]{:S(2)}) %collective-permute-start.7) | collective-permute-done | bytes 65568 | tf_op jit(solution)/shard_map/ppermute | solution.py:24
  93.1 2.3 %select_convert_fusion = bf16[16,16,128,32]{2,3,1,0:T(8,128)(2,1)S(1)} fusion(f32[32]{0:T(128)S(1)} %copy-done.8, f32[32]{0:T(128)S(1)} %copy-done.6, f32[16,16,128]{2,1,0:T(8,128)S(1)} %slice.285, pred[16,16]{1,0:T(8,128)(4,1)S(1)} %broadcast_and_fusion), kind=kLoop, calls=%fused_computation.1 | loop fusion | flops 4194304 | bytes 2228736 | tf_op jit(solution)/shard_map/convert_element_type | solution.py:86
  98.5 2.3 %fusion.5 = f32[14,14,128,32]{2,3,1,0:T(8,128)} fusion(bf16[16,16,128,32]{2,3,1,0:T(8,128)(2,1)S(1)} %select_convert_fusion, bf16[3,3,32,32]{3,2,1,0:T(8,128)(2,1)S(1)} %copy-done.4), kind=kOutput, calls=%fused_computation.13 | convolution fusion | flops 51380224 | bytes 4825088 | tf_op jit(solution)/shard_map/xybi,io->xybo/dot_general | solution.py:49
  100.8 2.3 %fusion.7 = f32[14,14,128,32]{2,3,1,0:T(8,128)} fusion(bf16[16,16,128,32]{2,3,1,0:T(8,128)(2,1)S(1)} %select_convert_fusion, bf16[3,3,32,32]{3,2,1,0:T(8,128)(2,1)S(1)} %copy-done.4), kind=kOutput, calls=%fused_computation.15 | convolution fusion | flops 51380224 | bytes 4825088 | tf_op jit(solution)/shard_map/xybi,io->xybo/dot_general | solution.py:49
  103.1 2.3 %fusion.9 = f32[14,14,128,32]{2,3,1,0:T(8,128)} fusion(bf16[16,16,128,32]{2,3,1,0:T(8,128)(2,1)S(1)} %select_convert_fusion, bf16[3,3,32,32]{3,2,1,0:T(8,128)(2,1)S(1)} %copy-done.4), kind=kOutput, calls=%fused_computation.17 | convolution fusion | flops 51380224 | bytes 4825088 | tf_op jit(solution)/shard_map/xybi,io->xybo/dot_general | solution.py:49
  105.4 5.2 %select_convert_fusion.1 = bf16[14,14,128,32]{2,3,1,0:T(8,128)(2,1)S(1)} fusion(f32[14,14,128,32]{2,3,1,0:T(8,128)S(1)} %fusion.1, f32[14,14,128,32]{2,3,1,0:T(8,128)S(1)} %fusion.3, f32[14,14,128,32]{2,3,1,0:T(8,128)} %fusion.5, f32[14,14,128,32]{2,3,1,0:T(8,128)} %fusion.7, f32[14,14,128,32]{2,3,1,0:T(8,128)} %fusion.9, ...), kind=kOutput, calls=%fused_computation.2 | convolution fusion | flops 60211200 | bytes 28912128 | tf_op jit(solution)/shard_map/xybi,io->xybo/dot_general | solution.py:49
  116.7 2.0 select_convert_fusion.2
  125.3 3.4 %convolution_bitcast_fusion = f32[4096,128]{0,1:T(8,128)} fusion(f32[8,8,128]{2,1,0:T(8,128)S(1)} %fusion.18, f32[8,8,4096]{2,1,0:T(8,128)S(1)} %copy-done), kind=kOutput, calls=%fused_computation | convolution fusion | flops 402653184 | bytes 3178496 | tf_op jit(solution)/shard_map/dot_general | solution.py:184
  128.7 1.9 copy.114
  131.7 1.9 collective-permute-start.8
  133.7 3.0 %collective-permute-done.8 = f32[2,2,2,2,2,2,2,2,8,128]{9,8,7,6,5,4,3,2,1,0:T(8,128)} collective-permute-done((f32[2,2,2,2,2,2,2,2,8,128]{9,8,7,6,5,4,3,2,1,0:T(8,128)}, f32[2,2,2,2,2,2,2,2,8,128]{9,8,7,6,5,4,3,2,1,0:T(8,128)}, u32[]{:S(2)}, u32[]{:S(2)}) %collective-permute-start.8) | collective-permute-done | bytes 1048608 | tf_op jit(solution)/shard_map/ppermute | solution.py:124
  139.1 2.0 %collective-permute-start.9 = (f32[2,2,2,2,2,2,2,8,128]{8,7,6,5,4,3,2,1,0:T(8,128)S(1)}, f32[2,2,2,2,2,2,2,8,128]{8,7,6,5,4,3,2,1,0:T(8,128)S(1)}, u32[]{:S(2)}, u32[]{:S(2)}) collective-permute-start(f32[2,2,2,2,2,2,2,8,128]{8,7,6,5,4,3,2,1,0:T(8,128)S(1)} %dynamic-slice_bitcast_fusion.1), channel_id=1, source_target_pairs={{0,2},{1,3},{2,0},{3,1},{4,6},{5,7},{6,4},{7,5},{8,10},{9,11},{10,... | collective-permute-start | bytes 1572872 | tf_op jit(solution)/shard_map/ppermute | solution.py:124
  141.2 13.2 %collective-permute-done.9 = f32[2,2,2,2,2,2,2,8,128]{8,7,6,5,4,3,2,1,0:T(8,128)S(1)} collective-permute-done((f32[2,2,2,2,2,2,2,8,128]{8,7,6,5,4,3,2,1,0:T(8,128)S(1)}, f32[2,2,2,2,2,2,2,8,128]{8,7,6,5,4,3,2,1,0:T(8,128)S(1)}, u32[]{:S(2)}, u32[]{:S(2)}) %collective-permute-start.9) | collective-permute-done | bytes 524320 | tf_op jit(solution)/shard_map/ppermute | solution.py:124
  155.6 2.4 %collective-permute-start.10 = (f32[2,2,2,2,2,2,8,128]{7,6,5,4,3,2,1,0:T(8,128)S(1)}, f32[2,2,2,2,2,2,8,128]{7,6,5,4,3,2,1,0:T(8,128)S(1)}, u32[]{:S(2)}, u32[]{:S(2)}) collective-permute-start(f32[2,2,2,2,2,2,8,128]{7,6,5,4,3,2,1,0:T(8,128)S(1)} %dynamic-slice_bitcast_fusion.2), channel_id=1, source_target_pairs={{0,16},{1,17},{2,18},{3,19},{4,20},{5,21},{6,22},{7,23},{8,24},{9,... | collective-permute-start | bytes 786440 | tf_op jit(solution)/shard_map/ppermute | solution.py:124
  158.0 6.4 %collective-permute-done.10 = f32[2,2,2,2,2,2,8,128]{7,6,5,4,3,2,1,0:T(8,128)S(1)} collective-permute-done((f32[2,2,2,2,2,2,8,128]{7,6,5,4,3,2,1,0:T(8,128)S(1)}, f32[2,2,2,2,2,2,8,128]{7,6,5,4,3,2,1,0:T(8,128)S(1)}, u32[]{:S(2)}, u32[]{:S(2)}) %collective-permute-start.10) | collective-permute-done | bytes 262176 | tf_op jit(solution)/shard_map/ppermute | solution.py:124
  164.4 1.9 collective-permute-start.11
  166.3 4.7 %collective-permute-done.11 = f32[2,2,2,2,2,8,128]{6,5,4,3,2,1,0:T(8,128)S(1)} collective-permute-done((f32[2,2,2,2,2,8,128]{6,5,4,3,2,1,0:T(8,128)S(1)}, f32[2,2,2,2,2,8,128]{6,5,4,3,2,1,0:T(8,128)S(1)}, u32[]{:S(2)}, u32[]{:S(2)}) %collective-permute-start.11) | collective-permute-done | bytes 131104 | tf_op jit(solution)/shard_map/ppermute | solution.py:124
  171.7 11.8 %all-to-all-start.1 = ((f32[32,8,128]{2,1,0:T(8,128)}), f32[32,8,128]{2,1,0:T(8,128)S(1)}, u32[]{:S(2)}, u32[]{:S(2)}) async-start(f32[32,8,128]{2,1,0:T(8,128)} %bitcast.103), calls=%async_computation.1 | async-start | bytes 262144 | tf_op jit(solution)/shard_map/all_to_all | solution.py:143
  184.1 13.5 %all-to-all-done.1 = f32[32,8,128]{2,1,0:T(8,128)S(1)} async-done(((f32[32,8,128]{2,1,0:T(8,128)}), f32[32,8,128]{2,1,0:T(8,128)S(1)}, u32[]{:S(2)}, u32[]{:S(2)}) %all-to-all-start.1) | async-done | bytes 131104 | tf_op jit(solution)/shard_map/all_to_all | solution.py:143
  (90 shorter events, 28.2 us)
Async XLA Ops:
  0.6 74.5 %copy-start = (f32[8,8,4096]{2,1,0:T(8,128)S(1)}, f32[8,8,4096]{2,1,0:T(8,128)}, u32[]{:S(2)}) copy-start(f32[8,8,4096]{2,1,0:T(8,128)} %param.11) | copy-start | bytes 3145732
  34.3 10.0 %collective-permute-start = (f32[2,2,2,2,2,8,128]{6,5,4,3,2,1,0:T(8,128)S(1)}, f32[2,2,2,2,2,8,128]{6,5,4,3,2,1,0:T(8,128)S(1)}, u32[]{:S(2)}, u32[]{:S(2)}) collective-permute-start(f32[2,2,2,2,2,8,128]{6,5,4,3,2,1,0:T(8,128)S(1)} %bitcast.321), channel_id=1, source_target_pairs={{0,128},{1,129},{2,130},{3,131},{4,132},{5,133},{6,134},{7,135},{8... | collective-permute-start | bytes 393224 | tf_op jit(solution)/shard_map/ppermute | solution.py:124
  44.4 8.3 %collective-permute-start.1 = (f32[2,2,2,2,2,2,8,128]{7,6,5,4,3,2,1,0:T(8,128)S(1)}, f32[2,2,2,2,2,2,8,128]{7,6,5,4,3,2,1,0:T(8,128)S(1)}, u32[]{:S(2)}, u32[]{:S(2)}) collective-permute-start(f32[2,2,2,2,2,2,8,128]{7,6,5,4,3,2,1,0:T(8,128)S(1)} %pad_maximum_fusion.3), channel_id=1, source_target_pairs={{0,16},{1,17},{2,18},{3,19},{4,20},{5,21},{6,22},{7,23},{8,24},{9,... | collective-permute-start | bytes 786440 | tf_op jit(solution)/shard_map/ppermute | solution.py:124
  52.7 13.0 %collective-permute-start.2 = (f32[2,2,2,2,2,2,2,8,128]{8,7,6,5,4,3,2,1,0:T(8,128)S(1)}, f32[2,2,2,2,2,2,2,8,128]{8,7,6,5,4,3,2,1,0:T(8,128)S(1)}, u32[]{:S(2)}, u32[]{:S(2)}) collective-permute-start(f32[2,2,2,2,2,2,2,8,128]{8,7,6,5,4,3,2,1,0:T(8,128)S(1)} %pad_maximum_fusion.2), channel_id=1, source_target_pairs={{0,2},{1,3},{2,0},{3,1},{4,6},{5,7},{6,4},{7,5},{8,10},{9,11},{10,... | collective-permute-start | bytes 1572872 | tf_op jit(solution)/shard_map/ppermute | solution.py:124
  67.0 7.6 %collective-permute-start.3 = (f32[2,2,2,2,2,2,2,2,8,128]{9,8,7,6,5,4,3,2,1,0:T(8,128)}, f32[2,2,2,2,2,2,2,2,8,128]{9,8,7,6,5,4,3,2,1,0:T(8,128)S(1)}, u32[]{:S(2)}, u32[]{:S(2)}) collective-permute-start(f32[2,2,2,2,2,2,2,2,8,128]{9,8,7,6,5,4,3,2,1,0:T(8,128)} %pad_maximum_fusion.1), channel_id=1, source_target_pairs={{0,1},{1,0},{2,3},{3,2},{4,5},{5,4},{6,7},{7,6},{8,9},{9,8},{10,11... | collective-permute-start | bytes 3145736 | tf_op jit(solution)/shard_map/ppermute | solution.py:124
  75.1 1.5 copy-start.2
  75.1 18.0 %copy-start.6 = (f32[32]{0:T(128)S(1)}, f32[32]{0:T(128)}, u32[]{:S(2)}) copy-start(f32[32]{0:T(128)} %param.13) | copy-start | bytes 388
  75.1 18.0 %copy-start.8 = (f32[32]{0:T(128)S(1)}, f32[32]{0:T(128)}, u32[]{:S(2)}) copy-start(f32[32]{0:T(128)} %param.14) | copy-start | bytes 388
  76.6 18.8 %copy-start.4 = (bf16[3,3,32,32]{3,2,1,0:T(8,128)(2,1)S(1)}, bf16[3,3,32,32]{3,2,1,0:T(8,128)(2,1)}, u32[]{:S(2)}) copy-start(bf16[3,3,32,32]{3,2,1,0:T(8,128)(2,1)} %param.15) | copy-start | bytes 55300
  76.7 3.6 %collective-permute-start.4 = (f32[4,8,256]{2,1,0:T(8,128)S(1)}, f32[4,8,256]{2,1,0:T(8,128)S(1)}, u32[]{:S(2)}, u32[]{:S(2)}) collective-permute-start(f32[4,8,256]{2,1,0:T(8,128)S(1)} %get-tuple-element.12), channel_id=1, source_target_pairs={{0,16},{16,32},{32,48},{48,64},{64,80},{80,96},{96,112},{112,128},... | collective-permute-start | bytes 98312 | tf_op jit(solution)/shard_map/ppermute | solution.py:21
  78.9 4.7 %collective-permute-start.5 = (f32[4,8,256]{2,1,0:T(8,128)S(1)}, f32[4,8,256]{2,1,0:T(8,128)S(1)}, u32[]{:S(2)}, u32[]{:S(2)}) collective-permute-start(f32[4,8,256]{2,1,0:T(8,128)S(1)} %get-tuple-element.13), channel_id=1, source_target_pairs={{16,0},{32,16},{48,32},{64,48},{80,64},{96,80},{112,96},{128,112},... | collective-permute-start | bytes 98312 | tf_op jit(solution)/shard_map/ppermute | solution.py:24
  83.6 5.8 %collective-permute-start.6 = (f32[16,4,256]{2,1,0:T(4,128)S(1)}, f32[16,4,256]{2,1,0:T(4,128)S(1)}, u32[]{:S(2)}, u32[]{:S(2)}) collective-permute-start(f32[16,4,256]{2,1,0:T(4,128)S(1)} %get-tuple-element.10), channel_id=1, source_target_pairs={{0,1},{1,2},{2,3},{3,4},{4,5},{5,6},{6,7},{7,8},{8,9},{9,10},{10,1... | collective-permute-start | bytes 196616 | tf_op jit(solution)/shard_map/ppermute | solution.py:21
  87.4 5.6 %collective-permute-start.7 = (f32[16,4,256]{2,1,0:T(4,128)S(1)}, f32[16,4,256]{2,1,0:T(4,128)S(1)}, u32[]{:S(2)}, u32[]{:S(2)}) collective-permute-start(f32[16,4,256]{2,1,0:T(4,128)S(1)} %get-tuple-element.11), channel_id=1, source_target_pairs={{1,0},{2,1},{3,2},{4,3},{5,4},{6,5},{7,6},{8,7},{9,8},{10,9},{11,1... | collective-permute-start | bytes 196616 | tf_op jit(solution)/shard_map/ppermute | solution.py:24
  103.1 2.4 %copy-start.9 = (f32[32]{0:T(128)S(1)}, f32[32]{0:T(128)}, u32[]{:S(2)}) copy-start(f32[32]{0:T(128)} %param.16) | copy-start | bytes 388
  105.4 5.2 %copy-start.3 = (bf16[3,3,32,32]{3,2,1,0:T(8,128)(2,1)S(1)}, bf16[3,3,32,32]{3,2,1,0:T(8,128)(2,1)}, u32[]{:S(2)}) copy-start(bf16[3,3,32,32]{3,2,1,0:T(8,128)(2,1)} %param.17) | copy-start | bytes 55300
  114.1 0.7 copy-start.7
  114.1 0.7 copy-start.10
  131.7 4.9 %collective-permute-start.8 = (f32[2,2,2,2,2,2,2,2,8,128]{9,8,7,6,5,4,3,2,1,0:T(8,128)}, f32[2,2,2,2,2,2,2,2,8,128]{9,8,7,6,5,4,3,2,1,0:T(8,128)}, u32[]{:S(2)}, u32[]{:S(2)}) collective-permute-start(f32[2,2,2,2,2,2,2,2,8,128]{9,8,7,6,5,4,3,2,1,0:T(8,128)} %dynamic-slice_bitcast_fusion), channel_id=1, source_target_pairs={{0,1},{1,0},{2,3},{3,2},{4,5},{5,4},{6,7},{7,6},{8,9},{9,8},{10,11... | collective-permute-start | bytes 3145736 | tf_op jit(solution)/shard_map/ppermute | solution.py:124
  138.1 1.0 copy-start.1
  139.1 58.5 %copy-start.5 = (f32[8,128]{1,0:T(8,128)S(1)}, f32[8,128]{1,0:T(8,128)}, u32[]{:S(2)}) copy-start(f32[8,128]{1,0:T(8,128)} %param.10) | copy-start | bytes 12292
  139.1 15.3 %collective-permute-start.9 = (f32[2,2,2,2,2,2,2,8,128]{8,7,6,5,4,3,2,1,0:T(8,128)S(1)}, f32[2,2,2,2,2,2,2,8,128]{8,7,6,5,4,3,2,1,0:T(8,128)S(1)}, u32[]{:S(2)}, u32[]{:S(2)}) collective-permute-start(f32[2,2,2,2,2,2,2,8,128]{8,7,6,5,4,3,2,1,0:T(8,128)S(1)} %dynamic-slice_bitcast_fusion.1), channel_id=1, source_target_pairs={{0,2},{1,3},{2,0},{3,1},{4,6},{5,7},{6,4},{7,5},{8,10},{9,11},{10,... | collective-permute-start | bytes 1572872 | tf_op jit(solution)/shard_map/ppermute | solution.py:124
  155.6 8.8 %collective-permute-start.10 = (f32[2,2,2,2,2,2,8,128]{7,6,5,4,3,2,1,0:T(8,128)S(1)}, f32[2,2,2,2,2,2,8,128]{7,6,5,4,3,2,1,0:T(8,128)S(1)}, u32[]{:S(2)}, u32[]{:S(2)}) collective-permute-start(f32[2,2,2,2,2,2,8,128]{7,6,5,4,3,2,1,0:T(8,128)S(1)} %dynamic-slice_bitcast_fusion.2), channel_id=1, source_target_pairs={{0,16},{1,17},{2,18},{3,19},{4,20},{5,21},{6,22},{7,23},{8,24},{9,... | collective-permute-start | bytes 786440 | tf_op jit(solution)/shard_map/ppermute | solution.py:124
  164.4 6.6 %collective-permute-start.11 = (f32[2,2,2,2,2,8,128]{6,5,4,3,2,1,0:T(8,128)S(1)}, f32[2,2,2,2,2,8,128]{6,5,4,3,2,1,0:T(8,128)S(1)}, u32[]{:S(2)}, u32[]{:S(2)}) collective-permute-start(f32[2,2,2,2,2,8,128]{6,5,4,3,2,1,0:T(8,128)S(1)} %dynamic-slice_bitcast_fusion.3), channel_id=1, source_target_pairs={{0,128},{1,129},{2,130},{3,131},{4,132},{5,133},{6,134},{7,135},{8... | collective-permute-start | bytes 393224 | tf_op jit(solution)/shard_map/ppermute | solution.py:124
  171.7 25.9 %all-to-all-start.1 = ((f32[32,8,128]{2,1,0:T(8,128)}), f32[32,8,128]{2,1,0:T(8,128)S(1)}, u32[]{:S(2)}, u32[]{:S(2)}) async-start(f32[32,8,128]{2,1,0:T(8,128)} %bitcast.103), calls=%async_computation.1 | async-start | bytes 262144 | tf_op jit(solution)/shard_map/all_to_all | solution.py:143

commit v5 on v4

--- a/solution.py
+++ b/solution.py
@@ -39,15 +39,19 @@
     return (row_ok[:, None] & col_ok[None, :])[:, :, None, None]
 
 
+def channels(vector):
+    return vector[:, None]
+
+
 def conv_valid(values, weights):
     nrow = values.shape[0] - 2
     ncol = values.shape[1] - 2
-    running = jnp.zeros((nrow, ncol) + values.shape[2:3] + (weights.shape[3],), jnp.float32)
+    running = jnp.zeros((nrow, ncol, weights.shape[3], values.shape[3]), jnp.float32)
     for shift_x in range(3):
         for shift_y in range(3):
             window = values[shift_x : shift_x + nrow, shift_y : shift_y + ncol]
             running = running + jnp.einsum(
-                "xybi,io->xybo",
+                "xyib,io->xyob",
                 window,
                 weights[shift_x, shift_y],
                 preferred_element_type=jnp.float32,
@@ -58,12 +62,12 @@
 def convt_valid(grads, weights):
     nrow = grads.shape[0] - 2
     ncol = grads.shape[1] - 2
-    running = jnp.zeros((nrow, ncol) + grads.shape[2:3] + (weights.shape[2],), jnp.float32)
+    running = jnp.zeros((nrow, ncol, weights.shape[2], grads.shape[3]), jnp.float32)
     for shift_x in range(3):
         for shift_y in range(3):
             window = grads[2 - shift_x : 2 - shift_x + nrow, 2 - shift_y : 2 - shift_y + ncol]
             running = running + jnp.einsum(
-                "xybo,io->xybi",
+                "xyob,io->xyib",
                 window,
                 weights[shift_x, shift_y],
                 preferred_element_type=jnp.float32,
@@ -83,21 +87,25 @@
     measured = trim(wide[..., batch_size:], 2)
     mask = inside_grid(tile_rows, tile_cols, HALO)
     zero = jnp.float32(0.0)
-    lifted = jnp.where(mask, field[..., None] * lift_w + lift_b, zero).astype(jnp.bfloat16)
+    lifted = jnp.where(
+        mask, field[:, :, None, :] * channels(lift_w) + channels(lift_b), zero
+    ).astype(jnp.bfloat16)
     hidden_one = jnp.where(
-        trim(mask, 1), jnp.tanh(conv_valid(lifted, w_one) + b_one), zero
-    ).astype(jnp.bfloat16)
-    hidden_two = jnp.tanh(conv_valid(hidden_one, w_two) + b_two)
-    pressure = jnp.sum(hidden_two * read_w, axis=-1)
+        trim(mask, 1), jnp.tanh(conv_valid(lifted, w_one) + channels(b_one)), zero
+    ).astype(jnp.bfloat16)
+    hidden_two = jnp.tanh(conv_valid(hidden_one, w_two) + channels(b_two))
+    pressure = jnp.sum(hidden_two * channels(read_w), axis=2)
     misfit = pressure - measured
     grad_two = jnp.where(
-        trim(mask, 2), misfit[..., None] * read_w * (1.0 - hidden_two * hidden_two), zero
+        trim(mask, 2),
+        misfit[:, :, None, :] * channels(read_w) * (1.0 - hidden_two * hidden_two),
+        zero,
     ).astype(jnp.bfloat16)
     h_one = trim(hidden_one, 2).astype(jnp.float32)
     grad_one = jnp.where(
         trim(mask, 3), convt_valid(grad_two, w_two) * (1.0 - h_one * h_one), zero
     ).astype(jnp.bfloat16)
-    grad_field = jnp.sum(convt_valid(grad_one, w_one) * lift_w, axis=-1)
+    grad_field = jnp.sum(convt_valid(grad_one, w_one) * channels(lift_w), axis=2)
     return (trim(pressure, 2), grad_field)
 
 

time: 200 us -> 200 us (level)
  no operation moved by 1% of the time
where the time goes in v5:
time: 200 us; the launch traced here: 198 us
  waiting for transfers between devices  72.7 us (36%)
  starting transfers between devices  42.8 us (21%)
  blocking collectives  32.9 us (16%)
  matrix products  32.4 us (16%)
  other arithmetic  10.3 us (5%)
  local copies, waits for them, and re-layouts  5.99 us (3%)
    ppermute x8, waiting for transfers between devices, exchange(): return lax.ppermute(values, ALL_AXES, pairs)  52.3 us
    all_to_all x1, blocking collectives, gather_all(): data = lax.all_to_all(data, group, 0, 0, tiled=False)  32.9 us
    ppermute x8, starting transfers between devices, exchange(): return lax.ppermute(values, ALL_AXES, pairs)  21.7 us
    dot_general x18, matrix products, conv_valid(): jnp.einsum('xyib,io->xyob', window, weights[shift_x, shift_y], preferred_...  21 us
    all_to_all x1, waiting for transfers between devices, scatter_sum(): data = lax.all_to_all(data, group, 0, 0, tiled=False)  13.5 us
    all_to_all x1, starting transfers between devices, scatter_sum(): data = lax.all_to_all(data, group, 0, 0, tiled=False)  11.8 us
    ppermute x2, waiting for transfers between devices, with_halo(): lax.ppermute(lax.slice_in_dim(block, 0, width, axis=dim), axis, backward)  6.86 us
    dot_general x18, matrix products, convt_valid(): jnp.einsum('xyob,io->xyib', window, weights[shift_x, shift_y], preferred_...  6.51 us
  transfers between devices with their start and end apart: 13, of which 11 were waited for; matrix products, arithmetic and copies ran while one was open for 1% of the time, Pallas kernels for 0%

profile of v5, /device:TPU:1, one launch (start us, length us, event | category | flops | bytes accessed | tf_op | source)
XLA Modules:
  0.0 198.3 jit_solution(11011597745025551138)
XLA Ops:
  1.4 32.9 %all_to_all.10 = f32[32,8,128]{2,1,0:T(8,128)S(1)} all-to-all(f32[32,8,128]{2,1,0:T(8,128)S(1)} %broadcast_in_dim.68), channel_id=1, replica_groups=mesh['b8'=2,'b7'=2,'b6'=2,'b5'=2,'b4'=2,'b3'=2,'b2'=2,'b1'=2,'b0'=2] {'b..., dimensions={0} | all-to-all | bytes 262144 | tf_op jit(solution)/shard_map/all_to_all | solution.py:163
  34.3 3.9 %collective-permute-start = (f32[2,2,2,2,2,8,128]{6,5,4,3,2,1,0:T(8,128)S(1)}, f32[2,2,2,2,2,8,128]{6,5,4,3,2,1,0:T(8,128)S(1)}, u32[]{:S(2)}, u32[]{:S(2)}) collective-permute-start(f32[2,2,2,2,2,8,128]{6,5,4,3,2,1,0:T(8,128)S(1)} %bitcast.335), channel_id=1, source_target_pairs={{0,128},{1,129},{2,130},{3,131},{4,132},{5,133},{6,134},{7,135},{8... | collective-permute-start | bytes 393224 | tf_op jit(solution)/shard_map/ppermute | solution.py:132
  38.3 6.0 %collective-permute-done = f32[2,2,2,2,2,8,128]{6,5,4,3,2,1,0:T(8,128)S(1)} collective-permute-done((f32[2,2,2,2,2,8,128]{6,5,4,3,2,1,0:T(8,128)S(1)}, f32[2,2,2,2,2,8,128]{6,5,4,3,2,1,0:T(8,128)S(1)}, u32[]{:S(2)}, u32[]{:S(2)}) %collective-permute-start) | collective-permute-done | bytes 131104 | tf_op jit(solution)/shard_map/ppermute | solution.py:132
  44.4 2.2 %collective-permute-start.1 = (f32[2,2,2,2,2,2,8,128]{7,6,5,4,3,2,1,0:T(8,128)S(1)}, f32[2,2,2,2,2,2,8,128]{7,6,5,4,3,2,1,0:T(8,128)S(1)}, u32[]{:S(2)}, u32[]{:S(2)}) collective-permute-start(f32[2,2,2,2,2,2,8,128]{7,6,5,4,3,2,1,0:T(8,128)S(1)} %pad_maximum_fusion.3), channel_id=1, source_target_pairs={{0,16},{1,17},{2,18},{3,19},{4,20},{5,21},{6,22},{7,23},{8,24},{9,... | collective-permute-start | bytes 786440 | tf_op jit(solution)/shard_map/ppermute | solution.py:132
  46.6 6.0 %collective-permute-done.1 = f32[2,2,2,2,2,2,8,128]{7,6,5,4,3,2,1,0:T(8,128)S(1)} collective-permute-done((f32[2,2,2,2,2,2,8,128]{7,6,5,4,3,2,1,0:T(8,128)S(1)}, f32[2,2,2,2,2,2,8,128]{7,6,5,4,3,2,1,0:T(8,128)S(1)}, u32[]{:S(2)}, u32[]{:S(2)}) %collective-permute-start.1) | collective-permute-done | bytes 262176 | tf_op jit(solution)/shard_map/ppermute | solution.py:132
  52.7 2.1 %collective-permute-start.2 = (f32[2,2,2,2,2,2,2,8,128]{8,7,6,5,4,3,2,1,0:T(8,128)S(1)}, f32[2,2,2,2,2,2,2,8,128]{8,7,6,5,4,3,2,1,0:T(8,128)S(1)}, u32[]{:S(2)}, u32[]{:S(2)}) collective-permute-start(f32[2,2,2,2,2,2,2,8,128]{8,7,6,5,4,3,2,1,0:T(8,128)S(1)} %pad_maximum_fusion.2), channel_id=1, source_target_pairs={{0,2},{1,3},{2,0},{3,1},{4,6},{5,7},{6,4},{7,5},{8,10},{9,11},{10,... | collective-permute-start | bytes 1572872 | tf_op jit(solution)/shard_map/ppermute | solution.py:132
  54.9 10.9 %collective-permute-done.2 = f32[2,2,2,2,2,2,2,8,128]{8,7,6,5,4,3,2,1,0:T(8,128)S(1)} collective-permute-done((f32[2,2,2,2,2,2,2,8,128]{8,7,6,5,4,3,2,1,0:T(8,128)S(1)}, f32[2,2,2,2,2,2,2,8,128]{8,7,6,5,4,3,2,1,0:T(8,128)S(1)}, u32[]{:S(2)}, u32[]{:S(2)}) %collective-permute-start.2) | collective-permute-done | bytes 524320 | tf_op jit(solution)/shard_map/ppermute | solution.py:132
  67.0 5.1 %collective-permute-start.3 = (f32[2,2,2,2,2,2,2,2,8,128]{9,8,7,6,5,4,3,2,1,0:T(8,128)}, f32[2,2,2,2,2,2,2,2,8,128]{9,8,7,6,5,4,3,2,1,0:T(8,128)S(1)}, u32[]{:S(2)}, u32[]{:S(2)}) collective-permute-start(f32[2,2,2,2,2,2,2,2,8,128]{9,8,7,6,5,4,3,2,1,0:T(8,128)} %pad_maximum_fusion.1), channel_id=1, source_target_pairs={{0,1},{1,0},{2,3},{3,2},{4,5},{5,4},{6,7},{7,6},{8,9},{9,8},{10,11... | collective-permute-start | bytes 3145736 | tf_op jit(solution)/shard_map/ppermute | solution.py:132
  72.4 2.2 %collective-permute-done.3 = f32[2,2,2,2,2,2,2,2,8,128]{9,8,7,6,5,4,3,2,1,0:T(8,128)S(1)} collective-permute-done((f32[2,2,2,2,2,2,2,2,8,128]{9,8,7,6,5,4,3,2,1,0:T(8,128)}, f32[2,2,2,2,2,2,2,2,8,128]{9,8,7,6,5,4,3,2,1,0:T(8,128)S(1)}, u32[]{:S(2)}, u32[]{:S(2)}) %collective-permute-start.3) | collective-permute-done | bytes 1048608 | tf_op jit(solution)/shard_map/ppermute | solution.py:132
  76.7 2.2 %collective-permute-start.4 = (f32[4,8,256]{2,1,0:T(8,128)S(1)}, f32[4,8,256]{2,1,0:T(8,128)S(1)}, u32[]{:S(2)}, u32[]{:S(2)}) collective-permute-start(f32[4,8,256]{2,1,0:T(8,128)S(1)} %get-tuple-element.12), channel_id=1, source_target_pairs={{0,16},{16,32},{32,48},{48,64},{64,80},{80,96},{96,112},{112,128},... | collective-permute-start | bytes 98312 | tf_op jit(solution)/shard_map/ppermute | solution.py:21
  80.3 3.3 %collective-permute-done.5 = f32[4,8,256]{2,1,0:T(8,128)S(1)} collective-permute-done((f32[4,8,256]{2,1,0:T(8,128)S(1)}, f32[4,8,256]{2,1,0:T(8,128)S(1)}, u32[]{:S(2)}, u32[]{:S(2)}) %collective-permute-start.5) | collective-permute-done | bytes 32800 | tf_op jit(solution)/shard_map/ppermute | solution.py:24
  83.6 3.8 %collective-permute-start.6 = (f32[16,4,256]{2,1,0:T(4,128)S(1)}, f32[16,4,256]{2,1,0:T(4,128)S(1)}, u32[]{:S(2)}, u32[]{:S(2)}) collective-permute-start(f32[16,4,256]{2,1,0:T(4,128)S(1)} %get-tuple-element.10), channel_id=1, source_target_pairs={{0,1},{1,2},{2,3},{3,4},{4,5},{5,6},{6,7},{7,8},{8,9},{9,10},{10,1... | collective-permute-start | bytes 196616 | tf_op jit(solution)/shard_map/ppermute | solution.py:21
  87.4 1.9 collective-permute-start.7
  89.4 3.6 %collective-permute-done.7 = f32[16,4,256]{2,1,0:T(4,128)S(1)} collective-permute-done((f32[16,4,256]{2,1,0:T(4,128)S(1)}, f32[16,4,256]{2,1,0:T(4,128)S(1)}, u32[]{:S(2)}, u32[]{:S(2)}) %collective-permute-start.7) | collective-permute-done | bytes 65568 | tf_op jit(solution)/shard_map/ppermute | solution.py:24
  93.1 2.3 %select_convert_fusion = bf16[16,16,32,128]{3,2,1,0:T(8,128)(2,1)S(1)} fusion(f32[32]{0:T(128)S(1)} %copy-done.8, f32[32]{0:T(128)S(1)} %copy-done.6, f32[16,16,128]{2,1,0:T(8,128)S(1)} %slice.285, pred[16,16]{1,0:T(8,128)(4,1)S(1)} %broadcast_and_fusion), kind=kLoop, calls=%fused_computation.1 | loop fusion | flops 4194304 | bytes 2228736 | tf_op jit(solution)/shard_map/convert_element_type | solution.py:92
  98.5 2.3 %fusion.5 = f32[14,14,128,32]{2,3,1,0:T(8,128)} fusion(bf16[16,16,32,128]{3,2,1,0:T(8,128)(2,1)S(1)} %select_convert_fusion, bf16[3,3,32,32]{3,2,1,0:T(8,128)(2,1)S(1)} %copy-done.4), kind=kOutput, calls=%fused_computation.13 | convolution fusion | flops 51380224 | bytes 4825088 | tf_op jit(solution)/shard_map/xyib,io->xyob/dot_general | solution.py:53
  100.8 2.3 %fusion.7 = f32[14,14,128,32]{2,3,1,0:T(8,128)} fusion(bf16[16,16,32,128]{3,2,1,0:T(8,128)(2,1)S(1)} %select_convert_fusion, bf16[3,3,32,32]{3,2,1,0:T(8,128)(2,1)S(1)} %copy-done.4), kind=kOutput, calls=%fused_computation.15 | convolution fusion | flops 51380224 | bytes 4825088 | tf_op jit(solution)/shard_map/xyib,io->xyob/dot_general | solution.py:53
  103.1 2.3 %fusion.9 = f32[14,14,128,32]{2,3,1,0:T(8,128)} fusion(bf16[16,16,32,128]{3,2,1,0:T(8,128)(2,1)S(1)} %select_convert_fusion, bf16[3,3,32,32]{3,2,1,0:T(8,128)(2,1)S(1)} %copy-done.4), kind=kOutput, calls=%fused_computation.17 | convolution fusion | flops 51380224 | bytes 4825088 | tf_op jit(solution)/shard_map/xyib,io->xyob/dot_general | solution.py:53
  105.4 5.3 %fusion.21 = bf16[14,14,32,128]{3,2,1,0:T(8,128)(2,1)S(1)} fusion(f32[32]{0:T(128)S(1)} %copy-done.9, bf16[16,16,32,128]{3,2,1,0:T(8,128)(2,1)S(1)} %select_convert_fusion, f32[14,14,128,32]{2,3,1,0:T(8,128)} %fusion.5, f32[14,14,128,32]{2,3,1,0:T(8,128)} %fusion.7, f32[14,14,128,32]{2,3,1,0:T(8,128)} %fusion.9, f32[14,14,128,32]{2,3,1,0:T(8,128)S(1)} %fusion.11, ...), kind=kOutput, calls=%fused_computation.29 | convolution fusion | flops 60211200 | bytes 28912128 | tf_op jit(solution)/shard_map/xyib,io->xyob/dot_general | solution.py:53
  116.7 2.0 fusion.1
  125.4 3.4 %convolution_bitcast_fusion = f32[4096,128]{0,1:T(8,128)} fusion(f32[8,8,128]{2,1,0:T(8,128)S(1)} %fusion.25, f32[8,8,4096]{2,1,0:T(8,128)S(1)} %copy-done), kind=kOutput, calls=%fused_computation | convolution fusion | flops 402653184 | bytes 3178496 | tf_op jit(solution)/shard_map/dot_general | solution.py:192
  128.8 1.9 copy.114
  131.8 1.9 collective-permute-start.8
  133.7 3.0 %collective-permute-done.8 = f32[2,2,2,2,2,2,2,2,8,128]{9,8,7,6,5,4,3,2,1,0:T(8,128)} collective-permute-done((f32[2,2,2,2,2,2,2,2,8,128]{9,8,7,6,5,4,3,2,1,0:T(8,128)}, f32[2,2,2,2,2,2,2,2,8,128]{9,8,7,6,5,4,3,2,1,0:T(8,128)}, u32[]{:S(2)}, u32[]{:S(2)}) %collective-permute-start.8) | collective-permute-done | bytes 1048608 | tf_op jit(solution)/shard_map/ppermute | solution.py:132
  139.2 2.0 %collective-permute-start.9 = (f32[2,2,2,2,2,2,2,8,128]{8,7,6,5,4,3,2,1,0:T(8,128)S(1)}, f32[2,2,2,2,2,2,2,8,128]{8,7,6,5,4,3,2,1,0:T(8,128)S(1)}, u32[]{:S(2)}, u32[]{:S(2)}) collective-permute-start(f32[2,2,2,2,2,2,2,8,128]{8,7,6,5,4,3,2,1,0:T(8,128)S(1)} %dynamic-slice_bitcast_fusion.1), channel_id=1, source_target_pairs={{0,2},{1,3},{2,0},{3,1},{4,6},{5,7},{6,4},{7,5},{8,10},{9,11},{10,... | collective-permute-start | bytes 1572872 | tf_op jit(solution)/shard_map/ppermute | solution.py:132
  141.2 13.2 %collective-permute-done.9 = f32[2,2,2,2,2,2,2,8,128]{8,7,6,5,4,3,2,1,0:T(8,128)S(1)} collective-permute-done((f32[2,2,2,2,2,2,2,8,128]{8,7,6,5,4,3,2,1,0:T(8,128)S(1)}, f32[2,2,2,2,2,2,2,8,128]{8,7,6,5,4,3,2,1,0:T(8,128)S(1)}, u32[]{:S(2)}, u32[]{:S(2)}) %collective-permute-start.9) | collective-permute-done | bytes 524320 | tf_op jit(solution)/shard_map/ppermute | solution.py:132
  155.6 2.5 %collective-permute-start.10 = (f32[2,2,2,2,2,2,8,128]{7,6,5,4,3,2,1,0:T(8,128)S(1)}, f32[2,2,2,2,2,2,8,128]{7,6,5,4,3,2,1,0:T(8,128)S(1)}, u32[]{:S(2)}, u32[]{:S(2)}) collective-permute-start(f32[2,2,2,2,2,2,8,128]{7,6,5,4,3,2,1,0:T(8,128)S(1)} %dynamic-slice_bitcast_fusion.2), channel_id=1, source_target_pairs={{0,16},{1,17},{2,18},{3,19},{4,20},{5,21},{6,22},{7,23},{8,24},{9,... | collective-permute-start | bytes 786440 | tf_op jit(solution)/shard_map/ppermute | solution.py:132
  158.1 6.3 %collective-permute-done.10 = f32[2,2,2,2,2,2,8,128]{7,6,5,4,3,2,1,0:T(8,128)S(1)} collective-permute-done((f32[2,2,2,2,2,2,8,128]{7,6,5,4,3,2,1,0:T(8,128)S(1)}, f32[2,2,2,2,2,2,8,128]{7,6,5,4,3,2,1,0:T(8,128)S(1)}, u32[]{:S(2)}, u32[]{:S(2)}) %collective-permute-start.10) | collective-permute-done | bytes 262176 | tf_op jit(solution)/shard_map/ppermute | solution.py:132
  164.5 1.9 collective-permute-start.11
  166.4 4.7 %collective-permute-done.11 = f32[2,2,2,2,2,8,128]{6,5,4,3,2,1,0:T(8,128)S(1)} collective-permute-done((f32[2,2,2,2,2,8,128]{6,5,4,3,2,1,0:T(8,128)S(1)}, f32[2,2,2,2,2,8,128]{6,5,4,3,2,1,0:T(8,128)S(1)}, u32[]{:S(2)}, u32[]{:S(2)}) %collective-permute-start.11) | collective-permute-done | bytes 131104 | tf_op jit(solution)/shard_map/ppermute | solution.py:132
  171.7 11.8 %all-to-all-start.1 = ((f32[32,8,128]{2,1,0:T(8,128)}), f32[32,8,128]{2,1,0:T(8,128)S(1)}, u32[]{:S(2)}, u32[]{:S(2)}) async-start(f32[32,8,128]{2,1,0:T(8,128)} %bitcast.106), calls=%async_computation.1 | async-start | bytes 262144 | tf_op jit(solution)/shard_map/all_to_all | solution.py:151
  184.2 13.5 %all-to-all-done.1 = f32[32,8,128]{2,1,0:T(8,128)S(1)} async-done(((f32[32,8,128]{2,1,0:T(8,128)}), f32[32,8,128]{2,1,0:T(8,128)S(1)}, u32[]{:S(2)}, u32[]{:S(2)}) %all-to-all-start.1) | async-done | bytes 131104 | tf_op jit(solution)/shard_map/all_to_all | solution.py:151
  (90 shorter events, 28.2 us)
Async XLA Ops:
  0.6 74.5 %copy-start = (f32[8,8,4096]{2,1,0:T(8,128)S(1)}, f32[8,8,4096]{2,1,0:T(8,128)}, u32[]{:S(2)}) copy-start(f32[8,8,4096]{2,1,0:T(8,128)} %param.11) | copy-start | bytes 3145732
  34.3 10.0 %collective-permute-start = (f32[2,2,2,2,2,8,128]{6,5,4,3,2,1,0:T(8,128)S(1)}, f32[2,2,2,2,2,8,128]{6,5,4,3,2,1,0:T(8,128)S(1)}, u32[]{:S(2)}, u32[]{:S(2)}) collective-permute-start(f32[2,2,2,2,2,8,128]{6,5,4,3,2,1,0:T(8,128)S(1)} %bitcast.335), channel_id=1, source_target_pairs={{0,128},{1,129},{2,130},{3,131},{4,132},{5,133},{6,134},{7,135},{8... | collective-permute-start | bytes 393224 | tf_op jit(solution)/shard_map/ppermute | solution.py:132
  44.4 8.3 %collective-permute-start.1 = (f32[2,2,2,2,2,2,8,128]{7,6,5,4,3,2,1,0:T(8,128)S(1)}, f32[2,2,2,2,2,2,8,128]{7,6,5,4,3,2,1,0:T(8,128)S(1)}, u32[]{:S(2)}, u32[]{:S(2)}) collective-permute-start(f32[2,2,2,2,2,2,8,128]{7,6,5,4,3,2,1,0:T(8,128)S(1)} %pad_maximum_fusion.3), channel_id=1, source_target_pairs={{0,16},{1,17},{2,18},{3,19},{4,20},{5,21},{6,22},{7,23},{8,24},{9,... | collective-permute-start | bytes 786440 | tf_op jit(solution)/shard_map/ppermute | solution.py:132
  52.7 13.0 %collective-permute-start.2 = (f32[2,2,2,2,2,2,2,8,128]{8,7,6,5,4,3,2,1,0:T(8,128)S(1)}, f32[2,2,2,2,2,2,2,8,128]{8,7,6,5,4,3,2,1,0:T(8,128)S(1)}, u32[]{:S(2)}, u32[]{:S(2)}) collective-permute-start(f32[2,2,2,2,2,2,2,8,128]{8,7,6,5,4,3,2,1,0:T(8,128)S(1)} %pad_maximum_fusion.2), channel_id=1, source_target_pairs={{0,2},{1,3},{2,0},{3,1},{4,6},{5,7},{6,4},{7,5},{8,10},{9,11},{10,... | collective-permute-start | bytes 1572872 | tf_op jit(solution)/shard_map/ppermute | solution.py:132
  67.0 7.6 %collective-permute-start.3 = (f32[2,2,2,2,2,2,2,2,8,128]{9,8,7,6,5,4,3,2,1,0:T(8,128)}, f32[2,2,2,2,2,2,2,2,8,128]{9,8,7,6,5,4,3,2,1,0:T(8,128)S(1)}, u32[]{:S(2)}, u32[]{:S(2)}) collective-permute-start(f32[2,2,2,2,2,2,2,2,8,128]{9,8,7,6,5,4,3,2,1,0:T(8,128)} %pad_maximum_fusion.1), channel_id=1, source_target_pairs={{0,1},{1,0},{2,3},{3,2},{4,5},{5,4},{6,7},{7,6},{8,9},{9,8},{10,11... | collective-permute-start | bytes 3145736 | tf_op jit(solution)/shard_map/ppermute | solution.py:132
  75.1 1.5 copy-start.2
  75.1 18.0 %copy-start.6 = (f32[32]{0:T(128)S(1)}, f32[32]{0:T(128)}, u32[]{:S(2)}) copy-start(f32[32]{0:T(128)} %param.13) | copy-start | bytes 388
  75.1 18.0 %copy-start.8 = (f32[32]{0:T(128)S(1)}, f32[32]{0:T(128)}, u32[]{:S(2)}) copy-start(f32[32]{0:T(128)} %param.14) | copy-start | bytes 388
  76.6 18.8 %copy-start.4 = (bf16[3,3,32,32]{3,2,1,0:T(8,128)(2,1)S(1)}, bf16[3,3,32,32]{3,2,1,0:T(8,128)(2,1)}, u32[]{:S(2)}) copy-start(bf16[3,3,32,32]{3,2,1,0:T(8,128)(2,1)} %param.15) | copy-start | bytes 55300
  76.7 3.6 %collective-permute-start.4 = (f32[4,8,256]{2,1,0:T(8,128)S(1)}, f32[4,8,256]{2,1,0:T(8,128)S(1)}, u32[]{:S(2)}, u32[]{:S(2)}) collective-permute-start(f32[4,8,256]{2,1,0:T(8,128)S(1)} %get-tuple-element.12), channel_id=1, source_target_pairs={{0,16},{16,32},{32,48},{48,64},{64,80},{80,96},{96,112},{112,128},... | collective-permute-start | bytes 98312 | tf_op jit(solution)/shard_map/ppermute | solution.py:21
  78.9 4.7 %collective-permute-start.5 = (f32[4,8,256]{2,1,0:T(8,128)S(1)}, f32[4,8,256]{2,1,0:T(8,128)S(1)}, u32[]{:S(2)}, u32[]{:S(2)}) collective-permute-start(f32[4,8,256]{2,1,0:T(8,128)S(1)} %get-tuple-element.13), channel_id=1, source_target_pairs={{16,0},{32,16},{48,32},{64,48},{80,64},{96,80},{112,96},{128,112},... | collective-permute-start | bytes 98312 | tf_op jit(solution)/shard_map/ppermute | solution.py:24
  83.6 5.8 %collective-permute-start.6 = (f32[16,4,256]{2,1,0:T(4,128)S(1)}, f32[16,4,256]{2,1,0:T(4,128)S(1)}, u32[]{:S(2)}, u32[]{:S(2)}) collective-permute-start(f32[16,4,256]{2,1,0:T(4,128)S(1)} %get-tuple-element.10), channel_id=1, source_target_pairs={{0,1},{1,2},{2,3},{3,4},{4,5},{5,6},{6,7},{7,8},{8,9},{9,10},{10,1... | collective-permute-start | bytes 196616 | tf_op jit(solution)/shard_map/ppermute | solution.py:21
  87.4 5.6 %collective-permute-start.7 = (f32[16,4,256]{2,1,0:T(4,128)S(1)}, f32[16,4,256]{2,1,0:T(4,128)S(1)}, u32[]{:S(2)}, u32[]{:S(2)}) collective-permute-start(f32[16,4,256]{2,1,0:T(4,128)S(1)} %get-tuple-element.11), channel_id=1, source_target_pairs={{1,0},{2,1},{3,2},{4,3},{5,4},{6,5},{7,6},{8,7},{9,8},{10,9},{11,1... | collective-permute-start | bytes 196616 | tf_op jit(solution)/shard_map/ppermute | solution.py:24
  103.1 2.4 %copy-start.9 = (f32[32]{0:T(128)S(1)}, f32[32]{0:T(128)}, u32[]{:S(2)}) copy-start(f32[32]{0:T(128)} %param.16) | copy-start | bytes 388
  105.4 5.3 %copy-start.3 = (bf16[3,3,32,32]{3,2,1,0:T(8,128)(2,1)S(1)}, bf16[3,3,32,32]{3,2,1,0:T(8,128)(2,1)}, u32[]{:S(2)}) copy-start(bf16[3,3,32,32]{3,2,1,0:T(8,128)(2,1)} %param.17) | copy-start | bytes 55300
  114.2 0.7 copy-start.7
  114.2 0.7 copy-start.10
  131.8 4.9 %collective-permute-start.8 = (f32[2,2,2,2,2,2,2,2,8,128]{9,8,7,6,5,4,3,2,1,0:T(8,128)}, f32[2,2,2,2,2,2,2,2,8,128]{9,8,7,6,5,4,3,2,1,0:T(8,128)}, u32[]{:S(2)}, u32[]{:S(2)}) collective-permute-start(f32[2,2,2,2,2,2,2,2,8,128]{9,8,7,6,5,4,3,2,1,0:T(8,128)} %dynamic-slice_bitcast_fusion), channel_id=1, source_target_pairs={{0,1},{1,0},{2,3},{3,2},{4,5},{5,4},{6,7},{7,6},{8,9},{9,8},{10,11... | collective-permute-start | bytes 3145736 | tf_op jit(solution)/shard_map/ppermute | solution.py:132
  138.1 1.0 copy-start.1
  139.2 58.5 %copy-start.5 = (f32[8,128]{1,0:T(8,128)S(1)}, f32[8,128]{1,0:T(8,128)}, u32[]{:S(2)}) copy-start(f32[8,128]{1,0:T(8,128)} %param.10) | copy-start | bytes 12292
  139.2 15.3 %collective-permute-start.9 = (f32[2,2,2,2,2,2,2,8,128]{8,7,6,5,4,3,2,1,0:T(8,128)S(1)}, f32[2,2,2,2,2,2,2,8,128]{8,7,6,5,4,3,2,1,0:T(8,128)S(1)}, u32[]{:S(2)}, u32[]{:S(2)}) collective-permute-start(f32[2,2,2,2,2,2,2,8,128]{8,7,6,5,4,3,2,1,0:T(8,128)S(1)} %dynamic-slice_bitcast_fusion.1), channel_id=1, source_target_pairs={{0,2},{1,3},{2,0},{3,1},{4,6},{5,7},{6,4},{7,5},{8,10},{9,11},{10,... | collective-permute-start | bytes 1572872 | tf_op jit(solution)/shard_map/ppermute | solution.py:132
  155.6 8.8 %collective-permute-start.10 = (f32[2,2,2,2,2,2,8,128]{7,6,5,4,3,2,1,0:T(8,128)S(1)}, f32[2,2,2,2,2,2,8,128]{7,6,5,4,3,2,1,0:T(8,128)S(1)}, u32[]{:S(2)}, u32[]{:S(2)}) collective-permute-start(f32[2,2,2,2,2,2,8,128]{7,6,5,4,3,2,1,0:T(8,128)S(1)} %dynamic-slice_bitcast_fusion.2), channel_id=1, source_target_pairs={{0,16},{1,17},{2,18},{3,19},{4,20},{5,21},{6,22},{7,23},{8,24},{9,... | collective-permute-start | bytes 786440 | tf_op jit(solution)/shard_map/ppermute | solution.py:132
  164.5 6.6 %collective-permute-start.11 = (f32[2,2,2,2,2,8,128]{6,5,4,3,2,1,0:T(8,128)S(1)}, f32[2,2,2,2,2,8,128]{6,5,4,3,2,1,0:T(8,128)S(1)}, u32[]{:S(2)}, u32[]{:S(2)}) collective-permute-start(f32[2,2,2,2,2,8,128]{6,5,4,3,2,1,0:T(8,128)S(1)} %dynamic-slice_bitcast_fusion.3), channel_id=1, source_target_pairs={{0,128},{1,129},{2,130},{3,131},{4,132},{5,133},{6,134},{7,135},{8... | collective-permute-start | bytes 393224 | tf_op jit(solution)/shard_map/ppermute | solution.py:132
  171.7 25.9 %all-to-all-start.1 = ((f32[32,8,128]{2,1,0:T(8,128)}), f32[32,8,128]{2,1,0:T(8,128)S(1)}, u32[]{:S(2)}, u32[]{:S(2)}) async-start(f32[32,8,128]{2,1,0:T(8,128)} %bitcast.106), calls=%async_computation.1 | async-start | bytes 262144 | tf_op jit(solution)/shard_map/all_to_all | solution.py:151

commit v6 on v5

--- a/solution.py
+++ b/solution.py
@@ -44,35 +44,25 @@
 
 
 def conv_valid(values, weights):
-    nrow = values.shape[0] - 2
-    ncol = values.shape[1] - 2
-    running = jnp.zeros((nrow, ncol, weights.shape[3], values.shape[3]), jnp.float32)
-    for shift_x in range(3):
-        for shift_y in range(3):
-            window = values[shift_x : shift_x + nrow, shift_y : shift_y + ncol]
-            running = running + jnp.einsum(
-                "xyib,io->xyob",
-                window,
-                weights[shift_x, shift_y],
-                preferred_element_type=jnp.float32,
-            )
-    return running
+    return lax.conv_general_dilated(
+        values,
+        weights,
+        (1, 1),
+        "VALID",
+        dimension_numbers=("HWCN", "HWIO", "HWCN"),
+        preferred_element_type=jnp.float32,
+    )
 
 
 def convt_valid(grads, weights):
-    nrow = grads.shape[0] - 2
-    ncol = grads.shape[1] - 2
-    running = jnp.zeros((nrow, ncol, weights.shape[2], grads.shape[3]), jnp.float32)
-    for shift_x in range(3):
-        for shift_y in range(3):
-            window = grads[2 - shift_x : 2 - shift_x + nrow, 2 - shift_y : 2 - shift_y + ncol]
-            running = running + jnp.einsum(
-                "xyob,io->xyib",
-                window,
-                weights[shift_x, shift_y],
-                preferred_element_type=jnp.float32,
-            )
-    return running
+    return lax.conv_general_dilated(
+        grads,
+        jnp.flip(weights, (0, 1)),
+        (1, 1),
+        "VALID",
+        dimension_numbers=("HWCN", "HWOI", "HWCN"),
+        preferred_element_type=jnp.float32,
+    )
 
 
 def trim(values, width):

time: 200 us -> 178 us (0.89)
  matrix products: 32.4 us -> 15.4 us
  other arithmetic: 10.3 us -> 6.03 us
    dot_general x36 -> x0, matrix products: 27.5 us -> none  [the longest x18 21 us: conv_valid(): jnp.einsum('xyib,io->xyob', window, weights[shift_x, shift_y], preferred_...]
    conv_general_dilated x0 -> x3, matrix products: none -> 10.7 us  [the longest x2 6.65 us: conv_valid(): lax.conv_general_dilated(values, weights, (1, 1), 'VALID', dimension_numb...]
    convert_element_type x2 -> x0, other arithmetic: 4.28 us -> none  [the longest x1 2.32 us: surrogate(): lifted = jnp.where(mask, field[:, :, None, :] * channels(lift_w) + channe...]
where the time goes in v6:
time: 178 us; the launch traced here: 177 us
  waiting for transfers between devices  72.9 us (41%)
  starting transfers between devices  42.6 us (24%)
  blocking collectives  32.9 us (18%)
  matrix products  15.4 us (9%)
  other arithmetic  6.03 us (3%)
  local copies, waits for them, and re-layouts  5.84 us (3%)
    ppermute x8, waiting for transfers between devices, exchange(): return lax.ppermute(values, ALL_AXES, pairs)  52.4 us
    all_to_all x1, blocking collectives, gather_all(): data = lax.all_to_all(data, group, 0, 0, tiled=False)  32.9 us
    ppermute x8, starting transfers between devices, exchange(): return lax.ppermute(values, ALL_AXES, pairs)  21.6 us
    all_to_all x1, waiting for transfers between devices, scatter_sum(): data = lax.all_to_all(data, group, 0, 0, tiled=False)  13.6 us
    all_to_all x1, starting transfers between devices, scatter_sum(): data = lax.all_to_all(data, group, 0, 0, tiled=False)  11.8 us
    ppermute x2, waiting for transfers between devices, with_halo(): lax.ppermute(lax.slice_in_dim(block, 0, width, axis=dim), axis, backward)  6.86 us
    conv_general_dilated x2, matrix products, conv_valid(): lax.conv_general_dilated(values, weights, (1, 1), 'VALID', dimension_numb...  6.65 us
    ppermute x2, starting transfers between devices, with_halo(): lax.ppermute(lax.slice_in_dim(block, block.shape[dim] - width, None, axis...  6.05 us
  transfers between devices with their start and end apart: 13, of which 11 were waited for; matrix products, arithmetic and copies ran while one was open for 1% of the time, Pallas kernels for 0%

profile of v6, /device:TPU:1, one launch (start us, length us, event | category | flops | bytes accessed | tf_op | source)
XLA Modules:
  0.0 176.8 jit_solution(14328961728055410083)
XLA Ops:
  1.4 32.9 %all_to_all.10 = f32[32,8,128]{2,1,0:T(8,128)S(1)} all-to-all(f32[32,8,128]{2,1,0:T(8,128)S(1)} %broadcast_in_dim.68), channel_id=1, replica_groups=mesh['b8'=2,'b7'=2,'b6'=2,'b5'=2,'b4'=2,'b3'=2,'b2'=2,'b1'=2,'b0'=2] {'b..., dimensions={0} | all-to-all | bytes 262144 | tf_op jit(solution)/shard_map/all_to_all | solution.py:153
  34.3 3.9 %collective-permute-start = (f32[2,2,2,2,2,8,128]{6,5,4,3,2,1,0:T(8,128)S(1)}, f32[2,2,2,2,2,8,128]{6,5,4,3,2,1,0:T(8,128)S(1)}, u32[]{:S(2)}, u32[]{:S(2)}) collective-permute-start(f32[2,2,2,2,2,8,128]{6,5,4,3,2,1,0:T(8,128)S(1)} %bitcast.72), channel_id=1, source_target_pairs={{0,128},{1,129},{2,130},{3,131},{4,132},{5,133},{6,134},{7,135},{8... | collective-permute-start | bytes 393224 | tf_op jit(solution)/shard_map/ppermute | solution.py:122
  38.3 6.0 %collective-permute-done = f32[2,2,2,2,2,8,128]{6,5,4,3,2,1,0:T(8,128)S(1)} collective-permute-done((f32[2,2,2,2,2,8,128]{6,5,4,3,2,1,0:T(8,128)S(1)}, f32[2,2,2,2,2,8,128]{6,5,4,3,2,1,0:T(8,128)S(1)}, u32[]{:S(2)}, u32[]{:S(2)}) %collective-permute-start) | collective-permute-done | bytes 131104 | tf_op jit(solution)/shard_map/ppermute | solution.py:122
  44.4 2.2 %collective-permute-start.1 = (f32[2,2,2,2,2,2,8,128]{7,6,5,4,3,2,1,0:T(8,128)S(1)}, f32[2,2,2,2,2,2,8,128]{7,6,5,4,3,2,1,0:T(8,128)S(1)}, u32[]{:S(2)}, u32[]{:S(2)}) collective-permute-start(f32[2,2,2,2,2,2,8,128]{7,6,5,4,3,2,1,0:T(8,128)S(1)} %pad_maximum_fusion.3), channel_id=1, source_target_pairs={{0,16},{1,17},{2,18},{3,19},{4,20},{5,21},{6,22},{7,23},{8,24},{9,... | collective-permute-start | bytes 786440 | tf_op jit(solution)/shard_map/ppermute | solution.py:122
  46.6 6.0 %collective-permute-done.1 = f32[2,2,2,2,2,2,8,128]{7,6,5,4,3,2,1,0:T(8,128)S(1)} collective-permute-done((f32[2,2,2,2,2,2,8,128]{7,6,5,4,3,2,1,0:T(8,128)S(1)}, f32[2,2,2,2,2,2,8,128]{7,6,5,4,3,2,1,0:T(8,128)S(1)}, u32[]{:S(2)}, u32[]{:S(2)}) %collective-permute-start.1) | collective-permute-done | bytes 262176 | tf_op jit(solution)/shard_map/ppermute | solution.py:122
  52.7 2.1 %collective-permute-start.2 = (f32[2,2,2,2,2,2,2,8,128]{8,7,6,5,4,3,2,1,0:T(8,128)S(1)}, f32[2,2,2,2,2,2,2,8,128]{8,7,6,5,4,3,2,1,0:T(8,128)S(1)}, u32[]{:S(2)}, u32[]{:S(2)}) collective-permute-start(f32[2,2,2,2,2,2,2,8,128]{8,7,6,5,4,3,2,1,0:T(8,128)S(1)} %pad_maximum_fusion.2), channel_id=1, source_target_pairs={{0,2},{1,3},{2,0},{3,1},{4,6},{5,7},{6,4},{7,5},{8,10},{9,11},{10,... | collective-permute-start | bytes 1572872 | tf_op jit(solution)/shard_map/ppermute | solution.py:122
  54.9 10.9 %collective-permute-done.2 = f32[2,2,2,2,2,2,2,8,128]{8,7,6,5,4,3,2,1,0:T(8,128)S(1)} collective-permute-done((f32[2,2,2,2,2,2,2,8,128]{8,7,6,5,4,3,2,1,0:T(8,128)S(1)}, f32[2,2,2,2,2,2,2,8,128]{8,7,6,5,4,3,2,1,0:T(8,128)S(1)}, u32[]{:S(2)}, u32[]{:S(2)}) %collective-permute-start.2) | collective-permute-done | bytes 524320 | tf_op jit(solution)/shard_map/ppermute | solution.py:122
  67.0 5.1 %collective-permute-start.3 = (f32[2,2,2,2,2,2,2,2,8,128]{9,8,7,6,5,4,3,2,1,0:T(8,128)}, f32[2,2,2,2,2,2,2,2,8,128]{9,8,7,6,5,4,3,2,1,0:T(8,128)S(1)}, u32[]{:S(2)}, u32[]{:S(2)}) collective-permute-start(f32[2,2,2,2,2,2,2,2,8,128]{9,8,7,6,5,4,3,2,1,0:T(8,128)} %pad_maximum_fusion.1), channel_id=1, source_target_pairs={{0,1},{1,0},{2,3},{3,2},{4,5},{5,4},{6,7},{7,6},{8,9},{9,8},{10,11... | collective-permute-start | bytes 3145736 | tf_op jit(solution)/shard_map/ppermute | solution.py:122
  72.4 2.2 %collective-permute-done.3 = f32[2,2,2,2,2,2,2,2,8,128]{9,8,7,6,5,4,3,2,1,0:T(8,128)S(1)} collective-permute-done((f32[2,2,2,2,2,2,2,2,8,128]{9,8,7,6,5,4,3,2,1,0:T(8,128)}, f32[2,2,2,2,2,2,2,2,8,128]{9,8,7,6,5,4,3,2,1,0:T(8,128)S(1)}, u32[]{:S(2)}, u32[]{:S(2)}) %collective-permute-start.3) | collective-permute-done | bytes 1048608 | tf_op jit(solution)/shard_map/ppermute | solution.py:122
  75.2 1.5 convolution_bitcast_fusion.1
  76.7 2.2 %collective-permute-start.4 = (f32[4,8,256]{2,1,0:T(8,128)S(1)}, f32[4,8,256]{2,1,0:T(8,128)S(1)}, u32[]{:S(2)}, u32[]{:S(2)}) collective-permute-start(f32[4,8,256]{2,1,0:T(8,128)S(1)} %get-tuple-element.12), channel_id=1, source_target_pairs={{0,16},{16,32},{32,48},{48,64},{64,80},{80,96},{96,112},{112,128},... | collective-permute-start | bytes 98312 | tf_op jit(solution)/shard_map/ppermute | solution.py:21
  78.9 1.3 collective-permute-start.5
  80.3 3.3 %collective-permute-done.5 = f32[4,8,256]{2,1,0:T(8,128)S(1)} collective-permute-done((f32[4,8,256]{2,1,0:T(8,128)S(1)}, f32[4,8,256]{2,1,0:T(8,128)S(1)}, u32[]{:S(2)}, u32[]{:S(2)}) %collective-permute-start.5) | collective-permute-done | bytes 32800 | tf_op jit(solution)/shard_map/ppermute | solution.py:24
  83.6 3.8 %collective-permute-start.6 = (f32[16,4,256]{2,1,0:T(4,128)S(1)}, f32[16,4,256]{2,1,0:T(4,128)S(1)}, u32[]{:S(2)}, u32[]{:S(2)}) collective-permute-start(f32[16,4,256]{2,1,0:T(4,128)S(1)} %get-tuple-element.10), channel_id=1, source_target_pairs={{0,1},{1,2},{2,3},{3,4},{4,5},{5,6},{6,7},{7,8},{8,9},{9,10},{10,1... | collective-permute-start | bytes 196616 | tf_op jit(solution)/shard_map/ppermute | solution.py:21
  87.5 1.9 %collective-permute-start.7 = (f32[16,4,256]{2,1,0:T(4,128)S(1)}, f32[16,4,256]{2,1,0:T(4,128)S(1)}, u32[]{:S(2)}, u32[]{:S(2)}) collective-permute-start(f32[16,4,256]{2,1,0:T(4,128)S(1)} %get-tuple-element.11), channel_id=1, source_target_pairs={{1,0},{2,1},{3,2},{4,3},{5,4},{6,5},{7,6},{8,7},{9,8},{10,9},{11,1... | collective-permute-start | bytes 196616 | tf_op jit(solution)/shard_map/ppermute | solution.py:24
  89.5 3.6 %collective-permute-done.7 = f32[16,4,256]{2,1,0:T(4,128)S(1)} collective-permute-done((f32[16,4,256]{2,1,0:T(4,128)S(1)}, f32[16,4,256]{2,1,0:T(4,128)S(1)}, u32[]{:S(2)}, u32[]{:S(2)}) %collective-permute-start.7) | collective-permute-done | bytes 65568 | tf_op jit(solution)/shard_map/ppermute | solution.py:24
  93.2 3.1 %select_convert_fusion.1 = bf16[14,14,32,128]{3,2,1,0:T(8,128)(2,1)S(1)} fusion(f32[32]{0:T(128)S(1)} %copy-done.6, pred[14,14]{1,0:T(8,128)(4,1)S(1)} %slice_bitcast_fusion.2, bf16[3,3,32,32]{3,2,1,0:T(8,128)(2,1)S(1)} %copy-done.4, f32[32]{0:T(128)S(1)} %copy-done.7, f32[32]{0:T(128)S(1)} %copy-done.10, f32[16,16,128]{2,1,0:T(8,128)S(1)} %slice.51, ...), kind=kOutput, calls=%fused_computation.2 | convolution fusion | flops 469024768 | bytes 1755972 | tf_op jit(solution)/shard_map/conv_general_dilated | solution.py:47
  96.4 3.5 %multiply_reduce_fusion = (f32[12,12,128]{2,1,0:T(8,128)S(1)}, f32[12,12,32,128]{3,2,1,0:T(8,128)}) fusion(f32[32]{0:T(128)S(1)} %copy-done.8, f32[32]{0:T(128)S(1)} %copy-done.9, bf16[14,14,32,128]{3,2,1,0:T(8,128)(2,1)S(1)} %select_convert_fusion.1, bf16[3,3,32,32]{3,2,1,0:T(8,128)(2,1)S(1)} %copy-done.5), kind=kOutput, calls=%fused_computation.4 | convolution fusion | flops 341489664 | bytes 4057344 | tf_op jit(solution)/shard_map/conv_general_dilated | solution.py:47
  99.9 4.1 %fusion.6 = f32[8,8,128]{2,1,0:T(8,128)S(1)} fusion(bf16[3,3,32,32]{3,2,1,0:T(8,128)(2,1)S(1)} %copy-done.4, bf16[3,3,32,32]{3,2,1,0:T(8,128)(2,1)S(1)} %copy-done.5, f32[12,12,32,128]{3,2,1,0:T(8,128)} %get-tuple-element.15, f32[12,12,128]{2,1,0:T(8,128)S(1)} %maximum_subtract_fusion, f32[32]{0:T(128)S(1)} %copy-done.8, f32[32]{0:T(128)S(1)} %copy-done.9, ...), kind=kOutput, calls=%fused_computation.15 | convolution fusion | flops 394027008 | bytes 3462656 | tf_op jit(solution)/shard_map/conv_general_dilated | solution.py:58
  104.0 3.2 %convolution_bitcast_fusion = f32[4096,128]{0,1:T(8,128)} fusion(f32[8,8,128]{2,1,0:T(8,128)S(1)} %fusion.6, f32[8,8,4096]{2,1,0:T(8,128)S(1)} %copy-done), kind=kOutput, calls=%fused_computation | convolution fusion | flops 402653184 | bytes 3178496 | tf_op jit(solution)/shard_map/dot_general | solution.py:182
  107.2 1.9 %copy.19 = f32[4096,128]{1,0:T(8,128)S(1)} copy(f32[4096,128]{0,1:T(8,128)} %convolution_bitcast_fusion) | data formatting | bytes 4194304 | tf_op jit(solution)/shard_map/dot_general | solution.py:182
  110.2 1.9 %collective-permute-start.8 = (f32[2,2,2,2,2,2,2,2,8,128]{9,8,7,6,5,4,3,2,1,0:T(8,128)}, f32[2,2,2,2,2,2,2,2,8,128]{9,8,7,6,5,4,3,2,1,0:T(8,128)}, u32[]{:S(2)}, u32[]{:S(2)}) collective-permute-start(f32[2,2,2,2,2,2,2,2,8,128]{9,8,7,6,5,4,3,2,1,0:T(8,128)} %dynamic-slice_bitcast_fusion), channel_id=1, source_target_pairs={{0,1},{1,0},{2,3},{3,2},{4,5},{5,4},{6,7},{7,6},{8,9},{9,8},{10,11... | collective-permute-start | bytes 3145736 | tf_op jit(solution)/shard_map/ppermute | solution.py:122
  112.1 3.0 %collective-permute-done.8 = f32[2,2,2,2,2,2,2,2,8,128]{9,8,7,6,5,4,3,2,1,0:T(8,128)} collective-permute-done((f32[2,2,2,2,2,2,2,2,8,128]{9,8,7,6,5,4,3,2,1,0:T(8,128)}, f32[2,2,2,2,2,2,2,2,8,128]{9,8,7,6,5,4,3,2,1,0:T(8,128)}, u32[]{:S(2)}, u32[]{:S(2)}) %collective-permute-start.8) | collective-permute-done | bytes 1048608 | tf_op jit(solution)/shard_map/ppermute | solution.py:122
  115.1 1.4 bitcast_add_fusion
  117.6 2.0 %collective-permute-start.9 = (f32[2,2,2,2,2,2,2,8,128]{8,7,6,5,4,3,2,1,0:T(8,128)S(1)}, f32[2,2,2,2,2,2,2,8,128]{8,7,6,5,4,3,2,1,0:T(8,128)S(1)}, u32[]{:S(2)}, u32[]{:S(2)}) collective-permute-start(f32[2,2,2,2,2,2,2,8,128]{8,7,6,5,4,3,2,1,0:T(8,128)S(1)} %dynamic-slice_bitcast_fusion.1), channel_id=1, source_target_pairs={{0,2},{1,3},{2,0},{3,1},{4,6},{5,7},{6,4},{7,5},{8,10},{9,11},{10,... | collective-permute-start | bytes 1572872 | tf_op jit(solution)/shard_map/ppermute | solution.py:122
  119.6 13.2 %collective-permute-done.9 = f32[2,2,2,2,2,2,2,8,128]{8,7,6,5,4,3,2,1,0:T(8,128)S(1)} collective-permute-done((f32[2,2,2,2,2,2,2,8,128]{8,7,6,5,4,3,2,1,0:T(8,128)S(1)}, f32[2,2,2,2,2,2,2,8,128]{8,7,6,5,4,3,2,1,0:T(8,128)S(1)}, u32[]{:S(2)}, u32[]{:S(2)}) %collective-permute-start.9) | collective-permute-done | bytes 524320 | tf_op jit(solution)/shard_map/ppermute | solution.py:122
  134.0 2.3 %collective-permute-start.10 = (f32[2,2,2,2,2,2,8,128]{7,6,5,4,3,2,1,0:T(8,128)S(1)}, f32[2,2,2,2,2,2,8,128]{7,6,5,4,3,2,1,0:T(8,128)S(1)}, u32[]{:S(2)}, u32[]{:S(2)}) collective-permute-start(f32[2,2,2,2,2,2,8,128]{7,6,5,4,3,2,1,0:T(8,128)S(1)} %dynamic-slice_bitcast_fusion.2), channel_id=1, source_target_pairs={{0,16},{1,17},{2,18},{3,19},{4,20},{5,21},{6,22},{7,23},{8,24},{9,... | collective-permute-start | bytes 786440 | tf_op jit(solution)/shard_map/ppermute | solution.py:122
  136.4 6.5 %collective-permute-done.10 = f32[2,2,2,2,2,2,8,128]{7,6,5,4,3,2,1,0:T(8,128)S(1)} collective-permute-done((f32[2,2,2,2,2,2,8,128]{7,6,5,4,3,2,1,0:T(8,128)S(1)}, f32[2,2,2,2,2,2,8,128]{7,6,5,4,3,2,1,0:T(8,128)S(1)}, u32[]{:S(2)}, u32[]{:S(2)}) %collective-permute-start.10) | collective-permute-done | bytes 262176 | tf_op jit(solution)/shard_map/ppermute | solution.py:122
  142.9 1.9 %collective-permute-start.11 = (f32[2,2,2,2,2,8,128]{6,5,4,3,2,1,0:T(8,128)S(1)}, f32[2,2,2,2,2,8,128]{6,5,4,3,2,1,0:T(8,128)S(1)}, u32[]{:S(2)}, u32[]{:S(2)}) collective-permute-start(f32[2,2,2,2,2,8,128]{6,5,4,3,2,1,0:T(8,128)S(1)} %dynamic-slice_bitcast_fusion.3), channel_id=1, source_target_pairs={{0,128},{1,129},{2,130},{3,131},{4,132},{5,133},{6,134},{7,135},{8... | collective-permute-start | bytes 393224 | tf_op jit(solution)/shard_map/ppermute | solution.py:122
  144.8 4.7 %collective-permute-done.11 = f32[2,2,2,2,2,8,128]{6,5,4,3,2,1,0:T(8,128)S(1)} collective-permute-done((f32[2,2,2,2,2,8,128]{6,5,4,3,2,1,0:T(8,128)S(1)}, f32[2,2,2,2,2,8,128]{6,5,4,3,2,1,0:T(8,128)S(1)}, u32[]{:S(2)}, u32[]{:S(2)}) %collective-permute-start.11) | collective-permute-done | bytes 131104 | tf_op jit(solution)/shard_map/ppermute | solution.py:122
  150.1 11.8 %all-to-all-start.1 = ((f32[32,8,128]{2,1,0:T(8,128)}), f32[32,8,128]{2,1,0:T(8,128)S(1)}, u32[]{:S(2)}, u32[]{:S(2)}) async-start(f32[32,8,128]{2,1,0:T(8,128)} %bitcast.31), calls=%async_computation.1 | async-start | bytes 262144 | tf_op jit(solution)/shard_map/all_to_all | solution.py:141
  162.6 13.6 %all-to-all-done.1 = f32[32,8,128]{2,1,0:T(8,128)S(1)} async-done(((f32[32,8,128]{2,1,0:T(8,128)}), f32[32,8,128]{2,1,0:T(8,128)S(1)}, u32[]{:S(2)}, u32[]{:S(2)}) %all-to-all-start.1) | async-done | bytes 131104 | tf_op jit(solution)/shard_map/all_to_all | solution.py:141
  (55 shorter events, 8.5 us)
Async XLA Ops:
  0.6 74.5 %copy-start = (f32[8,8,4096]{2,1,0:T(8,128)S(1)}, f32[8,8,4096]{2,1,0:T(8,128)}, u32[]{:S(2)}) copy-start(f32[8,8,4096]{2,1,0:T(8,128)} %param.11) | copy-start | bytes 3145732
  34.3 10.0 %collective-permute-start = (f32[2,2,2,2,2,8,128]{6,5,4,3,2,1,0:T(8,128)S(1)}, f32[2,2,2,2,2,8,128]{6,5,4,3,2,1,0:T(8,128)S(1)}, u32[]{:S(2)}, u32[]{:S(2)}) collective-permute-start(f32[2,2,2,2,2,8,128]{6,5,4,3,2,1,0:T(8,128)S(1)} %bitcast.72), channel_id=1, source_target_pairs={{0,128},{1,129},{2,130},{3,131},{4,132},{5,133},{6,134},{7,135},{8... | collective-permute-start | bytes 393224 | tf_op jit(solution)/shard_map/ppermute | solution.py:122
  44.4 8.3 %collective-permute-start.1 = (f32[2,2,2,2,2,2,8,128]{7,6,5,4,3,2,1,0:T(8,128)S(1)}, f32[2,2,2,2,2,2,8,128]{7,6,5,4,3,2,1,0:T(8,128)S(1)}, u32[]{:S(2)}, u32[]{:S(2)}) collective-permute-start(f32[2,2,2,2,2,2,8,128]{7,6,5,4,3,2,1,0:T(8,128)S(1)} %pad_maximum_fusion.3), channel_id=1, source_target_pairs={{0,16},{1,17},{2,18},{3,19},{4,20},{5,21},{6,22},{7,23},{8,24},{9,... | collective-permute-start | bytes 786440 | tf_op jit(solution)/shard_map/ppermute | solution.py:122
  52.7 13.0 %collective-permute-start.2 = (f32[2,2,2,2,2,2,2,8,128]{8,7,6,5,4,3,2,1,0:T(8,128)S(1)}, f32[2,2,2,2,2,2,2,8,128]{8,7,6,5,4,3,2,1,0:T(8,128)S(1)}, u32[]{:S(2)}, u32[]{:S(2)}) collective-permute-start(f32[2,2,2,2,2,2,2,8,128]{8,7,6,5,4,3,2,1,0:T(8,128)S(1)} %pad_maximum_fusion.2), channel_id=1, source_target_pairs={{0,2},{1,3},{2,0},{3,1},{4,6},{5,7},{6,4},{7,5},{8,10},{9,11},{10,... | collective-permute-start | bytes 1572872 | tf_op jit(solution)/shard_map/ppermute | solution.py:122
  67.0 7.6 %collective-permute-start.3 = (f32[2,2,2,2,2,2,2,2,8,128]{9,8,7,6,5,4,3,2,1,0:T(8,128)}, f32[2,2,2,2,2,2,2,2,8,128]{9,8,7,6,5,4,3,2,1,0:T(8,128)S(1)}, u32[]{:S(2)}, u32[]{:S(2)}) collective-permute-start(f32[2,2,2,2,2,2,2,2,8,128]{9,8,7,6,5,4,3,2,1,0:T(8,128)} %pad_maximum_fusion.1), channel_id=1, source_target_pairs={{0,1},{1,0},{2,3},{3,2},{4,5},{5,4},{6,7},{7,6},{8,9},{9,8},{10,11... | collective-permute-start | bytes 3145736 | tf_op jit(solution)/shard_map/ppermute | solution.py:122
  75.1 1.6 copy-start.2
  75.1 18.0 %copy-start.4 = (bf16[3,3,32,32]{3,2,1,0:T(8,128)(2,1)S(1)}, bf16[3,3,32,32]{3,2,1,0:T(8,128)(2,1)}, u32[]{:S(2)}) copy-start(bf16[3,3,32,32]{3,2,1,0:T(8,128)(2,1)} %param.15) | copy-start | bytes 55300
  75.1 18.0 %copy-start.6 = (f32[32]{0:T(128)S(1)}, f32[32]{0:T(128)}, u32[]{:S(2)}) copy-start(f32[32]{0:T(128)} %param.16) | copy-start | bytes 388
  75.1 18.0 %copy-start.7 = (f32[32]{0:T(128)S(1)}, f32[32]{0:T(128)}, u32[]{:S(2)}) copy-start(f32[32]{0:T(128)} %param.14) | copy-start | bytes 388
  75.2 18.0 %copy-start.10 = (f32[32]{0:T(128)S(1)}, f32[32]{0:T(128)}, u32[]{:S(2)}) copy-start(f32[32]{0:T(128)} %param.13) | copy-start | bytes 388
  76.7 3.6 %collective-permute-start.4 = (f32[4,8,256]{2,1,0:T(8,128)S(1)}, f32[4,8,256]{2,1,0:T(8,128)S(1)}, u32[]{:S(2)}, u32[]{:S(2)}) collective-permute-start(f32[4,8,256]{2,1,0:T(8,128)S(1)} %get-tuple-element.12), channel_id=1, source_target_pairs={{0,16},{16,32},{32,48},{48,64},{64,80},{80,96},{96,112},{112,128},... | collective-permute-start | bytes 98312 | tf_op jit(solution)/shard_map/ppermute | solution.py:21
  78.9 4.7 %collective-permute-start.5 = (f32[4,8,256]{2,1,0:T(8,128)S(1)}, f32[4,8,256]{2,1,0:T(8,128)S(1)}, u32[]{:S(2)}, u32[]{:S(2)}) collective-permute-start(f32[4,8,256]{2,1,0:T(8,128)S(1)} %get-tuple-element.13), channel_id=1, source_target_pairs={{16,0},{32,16},{48,32},{64,48},{80,64},{96,80},{112,96},{128,112},... | collective-permute-start | bytes 98312 | tf_op jit(solution)/shard_map/ppermute | solution.py:24
  83.6 5.8 %collective-permute-start.6 = (f32[16,4,256]{2,1,0:T(4,128)S(1)}, f32[16,4,256]{2,1,0:T(4,128)S(1)}, u32[]{:S(2)}, u32[]{:S(2)}) collective-permute-start(f32[16,4,256]{2,1,0:T(4,128)S(1)} %get-tuple-element.10), channel_id=1, source_target_pairs={{0,1},{1,2},{2,3},{3,4},{4,5},{5,6},{6,7},{7,8},{8,9},{9,10},{10,1... | collective-permute-start | bytes 196616 | tf_op jit(solution)/shard_map/ppermute | solution.py:21
  87.5 5.6 %collective-permute-start.7 = (f32[16,4,256]{2,1,0:T(4,128)S(1)}, f32[16,4,256]{2,1,0:T(4,128)S(1)}, u32[]{:S(2)}, u32[]{:S(2)}) collective-permute-start(f32[16,4,256]{2,1,0:T(4,128)S(1)} %get-tuple-element.11), channel_id=1, source_target_pairs={{1,0},{2,1},{3,2},{4,3},{5,4},{6,5},{7,6},{8,7},{9,8},{10,9},{11,1... | collective-permute-start | bytes 196616 | tf_op jit(solution)/shard_map/ppermute | solution.py:24
  93.2 3.2 %copy-start.5 = (bf16[3,3,32,32]{3,2,1,0:T(8,128)(2,1)S(1)}, bf16[3,3,32,32]{3,2,1,0:T(8,128)(2,1)}, u32[]{:S(2)}) copy-start(bf16[3,3,32,32]{3,2,1,0:T(8,128)(2,1)} %param.17) | copy-start | bytes 55300
  93.2 3.2 %copy-start.8 = (f32[32]{0:T(128)S(1)}, f32[32]{0:T(128)}, u32[]{:S(2)}) copy-start(f32[32]{0:T(128)} %param.19) | copy-start | bytes 388
  93.2 3.1 %copy-start.9 = (f32[32]{0:T(128)S(1)}, f32[32]{0:T(128)}, u32[]{:S(2)}) copy-start(f32[32]{0:T(128)} %param.18) | copy-start | bytes 388
  110.2 4.9 %collective-permute-start.8 = (f32[2,2,2,2,2,2,2,2,8,128]{9,8,7,6,5,4,3,2,1,0:T(8,128)}, f32[2,2,2,2,2,2,2,2,8,128]{9,8,7,6,5,4,3,2,1,0:T(8,128)}, u32[]{:S(2)}, u32[]{:S(2)}) collective-permute-start(f32[2,2,2,2,2,2,2,2,8,128]{9,8,7,6,5,4,3,2,1,0:T(8,128)} %dynamic-slice_bitcast_fusion), channel_id=1, source_target_pairs={{0,1},{1,0},{2,3},{3,2},{4,5},{5,4},{6,7},{7,6},{8,9},{9,8},{10,11... | collective-permute-start | bytes 3145736 | tf_op jit(solution)/shard_map/ppermute | solution.py:122
  116.5 1.0 copy-start.1
  117.5 58.6 %copy-start.3 = (f32[8,128]{1,0:T(8,128)S(1)}, f32[8,128]{1,0:T(8,128)}, u32[]{:S(2)}) copy-start(f32[8,128]{1,0:T(8,128)} %param.10) | copy-start | bytes 12292
  117.6 15.3 %collective-permute-start.9 = (f32[2,2,2,2,2,2,2,8,128]{8,7,6,5,4,3,2,1,0:T(8,128)S(1)}, f32[2,2,2,2,2,2,2,8,128]{8,7,6,5,4,3,2,1,0:T(8,128)S(1)}, u32[]{:S(2)}, u32[]{:S(2)}) collective-permute-start(f32[2,2,2,2,2,2,2,8,128]{8,7,6,5,4,3,2,1,0:T(8,128)S(1)} %dynamic-slice_bitcast_fusion.1), channel_id=1, source_target_pairs={{0,2},{1,3},{2,0},{3,1},{4,6},{5,7},{6,4},{7,5},{8,10},{9,11},{10,... | collective-permute-start | bytes 1572872 | tf_op jit(solution)/shard_map/ppermute | solution.py:122
  134.0 8.8 %collective-permute-start.10 = (f32[2,2,2,2,2,2,8,128]{7,6,5,4,3,2,1,0:T(8,128)S(1)}, f32[2,2,2,2,2,2,8,128]{7,6,5,4,3,2,1,0:T(8,128)S(1)}, u32[]{:S(2)}, u32[]{:S(2)}) collective-permute-start(f32[2,2,2,2,2,2,8,128]{7,6,5,4,3,2,1,0:T(8,128)S(1)} %dynamic-slice_bitcast_fusion.2), channel_id=1, source_target_pairs={{0,16},{1,17},{2,18},{3,19},{4,20},{5,21},{6,22},{7,23},{8,24},{9,... | collective-permute-start | bytes 786440 | tf_op jit(solution)/shard_map/ppermute | solution.py:122
  142.9 6.6 %collective-permute-start.11 = (f32[2,2,2,2,2,8,128]{6,5,4,3,2,1,0:T(8,128)S(1)}, f32[2,2,2,2,2,8,128]{6,5,4,3,2,1,0:T(8,128)S(1)}, u32[]{:S(2)}, u32[]{:S(2)}) collective-permute-start(f32[2,2,2,2,2,8,128]{6,5,4,3,2,1,0:T(8,128)S(1)} %dynamic-slice_bitcast_fusion.3), channel_id=1, source_target_pairs={{0,128},{1,129},{2,130},{3,131},{4,132},{5,133},{6,134},{7,135},{8... | collective-permute-start | bytes 393224 | tf_op jit(solution)/shard_map/ppermute | solution.py:122
  150.1 26.0 %all-to-all-start.1 = ((f32[32,8,128]{2,1,0:T(8,128)}), f32[32,8,128]{2,1,0:T(8,128)S(1)}, u32[]{:S(2)}, u32[]{:S(2)}) async-start(f32[32,8,128]{2,1,0:T(8,128)} %bitcast.31), calls=%async_computation.1 | async-start | bytes 262144 | tf_op jit(solution)/shard_map/all_to_all | solution.py:141

commit v7 on v6

--- a/solution.py
+++ b/solution.py
@@ -117,8 +117,14 @@
     return order, low
 
 
-def exchange(values, bit, count):
-    pairs = [(i, i ^ (1 << bit)) for i in range(count)]
+def core_orders(near):
+    swapped = list(near)
+    swapped[1], swapped[2] = near[2], near[1]
+    return (list(near), swapped)
+
+
+def exchange(values, bits, count):
+    pairs = [(i, i ^ (1 << bits[i & 1])) for i in range(count)]
     return lax.ppermute(values, ALL_AXES, pairs)
 
 
@@ -126,16 +132,24 @@
     order, nbits = bit_order(sizes)
     count = 1 << nbits
     me = lax.axis_index(ALL_AXES)
+    first_core = (me & 1) == 0
     data = projected.reshape((2,) * nbits + (mode_block, projected.shape[1]))
-    present = list(range(nbits - 1, -1, -1))
-    near, far = order[: nbits - FAR_COUNT], order[nbits - FAR_COUNT :]
-    for bit in near:
-        dim = present.index(bit)
-        mine = (me >> bit) & 1
-        keep = lax.dynamic_index_in_dim(data, mine, axis=dim, keepdims=False)
-        send = lax.dynamic_index_in_dim(data, 1 - mine, axis=dim, keepdims=False)
-        data = keep + exchange(send, bit, count)
-        present.pop(dim)
+    near = order[: nbits - FAR_COUNT]
+    orders = core_orders(near)
+    presents = [list(range(nbits - 1, -1, -1)) for _ in orders]
+    for step in range(len(near)):
+        bits = [variant[step] for variant in orders]
+        kept, sent = [], []
+        for bit, present in zip(bits, presents):
+            dim = present.index(bit)
+            mine = (me >> bit) & 1
+            kept.append(lax.dynamic_index_in_dim(data, mine, axis=dim, keepdims=False))
+            sent.append(lax.dynamic_index_in_dim(data, 1 - mine, axis=dim, keepdims=False))
+            present.pop(dim)
+        keep = kept[0] if bits[0] == bits[1] else jnp.where(first_core, kept[0], kept[1])
+        send = sent[0] if bits[0] == bits[1] else jnp.where(first_core, sent[0], sent[1])
+        data = keep + exchange(send, bits, count)
+    present = presents[0]
     group = tuple(f"b{bit}" for bit in present)
     data = data.reshape((1 << len(present), mode_block, projected.shape[1]))
     data = lax.all_to_all(data, group, 0, 0, tiled=False)
@@ -146,20 +160,26 @@
     order, nbits = bit_order(sizes)
     count = 1 << nbits
     me = lax.axis_index(ALL_AXES)
+    first_core = (me & 1) == 0
     near, far = order[: nbits - FAR_COUNT], order[nbits - FAR_COUNT :]
-    present = sorted(far, reverse=True)
-    group = tuple(f"b{bit}" for bit in present)
-    data = jnp.broadcast_to(block[None], (1 << len(present),) + block.shape)
+    orders = [list(reversed(variant)) for variant in core_orders(near)]
+    presents = [sorted(far, reverse=True) for _ in orders]
+    group = tuple(f"b{bit}" for bit in presents[0])
+    data = jnp.broadcast_to(block[None], (1 << len(presents[0]),) + block.shape)
     data = lax.all_to_all(data, group, 0, 0, tiled=False)
-    data = data.reshape((2,) * len(present) + block.shape)
-    for bit in reversed(near):
-        mine = (me >> bit) & 1
-        other = exchange(data, bit, count)
-        low = jnp.where(mine == 0, data, other)
-        high = jnp.where(mine == 0, other, data)
-        dim = sum(1 for b in present if b > bit)
-        data = jnp.stack([low, high], axis=dim)
-        present.insert(dim, bit)
+    data = data.reshape((2,) * len(presents[0]) + block.shape)
+    for step in range(len(near)):
+        bits = [variant[step] for variant in orders]
+        other = exchange(data, bits, count)
+        stacked = []
+        for bit, present in zip(bits, presents):
+            mine = (me >> bit) & 1
+            low = jnp.where(mine == 0, data, other)
+            high = jnp.where(mine == 0, other, data)
+            dim = sum(1 for b in present if b > bit)
+            stacked.append(jnp.stack([low, high], axis=dim))
+            present.insert(dim, bit)
+        data = stacked[0] if bits[0] == bits[1] else jnp.where(first_core, stacked[0], stacked[1])
     return data.reshape(count * block.shape[0], block.shape[1])
 
 

time: 178 us -> 168 us (0.944)
  waiting for transfers between devices: 72.9 us -> 63.3 us
    ppermute x8, waiting for transfers between devices: 52.4 us -> 42.9 us  [exchange(): return lax.ppermute(values, ALL_AXES, pairs)]
    all_to_all x1, starting transfers between devices: 11.8 us -> 8.2 us  [scatter_sum(): data = lax.all_to_all(data, group, 0, 0, tiled=False)]
where the time goes in v7:
time: 168 us; the launch traced here: 166 us
  waiting for transfers between devices  63.3 us (38%)
  starting transfers between devices  40.9 us (24%)
  blocking collectives  32.9 us (20%)
  matrix products  15.4 us (9%)
  other arithmetic  7.1 us (4%)
  local copies, waits for them, and re-layouts  4.9 us (3%)
    ppermute x8, waiting for transfers between devices, exchange(): return lax.ppermute(values, ALL_AXES, pairs)  42.9 us
    all_to_all x1, blocking collectives, gather_all(): data = lax.all_to_all(data, group, 0, 0, tiled=False)  32.9 us
    ppermute x8, starting transfers between devices, exchange(): return lax.ppermute(values, ALL_AXES, pairs)  23.1 us
    all_to_all x1, waiting for transfers between devices, scatter_sum(): data = lax.all_to_all(data, group, 0, 0, tiled=False)  13.5 us
    all_to_all x1, starting transfers between devices, scatter_sum(): data = lax.all_to_all(data, group, 0, 0, tiled=False)  8.2 us
    ppermute x2, waiting for transfers between devices, with_halo(): lax.ppermute(lax.slice_in_dim(block, 0, width, axis=dim), axis, backward)  6.86 us
    conv_general_dilated x2, matrix products, conv_valid(): lax.conv_general_dilated(values, weights, (1, 1), 'VALID', dimension_numb...  6.65 us
    ppermute x2, starting transfers between devices, with_halo(): lax.ppermute(lax.slice_in_dim(block, block.shape[dim] - width, None, axis...  6.36 us
  transfers between devices with their start and end apart: 13, of which 11 were waited for; matrix products, arithmetic and copies ran while one was open for 1% of the time, Pallas kernels for 0%

profile of v7, /device:TPU:1, one launch (start us, length us, event | category | flops | bytes accessed | tf_op | source)
XLA Modules:
  0.0 165.5 jit_solution(15775358954199583947)
XLA Ops:
  1.4 32.9 %all_to_all.10 = f32[32,8,128]{2,1,0:T(8,128)S(1)} all-to-all(f32[32,8,128]{2,1,0:T(8,128)S(1)} %broadcast_in_dim.68), channel_id=1, replica_groups=mesh['b8'=2,'b7'=2,'b6'=2,'b5'=2,'b4'=2,'b3'=2,'b2'=2,'b1'=2,'b0'=2] {'b..., dimensions={0} | all-to-all | bytes 262144 | tf_op jit(solution)/shard_map/all_to_all | solution.py:169
  34.3 3.9 %collective-permute-start = (f32[2,2,2,2,2,8,128]{6,5,4,3,2,1,0:T(8,128)S(1)}, f32[2,2,2,2,2,8,128]{6,5,4,3,2,1,0:T(8,128)S(1)}, u32[]{:S(2)}, u32[]{:S(2)}) collective-permute-start(f32[2,2,2,2,2,8,128]{6,5,4,3,2,1,0:T(8,128)S(1)} %bitcast.92), channel_id=1, source_target_pairs={{0,128},{1,129},{2,130},{3,131},{4,132},{5,133},{6,134},{7,135},{8... | collective-permute-start | bytes 393224 | tf_op jit(solution)/shard_map/ppermute | solution.py:128
  38.3 6.0 %collective-permute-done = f32[2,2,2,2,2,8,128]{6,5,4,3,2,1,0:T(8,128)S(1)} collective-permute-done((f32[2,2,2,2,2,8,128]{6,5,4,3,2,1,0:T(8,128)S(1)}, f32[2,2,2,2,2,8,128]{6,5,4,3,2,1,0:T(8,128)S(1)}, u32[]{:S(2)}, u32[]{:S(2)}) %collective-permute-start) | collective-permute-done | bytes 131104 | tf_op jit(solution)/shard_map/ppermute | solution.py:128
  44.4 2.3 %collective-permute-start.1 = (f32[2,2,2,2,2,2,8,128]{7,6,5,4,3,2,1,0:T(8,128)S(1)}, f32[2,2,2,2,2,2,8,128]{7,6,5,4,3,2,1,0:T(8,128)S(1)}, u32[]{:S(2)}, u32[]{:S(2)}) collective-permute-start(f32[2,2,2,2,2,2,8,128]{7,6,5,4,3,2,1,0:T(8,128)S(1)} %pad_maximum_fusion.3), channel_id=1, source_target_pairs={{0,16},{1,3},{2,18},{3,1},{4,20},{5,7},{6,22},{7,5},{8,24},{9,11},... | collective-permute-start | bytes 786440 | tf_op jit(solution)/shard_map/ppermute | solution.py:128
  46.7 5.1 %collective-permute-done.1 = f32[2,2,2,2,2,2,8,128]{7,6,5,4,3,2,1,0:T(8,128)S(1)} collective-permute-done((f32[2,2,2,2,2,2,8,128]{7,6,5,4,3,2,1,0:T(8,128)S(1)}, f32[2,2,2,2,2,2,8,128]{7,6,5,4,3,2,1,0:T(8,128)S(1)}, u32[]{:S(2)}, u32[]{:S(2)}) %collective-permute-start.1) | collective-permute-done | bytes 262176 | tf_op jit(solution)/shard_map/ppermute | solution.py:128
  52.0 2.2 %collective-permute-start.2 = (f32[2,2,2,2,2,2,2,8,128]{8,7,6,5,4,3,2,1,0:T(8,128)S(1)}, f32[2,2,2,2,2,2,2,8,128]{8,7,6,5,4,3,2,1,0:T(8,128)S(1)}, u32[]{:S(2)}, u32[]{:S(2)}) collective-permute-start(f32[2,2,2,2,2,2,2,8,128]{8,7,6,5,4,3,2,1,0:T(8,128)S(1)} %maximum_select_fusion.1), channel_id=1, source_target_pairs={{0,2},{1,17},{2,0},{3,19},{4,6},{5,21},{6,4},{7,23},{8,10},{9,25},... | collective-permute-start | bytes 1572872 | tf_op jit(solution)/shard_map/ppermute | solution.py:128
  54.2 8.0 %collective-permute-done.2 = f32[2,2,2,2,2,2,2,8,128]{8,7,6,5,4,3,2,1,0:T(8,128)S(1)} collective-permute-done((f32[2,2,2,2,2,2,2,8,128]{8,7,6,5,4,3,2,1,0:T(8,128)S(1)}, f32[2,2,2,2,2,2,2,8,128]{8,7,6,5,4,3,2,1,0:T(8,128)S(1)}, u32[]{:S(2)}, u32[]{:S(2)}) %collective-permute-start.2) | collective-permute-done | bytes 524320 | tf_op jit(solution)/shard_map/ppermute | solution.py:128
  63.7 5.1 %collective-permute-start.3 = (f32[2,2,2,2,2,2,2,2,8,128]{9,8,7,6,5,4,3,2,1,0:T(8,128)}, f32[2,2,2,2,2,2,2,2,8,128]{9,8,7,6,5,4,3,2,1,0:T(8,128)}, u32[]{:S(2)}, u32[]{:S(2)}) collective-permute-start(f32[2,2,2,2,2,2,2,2,8,128]{9,8,7,6,5,4,3,2,1,0:T(8,128)} %maximum_select_fusion), channel_id=1, source_target_pairs={{0,1},{1,0},{2,3},{3,2},{4,5},{5,4},{6,7},{7,6},{8,9},{9,8},{10,11... | collective-permute-start | bytes 3145736 | tf_op jit(solution)/shard_map/ppermute | solution.py:128
  69.1 2.3 %collective-permute-done.3 = f32[2,2,2,2,2,2,2,2,8,128]{9,8,7,6,5,4,3,2,1,0:T(8,128)} collective-permute-done((f32[2,2,2,2,2,2,2,2,8,128]{9,8,7,6,5,4,3,2,1,0:T(8,128)}, f32[2,2,2,2,2,2,2,2,8,128]{9,8,7,6,5,4,3,2,1,0:T(8,128)}, u32[]{:S(2)}, u32[]{:S(2)}) %collective-permute-start.3) | collective-permute-done | bytes 1048608 | tf_op jit(solution)/shard_map/ppermute | solution.py:128
  71.4 1.6 select_bitcast_fusion.1
  73.3 1.5 convolution_bitcast_fusion.1
  74.8 2.2 %collective-permute-start.4 = (f32[4,8,256]{2,1,0:T(8,128)S(1)}, f32[4,8,256]{2,1,0:T(8,128)S(1)}, u32[]{:S(2)}, u32[]{:S(2)}) collective-permute-start(f32[4,8,256]{2,1,0:T(8,128)S(1)} %get-tuple-element.16), channel_id=1, source_target_pairs={{0,16},{16,32},{32,48},{48,64},{64,80},{80,96},{96,112},{112,128},... | collective-permute-start | bytes 98312 | tf_op jit(solution)/shard_map/ppermute | solution.py:21
  78.4 3.3 %collective-permute-done.5 = f32[4,8,256]{2,1,0:T(8,128)S(1)} collective-permute-done((f32[4,8,256]{2,1,0:T(8,128)S(1)}, f32[4,8,256]{2,1,0:T(8,128)S(1)}, u32[]{:S(2)}, u32[]{:S(2)}) %collective-permute-start.5) | collective-permute-done | bytes 32800 | tf_op jit(solution)/shard_map/ppermute | solution.py:24
  81.7 4.1 %collective-permute-start.6 = (f32[16,4,256]{2,1,0:T(4,128)S(1)}, f32[16,4,256]{2,1,0:T(4,128)S(1)}, u32[]{:S(2)}, u32[]{:S(2)}) collective-permute-start(f32[16,4,256]{2,1,0:T(4,128)S(1)} %get-tuple-element.14), channel_id=1, source_target_pairs={{0,1},{1,2},{2,3},{3,4},{4,5},{5,6},{6,7},{7,8},{8,9},{9,10},{10,1... | collective-permute-start | bytes 196616 | tf_op jit(solution)/shard_map/ppermute | solution.py:21
  85.8 1.9 %collective-permute-start.7 = (f32[16,4,256]{2,1,0:T(4,128)S(1)}, f32[16,4,256]{2,1,0:T(4,128)S(1)}, u32[]{:S(2)}, u32[]{:S(2)}) collective-permute-start(f32[16,4,256]{2,1,0:T(4,128)S(1)} %get-tuple-element.15), channel_id=1, source_target_pairs={{1,0},{2,1},{3,2},{4,3},{5,4},{6,5},{7,6},{8,7},{9,8},{10,9},{11,1... | collective-permute-start | bytes 196616 | tf_op jit(solution)/shard_map/ppermute | solution.py:24
  87.9 3.6 %collective-permute-done.7 = f32[16,4,256]{2,1,0:T(4,128)S(1)} collective-permute-done((f32[16,4,256]{2,1,0:T(4,128)S(1)}, f32[16,4,256]{2,1,0:T(4,128)S(1)}, u32[]{:S(2)}, u32[]{:S(2)}) %collective-permute-start.7) | collective-permute-done | bytes 65568 | tf_op jit(solution)/shard_map/ppermute | solution.py:24
  91.6 3.1 %select_convert_fusion.1 = bf16[14,14,32,128]{3,2,1,0:T(8,128)(2,1)S(1)} fusion(f32[32]{0:T(128)S(1)} %copy-done.6, pred[14,14]{1,0:T(8,128)(4,1)S(1)} %slice_bitcast_fusion.2, bf16[3,3,32,32]{3,2,1,0:T(8,128)(2,1)S(1)} %copy-done.4, f32[32]{0:T(128)S(1)} %copy-done.7, f32[32]{0:T(128)S(1)} %copy-done.10, f32[16,16,128]{2,1,0:T(8,128)S(1)} %slice.51, ...), kind=kOutput, calls=%fused_computation.2 | convolution fusion | flops 469024768 | bytes 1755972 | tf_op jit(solution)/shard_map/conv_general_dilated | solution.py:47
  94.7 3.5 %multiply_reduce_fusion = (f32[12,12,128]{2,1,0:T(8,128)S(1)}, f32[12,12,32,128]{3,2,1,0:T(8,128)}) fusion(f32[32]{0:T(128)S(1)} %copy-done.8, f32[32]{0:T(128)S(1)} %copy-done.9, bf16[14,14,32,128]{3,2,1,0:T(8,128)(2,1)S(1)} %select_convert_fusion.1, bf16[3,3,32,32]{3,2,1,0:T(8,128)(2,1)S(1)} %copy-done.5), kind=kOutput, calls=%fused_computation.4 | convolution fusion | flops 341489664 | bytes 4057344 | tf_op jit(solution)/shard_map/conv_general_dilated | solution.py:47
  98.3 4.1 %fusion.6 = f32[8,8,128]{2,1,0:T(8,128)S(1)} fusion(bf16[3,3,32,32]{3,2,1,0:T(8,128)(2,1)S(1)} %copy-done.4, bf16[3,3,32,32]{3,2,1,0:T(8,128)(2,1)S(1)} %copy-done.5, f32[12,12,32,128]{3,2,1,0:T(8,128)} %get-tuple-element.19, f32[12,12,128]{2,1,0:T(8,128)S(1)} %maximum_subtract_fusion, f32[32]{0:T(128)S(1)} %copy-done.8, f32[32]{0:T(128)S(1)} %copy-done.9, ...), kind=kOutput, calls=%fused_computation.15 | convolution fusion | flops 394027008 | bytes 3462656 | tf_op jit(solution)/shard_map/conv_general_dilated | solution.py:58
  102.4 3.2 %convolution_bitcast_fusion = f32[4096,128]{0,1:T(8,128)} fusion(f32[8,8,128]{2,1,0:T(8,128)S(1)} %fusion.6, f32[8,8,4096]{2,1,0:T(8,128)S(1)} %copy-done), kind=kOutput, calls=%fused_computation | convolution fusion | flops 402653184 | bytes 3178496 | tf_op jit(solution)/shard_map/dot_general | solution.py:202
  105.5 1.9 %copy.39 = f32[4096,128]{1,0:T(8,128)S(1)} copy(f32[4096,128]{0,1:T(8,128)} %convolution_bitcast_fusion) | data formatting | bytes 4194304 | tf_op jit(solution)/shard_map/dot_general | solution.py:202
  108.7 1.9 %collective-permute-start.8 = (f32[2,2,2,2,2,2,2,2,8,128]{9,8,7,6,5,4,3,2,1,0:T(8,128)}, f32[2,2,2,2,2,2,2,2,8,128]{9,8,7,6,5,4,3,2,1,0:T(8,128)}, u32[]{:S(2)}, u32[]{:S(2)}) collective-permute-start(f32[2,2,2,2,2,2,2,2,8,128]{9,8,7,6,5,4,3,2,1,0:T(8,128)} %dynamic-slice_bitcast_fusion), channel_id=1, source_target_pairs={{0,1},{1,0},{2,3},{3,2},{4,5},{5,4},{6,7},{7,6},{8,9},{9,8},{10,11... | collective-permute-start | bytes 3145736 | tf_op jit(solution)/shard_map/ppermute | solution.py:128
  110.6 3.0 %collective-permute-done.8 = f32[2,2,2,2,2,2,2,2,8,128]{9,8,7,6,5,4,3,2,1,0:T(8,128)} collective-permute-done((f32[2,2,2,2,2,2,2,2,8,128]{9,8,7,6,5,4,3,2,1,0:T(8,128)}, f32[2,2,2,2,2,2,2,2,8,128]{9,8,7,6,5,4,3,2,1,0:T(8,128)}, u32[]{:S(2)}, u32[]{:S(2)}) %collective-permute-start.8) | collective-permute-done | bytes 1048608 | tf_op jit(solution)/shard_map/ppermute | solution.py:128
  113.6 1.7 %bitcast_add_fusion = f32[2,2,2,2,2,2,2,2,8,128]{9,8,7,6,5,4,3,2,1,0:T(8,128)S(1)} fusion(f32[2,2,2,2,2,2,2,2,8,128]{9,8,7,6,5,4,3,2,1,0:T(8,128)} %collective-permute-done.8, f32[2,2,2,2,2,2,2,2,2,8,128]{10,9,8,7,6,5,4,3,2,1,0:T(8,128)} %bitcast.90, s32[]{:T(128)S(6)} %select_n.175), kind=kLoop, calls=%fused_computation.24 | loop fusion | flops 262144 | bytes 3145732 | tf_op jit(solution)/shard_map/add | solution.py:151
  115.5 1.9 %collective-permute-start.9 = (f32[2,2,2,2,2,2,2,8,128]{8,7,6,5,4,3,2,1,0:T(8,128)S(1)}, f32[2,2,2,2,2,2,2,8,128]{8,7,6,5,4,3,2,1,0:T(8,128)S(1)}, u32[]{:S(2)}, u32[]{:S(2)}) collective-permute-start(f32[2,2,2,2,2,2,2,8,128]{8,7,6,5,4,3,2,1,0:T(8,128)S(1)} %bitcast_select_fusion), channel_id=1, source_target_pairs={{0,2},{1,17},{2,0},{3,19},{4,6},{5,21},{6,4},{7,23},{8,10},{9,25},... | collective-permute-start | bytes 1572872 | tf_op jit(solution)/shard_map/ppermute | solution.py:128
  117.4 8.3 %collective-permute-done.9 = f32[2,2,2,2,2,2,2,8,128]{8,7,6,5,4,3,2,1,0:T(8,128)S(1)} collective-permute-done((f32[2,2,2,2,2,2,2,8,128]{8,7,6,5,4,3,2,1,0:T(8,128)S(1)}, f32[2,2,2,2,2,2,2,8,128]{8,7,6,5,4,3,2,1,0:T(8,128)S(1)}, u32[]{:S(2)}, u32[]{:S(2)}) %collective-permute-start.9) | collective-permute-done | bytes 524320 | tf_op jit(solution)/shard_map/ppermute | solution.py:128
  125.9 1.9 %collective-permute-start.10 = (f32[2,2,2,2,2,2,8,128]{7,6,5,4,3,2,1,0:T(8,128)S(1)}, f32[2,2,2,2,2,2,8,128]{7,6,5,4,3,2,1,0:T(8,128)S(1)}, u32[]{:S(2)}, u32[]{:S(2)}) collective-permute-start(f32[2,2,2,2,2,2,8,128]{7,6,5,4,3,2,1,0:T(8,128)S(1)} %bitcast_select_fusion.2), channel_id=1, source_target_pairs={{0,16},{1,3},{2,18},{3,1},{4,20},{5,7},{6,22},{7,5},{8,24},{9,11},... | collective-permute-start | bytes 786440 | tf_op jit(solution)/shard_map/ppermute | solution.py:128
  127.8 5.5 %collective-permute-done.10 = f32[2,2,2,2,2,2,8,128]{7,6,5,4,3,2,1,0:T(8,128)S(1)} collective-permute-done((f32[2,2,2,2,2,2,8,128]{7,6,5,4,3,2,1,0:T(8,128)S(1)}, f32[2,2,2,2,2,2,8,128]{7,6,5,4,3,2,1,0:T(8,128)S(1)}, u32[]{:S(2)}, u32[]{:S(2)}) %collective-permute-start.10) | collective-permute-done | bytes 262176 | tf_op jit(solution)/shard_map/ppermute | solution.py:128
  133.4 3.8 %collective-permute-start.11 = (f32[2,2,2,2,2,8,128]{6,5,4,3,2,1,0:T(8,128)S(1)}, f32[2,2,2,2,2,8,128]{6,5,4,3,2,1,0:T(8,128)S(1)}, u32[]{:S(2)}, u32[]{:S(2)}) collective-permute-start(f32[2,2,2,2,2,8,128]{6,5,4,3,2,1,0:T(8,128)S(1)} %dynamic-slice_bitcast_fusion.1), channel_id=1, source_target_pairs={{0,128},{1,129},{2,130},{3,131},{4,132},{5,133},{6,134},{7,135},{8... | collective-permute-start | bytes 393224 | tf_op jit(solution)/shard_map/ppermute | solution.py:128
  137.2 4.7 %collective-permute-done.11 = f32[2,2,2,2,2,8,128]{6,5,4,3,2,1,0:T(8,128)S(1)} collective-permute-done((f32[2,2,2,2,2,8,128]{6,5,4,3,2,1,0:T(8,128)S(1)}, f32[2,2,2,2,2,8,128]{6,5,4,3,2,1,0:T(8,128)S(1)}, u32[]{:S(2)}, u32[]{:S(2)}) %collective-permute-start.11) | collective-permute-done | bytes 131104 | tf_op jit(solution)/shard_map/ppermute | solution.py:128
  142.5 8.2 %all-to-all-start.1 = ((f32[32,8,128]{2,1,0:T(8,128)}), f32[32,8,128]{2,1,0:T(8,128)S(1)}, u32[]{:S(2)}, u32[]{:S(2)}) async-start(f32[32,8,128]{2,1,0:T(8,128)} %bitcast.39), calls=%async_computation.1 | async-start | bytes 262144 | tf_op jit(solution)/shard_map/all_to_all | solution.py:155
  151.3 13.5 %all-to-all-done.1 = f32[32,8,128]{2,1,0:T(8,128)S(1)} async-done(((f32[32,8,128]{2,1,0:T(8,128)}), f32[32,8,128]{2,1,0:T(8,128)S(1)}, u32[]{:S(2)}, u32[]{:S(2)}) %all-to-all-start.1) | async-done | bytes 131104 | tf_op jit(solution)/shard_map/all_to_all | solution.py:155
  (55 shorter events, 8.1 us)
Async XLA Ops:
  0.6 72.6 %copy-start = (f32[8,8,4096]{2,1,0:T(8,128)S(1)}, f32[8,8,4096]{2,1,0:T(8,128)}, u32[]{:S(2)}) copy-start(f32[8,8,4096]{2,1,0:T(8,128)} %param.11) | copy-start | bytes 3145732
  34.3 10.0 %collective-permute-start = (f32[2,2,2,2,2,8,128]{6,5,4,3,2,1,0:T(8,128)S(1)}, f32[2,2,2,2,2,8,128]{6,5,4,3,2,1,0:T(8,128)S(1)}, u32[]{:S(2)}, u32[]{:S(2)}) collective-permute-start(f32[2,2,2,2,2,8,128]{6,5,4,3,2,1,0:T(8,128)S(1)} %bitcast.92), channel_id=1, source_target_pairs={{0,128},{1,129},{2,130},{3,131},{4,132},{5,133},{6,134},{7,135},{8... | collective-permute-start | bytes 393224 | tf_op jit(solution)/shard_map/ppermute | solution.py:128
  44.4 7.4 %collective-permute-start.1 = (f32[2,2,2,2,2,2,8,128]{7,6,5,4,3,2,1,0:T(8,128)S(1)}, f32[2,2,2,2,2,2,8,128]{7,6,5,4,3,2,1,0:T(8,128)S(1)}, u32[]{:S(2)}, u32[]{:S(2)}) collective-permute-start(f32[2,2,2,2,2,2,8,128]{7,6,5,4,3,2,1,0:T(8,128)S(1)} %pad_maximum_fusion.3), channel_id=1, source_target_pairs={{0,16},{1,3},{2,18},{3,1},{4,20},{5,7},{6,22},{7,5},{8,24},{9,11},... | collective-permute-start | bytes 786440 | tf_op jit(solution)/shard_map/ppermute | solution.py:128
  52.0 10.2 %collective-permute-start.2 = (f32[2,2,2,2,2,2,2,8,128]{8,7,6,5,4,3,2,1,0:T(8,128)S(1)}, f32[2,2,2,2,2,2,2,8,128]{8,7,6,5,4,3,2,1,0:T(8,128)S(1)}, u32[]{:S(2)}, u32[]{:S(2)}) collective-permute-start(f32[2,2,2,2,2,2,2,8,128]{8,7,6,5,4,3,2,1,0:T(8,128)S(1)} %maximum_select_fusion.1), channel_id=1, source_target_pairs={{0,2},{1,17},{2,0},{3,19},{4,6},{5,21},{6,4},{7,23},{8,10},{9,25},... | collective-permute-start | bytes 1572872 | tf_op jit(solution)/shard_map/ppermute | solution.py:128
  63.7 7.7 %collective-permute-start.3 = (f32[2,2,2,2,2,2,2,2,8,128]{9,8,7,6,5,4,3,2,1,0:T(8,128)}, f32[2,2,2,2,2,2,2,2,8,128]{9,8,7,6,5,4,3,2,1,0:T(8,128)}, u32[]{:S(2)}, u32[]{:S(2)}) collective-permute-start(f32[2,2,2,2,2,2,2,2,8,128]{9,8,7,6,5,4,3,2,1,0:T(8,128)} %maximum_select_fusion), channel_id=1, source_target_pairs={{0,1},{1,0},{2,3},{3,2},{4,5},{5,4},{6,7},{7,6},{8,9},{9,8},{10,11... | collective-permute-start | bytes 3145736 | tf_op jit(solution)/shard_map/ppermute | solution.py:128
  73.2 1.6 copy-start.2
  73.2 18.3 %copy-start.4 = (bf16[3,3,32,32]{3,2,1,0:T(8,128)(2,1)S(1)}, bf16[3,3,32,32]{3,2,1,0:T(8,128)(2,1)}, u32[]{:S(2)}) copy-start(bf16[3,3,32,32]{3,2,1,0:T(8,128)(2,1)} %param.15) | copy-start | bytes 55300
  73.2 18.3 %copy-start.6 = (f32[32]{0:T(128)S(1)}, f32[32]{0:T(128)}, u32[]{:S(2)}) copy-start(f32[32]{0:T(128)} %param.16) | copy-start | bytes 388
  73.2 18.3 %copy-start.7 = (f32[32]{0:T(128)S(1)}, f32[32]{0:T(128)}, u32[]{:S(2)}) copy-start(f32[32]{0:T(128)} %param.14) | copy-start | bytes 388
  73.2 18.3 %copy-start.10 = (f32[32]{0:T(128)S(1)}, f32[32]{0:T(128)}, u32[]{:S(2)}) copy-start(f32[32]{0:T(128)} %param.13) | copy-start | bytes 388
  74.8 3.6 %collective-permute-start.4 = (f32[4,8,256]{2,1,0:T(8,128)S(1)}, f32[4,8,256]{2,1,0:T(8,128)S(1)}, u32[]{:S(2)}, u32[]{:S(2)}) collective-permute-start(f32[4,8,256]{2,1,0:T(8,128)S(1)} %get-tuple-element.16), channel_id=1, source_target_pairs={{0,16},{16,32},{32,48},{48,64},{64,80},{80,96},{96,112},{112,128},... | collective-permute-start | bytes 98312 | tf_op jit(solution)/shard_map/ppermute | solution.py:21
  77.0 4.7 %collective-permute-start.5 = (f32[4,8,256]{2,1,0:T(8,128)S(1)}, f32[4,8,256]{2,1,0:T(8,128)S(1)}, u32[]{:S(2)}, u32[]{:S(2)}) collective-permute-start(f32[4,8,256]{2,1,0:T(8,128)S(1)} %get-tuple-element.17), channel_id=1, source_target_pairs={{16,0},{32,16},{48,32},{64,48},{80,64},{96,80},{112,96},{128,112},... | collective-permute-start | bytes 98312 | tf_op jit(solution)/shard_map/ppermute | solution.py:24
  81.7 6.2 %collective-permute-start.6 = (f32[16,4,256]{2,1,0:T(4,128)S(1)}, f32[16,4,256]{2,1,0:T(4,128)S(1)}, u32[]{:S(2)}, u32[]{:S(2)}) collective-permute-start(f32[16,4,256]{2,1,0:T(4,128)S(1)} %get-tuple-element.14), channel_id=1, source_target_pairs={{0,1},{1,2},{2,3},{3,4},{4,5},{5,6},{6,7},{7,8},{8,9},{9,10},{10,1... | collective-permute-start | bytes 196616 | tf_op jit(solution)/shard_map/ppermute | solution.py:21
  85.8 5.6 %collective-permute-start.7 = (f32[16,4,256]{2,1,0:T(4,128)S(1)}, f32[16,4,256]{2,1,0:T(4,128)S(1)}, u32[]{:S(2)}, u32[]{:S(2)}) collective-permute-start(f32[16,4,256]{2,1,0:T(4,128)S(1)} %get-tuple-element.15), channel_id=1, source_target_pairs={{1,0},{2,1},{3,2},{4,3},{5,4},{6,5},{7,6},{8,7},{9,8},{10,9},{11,1... | collective-permute-start | bytes 196616 | tf_op jit(solution)/shard_map/ppermute | solution.py:24
  91.5 3.2 %copy-start.5 = (bf16[3,3,32,32]{3,2,1,0:T(8,128)(2,1)S(1)}, bf16[3,3,32,32]{3,2,1,0:T(8,128)(2,1)}, u32[]{:S(2)}) copy-start(bf16[3,3,32,32]{3,2,1,0:T(8,128)(2,1)} %param.17) | copy-start | bytes 55300
  91.6 3.2 %copy-start.8 = (f32[32]{0:T(128)S(1)}, f32[32]{0:T(128)}, u32[]{:S(2)}) copy-start(f32[32]{0:T(128)} %param.19) | copy-start | bytes 388
  91.6 3.2 %copy-start.9 = (f32[32]{0:T(128)S(1)}, f32[32]{0:T(128)}, u32[]{:S(2)}) copy-start(f32[32]{0:T(128)} %param.18) | copy-start | bytes 388
  107.5 3.2 %copy-start.1 = (f32[4096,128]{1,0:T(8,128)}, f32[4096,128]{1,0:T(8,128)S(1)}, u32[]{:S(2)}) copy-start(f32[4096,128]{1,0:T(8,128)S(1)} %copy.39) | copy-start | bytes 6291460
  108.7 4.9 %collective-permute-start.8 = (f32[2,2,2,2,2,2,2,2,8,128]{9,8,7,6,5,4,3,2,1,0:T(8,128)}, f32[2,2,2,2,2,2,2,2,8,128]{9,8,7,6,5,4,3,2,1,0:T(8,128)}, u32[]{:S(2)}, u32[]{:S(2)}) collective-permute-start(f32[2,2,2,2,2,2,2,2,8,128]{9,8,7,6,5,4,3,2,1,0:T(8,128)} %dynamic-slice_bitcast_fusion), channel_id=1, source_target_pairs={{0,1},{1,0},{2,3},{3,2},{4,5},{5,4},{6,7},{7,6},{8,9},{9,8},{10,11... | collective-permute-start | bytes 3145736 | tf_op jit(solution)/shard_map/ppermute | solution.py:128
  115.5 10.2 %collective-permute-start.9 = (f32[2,2,2,2,2,2,2,8,128]{8,7,6,5,4,3,2,1,0:T(8,128)S(1)}, f32[2,2,2,2,2,2,2,8,128]{8,7,6,5,4,3,2,1,0:T(8,128)S(1)}, u32[]{:S(2)}, u32[]{:S(2)}) collective-permute-start(f32[2,2,2,2,2,2,2,8,128]{8,7,6,5,4,3,2,1,0:T(8,128)S(1)} %bitcast_select_fusion), channel_id=1, source_target_pairs={{0,2},{1,17},{2,0},{3,19},{4,6},{5,21},{6,4},{7,23},{8,10},{9,25},... | collective-permute-start | bytes 1572872 | tf_op jit(solution)/shard_map/ppermute | solution.py:128
  117.4 47.5 %copy-start.3 = (f32[8,128]{1,0:T(8,128)S(1)}, f32[8,128]{1,0:T(8,128)}, u32[]{:S(2)}) copy-start(f32[8,128]{1,0:T(8,128)} %param.10) | copy-start | bytes 12292
  125.9 7.4 %collective-permute-start.10 = (f32[2,2,2,2,2,2,8,128]{7,6,5,4,3,2,1,0:T(8,128)S(1)}, f32[2,2,2,2,2,2,8,128]{7,6,5,4,3,2,1,0:T(8,128)S(1)}, u32[]{:S(2)}, u32[]{:S(2)}) collective-permute-start(f32[2,2,2,2,2,2,8,128]{7,6,5,4,3,2,1,0:T(8,128)S(1)} %bitcast_select_fusion.2), channel_id=1, source_target_pairs={{0,16},{1,3},{2,18},{3,1},{4,20},{5,7},{6,22},{7,5},{8,24},{9,11},... | collective-permute-start | bytes 786440 | tf_op jit(solution)/shard_map/ppermute | solution.py:128
  133.4 8.5 %collective-permute-start.11 = (f32[2,2,2,2,2,8,128]{6,5,4,3,2,1,0:T(8,128)S(1)}, f32[2,2,2,2,2,8,128]{6,5,4,3,2,1,0:T(8,128)S(1)}, u32[]{:S(2)}, u32[]{:S(2)}) collective-permute-start(f32[2,2,2,2,2,8,128]{6,5,4,3,2,1,0:T(8,128)S(1)} %dynamic-slice_bitcast_fusion.1), channel_id=1, source_target_pairs={{0,128},{1,129},{2,130},{3,131},{4,132},{5,133},{6,134},{7,135},{8... | collective-permute-start | bytes 393224 | tf_op jit(solution)/shard_map/ppermute | solution.py:128
  142.5 22.4 %all-to-all-start.1 = ((f32[32,8,128]{2,1,0:T(8,128)}), f32[32,8,128]{2,1,0:T(8,128)S(1)}, u32[]{:S(2)}, u32[]{:S(2)}) async-start(f32[32,8,128]{2,1,0:T(8,128)} %bitcast.39), calls=%async_computation.1 | async-start | bytes 262144 | tf_op jit(solution)/shard_map/all_to_all | solution.py:155

commit v8 on v7

--- a/solution.py
+++ b/solution.py
@@ -69,12 +69,9 @@
     return values[width : values.shape[0] - width, width : values.shape[1] - width]
 
 
-def surrogate(logperm, observed, lift_w, lift_b, w_one, b_one, w_two, b_two, read_w):
-    tile_rows, tile_cols, batch_size = logperm.shape
-    both = jnp.concatenate([logperm, observed], axis=-1)
-    wide = with_halo(both, ((ROW_AXES, 0), (COL_AXES, 1)), HALO)
-    field = wide[..., :batch_size]
-    measured = trim(wide[..., batch_size:], 2)
+def surrogate(field, measured, lift_w, lift_b, w_one, b_one, w_two, b_two, read_w):
+    tile_rows = field.shape[0] - 2 * HALO
+    tile_cols = field.shape[1] - 2 * HALO
     mask = inside_grid(tile_rows, tile_cols, HALO)
     zero = jnp.float32(0.0)
     lifted = jnp.where(
@@ -188,15 +185,18 @@
     batch_size = coeffs.shape[1]
     sizes = (4, 8, 8, 2)
     flat_basis = basis.reshape(tile_rows * tile_cols, mode_count)
-    logperm = jnp.dot(
-        flat_basis,
+    sides = ((ROW_AXES, 0), (COL_AXES, 1))
+    wide_basis = with_halo(basis, sides, HALO)
+    measured = with_halo(observed, sides, 2)
+    field = jnp.dot(
+        wide_basis.reshape(-1, mode_count),
         gather_all(coeffs, sizes),
         precision=lax.Precision.HIGHEST,
         preferred_element_type=jnp.float32,
     )
-    logperm = logperm.reshape(tile_rows, tile_cols, batch_size)
+    field = field.reshape(wide_basis.shape[0], wide_basis.shape[1], batch_size)
     pressure, grad_field = surrogate(
-        logperm, observed, lift_w, lift_b, w_one, b_one, w_two, b_two, read_w
+        field, measured, lift_w, lift_b, w_one, b_one, w_two, b_two, read_w
     )
     grad_flat = grad_field.reshape(tile_rows * tile_cols, batch_size)
     projected = lax.dot_general(

time: 168 us -> 180 us (1.071)
  starting transfers between devices: 40.9 us -> 75.4 us
  blocking collectives: 32.9 us -> 0 us
  local copies, waits for them, and re-layouts: 4.9 us -> 11.3 us
  matrix products: 15.4 us -> 19.5 us
    all_to_all x1 -> x0, blocking collectives: 32.9 us -> none  [gather_all(): data = lax.all_to_all(data, group, 0, 0, tiled=False)]
    all_to_all x0 -> x1, starting transfers between devices: none -> 18.9 us  [gather_all(): data = lax.all_to_all(data, group, 0, 0, tiled=False)]
    ppermute x2 -> x4, starting transfers between devices: 6.36 us -> 11.6 us  [with_halo(): lax.ppermute(lax.slice_in_dim(block, block.shape[dim] - width, None, axis...]
    ppermute x2 -> x4, starting transfers between devices: 3.21 us -> 7.82 us  [with_halo(): lax.ppermute(lax.slice_in_dim(block, 0, width, axis=dim), axis, backward)]
    dot_general x1, matrix products: 1.48 us -> 5.63 us  [shards(): jnp.dot(wide_basis.reshape(-1, mode_count), gather_all(coeffs, sizes), pr...]
    ppermute x8, starting transfers between devices: 23.1 us -> 26.8 us  [exchange(): return lax.ppermute(values, ALL_AXES, pairs)]
    ppermute x2 -> x4, waiting for transfers between devices: 6.86 us -> 4.4 us  [with_halo(): lax.ppermute(lax.slice_in_dim(block, 0, width, axis=dim), axis, backward)]
    all_to_all x0 -> x1, waiting for transfers between devices: none -> 2.24 us  [gather_all(): data = lax.all_to_all(data, group, 0, 0, tiled=False)]
  transfers between devices with their start and end apart: 13 -> 18, of which waited for: 11 -> 11; matrix products, arithmetic and copies ran while one was open for 1% -> 13% of each run, Pallas kernels for 0% -> 0%
where the time goes in v8:
time: 180 us; the launch traced here: 178 us
  starting transfers between devices  75.4 us (42%)
  waiting for transfers between devices  63 us (35%)
  matrix products  19.5 us (11%)
  local copies, waits for them, and re-layouts  11.3 us (6%)
  other arithmetic  7.36 us (4%)
    ppermute x8, waiting for transfers between devices, exchange(): return lax.ppermute(values, ALL_AXES, pairs)  41 us
    ppermute x8, starting transfers between devices, exchange(): return lax.ppermute(values, ALL_AXES, pairs)  26.8 us
    all_to_all x1, starting transfers between devices, gather_all(): data = lax.all_to_all(data, group, 0, 0, tiled=False)  18.9 us
    all_to_all x1, waiting for transfers between devices, scatter_sum(): data = lax.all_to_all(data, group, 0, 0, tiled=False)  13.6 us
    ppermute x4, starting transfers between devices, with_halo(): lax.ppermute(lax.slice_in_dim(block, block.shape[dim] - width, None, axis...  11.6 us
    all_to_all x1, starting transfers between devices, scatter_sum(): data = lax.all_to_all(data, group, 0, 0, tiled=False)  10.3 us
    ppermute x4, starting transfers between devices, with_halo(): lax.ppermute(lax.slice_in_dim(block, 0, width, axis=dim), axis, backward)  7.82 us
    conv_general_dilated x2, matrix products, conv_valid(): lax.conv_general_dilated(values, weights, (1, 1), 'VALID', dimension_numb...  6.64 us
  transfers between devices with their start and end apart: 18, of which 11 were waited for; matrix products, arithmetic and copies ran while one was open for 13% of the time, Pallas kernels for 0%

profile of v8, /device:TPU:1, one launch (start us, length us, event | category | flops | bytes accessed | tf_op | source)
XLA Modules:
  0.0 177.8 jit_solution(8003153722705762166)
XLA Ops:
  2.0 18.9 %all-to-all-start = ((f32[32,8,128]{2,1,0:T(8,128)}), f32[32,8,128]{2,1,0:T(8,128)S(1)}, u32[]{:S(2)}, u32[]{:S(2)}) async-start(f32[32,8,128]{2,1,0:T(8,128)} %broadcast_in_dim.67), calls=%async_computation | async-start | bytes 262144 | tf_op jit(solution)/shard_map/all_to_all | solution.py:166
  21.0 2.1 %fusion.27 = (f32[4,8,4096]{2,1,0:T(8,128)}, f32[4,8,4096]{2,1,0:T(8,128)S(1)}) fusion(f32[8,8,4096]{2,1,0:T(8,128)} %param.11), kind=kLoop, calls=%fused_computation.74 | loop fusion | bytes 2097152 | tf_op jit(solution)/shard_map/slice | solution.py:24
  23.0 3.0 %collective-permute-start = (f32[4,8,4096]{2,1,0:T(8,128)S(1)}, f32[4,8,4096]{2,1,0:T(8,128)}, u32[]{:S(2)}, u32[]{:S(2)}) collective-permute-start(f32[4,8,4096]{2,1,0:T(8,128)S(1)} %get-tuple-element.7), channel_id=1, source_target_pairs={{0,16},{16,32},{32,48},{48,64},{64,80},{80,96},{96,112},{112,128},... | collective-permute-start | bytes 1572872 | tf_op jit(solution)/shard_map/ppermute | solution.py:21
  27.4 4.0 %collective-permute-start.8 = (f32[2,8,128]{2,1,0:T(8,128)S(1)}, f32[2,8,128]{2,1,0:T(8,128)S(1)}, u32[]{:S(2)}, u32[]{:S(2)}) collective-permute-start(f32[2,8,128]{2,1,0:T(8,128)S(1)} %get-tuple-element.21), channel_id=1, source_target_pairs={{0,16},{16,32},{32,48},{48,64},{64,80},{80,96},{96,112},{112,128},... | collective-permute-start | bytes 24584 | tf_op jit(solution)/shard_map/ppermute | solution.py:21
  32.9 2.2 %all-to-all-done = f32[32,8,128]{2,1,0:T(8,128)S(1)} async-done(((f32[32,8,128]{2,1,0:T(8,128)}), f32[32,8,128]{2,1,0:T(8,128)S(1)}, u32[]{:S(2)}, u32[]{:S(2)}) %all-to-all-start) | async-done | bytes 131104 | tf_op jit(solution)/shard_map/all_to_all | solution.py:166
  35.2 7.0 %collective-permute-start.4 = (f32[2,2,2,2,2,8,128]{6,5,4,3,2,1,0:T(8,128)S(1)}, f32[2,2,2,2,2,8,128]{6,5,4,3,2,1,0:T(8,128)S(1)}, u32[]{:S(2)}, u32[]{:S(2)}) collective-permute-start(f32[2,2,2,2,2,8,128]{6,5,4,3,2,1,0:T(8,128)S(1)} %bitcast.87), channel_id=1, source_target_pairs={{0,128},{1,129},{2,130},{3,131},{4,132},{5,133},{6,134},{7,135},{8... | collective-permute-start | bytes 393224 | tf_op jit(solution)/shard_map/ppermute | solution.py:125
  42.2 7.0 %collective-permute-done.4 = f32[2,2,2,2,2,8,128]{6,5,4,3,2,1,0:T(8,128)S(1)} collective-permute-done((f32[2,2,2,2,2,8,128]{6,5,4,3,2,1,0:T(8,128)S(1)}, f32[2,2,2,2,2,8,128]{6,5,4,3,2,1,0:T(8,128)S(1)}, u32[]{:S(2)}, u32[]{:S(2)}) %collective-permute-start.4) | collective-permute-done | bytes 131104 | tf_op jit(solution)/shard_map/ppermute | solution.py:125
  49.3 2.4 %collective-permute-start.5 = (f32[2,2,2,2,2,2,8,128]{7,6,5,4,3,2,1,0:T(8,128)S(1)}, f32[2,2,2,2,2,2,8,128]{7,6,5,4,3,2,1,0:T(8,128)S(1)}, u32[]{:S(2)}, u32[]{:S(2)}) collective-permute-start(f32[2,2,2,2,2,2,8,128]{7,6,5,4,3,2,1,0:T(8,128)S(1)} %pad_maximum_fusion.3), channel_id=1, source_target_pairs={{0,16},{1,3},{2,18},{3,1},{4,20},{5,7},{6,22},{7,5},{8,24},{9,11},... | collective-permute-start | bytes 786440 | tf_op jit(solution)/shard_map/ppermute | solution.py:125
  52.9 4.0 %collective-permute-done.5 = f32[2,2,2,2,2,2,8,128]{7,6,5,4,3,2,1,0:T(8,128)S(1)} collective-permute-done((f32[2,2,2,2,2,2,8,128]{7,6,5,4,3,2,1,0:T(8,128)S(1)}, f32[2,2,2,2,2,2,8,128]{7,6,5,4,3,2,1,0:T(8,128)S(1)}, u32[]{:S(2)}, u32[]{:S(2)}) %collective-permute-start.5) | collective-permute-done | bytes 262176 | tf_op jit(solution)/shard_map/ppermute | solution.py:125
  57.1 1.9 %collective-permute-start.6 = (f32[2,2,2,2,2,2,2,8,128]{8,7,6,5,4,3,2,1,0:T(8,128)S(1)}, f32[2,2,2,2,2,2,2,8,128]{8,7,6,5,4,3,2,1,0:T(8,128)S(1)}, u32[]{:S(2)}, u32[]{:S(2)}) collective-permute-start(f32[2,2,2,2,2,2,2,8,128]{8,7,6,5,4,3,2,1,0:T(8,128)S(1)} %maximum_select_fusion.1), channel_id=1, source_target_pairs={{0,2},{1,17},{2,0},{3,19},{4,6},{5,21},{6,4},{7,23},{8,10},{9,25},... | collective-permute-start | bytes 1572872 | tf_op jit(solution)/shard_map/ppermute | solution.py:125
  60.2 7.1 %collective-permute-done.6 = f32[2,2,2,2,2,2,2,8,128]{8,7,6,5,4,3,2,1,0:T(8,128)S(1)} collective-permute-done((f32[2,2,2,2,2,2,2,8,128]{8,7,6,5,4,3,2,1,0:T(8,128)S(1)}, f32[2,2,2,2,2,2,2,8,128]{8,7,6,5,4,3,2,1,0:T(8,128)S(1)}, u32[]{:S(2)}, u32[]{:S(2)}) %collective-permute-start.6) | collective-permute-done | bytes 524320 | tf_op jit(solution)/shard_map/ppermute | solution.py:125
  69.7 5.9 %collective-permute-start.7 = (f32[2,2,2,2,2,2,2,2,8,128]{9,8,7,6,5,4,3,2,1,0:T(8,128)}, f32[2,2,2,2,2,2,2,2,8,128]{9,8,7,6,5,4,3,2,1,0:T(8,128)}, u32[]{:S(2)}, u32[]{:S(2)}) collective-permute-start(f32[2,2,2,2,2,2,2,2,8,128]{9,8,7,6,5,4,3,2,1,0:T(8,128)} %maximum_select_fusion), channel_id=1, source_target_pairs={{0,1},{1,0},{2,3},{3,2},{4,5},{5,4},{6,7},{7,6},{8,9},{9,8},{10,11... | collective-permute-start | bytes 3145736 | tf_op jit(solution)/shard_map/ppermute | solution.py:125
  77.4 2.2 %collective-permute-start.2 = (f32[16,4,4096]{2,1,0:T(4,128)}, f32[16,4,4096]{2,1,0:T(4,128)}, u32[]{:S(2)}, u32[]{:S(2)}) collective-permute-start(f32[16,4,4096]{2,1,0:T(4,128)} %get-tuple-element.2), channel_id=1, source_target_pairs={{0,1},{1,2},{2,3},{3,4},{4,5},{5,6},{6,7},{7,8},{8,9},{9,10},{10,1... | collective-permute-start | bytes 3145736 | tf_op jit(solution)/shard_map/ppermute | solution.py:21
  79.6 3.1 %collective-permute-start.3 = (f32[16,4,4096]{2,1,0:T(4,128)}, f32[16,4,4096]{2,1,0:T(4,128)}, u32[]{:S(2)}, u32[]{:S(2)}) collective-permute-start(f32[16,4,4096]{2,1,0:T(4,128)} %get-tuple-element.3), channel_id=1, source_target_pairs={{1,0},{2,1},{3,2},{4,3},{5,4},{6,5},{7,6},{8,7},{9,8},{10,9},{11,1... | collective-permute-start | bytes 3145736 | tf_op jit(solution)/shard_map/ppermute | solution.py:24
  82.8 2.4 %collective-permute-start.10 = (f32[12,2,128]{2,1,0:T(2,128)S(1)}, f32[12,2,128]{2,1,0:T(2,128)S(1)}, u32[]{:S(2)}, u32[]{:S(2)}) collective-permute-start(f32[12,2,128]{2,1,0:T(2,128)S(1)} %get-tuple-element.18), channel_id=1, source_target_pairs={{0,1},{1,2},{2,3},{3,4},{4,5},{5,6},{6,7},{7,8},{8,9},{9,10},{10,1... | collective-permute-start | bytes 36872 | tf_op jit(solution)/shard_map/ppermute | solution.py:21
  85.3 2.1 %collective-permute-start.11 = (f32[12,2,128]{2,1,0:T(2,128)S(1)}, f32[12,2,128]{2,1,0:T(2,128)S(1)}, u32[]{:S(2)}, u32[]{:S(2)}) collective-permute-start(f32[12,2,128]{2,1,0:T(2,128)S(1)} %get-tuple-element.19), channel_id=1, source_target_pairs={{1,0},{2,1},{3,2},{4,3},{5,4},{6,5},{7,6},{8,7},{9,8},{10,9},{11,1... | collective-permute-start | bytes 36872 | tf_op jit(solution)/shard_map/ppermute | solution.py:24
  87.4 2.2 %select_bitcast_fusion.1 = (f32[2,2,2,2,2,2,2,2,1,8,128]{10,9,8,7,6,5,4,3,2,1,0:T(8,128)S(1)}, f32[2,2,2,2,2,2,2,2,1,8,128]{10,9,8,7,6,5,4,3,2,1,0:T(8,128)S(1)}) fusion(f32[2,2,2,2,2,2,2,2,8,128]{9,8,7,6,5,4,3,2,1,0:T(8,128)} %collective-permute-done.7, pred[]{:T(512)S(6)} %eq.10, f32[2,2,2,2,1,2,2,2,8,128]{9,8,7,6,5,4,3,2,1,0:T(8,128)} %copy-done.3, ...), kind=kLoop, calls=%fused_computation.32 | loop fusion | flops 1310720 | bytes 5242882 | tf_op jit(solution)/shard_map/stack | solution.py:177
  91.6 4.4 %collective-permute-done.3 = f32[16,4,4096]{2,1,0:T(4,128)} collective-permute-done((f32[16,4,4096]{2,1,0:T(4,128)}, f32[16,4,4096]{2,1,0:T(4,128)}, u32[]{:S(2)}, u32[]{:S(2)}) %collective-permute-start.3) | collective-permute-done | bytes 1048608 | tf_op jit(solution)/shard_map/ppermute | solution.py:24
  96.0 5.6 %fusion = f32[16,16,128]{2,1,0:T(8,128)S(1)} fusion(f32[4096,128,1]{1,0,2:T(8,128)S(1)} %bitcast.84, f32[16,4,4096]{2,1,0:T(4,128)} %collective-permute-done.3, f32[16,8,4096]{2,1,0:T(8,128)S(1)} %constant_dynamic-update-slice_fusion, f32[16,4,4096]{2,1,0:T(4,128)} %collective-permute-done.2), kind=kOutput, calls=%fused_computation.1 | convolution fusion | flops 1612709888 | bytes 6422528 | tf_op jit(solution)/shard_map/dot_general | solution.py:191
  101.7 3.1 %select_convert_fusion.1 = bf16[14,14,32,128]{3,2,1,0:T(8,128)(2,1)S(1)} fusion(f32[32]{0:T(128)S(1)} %copy-done.9, pred[14,14]{1,0:T(8,128)(4,1)S(1)} %slice_bitcast_fusion.2, bf16[3,3,32,32]{3,2,1,0:T(8,128)(2,1)S(1)} %copy-done, f32[32]{0:T(128)S(1)} %copy-done.10, f32[32]{0:T(128)S(1)} %copy-done.13, f32[16,16,128]{2,1,0:T(8,128)S(1)} %fusion, ...), kind=kOutput, calls=%fused_computation.8 | convolution fusion | flops 469024768 | bytes 1755972 | tf_op jit(solution)/shard_map/conv_general_dilated | solution.py:47
  104.9 3.5 %multiply_reduce_fusion = (f32[12,12,128]{2,1,0:T(8,128)S(1)}, f32[12,12,32,128]{3,2,1,0:T(8,128)}) fusion(f32[32]{0:T(128)S(1)} %copy-done.11, f32[32]{0:T(128)S(1)} %copy-done.12, bf16[14,14,32,128]{3,2,1,0:T(8,128)(2,1)S(1)} %select_convert_fusion.1, bf16[3,3,32,32]{3,2,1,0:T(8,128)(2,1)S(1)} %copy-done.8), kind=kOutput, calls=%fused_computation.10 | convolution fusion | flops 341489664 | bytes 4057344 | tf_op jit(solution)/shard_map/conv_general_dilated | solution.py:47
  108.4 4.1 %fusion.12 = f32[8,8,128]{2,1,0:T(8,128)S(1)} fusion(bf16[3,3,32,32]{3,2,1,0:T(8,128)(2,1)S(1)} %copy-done, bf16[3,3,32,32]{3,2,1,0:T(8,128)(2,1)S(1)} %copy-done.8, f32[12,12,32,128]{3,2,1,0:T(8,128)} %get-tuple-element.23, f32[12,12,128]{2,1,0:T(8,128)S(1)} %maximum_subtract_fusion, f32[32]{0:T(128)S(1)} %copy-done.11, f32[32]{0:T(128)S(1)} %copy-done.12, ...), kind=kOutput, calls=%fused_computation.21 | convolution fusion | flops 394027008 | bytes 3462656 | tf_op jit(solution)/shard_map/conv_general_dilated | solution.py:58
  112.5 3.2 %convolution_bitcast_fusion = f32[4096,128]{0,1:T(8,128)} fusion(f32[8,8,128]{2,1,0:T(8,128)S(1)} %fusion.12, f32[8,8,4096]{2,1,0:T(8,128)S(1)} %copy-done.1), kind=kOutput, calls=%fused_computation | convolution fusion | flops 402653184 | bytes 3178496 | tf_op jit(solution)/shard_map/dot_general | solution.py:202
  117.8 1.9 %collective-permute-start.12 = (f32[2,2,2,2,2,2,2,2,8,128]{9,8,7,6,5,4,3,2,1,0:T(8,128)S(1)}, f32[2,2,2,2,2,2,2,2,8,128]{9,8,7,6,5,4,3,2,1,0:T(8,128)}, u32[]{:S(2)}, u32[]{:S(2)}) collective-permute-start(f32[2,2,2,2,2,2,2,2,8,128]{9,8,7,6,5,4,3,2,1,0:T(8,128)S(1)} %dynamic-slice_bitcast_fusion), channel_id=1, source_target_pairs={{0,1},{1,0},{2,3},{3,2},{4,5},{5,4},{6,7},{7,6},{8,9},{9,8},{10,11... | collective-permute-start | bytes 3145736 | tf_op jit(solution)/shard_map/ppermute | solution.py:125
  119.7 2.8 %collective-permute-done.12 = f32[2,2,2,2,2,2,2,2,8,128]{9,8,7,6,5,4,3,2,1,0:T(8,128)} collective-permute-done((f32[2,2,2,2,2,2,2,2,8,128]{9,8,7,6,5,4,3,2,1,0:T(8,128)S(1)}, f32[2,2,2,2,2,2,2,2,8,128]{9,8,7,6,5,4,3,2,1,0:T(8,128)}, u32[]{:S(2)}, u32[]{:S(2)}) %collective-permute-start.12) | collective-permute-done | bytes 1048608 | tf_op jit(solution)/shard_map/ppermute | solution.py:125
  124.0 1.9 %collective-permute-start.13 = (f32[2,2,2,2,2,2,2,8,128]{8,7,6,5,4,3,2,1,0:T(8,128)S(1)}, f32[2,2,2,2,2,2,2,8,128]{8,7,6,5,4,3,2,1,0:T(8,128)S(1)}, u32[]{:S(2)}, u32[]{:S(2)}) collective-permute-start(f32[2,2,2,2,2,2,2,8,128]{8,7,6,5,4,3,2,1,0:T(8,128)S(1)} %bitcast_select_fusion), channel_id=1, source_target_pairs={{0,2},{1,17},{2,0},{3,19},{4,6},{5,21},{6,4},{7,23},{8,10},{9,25},... | collective-permute-start | bytes 1572872 | tf_op jit(solution)/shard_map/ppermute | solution.py:125
  125.9 8.3 %collective-permute-done.13 = f32[2,2,2,2,2,2,2,8,128]{8,7,6,5,4,3,2,1,0:T(8,128)S(1)} collective-permute-done((f32[2,2,2,2,2,2,2,8,128]{8,7,6,5,4,3,2,1,0:T(8,128)S(1)}, f32[2,2,2,2,2,2,2,8,128]{8,7,6,5,4,3,2,1,0:T(8,128)S(1)}, u32[]{:S(2)}, u32[]{:S(2)}) %collective-permute-start.13) | collective-permute-done | bytes 524320 | tf_op jit(solution)/shard_map/ppermute | solution.py:125
  134.4 3.8 %collective-permute-start.14 = (f32[2,2,2,2,2,2,8,128]{7,6,5,4,3,2,1,0:T(8,128)S(1)}, f32[2,2,2,2,2,2,8,128]{7,6,5,4,3,2,1,0:T(8,128)S(1)}, u32[]{:S(2)}, u32[]{:S(2)}) collective-permute-start(f32[2,2,2,2,2,2,8,128]{7,6,5,4,3,2,1,0:T(8,128)S(1)} %bitcast_select_fusion.2), channel_id=1, source_target_pairs={{0,16},{1,3},{2,18},{3,1},{4,20},{5,7},{6,22},{7,5},{8,24},{9,11},... | collective-permute-start | bytes 786440 | tf_op jit(solution)/shard_map/ppermute | solution.py:125
  138.2 4.0 %collective-permute-done.14 = f32[2,2,2,2,2,2,8,128]{7,6,5,4,3,2,1,0:T(8,128)S(1)} collective-permute-done((f32[2,2,2,2,2,2,8,128]{7,6,5,4,3,2,1,0:T(8,128)S(1)}, f32[2,2,2,2,2,2,8,128]{7,6,5,4,3,2,1,0:T(8,128)S(1)}, u32[]{:S(2)}, u32[]{:S(2)}) %collective-permute-start.14) | collective-permute-done | bytes 262176 | tf_op jit(solution)/shard_map/ppermute | solution.py:125
  144.3 7.8 %collective-permute-done.15 = f32[2,2,2,2,2,8,128]{6,5,4,3,2,1,0:T(8,128)S(1)} collective-permute-done((f32[2,2,2,2,2,8,128]{6,5,4,3,2,1,0:T(8,128)S(1)}, f32[2,2,2,2,2,8,128]{6,5,4,3,2,1,0:T(8,128)S(1)}, u32[]{:S(2)}, u32[]{:S(2)}) %collective-permute-start.15) | collective-permute-done | bytes 131104 | tf_op jit(solution)/shard_map/ppermute | solution.py:125
  152.7 10.3 %all-to-all-start.1 = ((f32[32,8,128]{2,1,0:T(8,128)}), f32[32,8,128]{2,1,0:T(8,128)S(1)}, u32[]{:S(2)}, u32[]{:S(2)}) async-start(f32[32,8,128]{2,1,0:T(8,128)} %bitcast.37), calls=%async_computation.1 | async-start | bytes 262144 | tf_op jit(solution)/shard_map/all_to_all | solution.py:152
  163.6 13.6 %all-to-all-done.1 = f32[32,8,128]{2,1,0:T(8,128)S(1)} async-done(((f32[32,8,128]{2,1,0:T(8,128)}), f32[32,8,128]{2,1,0:T(8,128)S(1)}, u32[]{:S(2)}, u32[]{:S(2)}) %all-to-all-start.1) | async-done | bytes 131104 | tf_op jit(solution)/shard_map/all_to_all | solution.py:152
  (75 shorter events, 20.8 us)
Async XLA Ops:
  0.6 101.0 %copy-start = (bf16[3,3,32,32]{3,2,1,0:T(8,128)(2,1)S(1)}, bf16[3,3,32,32]{3,2,1,0:T(8,128)(2,1)}, u32[]{:S(2)}) copy-start(bf16[3,3,32,32]{3,2,1,0:T(8,128)(2,1)} %param.15) | copy-start | bytes 55300
  0.6 26.7 %copy-start.6 = (f32[8,8,128]{2,1,0:T(8,128)S(1)}, f32[8,8,128]{2,1,0:T(8,128)}, u32[]{:S(2)}) copy-start(f32[8,8,128]{2,1,0:T(8,128)} %param.12) | copy-start | bytes 98308
  2.0 33.1 %all-to-all-start = ((f32[32,8,128]{2,1,0:T(8,128)}), f32[32,8,128]{2,1,0:T(8,128)S(1)}, u32[]{:S(2)}, u32[]{:S(2)}) async-start(f32[32,8,128]{2,1,0:T(8,128)} %broadcast_in_dim.67), calls=%async_computation | async-start | bytes 262144 | tf_op jit(solution)/shard_map/all_to_all | solution.py:166
  23.0 28.7 %collective-permute-start = (f32[4,8,4096]{2,1,0:T(8,128)S(1)}, f32[4,8,4096]{2,1,0:T(8,128)}, u32[]{:S(2)}, u32[]{:S(2)}) collective-permute-start(f32[4,8,4096]{2,1,0:T(8,128)S(1)} %get-tuple-element.7), channel_id=1, source_target_pairs={{0,16},{16,32},{32,48},{48,64},{64,80},{80,96},{96,112},{112,128},... | collective-permute-start | bytes 1572872 | tf_op jit(solution)/shard_map/ppermute | solution.py:21
  26.0 33.1 %collective-permute-start.1 = (f32[4,8,4096]{2,1,0:T(8,128)}, f32[4,8,4096]{2,1,0:T(8,128)}, u32[]{:S(2)}, u32[]{:S(2)}) collective-permute-start(f32[4,8,4096]{2,1,0:T(8,128)} %get-tuple-element.6), channel_id=1, source_target_pairs={{16,0},{32,16},{48,32},{64,48},{80,64},{96,80},{112,96},{128,112},... | collective-permute-start | bytes 1572872 | tf_op jit(solution)/shard_map/ppermute | solution.py:24
  27.4 55.4 %collective-permute-start.8 = (f32[2,8,128]{2,1,0:T(8,128)S(1)}, f32[2,8,128]{2,1,0:T(8,128)S(1)}, u32[]{:S(2)}, u32[]{:S(2)}) collective-permute-start(f32[2,8,128]{2,1,0:T(8,128)S(1)} %get-tuple-element.21), channel_id=1, source_target_pairs={{0,16},{16,32},{32,48},{48,64},{64,80},{80,96},{96,112},{112,128},... | collective-permute-start | bytes 24584 | tf_op jit(solution)/shard_map/ppermute | solution.py:21
  31.4 51.5 %collective-permute-start.9 = (f32[2,8,128]{2,1,0:T(8,128)S(1)}, f32[2,8,128]{2,1,0:T(8,128)S(1)}, u32[]{:S(2)}, u32[]{:S(2)}) collective-permute-start(f32[2,8,128]{2,1,0:T(8,128)S(1)} %get-tuple-element.20), channel_id=1, source_target_pairs={{16,0},{32,16},{48,32},{64,48},{80,64},{96,80},{112,96},{128,112},... | collective-permute-start | bytes 24584 | tf_op jit(solution)/shard_map/ppermute | solution.py:24
  35.2 14.1 %collective-permute-start.4 = (f32[2,2,2,2,2,8,128]{6,5,4,3,2,1,0:T(8,128)S(1)}, f32[2,2,2,2,2,8,128]{6,5,4,3,2,1,0:T(8,128)S(1)}, u32[]{:S(2)}, u32[]{:S(2)}) collective-permute-start(f32[2,2,2,2,2,8,128]{6,5,4,3,2,1,0:T(8,128)S(1)} %bitcast.87), channel_id=1, source_target_pairs={{0,128},{1,129},{2,130},{3,131},{4,132},{5,133},{6,134},{7,135},{8... | collective-permute-start | bytes 393224 | tf_op jit(solution)/shard_map/ppermute | solution.py:125
  49.3 9.7 %copy-start.1 = (f32[8,8,4096]{2,1,0:T(8,128)S(1)}, f32[8,8,4096]{2,1,0:T(8,128)}, u32[]{:S(2)}) copy-start(f32[8,8,4096]{2,1,0:T(8,128)} %param.11) | copy-start | bytes 3145732
  49.3 7.5 %collective-permute-start.5 = (f32[2,2,2,2,2,2,8,128]{7,6,5,4,3,2,1,0:T(8,128)S(1)}, f32[2,2,2,2,2,2,8,128]{7,6,5,4,3,2,1,0:T(8,128)S(1)}, u32[]{:S(2)}, u32[]{:S(2)}) collective-permute-start(f32[2,2,2,2,2,2,8,128]{7,6,5,4,3,2,1,0:T(8,128)S(1)} %pad_maximum_fusion.3), channel_id=1, source_target_pairs={{0,16},{1,3},{2,18},{3,1},{4,20},{5,7},{6,22},{7,5},{8,24},{9,11},... | collective-permute-start | bytes 786440 | tf_op jit(solution)/shard_map/ppermute | solution.py:125
  57.1 10.2 %collective-permute-start.6 = (f32[2,2,2,2,2,2,2,8,128]{8,7,6,5,4,3,2,1,0:T(8,128)S(1)}, f32[2,2,2,2,2,2,2,8,128]{8,7,6,5,4,3,2,1,0:T(8,128)S(1)}, u32[]{:S(2)}, u32[]{:S(2)}) collective-permute-start(f32[2,2,2,2,2,2,2,8,128]{8,7,6,5,4,3,2,1,0:T(8,128)S(1)} %maximum_select_fusion.1), channel_id=1, source_target_pairs={{0,2},{1,17},{2,0},{3,19},{4,6},{5,21},{6,4},{7,23},{8,10},{9,25},... | collective-permute-start | bytes 1572872 | tf_op jit(solution)/shard_map/ppermute | solution.py:125
  67.7 0.8 copy-start.2
  67.7 2.0 %copy-start.3 = (f32[2,2,2,2,1,2,2,2,8,128]{9,8,7,6,5,4,3,2,1,0:T(8,128)}, f32[2,2,2,2,1,2,2,2,8,128]{9,8,7,6,5,4,3,2,1,0:T(8,128)S(1)}, u32[]{:S(2)}) copy-start(f32[2,2,2,2,1,2,2,2,8,128]{9,8,7,6,5,4,3,2,1,0:T(8,128)S(1)} %get-tuple-element.9) | copy-start | bytes 1572868
  67.7 2.0 %copy-start.4 = (f32[2,2,2,2,1,2,2,2,8,128]{9,8,7,6,5,4,3,2,1,0:T(8,128)}, f32[2,2,2,2,1,2,2,2,8,128]{9,8,7,6,5,4,3,2,1,0:T(8,128)S(1)}, u32[]{:S(2)}) copy-start(f32[2,2,2,2,1,2,2,2,8,128]{9,8,7,6,5,4,3,2,1,0:T(8,128)S(1)} %get-tuple-element.10) | copy-start | bytes 1572868
  67.7 2.0 %copy-start.5 = (f32[2,2,2,2,2,2,2,1,8,128]{9,8,6,5,4,3,2,1,0,7:T(8,128)}, f32[2,2,2,2,2,2,2,1,8,128]{9,8,6,5,4,3,2,1,0,7:T(8,128)S(1)}, u32[]{:S(2)}) copy-start(f32[2,2,2,2,2,2,2,1,8,128]{9,8,6,5,4,3,2,1,0,7:T(8,128)S(1)} %get-tuple-element.11) | copy-start | bytes 1572868
  69.7 17.7 %collective-permute-start.7 = (f32[2,2,2,2,2,2,2,2,8,128]{9,8,7,6,5,4,3,2,1,0:T(8,128)}, f32[2,2,2,2,2,2,2,2,8,128]{9,8,7,6,5,4,3,2,1,0:T(8,128)}, u32[]{:S(2)}, u32[]{:S(2)}) collective-permute-start(f32[2,2,2,2,2,2,2,2,8,128]{9,8,7,6,5,4,3,2,1,0:T(8,128)} %maximum_select_fusion), channel_id=1, source_target_pairs={{0,1},{1,0},{2,3},{3,2},{4,5},{5,4},{6,7},{7,6},{8,9},{9,8},{10,11... | collective-permute-start | bytes 3145736 | tf_op jit(solution)/shard_map/ppermute | solution.py:125
  77.4 14.2 %collective-permute-start.2 = (f32[16,4,4096]{2,1,0:T(4,128)}, f32[16,4,4096]{2,1,0:T(4,128)}, u32[]{:S(2)}, u32[]{:S(2)}) collective-permute-start(f32[16,4,4096]{2,1,0:T(4,128)} %get-tuple-element.2), channel_id=1, source_target_pairs={{0,1},{1,2},{2,3},{3,4},{4,5},{5,6},{6,7},{7,8},{8,9},{9,10},{10,1... | collective-permute-start | bytes 3145736 | tf_op jit(solution)/shard_map/ppermute | solution.py:21
  79.6 16.4 %collective-permute-start.3 = (f32[16,4,4096]{2,1,0:T(4,128)}, f32[16,4,4096]{2,1,0:T(4,128)}, u32[]{:S(2)}, u32[]{:S(2)}) collective-permute-start(f32[16,4,4096]{2,1,0:T(4,128)} %get-tuple-element.3), channel_id=1, source_target_pairs={{1,0},{2,1},{3,2},{4,3},{5,4},{6,5},{7,6},{8,7},{9,8},{10,9},{11,1... | collective-permute-start | bytes 3145736 | tf_op jit(solution)/shard_map/ppermute | solution.py:24
  82.8 25.5 %collective-permute-start.10 = (f32[12,2,128]{2,1,0:T(2,128)S(1)}, f32[12,2,128]{2,1,0:T(2,128)S(1)}, u32[]{:S(2)}, u32[]{:S(2)}) collective-permute-start(f32[12,2,128]{2,1,0:T(2,128)S(1)} %get-tuple-element.18), channel_id=1, source_target_pairs={{0,1},{1,2},{2,3},{3,4},{4,5},{5,6},{6,7},{7,8},{8,9},{9,10},{10,1... | collective-permute-start | bytes 36872 | tf_op jit(solution)/shard_map/ppermute | solution.py:21
  85.3 23.1 %collective-permute-start.11 = (f32[12,2,128]{2,1,0:T(2,128)S(1)}, f32[12,2,128]{2,1,0:T(2,128)S(1)}, u32[]{:S(2)}, u32[]{:S(2)}) collective-permute-start(f32[12,2,128]{2,1,0:T(2,128)S(1)} %get-tuple-element.19), channel_id=1, source_target_pairs={{1,0},{2,1},{3,2},{4,3},{5,4},{6,5},{7,6},{8,7},{9,8},{10,9},{11,1... | collective-permute-start | bytes 36872 | tf_op jit(solution)/shard_map/ppermute | solution.py:24
  96.0 5.7 %copy-start.9 = (f32[32]{0:T(128)S(1)}, f32[32]{0:T(128)}, u32[]{:S(2)}) copy-start(f32[32]{0:T(128)} %param.16) | copy-start | bytes 388
  96.0 5.7 %copy-start.10 = (f32[32]{0:T(128)S(1)}, f32[32]{0:T(128)}, u32[]{:S(2)}) copy-start(f32[32]{0:T(128)} %param.14) | copy-start | bytes 388
  96.0 5.7 %copy-start.13 = (f32[32]{0:T(128)S(1)}, f32[32]{0:T(128)}, u32[]{:S(2)}) copy-start(f32[32]{0:T(128)} %param.13) | copy-start | bytes 388
  101.7 3.2 %copy-start.8 = (bf16[3,3,32,32]{3,2,1,0:T(8,128)(2,1)S(1)}, bf16[3,3,32,32]{3,2,1,0:T(8,128)(2,1)}, u32[]{:S(2)}) copy-start(bf16[3,3,32,32]{3,2,1,0:T(8,128)(2,1)} %param.17) | copy-start | bytes 55300
  101.7 3.2 %copy-start.11 = (f32[32]{0:T(128)S(1)}, f32[32]{0:T(128)}, u32[]{:S(2)}) copy-start(f32[32]{0:T(128)} %param.19) | copy-start | bytes 388
  101.7 3.1 %copy-start.12 = (f32[32]{0:T(128)S(1)}, f32[32]{0:T(128)}, u32[]{:S(2)}) copy-start(f32[32]{0:T(128)} %param.18) | copy-start | bytes 388
  117.8 4.7 %collective-permute-start.12 = (f32[2,2,2,2,2,2,2,2,8,128]{9,8,7,6,5,4,3,2,1,0:T(8,128)S(1)}, f32[2,2,2,2,2,2,2,2,8,128]{9,8,7,6,5,4,3,2,1,0:T(8,128)}, u32[]{:S(2)}, u32[]{:S(2)}) collective-permute-start(f32[2,2,2,2,2,2,2,2,8,128]{9,8,7,6,5,4,3,2,1,0:T(8,128)S(1)} %dynamic-slice_bitcast_fusion), channel_id=1, source_target_pairs={{0,1},{1,0},{2,3},{3,2},{4,5},{5,4},{6,7},{7,6},{8,9},{9,8},{10,11... | collective-permute-start | bytes 3145736 | tf_op jit(solution)/shard_map/ppermute | solution.py:125
  124.0 10.2 %collective-permute-start.13 = (f32[2,2,2,2,2,2,2,8,128]{8,7,6,5,4,3,2,1,0:T(8,128)S(1)}, f32[2,2,2,2,2,2,2,8,128]{8,7,6,5,4,3,2,1,0:T(8,128)S(1)}, u32[]{:S(2)}, u32[]{:S(2)}) collective-permute-start(f32[2,2,2,2,2,2,2,8,128]{8,7,6,5,4,3,2,1,0:T(8,128)S(1)} %bitcast_select_fusion), channel_id=1, source_target_pairs={{0,2},{1,17},{2,0},{3,19},{4,6},{5,21},{6,4},{7,23},{8,10},{9,25},... | collective-permute-start | bytes 1572872 | tf_op jit(solution)/shard_map/ppermute | solution.py:125
  125.9 51.3 %copy-start.7 = (f32[8,128]{1,0:T(8,128)S(1)}, f32[8,128]{1,0:T(8,128)}, u32[]{:S(2)}) copy-start(f32[8,128]{1,0:T(8,128)} %param.10) | copy-start | bytes 12292
  134.4 7.8 %collective-permute-start.14 = (f32[2,2,2,2,2,2,8,128]{7,6,5,4,3,2,1,0:T(8,128)S(1)}, f32[2,2,2,2,2,2,8,128]{7,6,5,4,3,2,1,0:T(8,128)S(1)}, u32[]{:S(2)}, u32[]{:S(2)}) collective-permute-start(f32[2,2,2,2,2,2,8,128]{7,6,5,4,3,2,1,0:T(8,128)S(1)} %bitcast_select_fusion.2), channel_id=1, source_target_pairs={{0,16},{1,3},{2,18},{3,1},{4,20},{5,7},{6,22},{7,5},{8,24},{9,11},... | collective-permute-start | bytes 786440 | tf_op jit(solution)/shard_map/ppermute | solution.py:125
  142.3 9.7 %collective-permute-start.15 = (f32[2,2,2,2,2,8,128]{6,5,4,3,2,1,0:T(8,128)S(1)}, f32[2,2,2,2,2,8,128]{6,5,4,3,2,1,0:T(8,128)S(1)}, u32[]{:S(2)}, u32[]{:S(2)}) collective-permute-start(f32[2,2,2,2,2,8,128]{6,5,4,3,2,1,0:T(8,128)S(1)} %dynamic-slice_bitcast_fusion.1), channel_id=1, source_target_pairs={{0,128},{1,129},{2,130},{3,131},{4,132},{5,133},{6,134},{7,135},{8... | collective-permute-start | bytes 393224 | tf_op jit(solution)/shard_map/ppermute | solution.py:125
  152.7 24.5 %all-to-all-start.1 = ((f32[32,8,128]{2,1,0:T(8,128)}), f32[32,8,128]{2,1,0:T(8,128)S(1)}, u32[]{:S(2)}, u32[]{:S(2)}) async-start(f32[32,8,128]{2,1,0:T(8,128)} %bitcast.37), calls=%async_computation.1 | async-start | bytes 262144 | tf_op jit(solution)/shard_map/all_to_all | solution.py:152

commit v9 on v7

--- a/solution.py
+++ b/solution.py
@@ -10,7 +10,7 @@
 ALL_AXES = tuple(f"b{bit}" for bit in range(8, -1, -1))
 ROW_AXES = ALL_AXES[:5]
 COL_AXES = ALL_AXES[5:]
-FAR_COUNT = 5
+FAR_COUNT = 6
 
 
 def with_halo(block, sides, width):

time: 168 us -> 154 us (0.917)
  waiting for transfers between devices: 63.3 us -> 50.7 us
  starting transfers between devices: 40.9 us -> 38.4 us
    ppermute x8 -> x6, waiting for transfers between devices: 42.9 us -> 29.9 us  [exchange(): return lax.ppermute(values, ALL_AXES, pairs)]
    ppermute x8 -> x6, starting transfers between devices: 23.1 us -> 19.9 us  [exchange(): return lax.ppermute(values, ALL_AXES, pairs)]
  transfers between devices with their start and end apart: 13 -> 11, of which waited for: 11 -> 9; matrix products, arithmetic and copies ran while one was open for 1% -> 1% of each run, Pallas kernels for 0% -> 0%
where the time goes in v9:
time: 154 us; the launch traced here: 152 us
  waiting for transfers between devices  50.7 us (33%)
  starting transfers between devices  38.4 us (25%)
  blocking collectives  34 us (22%)
  matrix products  15.4 us (10%)
  other arithmetic  7.13 us (5%)
  local copies, waits for them, and re-layouts  4.88 us (3%)
    all_to_all x1, blocking collectives, gather_all(): data = lax.all_to_all(data, group, 0, 0, tiled=False)  34 us
    ppermute x6, waiting for transfers between devices, exchange(): return lax.ppermute(values, ALL_AXES, pairs)  29.9 us
    ppermute x6, starting transfers between devices, exchange(): return lax.ppermute(values, ALL_AXES, pairs)  19.9 us
    all_to_all x1, waiting for transfers between devices, scatter_sum(): data = lax.all_to_all(data, group, 0, 0, tiled=False)  14 us
    all_to_all x1, starting transfers between devices, scatter_sum(): data = lax.all_to_all(data, group, 0, 0, tiled=False)  9.47 us
    ppermute x2, waiting for transfers between devices, with_halo(): lax.ppermute(lax.slice_in_dim(block, 0, width, axis=dim), axis, backward)  6.86 us
    conv_general_dilated x2, matrix products, conv_valid(): lax.conv_general_dilated(values, weights, (1, 1), 'VALID', dimension_numb...  6.64 us
    ppermute x2, starting transfers between devices, with_halo(): lax.ppermute(lax.slice_in_dim(block, block.shape[dim] - width, None, axis...  5.8 us
  transfers between devices with their start and end apart: 11, of which 9 were waited for; matrix products, arithmetic and copies ran while one was open for 1% of the time, Pallas kernels for 0%

profile of v9, /device:TPU:1, one launch (start us, length us, event | category | flops | bytes accessed | tf_op | source)
XLA Modules:
  0.0 151.6 jit_solution(1965643431458893748)
XLA Ops:
  0.6 0.8 broadcast_in_dim.68
  1.4 34.0 %all_to_all.10 = f32[64,8,128]{2,1,0:T(8,128)S(1)} all-to-all(f32[64,8,128]{2,1,0:T(8,128)S(1)} %broadcast_in_dim.68), channel_id=1, replica_groups=mesh['b8'=2,'b7'=2,'b6'=2,'b5'=2,'b4'=2,'b3'=2,'b2'=2,'b1'=2,'b0'=2] {'b..., dimensions={0} | all-to-all | bytes 524288 | tf_op jit(solution)/shard_map/all_to_all | solution.py:169
  35.4 2.5 %collective-permute-start = (f32[2,2,2,2,2,2,8,128]{7,6,5,4,3,2,1,0:T(8,128)S(1)}, f32[2,2,2,2,2,2,8,128]{7,6,5,4,3,2,1,0:T(8,128)S(1)}, u32[]{:S(2)}, u32[]{:S(2)}) collective-permute-start(f32[2,2,2,2,2,2,8,128]{7,6,5,4,3,2,1,0:T(8,128)S(1)} %bitcast.82), channel_id=1, source_target_pairs={{0,16},{1,3},{2,18},{3,1},{4,20},{5,7},{6,22},{7,5},{8,24},{9,11},... | collective-permute-start | bytes 786440 | tf_op jit(solution)/shard_map/ppermute | solution.py:128
  38.0 4.6 %collective-permute-done = f32[2,2,2,2,2,2,8,128]{7,6,5,4,3,2,1,0:T(8,128)S(1)} collective-permute-done((f32[2,2,2,2,2,2,8,128]{7,6,5,4,3,2,1,0:T(8,128)S(1)}, f32[2,2,2,2,2,2,8,128]{7,6,5,4,3,2,1,0:T(8,128)S(1)}, u32[]{:S(2)}, u32[]{:S(2)}) %collective-permute-start) | collective-permute-done | bytes 262176 | tf_op jit(solution)/shard_map/ppermute | solution.py:128
  42.7 2.2 %collective-permute-start.1 = (f32[2,2,2,2,2,2,2,8,128]{8,7,6,5,4,3,2,1,0:T(8,128)S(1)}, f32[2,2,2,2,2,2,2,8,128]{8,7,6,5,4,3,2,1,0:T(8,128)S(1)}, u32[]{:S(2)}, u32[]{:S(2)}) collective-permute-start(f32[2,2,2,2,2,2,2,8,128]{8,7,6,5,4,3,2,1,0:T(8,128)S(1)} %maximum_select_fusion.1), channel_id=1, source_target_pairs={{0,2},{1,17},{2,0},{3,19},{4,6},{5,21},{6,4},{7,23},{8,10},{9,25},... | collective-permute-start | bytes 1572872 | tf_op jit(solution)/shard_map/ppermute | solution.py:128
  45.0 8.0 %collective-permute-done.1 = f32[2,2,2,2,2,2,2,8,128]{8,7,6,5,4,3,2,1,0:T(8,128)S(1)} collective-permute-done((f32[2,2,2,2,2,2,2,8,128]{8,7,6,5,4,3,2,1,0:T(8,128)S(1)}, f32[2,2,2,2,2,2,2,8,128]{8,7,6,5,4,3,2,1,0:T(8,128)S(1)}, u32[]{:S(2)}, u32[]{:S(2)}) %collective-permute-start.1) | collective-permute-done | bytes 524320 | tf_op jit(solution)/shard_map/ppermute | solution.py:128
  53.3 1.2 maximum_select_fusion
  54.4 6.9 %collective-permute-start.2 = (f32[2,2,2,2,2,2,2,2,8,128]{9,8,7,6,5,4,3,2,1,0:T(8,128)}, f32[2,2,2,2,2,2,2,2,8,128]{9,8,7,6,5,4,3,2,1,0:T(8,128)}, u32[]{:S(2)}, u32[]{:S(2)}) collective-permute-start(f32[2,2,2,2,2,2,2,2,8,128]{9,8,7,6,5,4,3,2,1,0:T(8,128)} %maximum_select_fusion), channel_id=1, source_target_pairs={{0,1},{1,0},{2,3},{3,2},{4,5},{5,4},{6,7},{7,6},{8,9},{9,8},{10,11... | collective-permute-start | bytes 3145736 | tf_op jit(solution)/shard_map/ppermute | solution.py:128
  61.6 2.3 %collective-permute-done.2 = f32[2,2,2,2,2,2,2,2,8,128]{9,8,7,6,5,4,3,2,1,0:T(8,128)} collective-permute-done((f32[2,2,2,2,2,2,2,2,8,128]{9,8,7,6,5,4,3,2,1,0:T(8,128)}, f32[2,2,2,2,2,2,2,2,8,128]{9,8,7,6,5,4,3,2,1,0:T(8,128)}, u32[]{:S(2)}, u32[]{:S(2)}) %collective-permute-start.2) | collective-permute-done | bytes 1048608 | tf_op jit(solution)/shard_map/ppermute | solution.py:128
  64.0 1.6 %select_bitcast_fusion.1 = (f32[2,2,2,2,2,2,2,2,1,8,128]{10,9,8,7,6,5,4,3,2,1,0:T(8,128)S(1)}, f32[2,2,2,2,2,2,2,2,1,8,128]{10,9,8,7,6,5,4,3,2,1,0:T(8,128)S(1)}) fusion(f32[2,2,2,2,2,2,2,2,8,128]{9,8,7,6,5,4,3,2,1,0:T(8,128)} %collective-permute-done.2, pred[]{:T(512)S(6)} %eq.8, f32[2,2,2,2,1,2,2,2,8,128]{9,8,7,6,5,4,3,2,1,0:T(8,128)S(1)} %get-tuple-element.5, ...), kind=kLoop, calls=%fused_computation.28 | loop fusion | flops 1310720 | bytes 5242882 | tf_op jit(solution)/shard_map/stack | solution.py:180
  65.8 1.5 convolution_bitcast_fusion.1
  67.3 2.2 %collective-permute-start.3 = (f32[4,8,256]{2,1,0:T(8,128)S(1)}, f32[4,8,256]{2,1,0:T(8,128)S(1)}, u32[]{:S(2)}, u32[]{:S(2)}) collective-permute-start(f32[4,8,256]{2,1,0:T(8,128)S(1)} %get-tuple-element.14), channel_id=1, source_target_pairs={{0,16},{16,32},{32,48},{48,64},{64,80},{80,96},{96,112},{112,128},... | collective-permute-start | bytes 98312 | tf_op jit(solution)/shard_map/ppermute | solution.py:21
  69.6 1.3 collective-permute-start.4
  71.0 3.3 %collective-permute-done.4 = f32[4,8,256]{2,1,0:T(8,128)S(1)} collective-permute-done((f32[4,8,256]{2,1,0:T(8,128)S(1)}, f32[4,8,256]{2,1,0:T(8,128)S(1)}, u32[]{:S(2)}, u32[]{:S(2)}) %collective-permute-start.4) | collective-permute-done | bytes 32800 | tf_op jit(solution)/shard_map/ppermute | solution.py:24
  74.3 3.6 %collective-permute-start.5 = (f32[16,4,256]{2,1,0:T(4,128)S(1)}, f32[16,4,256]{2,1,0:T(4,128)S(1)}, u32[]{:S(2)}, u32[]{:S(2)}) collective-permute-start(f32[16,4,256]{2,1,0:T(4,128)S(1)} %get-tuple-element.12), channel_id=1, source_target_pairs={{0,1},{1,2},{2,3},{3,4},{4,5},{5,6},{6,7},{7,8},{8,9},{9,10},{10,1... | collective-permute-start | bytes 196616 | tf_op jit(solution)/shard_map/ppermute | solution.py:21
  77.9 1.9 %collective-permute-start.6 = (f32[16,4,256]{2,1,0:T(4,128)S(1)}, f32[16,4,256]{2,1,0:T(4,128)S(1)}, u32[]{:S(2)}, u32[]{:S(2)}) collective-permute-start(f32[16,4,256]{2,1,0:T(4,128)S(1)} %get-tuple-element.13), channel_id=1, source_target_pairs={{1,0},{2,1},{3,2},{4,3},{5,4},{6,5},{7,6},{8,7},{9,8},{10,9},{11,1... | collective-permute-start | bytes 196616 | tf_op jit(solution)/shard_map/ppermute | solution.py:24
  79.9 3.6 %collective-permute-done.6 = f32[16,4,256]{2,1,0:T(4,128)S(1)} collective-permute-done((f32[16,4,256]{2,1,0:T(4,128)S(1)}, f32[16,4,256]{2,1,0:T(4,128)S(1)}, u32[]{:S(2)}, u32[]{:S(2)}) %collective-permute-start.6) | collective-permute-done | bytes 65568 | tf_op jit(solution)/shard_map/ppermute | solution.py:24
  83.6 3.1 %select_convert_fusion.1 = bf16[14,14,32,128]{3,2,1,0:T(8,128)(2,1)S(1)} fusion(f32[32]{0:T(128)S(1)} %copy-done.6, pred[14,14]{1,0:T(8,128)(4,1)S(1)} %slice_bitcast_fusion.2, bf16[3,3,32,32]{3,2,1,0:T(8,128)(2,1)S(1)} %copy-done.4, f32[32]{0:T(128)S(1)} %copy-done.7, f32[32]{0:T(128)S(1)} %copy-done.10, f32[16,16,128]{2,1,0:T(8,128)S(1)} %slice.51, ...), kind=kOutput, calls=%fused_computation.2 | convolution fusion | flops 469024768 | bytes 1755972 | tf_op jit(solution)/shard_map/conv_general_dilated | solution.py:47
  86.7 3.5 %multiply_reduce_fusion = (f32[12,12,128]{2,1,0:T(8,128)S(1)}, f32[12,12,32,128]{3,2,1,0:T(8,128)}) fusion(f32[32]{0:T(128)S(1)} %copy-done.8, f32[32]{0:T(128)S(1)} %copy-done.9, bf16[14,14,32,128]{3,2,1,0:T(8,128)(2,1)S(1)} %select_convert_fusion.1, bf16[3,3,32,32]{3,2,1,0:T(8,128)(2,1)S(1)} %copy-done.5), kind=kOutput, calls=%fused_computation.4 | convolution fusion | flops 341489664 | bytes 4057344 | tf_op jit(solution)/shard_map/conv_general_dilated | solution.py:47
  90.3 4.1 %fusion.6 = f32[8,8,128]{2,1,0:T(8,128)S(1)} fusion(bf16[3,3,32,32]{3,2,1,0:T(8,128)(2,1)S(1)} %copy-done.4, bf16[3,3,32,32]{3,2,1,0:T(8,128)(2,1)S(1)} %copy-done.5, f32[12,12,32,128]{3,2,1,0:T(8,128)} %get-tuple-element.17, f32[12,12,128]{2,1,0:T(8,128)S(1)} %maximum_subtract_fusion, f32[32]{0:T(128)S(1)} %copy-done.8, f32[32]{0:T(128)S(1)} %copy-done.9, ...), kind=kOutput, calls=%fused_computation.15 | convolution fusion | flops 394027008 | bytes 3462656 | tf_op jit(solution)/shard_map/conv_general_dilated | solution.py:58
  94.4 3.2 %convolution_bitcast_fusion = f32[4096,128]{0,1:T(8,128)} fusion(f32[8,8,128]{2,1,0:T(8,128)S(1)} %fusion.6, f32[8,8,4096]{2,1,0:T(8,128)S(1)} %copy-done), kind=kOutput, calls=%fused_computation | convolution fusion | flops 402653184 | bytes 3178496 | tf_op jit(solution)/shard_map/dot_general | solution.py:202
  97.6 1.9 %copy.36 = f32[4096,128]{1,0:T(8,128)S(1)} copy(f32[4096,128]{0,1:T(8,128)} %convolution_bitcast_fusion) | data formatting | bytes 4194304 | tf_op jit(solution)/shard_map/dot_general | solution.py:202
  99.5 1.2 dynamic-slice_bitcast_fusion
  100.7 1.9 %collective-permute-start.7 = (f32[2,2,2,2,2,2,2,2,8,128]{9,8,7,6,5,4,3,2,1,0:T(8,128)}, f32[2,2,2,2,2,2,2,2,8,128]{9,8,7,6,5,4,3,2,1,0:T(8,128)}, u32[]{:S(2)}, u32[]{:S(2)}) collective-permute-start(f32[2,2,2,2,2,2,2,2,8,128]{9,8,7,6,5,4,3,2,1,0:T(8,128)} %dynamic-slice_bitcast_fusion), channel_id=1, source_target_pairs={{0,1},{1,0},{2,3},{3,2},{4,5},{5,4},{6,7},{7,6},{8,9},{9,8},{10,11... | collective-permute-start | bytes 3145736 | tf_op jit(solution)/shard_map/ppermute | solution.py:128
  102.6 3.0 %collective-permute-done.7 = f32[2,2,2,2,2,2,2,2,8,128]{9,8,7,6,5,4,3,2,1,0:T(8,128)} collective-permute-done((f32[2,2,2,2,2,2,2,2,8,128]{9,8,7,6,5,4,3,2,1,0:T(8,128)}, f32[2,2,2,2,2,2,2,2,8,128]{9,8,7,6,5,4,3,2,1,0:T(8,128)}, u32[]{:S(2)}, u32[]{:S(2)}) %collective-permute-start.7) | collective-permute-done | bytes 1048608 | tf_op jit(solution)/shard_map/ppermute | solution.py:128
  105.6 1.7 %bitcast_add_fusion = f32[2,2,2,2,2,2,2,2,8,128]{9,8,7,6,5,4,3,2,1,0:T(8,128)S(1)} fusion(f32[2,2,2,2,2,2,2,2,8,128]{9,8,7,6,5,4,3,2,1,0:T(8,128)} %collective-permute-done.7, f32[2,2,2,2,2,2,2,2,2,8,128]{10,9,8,7,6,5,4,3,2,1,0:T(8,128)} %bitcast.80, s32[]{:T(128)S(6)} %select_n.153), kind=kLoop, calls=%fused_computation.24 | loop fusion | flops 262144 | bytes 3145732 | tf_op jit(solution)/shard_map/add | solution.py:151
  107.5 2.2 %collective-permute-start.8 = (f32[2,2,2,2,2,2,2,8,128]{8,7,6,5,4,3,2,1,0:T(8,128)S(1)}, f32[2,2,2,2,2,2,2,8,128]{8,7,6,5,4,3,2,1,0:T(8,128)S(1)}, u32[]{:S(2)}, u32[]{:S(2)}) collective-permute-start(f32[2,2,2,2,2,2,2,8,128]{8,7,6,5,4,3,2,1,0:T(8,128)S(1)} %bitcast_select_fusion), channel_id=1, source_target_pairs={{0,2},{1,17},{2,0},{3,19},{4,6},{5,21},{6,4},{7,23},{8,10},{9,25},... | collective-permute-start | bytes 1572872 | tf_op jit(solution)/shard_map/ppermute | solution.py:128
  109.7 8.0 %collective-permute-done.8 = f32[2,2,2,2,2,2,2,8,128]{8,7,6,5,4,3,2,1,0:T(8,128)S(1)} collective-permute-done((f32[2,2,2,2,2,2,2,8,128]{8,7,6,5,4,3,2,1,0:T(8,128)S(1)}, f32[2,2,2,2,2,2,2,8,128]{8,7,6,5,4,3,2,1,0:T(8,128)S(1)}, u32[]{:S(2)}, u32[]{:S(2)}) %collective-permute-start.8) | collective-permute-done | bytes 524320 | tf_op jit(solution)/shard_map/ppermute | solution.py:128
  117.9 4.2 %collective-permute-start.9 = (f32[2,2,2,2,2,2,8,128]{7,6,5,4,3,2,1,0:T(8,128)S(1)}, f32[2,2,2,2,2,2,8,128]{7,6,5,4,3,2,1,0:T(8,128)S(1)}, u32[]{:S(2)}, u32[]{:S(2)}) collective-permute-start(f32[2,2,2,2,2,2,8,128]{7,6,5,4,3,2,1,0:T(8,128)S(1)} %bitcast_select_fusion.2), channel_id=1, source_target_pairs={{0,16},{1,3},{2,18},{3,1},{4,20},{5,7},{6,22},{7,5},{8,24},{9,11},... | collective-permute-start | bytes 786440 | tf_op jit(solution)/shard_map/ppermute | solution.py:128
  122.1 4.0 %collective-permute-done.9 = f32[2,2,2,2,2,2,8,128]{7,6,5,4,3,2,1,0:T(8,128)S(1)} collective-permute-done((f32[2,2,2,2,2,2,8,128]{7,6,5,4,3,2,1,0:T(8,128)S(1)}, f32[2,2,2,2,2,2,8,128]{7,6,5,4,3,2,1,0:T(8,128)S(1)}, u32[]{:S(2)}, u32[]{:S(2)}) %collective-permute-start.9) | collective-permute-done | bytes 262176 | tf_op jit(solution)/shard_map/ppermute | solution.py:128
  126.9 9.5 %all-to-all-start.1 = ((f32[64,8,128]{2,1,0:T(8,128)}), f32[64,8,128]{2,1,0:T(8,128)S(1)}, u32[]{:S(2)}, u32[]{:S(2)}) async-start(f32[64,8,128]{2,1,0:T(8,128)} %bitcast.34), calls=%async_computation.1 | async-start | bytes 524288 | tf_op jit(solution)/shard_map/all_to_all | solution.py:155
  137.0 14.0 %all-to-all-done.1 = f32[64,8,128]{2,1,0:T(8,128)S(1)} async-done(((f32[64,8,128]{2,1,0:T(8,128)}), f32[64,8,128]{2,1,0:T(8,128)S(1)}, u32[]{:S(2)}, u32[]{:S(2)}) %all-to-all-start.1) | async-done | bytes 262176 | tf_op jit(solution)/shard_map/all_to_all | solution.py:155
  (47 shorter events, 3.6 us)
Async XLA Ops:
  0.6 65.2 %copy-start = (f32[8,8,4096]{2,1,0:T(8,128)S(1)}, f32[8,8,4096]{2,1,0:T(8,128)}, u32[]{:S(2)}) copy-start(f32[8,8,4096]{2,1,0:T(8,128)} %param.11) | copy-start | bytes 3145732
  35.4 7.1 %collective-permute-start = (f32[2,2,2,2,2,2,8,128]{7,6,5,4,3,2,1,0:T(8,128)S(1)}, f32[2,2,2,2,2,2,8,128]{7,6,5,4,3,2,1,0:T(8,128)S(1)}, u32[]{:S(2)}, u32[]{:S(2)}) collective-permute-start(f32[2,2,2,2,2,2,8,128]{7,6,5,4,3,2,1,0:T(8,128)S(1)} %bitcast.82), channel_id=1, source_target_pairs={{0,16},{1,3},{2,18},{3,1},{4,20},{5,7},{6,22},{7,5},{8,24},{9,11},... | collective-permute-start | bytes 786440 | tf_op jit(solution)/shard_map/ppermute | solution.py:128
  42.7 10.2 %collective-permute-start.1 = (f32[2,2,2,2,2,2,2,8,128]{8,7,6,5,4,3,2,1,0:T(8,128)S(1)}, f32[2,2,2,2,2,2,2,8,128]{8,7,6,5,4,3,2,1,0:T(8,128)S(1)}, u32[]{:S(2)}, u32[]{:S(2)}) collective-permute-start(f32[2,2,2,2,2,2,2,8,128]{8,7,6,5,4,3,2,1,0:T(8,128)S(1)} %maximum_select_fusion.1), channel_id=1, source_target_pairs={{0,2},{1,17},{2,0},{3,19},{4,6},{5,21},{6,4},{7,23},{8,10},{9,25},... | collective-permute-start | bytes 1572872 | tf_op jit(solution)/shard_map/ppermute | solution.py:128
  54.4 9.6 %collective-permute-start.2 = (f32[2,2,2,2,2,2,2,2,8,128]{9,8,7,6,5,4,3,2,1,0:T(8,128)}, f32[2,2,2,2,2,2,2,2,8,128]{9,8,7,6,5,4,3,2,1,0:T(8,128)}, u32[]{:S(2)}, u32[]{:S(2)}) collective-permute-start(f32[2,2,2,2,2,2,2,2,8,128]{9,8,7,6,5,4,3,2,1,0:T(8,128)} %maximum_select_fusion), channel_id=1, source_target_pairs={{0,1},{1,0},{2,3},{3,2},{4,5},{5,4},{6,7},{7,6},{8,9},{9,8},{10,11... | collective-permute-start | bytes 3145736 | tf_op jit(solution)/shard_map/ppermute | solution.py:128
  65.8 1.6 %copy-start.2 = (f32[8,8,128]{2,1,0:T(8,128)S(1)}, f32[8,8,128]{2,1,0:T(8,128)}, u32[]{:S(2)}) copy-start(f32[8,8,128]{2,1,0:T(8,128)} %param.12) | copy-start | bytes 98308
  65.8 17.8 %copy-start.4 = (bf16[3,3,32,32]{3,2,1,0:T(8,128)(2,1)S(1)}, bf16[3,3,32,32]{3,2,1,0:T(8,128)(2,1)}, u32[]{:S(2)}) copy-start(bf16[3,3,32,32]{3,2,1,0:T(8,128)(2,1)} %param.15) | copy-start | bytes 55300
  65.8 17.7 %copy-start.6 = (f32[32]{0:T(128)S(1)}, f32[32]{0:T(128)}, u32[]{:S(2)}) copy-start(f32[32]{0:T(128)} %param.16) | copy-start | bytes 388
  65.8 17.7 %copy-start.7 = (f32[32]{0:T(128)S(1)}, f32[32]{0:T(128)}, u32[]{:S(2)}) copy-start(f32[32]{0:T(128)} %param.14) | copy-start | bytes 388
  65.8 17.7 %copy-start.10 = (f32[32]{0:T(128)S(1)}, f32[32]{0:T(128)}, u32[]{:S(2)}) copy-start(f32[32]{0:T(128)} %param.13) | copy-start | bytes 388
  67.3 3.6 %collective-permute-start.3 = (f32[4,8,256]{2,1,0:T(8,128)S(1)}, f32[4,8,256]{2,1,0:T(8,128)S(1)}, u32[]{:S(2)}, u32[]{:S(2)}) collective-permute-start(f32[4,8,256]{2,1,0:T(8,128)S(1)} %get-tuple-element.14), channel_id=1, source_target_pairs={{0,16},{16,32},{32,48},{48,64},{64,80},{80,96},{96,112},{112,128},... | collective-permute-start | bytes 98312 | tf_op jit(solution)/shard_map/ppermute | solution.py:21
  69.6 4.7 %collective-permute-start.4 = (f32[4,8,256]{2,1,0:T(8,128)S(1)}, f32[4,8,256]{2,1,0:T(8,128)S(1)}, u32[]{:S(2)}, u32[]{:S(2)}) collective-permute-start(f32[4,8,256]{2,1,0:T(8,128)S(1)} %get-tuple-element.15), channel_id=1, source_target_pairs={{16,0},{32,16},{48,32},{64,48},{80,64},{96,80},{112,96},{128,112},... | collective-permute-start | bytes 98312 | tf_op jit(solution)/shard_map/ppermute | solution.py:24
  74.3 5.6 %collective-permute-start.5 = (f32[16,4,256]{2,1,0:T(4,128)S(1)}, f32[16,4,256]{2,1,0:T(4,128)S(1)}, u32[]{:S(2)}, u32[]{:S(2)}) collective-permute-start(f32[16,4,256]{2,1,0:T(4,128)S(1)} %get-tuple-element.12), channel_id=1, source_target_pairs={{0,1},{1,2},{2,3},{3,4},{4,5},{5,6},{6,7},{7,8},{8,9},{9,10},{10,1... | collective-permute-start | bytes 196616 | tf_op jit(solution)/shard_map/ppermute | solution.py:21
  77.9 5.6 %collective-permute-start.6 = (f32[16,4,256]{2,1,0:T(4,128)S(1)}, f32[16,4,256]{2,1,0:T(4,128)S(1)}, u32[]{:S(2)}, u32[]{:S(2)}) collective-permute-start(f32[16,4,256]{2,1,0:T(4,128)S(1)} %get-tuple-element.13), channel_id=1, source_target_pairs={{1,0},{2,1},{3,2},{4,3},{5,4},{6,5},{7,6},{8,7},{9,8},{10,9},{11,1... | collective-permute-start | bytes 196616 | tf_op jit(solution)/shard_map/ppermute | solution.py:24
  83.6 3.2 %copy-start.5 = (bf16[3,3,32,32]{3,2,1,0:T(8,128)(2,1)S(1)}, bf16[3,3,32,32]{3,2,1,0:T(8,128)(2,1)}, u32[]{:S(2)}) copy-start(bf16[3,3,32,32]{3,2,1,0:T(8,128)(2,1)} %param.17) | copy-start | bytes 55300
  83.6 3.2 %copy-start.8 = (f32[32]{0:T(128)S(1)}, f32[32]{0:T(128)}, u32[]{:S(2)}) copy-start(f32[32]{0:T(128)} %param.19) | copy-start | bytes 388
  83.6 3.1 %copy-start.9 = (f32[32]{0:T(128)S(1)}, f32[32]{0:T(128)}, u32[]{:S(2)}) copy-start(f32[32]{0:T(128)} %param.18) | copy-start | bytes 388
  99.5 3.2 %copy-start.1 = (f32[4096,128]{1,0:T(8,128)}, f32[4096,128]{1,0:T(8,128)S(1)}, u32[]{:S(2)}) copy-start(f32[4096,128]{1,0:T(8,128)S(1)} %copy.36) | copy-start | bytes 6291460
  100.7 4.9 %collective-permute-start.7 = (f32[2,2,2,2,2,2,2,2,8,128]{9,8,7,6,5,4,3,2,1,0:T(8,128)}, f32[2,2,2,2,2,2,2,2,8,128]{9,8,7,6,5,4,3,2,1,0:T(8,128)}, u32[]{:S(2)}, u32[]{:S(2)}) collective-permute-start(f32[2,2,2,2,2,2,2,2,8,128]{9,8,7,6,5,4,3,2,1,0:T(8,128)} %dynamic-slice_bitcast_fusion), channel_id=1, source_target_pairs={{0,1},{1,0},{2,3},{3,2},{4,5},{5,4},{6,7},{7,6},{8,9},{9,8},{10,11... | collective-permute-start | bytes 3145736 | tf_op jit(solution)/shard_map/ppermute | solution.py:128
  107.5 10.2 %collective-permute-start.8 = (f32[2,2,2,2,2,2,2,8,128]{8,7,6,5,4,3,2,1,0:T(8,128)S(1)}, f32[2,2,2,2,2,2,2,8,128]{8,7,6,5,4,3,2,1,0:T(8,128)S(1)}, u32[]{:S(2)}, u32[]{:S(2)}) collective-permute-start(f32[2,2,2,2,2,2,2,8,128]{8,7,6,5,4,3,2,1,0:T(8,128)S(1)} %bitcast_select_fusion), channel_id=1, source_target_pairs={{0,2},{1,17},{2,0},{3,19},{4,6},{5,21},{6,4},{7,23},{8,10},{9,25},... | collective-permute-start | bytes 1572872 | tf_op jit(solution)/shard_map/ppermute | solution.py:128
  109.6 41.3 %copy-start.3 = (f32[8,128]{1,0:T(8,128)S(1)}, f32[8,128]{1,0:T(8,128)}, u32[]{:S(2)}) copy-start(f32[8,128]{1,0:T(8,128)} %param.10) | copy-start | bytes 12292
  117.9 8.2 %collective-permute-start.9 = (f32[2,2,2,2,2,2,8,128]{7,6,5,4,3,2,1,0:T(8,128)S(1)}, f32[2,2,2,2,2,2,8,128]{7,6,5,4,3,2,1,0:T(8,128)S(1)}, u32[]{:S(2)}, u32[]{:S(2)}) collective-permute-start(f32[2,2,2,2,2,2,8,128]{7,6,5,4,3,2,1,0:T(8,128)S(1)} %bitcast_select_fusion.2), channel_id=1, source_target_pairs={{0,16},{1,3},{2,18},{3,1},{4,20},{5,7},{6,22},{7,5},{8,24},{9,11},... | collective-permute-start | bytes 786440 | tf_op jit(solution)/shard_map/ppermute | solution.py:128
  126.9 24.1 %all-to-all-start.1 = ((f32[64,8,128]{2,1,0:T(8,128)}), f32[64,8,128]{2,1,0:T(8,128)S(1)}, u32[]{:S(2)}, u32[]{:S(2)}) async-start(f32[64,8,128]{2,1,0:T(8,128)} %bitcast.34), calls=%async_computation.1 | async-start | bytes 524288 | tf_op jit(solution)/shard_map/all_to_all | solution.py:155

commit v10 on v9

--- a/solution.py
+++ b/solution.py
@@ -121,6 +121,11 @@
     swapped = list(near)
     swapped[1], swapped[2] = near[2], near[1]
     return (list(near), swapped)
+
+
+def far_groups(present):
+    longest = [bit for bit in present if bit in (8, 6, 3)]
+    return [[bit for bit in present if bit not in longest], longest]
 
 
 def exchange(values, bits, count):
@@ -150,10 +155,18 @@
         send = sent[0] if bits[0] == bits[1] else jnp.where(first_core, sent[0], sent[1])
         data = keep + exchange(send, bits, count)
     present = presents[0]
-    group = tuple(f"b{bit}" for bit in present)
-    data = data.reshape((1 << len(present), mode_block, projected.shape[1]))
-    data = lax.all_to_all(data, group, 0, 0, tiled=False)
-    return jnp.sum(data, axis=0)
+    for group_bits in far_groups(present):
+        others = [bit for bit in present if bit not in group_bits]
+        data = jnp.transpose(
+            data,
+            [present.index(bit) for bit in group_bits + others]
+            + [len(present), len(present) + 1],
+        )
+        data = data.reshape((1 << len(group_bits), -1, mode_block, projected.shape[1]))
+        data = lax.all_to_all(data, tuple(f"b{bit}" for bit in group_bits), 0, 0, tiled=False)
+        data = jnp.sum(data, axis=0).reshape((2,) * len(others) + (mode_block, projected.shape[1]))
+        present = others
+    return data.reshape(mode_block, projected.shape[1])
 
 
 def gather_all(block, sizes):
@@ -163,11 +176,18 @@
     first_core = (me & 1) == 0
     near, far = order[: nbits - FAR_COUNT], order[nbits - FAR_COUNT :]
     orders = [list(reversed(variant)) for variant in core_orders(near)]
-    presents = [sorted(far, reverse=True) for _ in orders]
-    group = tuple(f"b{bit}" for bit in presents[0])
-    data = jnp.broadcast_to(block[None], (1 << len(presents[0]),) + block.shape)
-    data = lax.all_to_all(data, group, 0, 0, tiled=False)
-    data = data.reshape((2,) * len(presents[0]) + block.shape)
+    present = []
+    data = block
+    for group_bits in reversed(far_groups(sorted(far, reverse=True))):
+        data = jnp.broadcast_to(data[None], (1 << len(group_bits),) + data.shape)
+        data = lax.all_to_all(data, tuple(f"b{bit}" for bit in group_bits), 0, 0, tiled=False)
+        data = data.reshape((2,) * len(group_bits) + data.shape[1:])
+        present = group_bits + present
+    ranked = sorted(present, reverse=True)
+    data = jnp.transpose(
+        data, [present.index(bit) for bit in ranked] + [len(present), len(present) + 1]
+    )
+    presents = [list(ranked) for _ in orders]
     for step in range(len(near)):
         bits = [variant[step] for variant in orders]
         other = exchange(data, bits, count)

time: 154 us -> 172 us (1.12)
  blocking collectives: 34 us -> 60.7 us
  starting transfers between devices: 38.4 us -> 30.8 us
    all_to_all x1 -> x3, blocking collectives: 34 us -> 60.7 us  [the longest x2 44.2 us: gather_all(): lax.all_to_all(data, tuple((f'b{bit}' for bit in group_bits)), 0, 0, tile...]
    all_to_all x1, starting transfers between devices: 9.47 us -> 4.68 us  [scatter_sum(): lax.all_to_all(data, tuple((f'b{bit}' for bit in group_bits)), 0, 0, tile...]
    all_to_all x1, waiting for transfers between devices: 14 us -> 10.8 us  [scatter_sum(): lax.all_to_all(data, tuple((f'b{bit}' for bit in group_bits)), 0, 0, tile...]
    ppermute x6, starting transfers between devices: 19.9 us -> 17.4 us  [exchange(): return lax.ppermute(values, ALL_AXES, pairs)]
    ppermute x6, waiting for transfers between devices: 29.9 us -> 32.1 us  [exchange(): return lax.ppermute(values, ALL_AXES, pairs)]
where the time goes in v10:
time: 172 us; the launch traced here: 170 us
  blocking collectives  60.7 us (35%)
  waiting for transfers between devices  49.7 us (29%)
  starting transfers between devices  30.8 us (18%)
  matrix products  15.4 us (9%)
  other arithmetic  6.72 us (4%)
  local copies, waits for them, and re-layouts  5.48 us (3%)
    all_to_all x2, blocking collectives, gather_all(): lax.all_to_all(data, tuple((f'b{bit}' for bit in group_bits)), 0, 0, tile...  44.2 us
    ppermute x6, waiting for transfers between devices, exchange(): return lax.ppermute(values, ALL_AXES, pairs)  32.1 us
    ppermute x6, starting transfers between devices, exchange(): return lax.ppermute(values, ALL_AXES, pairs)  17.4 us
    all_to_all x1, blocking collectives, scatter_sum(): lax.all_to_all(data, tuple((f'b{bit}' for bit in group_bits)), 0, 0, tile...  16.6 us
    all_to_all x1, waiting for transfers between devices, scatter_sum(): lax.all_to_all(data, tuple((f'b{bit}' for bit in group_bits)), 0, 0, tile...  10.8 us
    ppermute x2, waiting for transfers between devices, with_halo(): lax.ppermute(lax.slice_in_dim(block, 0, width, axis=dim), axis, backward)  6.86 us
    conv_general_dilated x2, matrix products, conv_valid(): lax.conv_general_dilated(values, weights, (1, 1), 'VALID', dimension_numb...  6.64 us
    ppermute x2, starting transfers between devices, with_halo(): lax.ppermute(lax.slice_in_dim(block, block.shape[dim] - width, None, axis...  5.55 us
  transfers between devices with their start and end apart: 11, of which 9 were waited for; matrix products, arithmetic and copies ran while one was open for 1% of the time, Pallas kernels for 0%

profile of v10, /device:TPU:1, one launch (start us, length us, event | category | flops | bytes accessed | tf_op | source)
XLA Modules:
  0.0 170.0 jit_solution(10460685403010946046)
XLA Ops:
  1.4 27.4 %all_to_all.20 = f32[8,8,128]{2,1,0:T(8,128)S(1)} all-to-all(f32[8,8,128]{2,1,0:T(8,128)S(1)} %broadcast_in_dim.75), channel_id=1, replica_groups=mesh['b8'=2,'b7'=2,'b6'=2,'b5'=2,'b4'=2,'b3'=2,'b2'=2,'b1'=2,'b0'=2] {'b..., dimensions={0} | all-to-all | bytes 65536 | tf_op jit(solution)/shard_map/all_to_all | solution.py:183
  28.8 16.8 %all_to_all.21 = f32[8,2,2,2,8,128]{5,4,3,2,1,0:T(8,128)S(1)} all-to-all(f32[8,2,2,2,8,128]{5,4,3,2,1,0:T(8,128)S(1)} %broadcast_in_dim.77), channel_id=1, replica_groups=mesh['b8'=2,'b7'=2,'b6'=2,'b5'=2,'b4'=2,'b3'=2,'b2'=2,'b1'=2,'b0'=2] {'b..., dimensions={0} | all-to-all | bytes 524288 | tf_op jit(solution)/shard_map/all_to_all | solution.py:183
  45.6 1.9 %collective-permute-start = (f32[2,2,2,2,2,2,8,128]{7,6,2,0,4,3,1,5:T(8,128)S(1)}, f32[2,2,2,2,2,2,8,128]{7,6,2,0,4,3,1,5:T(8,128)S(1)}, u32[]{:S(2)}, u32[]{:S(2)}) collective-permute-start(f32[2,2,2,2,2,2,8,128]{7,6,2,0,4,3,1,5:T(8,128)S(1)} %copy.95), channel_id=1, source_target_pairs={{0,16},{1,3},{2,18},{3,1},{4,20},{5,7},{6,22},{7,5},{8,24},{9,11},... | collective-permute-start | bytes 786440 | tf_op jit(solution)/shard_map/ppermute | solution.py:133
  47.6 5.1 %collective-permute-done = f32[2,2,2,2,2,2,8,128]{7,6,2,0,4,3,1,5:T(8,128)S(1)} collective-permute-done((f32[2,2,2,2,2,2,8,128]{7,6,2,0,4,3,1,5:T(8,128)S(1)}, f32[2,2,2,2,2,2,8,128]{7,6,2,0,4,3,1,5:T(8,128)S(1)}, u32[]{:S(2)}, u32[]{:S(2)}) %collective-permute-start) | collective-permute-done | bytes 262176 | tf_op jit(solution)/shard_map/ppermute | solution.py:133
  53.0 2.2 %collective-permute-start.1 = (f32[2,2,2,2,2,2,2,8,128]{8,7,5,2,0,6,3,1,4:T(8,128)S(1)}, f32[2,2,2,2,2,2,2,8,128]{8,7,5,2,0,6,3,1,4:T(8,128)S(1)}, u32[]{:S(2)}, u32[]{:S(2)}) collective-permute-start(f32[2,2,2,2,2,2,2,8,128]{8,7,5,2,0,6,3,1,4:T(8,128)S(1)} %copy.103), channel_id=1, source_target_pairs={{0,2},{1,17},{2,0},{3,19},{4,6},{5,21},{6,4},{7,23},{8,10},{9,25},... | collective-permute-start | bytes 1572872 | tf_op jit(solution)/shard_map/ppermute | solution.py:133
  55.3 8.0 %collective-permute-done.1 = f32[2,2,2,2,2,2,2,8,128]{8,7,5,2,0,6,3,1,4:T(8,128)S(1)} collective-permute-done((f32[2,2,2,2,2,2,2,8,128]{8,7,5,2,0,6,3,1,4:T(8,128)S(1)}, f32[2,2,2,2,2,2,2,8,128]{8,7,5,2,0,6,3,1,4:T(8,128)S(1)}, u32[]{:S(2)}, u32[]{:S(2)}) %collective-permute-start.1) | collective-permute-done | bytes 524320 | tf_op jit(solution)/shard_map/ppermute | solution.py:133
  63.6 1.2 maximum_select_fusion
  64.8 7.3 %collective-permute-start.2 = (f32[2,2,2,2,2,2,2,2,8,128]{9,8,5,2,0,6,3,1,7,4:T(8,128)}, f32[2,2,2,2,2,2,2,2,8,128]{9,8,5,2,0,6,3,1,7,4:T(8,128)}, u32[]{:S(2)}, u32[]{:S(2)}) collective-permute-start(f32[2,2,2,2,2,2,2,2,8,128]{9,8,5,2,0,6,3,1,7,4:T(8,128)} %maximum_select_fusion), channel_id=1, source_target_pairs={{0,1},{1,0},{2,3},{3,2},{4,5},{5,4},{6,7},{7,6},{8,9},{9,8},{10,11... | collective-permute-start | bytes 3145736 | tf_op jit(solution)/shard_map/ppermute | solution.py:133
  72.4 2.3 %collective-permute-done.2 = f32[2,2,2,2,2,2,2,2,8,128]{9,8,5,2,0,6,3,1,7,4:T(8,128)} collective-permute-done((f32[2,2,2,2,2,2,2,2,8,128]{9,8,5,2,0,6,3,1,7,4:T(8,128)}, f32[2,2,2,2,2,2,2,2,8,128]{9,8,5,2,0,6,3,1,7,4:T(8,128)}, u32[]{:S(2)}, u32[]{:S(2)}) %collective-permute-start.2) | collective-permute-done | bytes 1048608 | tf_op jit(solution)/shard_map/ppermute | solution.py:133
  74.7 1.6 select_bitcast_fusion.1
  76.9 1.5 convolution_bitcast_fusion.1
  78.5 2.2 %collective-permute-start.3 = (f32[4,8,256]{2,1,0:T(8,128)S(1)}, f32[4,8,256]{2,1,0:T(8,128)S(1)}, u32[]{:S(2)}, u32[]{:S(2)}) collective-permute-start(f32[4,8,256]{2,1,0:T(8,128)S(1)} %get-tuple-element.20), channel_id=1, source_target_pairs={{0,16},{16,32},{32,48},{48,64},{64,80},{80,96},{96,112},{112,128},... | collective-permute-start | bytes 98312 | tf_op jit(solution)/shard_map/ppermute | solution.py:21
  80.7 1.3 collective-permute-start.4
  82.1 3.3 %collective-permute-done.4 = f32[4,8,256]{2,1,0:T(8,128)S(1)} collective-permute-done((f32[4,8,256]{2,1,0:T(8,128)S(1)}, f32[4,8,256]{2,1,0:T(8,128)S(1)}, u32[]{:S(2)}, u32[]{:S(2)}) %collective-permute-start.4) | collective-permute-done | bytes 32800 | tf_op jit(solution)/shard_map/ppermute | solution.py:24
  85.4 3.3 %collective-permute-start.5 = (f32[16,4,256]{2,1,0:T(4,128)S(1)}, f32[16,4,256]{2,1,0:T(4,128)S(1)}, u32[]{:S(2)}, u32[]{:S(2)}) collective-permute-start(f32[16,4,256]{2,1,0:T(4,128)S(1)} %get-tuple-element.18), channel_id=1, source_target_pairs={{0,1},{1,2},{2,3},{3,4},{4,5},{5,6},{6,7},{7,8},{8,9},{9,10},{10,1... | collective-permute-start | bytes 196616 | tf_op jit(solution)/shard_map/ppermute | solution.py:21
  88.7 1.9 %collective-permute-start.6 = (f32[16,4,256]{2,1,0:T(4,128)S(1)}, f32[16,4,256]{2,1,0:T(4,128)S(1)}, u32[]{:S(2)}, u32[]{:S(2)}) collective-permute-start(f32[16,4,256]{2,1,0:T(4,128)S(1)} %get-tuple-element.19), channel_id=1, source_target_pairs={{1,0},{2,1},{3,2},{4,3},{5,4},{6,5},{7,6},{8,7},{9,8},{10,9},{11,1... | collective-permute-start | bytes 196616 | tf_op jit(solution)/shard_map/ppermute | solution.py:24
  90.7 3.6 %collective-permute-done.6 = f32[16,4,256]{2,1,0:T(4,128)S(1)} collective-permute-done((f32[16,4,256]{2,1,0:T(4,128)S(1)}, f32[16,4,256]{2,1,0:T(4,128)S(1)}, u32[]{:S(2)}, u32[]{:S(2)}) %collective-permute-start.6) | collective-permute-done | bytes 65568 | tf_op jit(solution)/shard_map/ppermute | solution.py:24
  94.5 3.1 %select_convert_fusion.1 = bf16[14,14,32,128]{3,2,1,0:T(8,128)(2,1)S(1)} fusion(f32[32]{0:T(128)S(1)} %copy-done.5, pred[14,14]{1,0:T(8,128)(4,1)S(1)} %slice_bitcast_fusion.2, bf16[3,3,32,32]{3,2,1,0:T(8,128)(2,1)S(1)} %copy-done.3, f32[32]{0:T(128)S(1)} %copy-done.6, f32[32]{0:T(128)S(1)} %copy-done.9, f32[16,16,128]{2,1,0:T(8,128)S(1)} %slice.51, ...), kind=kOutput, calls=%fused_computation.2 | convolution fusion | flops 469024768 | bytes 1755972 | tf_op jit(solution)/shard_map/conv_general_dilated | solution.py:47
  97.6 3.5 %multiply_reduce_fusion = (f32[12,12,128]{2,1,0:T(8,128)S(1)}, f32[12,12,32,128]{3,2,1,0:T(8,128)}) fusion(f32[32]{0:T(128)S(1)} %copy-done.7, f32[32]{0:T(128)S(1)} %copy-done.8, bf16[14,14,32,128]{3,2,1,0:T(8,128)(2,1)S(1)} %select_convert_fusion.1, bf16[3,3,32,32]{3,2,1,0:T(8,128)(2,1)S(1)} %copy-done.4), kind=kOutput, calls=%fused_computation.4 | convolution fusion | flops 341489664 | bytes 4057344 | tf_op jit(solution)/shard_map/conv_general_dilated | solution.py:47
  101.2 4.1 %fusion.6 = f32[8,8,128]{2,1,0:T(8,128)S(1)} fusion(bf16[3,3,32,32]{3,2,1,0:T(8,128)(2,1)S(1)} %copy-done.3, bf16[3,3,32,32]{3,2,1,0:T(8,128)(2,1)S(1)} %copy-done.4, f32[12,12,32,128]{3,2,1,0:T(8,128)} %get-tuple-element.23, f32[12,12,128]{2,1,0:T(8,128)S(1)} %maximum_subtract_fusion, f32[32]{0:T(128)S(1)} %copy-done.7, f32[32]{0:T(128)S(1)} %copy-done.8, ...), kind=kOutput, calls=%fused_computation.15 | convolution fusion | flops 394027008 | bytes 3462656 | tf_op jit(solution)/shard_map/conv_general_dilated | solution.py:58
  105.2 3.2 %convolution_bitcast_fusion = f32[4096,128]{0,1:T(8,128)} fusion(f32[8,8,128]{2,1,0:T(8,128)S(1)} %fusion.6, f32[8,8,4096]{2,1,0:T(8,128)S(1)} %copy-done), kind=kOutput, calls=%fused_computation | convolution fusion | flops 402653184 | bytes 3178496 | tf_op jit(solution)/shard_map/dot_general | solution.py:222
  108.4 1.9 %copy.111 = f32[4096,128]{1,0:T(8,128)S(1)} copy(f32[4096,128]{0,1:T(8,128)} %convolution_bitcast_fusion) | data formatting | bytes 4194304 | tf_op jit(solution)/shard_map/dot_general | solution.py:222
  111.5 1.9 %collective-permute-start.7 = (f32[2,2,2,2,2,2,2,2,8,128]{9,8,7,6,5,4,3,2,1,0:T(8,128)}, f32[2,2,2,2,2,2,2,2,8,128]{9,8,7,6,5,4,3,2,1,0:T(8,128)}, u32[]{:S(2)}, u32[]{:S(2)}) collective-permute-start(f32[2,2,2,2,2,2,2,2,8,128]{9,8,7,6,5,4,3,2,1,0:T(8,128)} %dynamic-slice_bitcast_fusion), channel_id=1, source_target_pairs={{0,1},{1,0},{2,3},{3,2},{4,5},{5,4},{6,7},{7,6},{8,9},{9,8},{10,11... | collective-permute-start | bytes 3145736 | tf_op jit(solution)/shard_map/ppermute | solution.py:133
  113.4 3.0 %collective-permute-done.7 = f32[2,2,2,2,2,2,2,2,8,128]{9,8,7,6,5,4,3,2,1,0:T(8,128)} collective-permute-done((f32[2,2,2,2,2,2,2,2,8,128]{9,8,7,6,5,4,3,2,1,0:T(8,128)}, f32[2,2,2,2,2,2,2,2,8,128]{9,8,7,6,5,4,3,2,1,0:T(8,128)}, u32[]{:S(2)}, u32[]{:S(2)}) %collective-permute-start.7) | collective-permute-done | bytes 1048608 | tf_op jit(solution)/shard_map/ppermute | solution.py:133
  116.3 1.4 bitcast_add_fusion
  118.1 1.9 %collective-permute-start.8 = (f32[2,2,2,2,2,2,2,8,128]{8,7,4,2,0,5,3,1,6:T(8,128)S(1)}, f32[2,2,2,2,2,2,2,8,128]{8,7,4,2,0,5,3,1,6:T(8,128)S(1)}, u32[]{:S(2)}, u32[]{:S(2)}) collective-permute-start(f32[2,2,2,2,2,2,2,8,128]{8,7,4,2,0,5,3,1,6:T(8,128)S(1)} %bitcast_select_fusion), channel_id=1, source_target_pairs={{0,2},{1,17},{2,0},{3,19},{4,6},{5,21},{6,4},{7,23},{8,10},{9,25},... | collective-permute-start | bytes 1572872 | tf_op jit(solution)/shard_map/ppermute | solution.py:133
  120.0 8.3 %collective-permute-done.8 = f32[2,2,2,2,2,2,2,8,128]{8,7,4,2,0,5,3,1,6:T(8,128)S(1)} collective-permute-done((f32[2,2,2,2,2,2,2,8,128]{8,7,4,2,0,5,3,1,6:T(8,128)S(1)}, f32[2,2,2,2,2,2,2,8,128]{8,7,4,2,0,5,3,1,6:T(8,128)S(1)}, u32[]{:S(2)}, u32[]{:S(2)}) %collective-permute-start.8) | collective-permute-done | bytes 524320 | tf_op jit(solution)/shard_map/ppermute | solution.py:133
  128.6 2.1 %collective-permute-start.9 = (f32[2,2,2,2,2,2,8,128]{7,6,5,4,3,2,1,0:T(8,128)S(1)}, f32[2,2,2,2,2,2,8,128]{7,6,5,4,3,2,1,0:T(8,128)S(1)}, u32[]{:S(2)}, u32[]{:S(2)}) collective-permute-start(f32[2,2,2,2,2,2,8,128]{7,6,5,4,3,2,1,0:T(8,128)S(1)} %bitcast_select_fusion.2), channel_id=1, source_target_pairs={{0,16},{1,3},{2,18},{3,1},{4,20},{5,7},{6,22},{7,5},{8,24},{9,11},... | collective-permute-start | bytes 786440 | tf_op jit(solution)/shard_map/ppermute | solution.py:133
  130.7 5.3 %collective-permute-done.9 = f32[2,2,2,2,2,2,8,128]{7,6,5,4,3,2,1,0:T(8,128)S(1)} collective-permute-done((f32[2,2,2,2,2,2,8,128]{7,6,5,4,3,2,1,0:T(8,128)S(1)}, f32[2,2,2,2,2,2,8,128]{7,6,5,4,3,2,1,0:T(8,128)S(1)}, u32[]{:S(2)}, u32[]{:S(2)}) %collective-permute-start.9) | collective-permute-done | bytes 262176 | tf_op jit(solution)/shard_map/ppermute | solution.py:133
  136.1 16.6 %all_to_all.22 = f32[8,8,8,128]{3,2,1,0:T(8,128)S(1)} all-to-all(f32[8,8,8,128]{3,2,1,0:T(8,128)S(1)} %bitcast.91), channel_id=1, replica_groups=mesh['b8'=2,'b7'=2,'b6'=2,'b5'=2,'b4'=2,'b3'=2,'b2'=2,'b1'=2,'b0'=2] {'b..., dimensions={0} | all-to-all | bytes 524288 | tf_op jit(solution)/shard_map/all_to_all | solution.py:166
  153.3 4.7 %all-to-all-start.3 = ((f32[8,1,8,128]{3,2,1,0:T(8,128)}), f32[8,1,8,128]{3,2,1,0:T(8,128)S(1)}, u32[]{:S(2)}, u32[]{:S(2)}) async-start(f32[8,1,8,128]{3,2,1,0:T(8,128)} %bitcast.38), calls=%async_computation.3 | async-start | bytes 65536 | tf_op jit(solution)/shard_map/all_to_all | solution.py:166
  158.6 10.8 %all-to-all-done.3 = f32[8,1,8,128]{3,2,1,0:T(8,128)S(1)} async-done(((f32[8,1,8,128]{3,2,1,0:T(8,128)}), f32[8,1,8,128]{3,2,1,0:T(8,128)S(1)}, u32[]{:S(2)}, u32[]{:S(2)}) %all-to-all-start.3) | async-done | bytes 32800 | tf_op jit(solution)/shard_map/all_to_all | solution.py:166
  (59 shorter events, 6.1 us)
Async XLA Ops:
  0.6 76.3 %copy-start = (f32[8,8,4096]{2,1,0:T(8,128)S(1)}, f32[8,8,4096]{2,1,0:T(8,128)}, u32[]{:S(2)}) copy-start(f32[8,8,4096]{2,1,0:T(8,128)} %param.11) | copy-start | bytes 3145732
  45.6 7.1 %collective-permute-start = (f32[2,2,2,2,2,2,8,128]{7,6,2,0,4,3,1,5:T(8,128)S(1)}, f32[2,2,2,2,2,2,8,128]{7,6,2,0,4,3,1,5:T(8,128)S(1)}, u32[]{:S(2)}, u32[]{:S(2)}) collective-permute-start(f32[2,2,2,2,2,2,8,128]{7,6,2,0,4,3,1,5:T(8,128)S(1)} %copy.95), channel_id=1, source_target_pairs={{0,16},{1,3},{2,18},{3,1},{4,20},{5,7},{6,22},{7,5},{8,24},{9,11},... | collective-permute-start | bytes 786440 | tf_op jit(solution)/shard_map/ppermute | solution.py:133
  53.0 10.2 %collective-permute-start.1 = (f32[2,2,2,2,2,2,2,8,128]{8,7,5,2,0,6,3,1,4:T(8,128)S(1)}, f32[2,2,2,2,2,2,2,8,128]{8,7,5,2,0,6,3,1,4:T(8,128)S(1)}, u32[]{:S(2)}, u32[]{:S(2)}) collective-permute-start(f32[2,2,2,2,2,2,2,8,128]{8,7,5,2,0,6,3,1,4:T(8,128)S(1)} %copy.103), channel_id=1, source_target_pairs={{0,2},{1,17},{2,0},{3,19},{4,6},{5,21},{6,4},{7,23},{8,10},{9,25},... | collective-permute-start | bytes 1572872 | tf_op jit(solution)/shard_map/ppermute | solution.py:133
  64.8 9.9 %collective-permute-start.2 = (f32[2,2,2,2,2,2,2,2,8,128]{9,8,5,2,0,6,3,1,7,4:T(8,128)}, f32[2,2,2,2,2,2,2,2,8,128]{9,8,5,2,0,6,3,1,7,4:T(8,128)}, u32[]{:S(2)}, u32[]{:S(2)}) collective-permute-start(f32[2,2,2,2,2,2,2,2,8,128]{9,8,5,2,0,6,3,1,7,4:T(8,128)} %maximum_select_fusion), channel_id=1, source_target_pairs={{0,1},{1,0},{2,3},{3,2},{4,5},{5,4},{6,7},{7,6},{8,9},{9,8},{10,11... | collective-permute-start | bytes 3145736 | tf_op jit(solution)/shard_map/ppermute | solution.py:133
  76.9 1.6 copy-start.1
  76.9 17.5 %copy-start.3 = (bf16[3,3,32,32]{3,2,1,0:T(8,128)(2,1)S(1)}, bf16[3,3,32,32]{3,2,1,0:T(8,128)(2,1)}, u32[]{:S(2)}) copy-start(bf16[3,3,32,32]{3,2,1,0:T(8,128)(2,1)} %param.15) | copy-start | bytes 55300
  76.9 17.5 %copy-start.5 = (f32[32]{0:T(128)S(1)}, f32[32]{0:T(128)}, u32[]{:S(2)}) copy-start(f32[32]{0:T(128)} %param.16) | copy-start | bytes 388
  76.9 17.5 %copy-start.6 = (f32[32]{0:T(128)S(1)}, f32[32]{0:T(128)}, u32[]{:S(2)}) copy-start(f32[32]{0:T(128)} %param.14) | copy-start | bytes 388
  76.9 17.5 %copy-start.9 = (f32[32]{0:T(128)S(1)}, f32[32]{0:T(128)}, u32[]{:S(2)}) copy-start(f32[32]{0:T(128)} %param.13) | copy-start | bytes 388
  78.5 3.6 %collective-permute-start.3 = (f32[4,8,256]{2,1,0:T(8,128)S(1)}, f32[4,8,256]{2,1,0:T(8,128)S(1)}, u32[]{:S(2)}, u32[]{:S(2)}) collective-permute-start(f32[4,8,256]{2,1,0:T(8,128)S(1)} %get-tuple-element.20), channel_id=1, source_target_pairs={{0,16},{16,32},{32,48},{48,64},{64,80},{80,96},{96,112},{112,128},... | collective-permute-start | bytes 98312 | tf_op jit(solution)/shard_map/ppermute | solution.py:21
  80.7 4.7 %collective-permute-start.4 = (f32[4,8,256]{2,1,0:T(8,128)S(1)}, f32[4,8,256]{2,1,0:T(8,128)S(1)}, u32[]{:S(2)}, u32[]{:S(2)}) collective-permute-start(f32[4,8,256]{2,1,0:T(8,128)S(1)} %get-tuple-element.21), channel_id=1, source_target_pairs={{16,0},{32,16},{48,32},{64,48},{80,64},{96,80},{112,96},{128,112},... | collective-permute-start | bytes 98312 | tf_op jit(solution)/shard_map/ppermute | solution.py:24
  85.4 5.3 %collective-permute-start.5 = (f32[16,4,256]{2,1,0:T(4,128)S(1)}, f32[16,4,256]{2,1,0:T(4,128)S(1)}, u32[]{:S(2)}, u32[]{:S(2)}) collective-permute-start(f32[16,4,256]{2,1,0:T(4,128)S(1)} %get-tuple-element.18), channel_id=1, source_target_pairs={{0,1},{1,2},{2,3},{3,4},{4,5},{5,6},{6,7},{7,8},{8,9},{9,10},{10,1... | collective-permute-start | bytes 196616 | tf_op jit(solution)/shard_map/ppermute | solution.py:21
  88.7 5.6 %collective-permute-start.6 = (f32[16,4,256]{2,1,0:T(4,128)S(1)}, f32[16,4,256]{2,1,0:T(4,128)S(1)}, u32[]{:S(2)}, u32[]{:S(2)}) collective-permute-start(f32[16,4,256]{2,1,0:T(4,128)S(1)} %get-tuple-element.19), channel_id=1, source_target_pairs={{1,0},{2,1},{3,2},{4,3},{5,4},{6,5},{7,6},{8,7},{9,8},{10,9},{11,1... | collective-permute-start | bytes 196616 | tf_op jit(solution)/shard_map/ppermute | solution.py:24
  94.4 3.2 %copy-start.4 = (bf16[3,3,32,32]{3,2,1,0:T(8,128)(2,1)S(1)}, bf16[3,3,32,32]{3,2,1,0:T(8,128)(2,1)}, u32[]{:S(2)}) copy-start(bf16[3,3,32,32]{3,2,1,0:T(8,128)(2,1)} %param.17) | copy-start | bytes 55300
  94.4 3.2 %copy-start.7 = (f32[32]{0:T(128)S(1)}, f32[32]{0:T(128)}, u32[]{:S(2)}) copy-start(f32[32]{0:T(128)} %param.19) | copy-start | bytes 388
  94.5 3.2 %copy-start.8 = (f32[32]{0:T(128)S(1)}, f32[32]{0:T(128)}, u32[]{:S(2)}) copy-start(f32[32]{0:T(128)} %param.18) | copy-start | bytes 388
  111.5 4.9 %collective-permute-start.7 = (f32[2,2,2,2,2,2,2,2,8,128]{9,8,7,6,5,4,3,2,1,0:T(8,128)}, f32[2,2,2,2,2,2,2,2,8,128]{9,8,7,6,5,4,3,2,1,0:T(8,128)}, u32[]{:S(2)}, u32[]{:S(2)}) collective-permute-start(f32[2,2,2,2,2,2,2,2,8,128]{9,8,7,6,5,4,3,2,1,0:T(8,128)} %dynamic-slice_bitcast_fusion), channel_id=1, source_target_pairs={{0,1},{1,0},{2,3},{3,2},{4,5},{5,4},{6,7},{7,6},{8,9},{9,8},{10,11... | collective-permute-start | bytes 3145736 | tf_op jit(solution)/shard_map/ppermute | solution.py:133
  118.1 10.2 %collective-permute-start.8 = (f32[2,2,2,2,2,2,2,8,128]{8,7,4,2,0,5,3,1,6:T(8,128)S(1)}, f32[2,2,2,2,2,2,2,8,128]{8,7,4,2,0,5,3,1,6:T(8,128)S(1)}, u32[]{:S(2)}, u32[]{:S(2)}) collective-permute-start(f32[2,2,2,2,2,2,2,8,128]{8,7,4,2,0,5,3,1,6:T(8,128)S(1)} %bitcast_select_fusion), channel_id=1, source_target_pairs={{0,2},{1,17},{2,0},{3,19},{4,6},{5,21},{6,4},{7,23},{8,10},{9,25},... | collective-permute-start | bytes 1572872 | tf_op jit(solution)/shard_map/ppermute | solution.py:133
  128.5 40.9 %copy-start.2 = (f32[8,128]{1,0:T(8,128)S(1)}, f32[8,128]{1,0:T(8,128)}, u32[]{:S(2)}) copy-start(f32[8,128]{1,0:T(8,128)} %param.10) | copy-start | bytes 12292
  128.6 7.4 %collective-permute-start.9 = (f32[2,2,2,2,2,2,8,128]{7,6,5,4,3,2,1,0:T(8,128)S(1)}, f32[2,2,2,2,2,2,8,128]{7,6,5,4,3,2,1,0:T(8,128)S(1)}, u32[]{:S(2)}, u32[]{:S(2)}) collective-permute-start(f32[2,2,2,2,2,2,8,128]{7,6,5,4,3,2,1,0:T(8,128)S(1)} %bitcast_select_fusion.2), channel_id=1, source_target_pairs={{0,16},{1,3},{2,18},{3,1},{4,20},{5,7},{6,22},{7,5},{8,24},{9,11},... | collective-permute-start | bytes 786440 | tf_op jit(solution)/shard_map/ppermute | solution.py:133
  153.3 16.1 %all-to-all-start.3 = ((f32[8,1,8,128]{3,2,1,0:T(8,128)}), f32[8,1,8,128]{3,2,1,0:T(8,128)S(1)}, u32[]{:S(2)}, u32[]{:S(2)}) async-start(f32[8,1,8,128]{3,2,1,0:T(8,128)} %bitcast.38), calls=%async_computation.3 | async-start | bytes 65536 | tf_op jit(solution)/shard_map/all_to_all | solution.py:166

commit v11 on v9

--- a/solution.py
+++ b/solution.py
@@ -10,7 +10,7 @@
 ALL_AXES = tuple(f"b{bit}" for bit in range(8, -1, -1))
 ROW_AXES = ALL_AXES[:5]
 COL_AXES = ALL_AXES[5:]
-FAR_COUNT = 6
+FAR_COUNT = 7
 
 
 def with_halo(block, sides, width):
@@ -119,7 +119,8 @@
 
 def core_orders(near):
     swapped = list(near)
-    swapped[1], swapped[2] = near[2], near[1]
+    if len(near) > 2:
+        swapped[1], swapped[2] = near[2], near[1]
     return (list(near), swapped)
 
 

time: 154 us -> 161 us (1.045)
  the two profiles are of different devices: /device:TPU:1 before, /device:TPU:8 now
where the time goes in v11:
time: 161 us; the launch traced here: 160 us
  waiting for transfers between devices  57.7 us (36%)
  blocking collectives  40.1 us (25%)
  starting transfers between devices  34.3 us (21%)
  matrix products  15.5 us (10%)
  other arithmetic  6.04 us (4%)
  local copies, waits for them, and re-layouts  5.8 us (4%)
    all_to_all x1, blocking collectives, gather_all(): data = lax.all_to_all(data, group, 0, 0, tiled=False)  40.1 us
    ppermute x4, waiting for transfers between devices, exchange(): return lax.ppermute(values, ALL_AXES, pairs)  29.9 us
    all_to_all x1, waiting for transfers between devices, scatter_sum(): data = lax.all_to_all(data, group, 0, 0, tiled=False)  21.5 us
    all_to_all x1, starting transfers between devices, scatter_sum(): data = lax.all_to_all(data, group, 0, 0, tiled=False)  12.7 us
    ppermute x4, starting transfers between devices, exchange(): return lax.ppermute(values, ALL_AXES, pairs)  12.4 us
    conv_general_dilated x2, matrix products, conv_valid(): lax.conv_general_dilated(values, weights, (1, 1), 'VALID', dimension_numb...  6.64 us
    ppermute x2, waiting for transfers between devices, with_halo(): lax.ppermute(lax.slice_in_dim(block, 0, width, axis=dim), axis, backward)  6.03 us
    ppermute x2, starting transfers between devices, with_halo(): lax.ppermute(lax.slice_in_dim(block, 0, width, axis=dim), axis, backward)  4.93 us
  transfers between devices with their start and end apart: 9, of which 8 were waited for; matrix products, arithmetic and copies ran while one was open for 1% of the time, Pallas kernels for 0%

profile of v11, /device:TPU:8, one launch (start us, length us, event | category | flops | bytes accessed | tf_op | source)
XLA Modules:
  0.0 160.5 jit_solution(3772110295304338167)
XLA Ops:
  0.6 0.8 broadcast_in_dim.68
  1.5 40.1 %all_to_all.10 = f32[128,8,128]{2,1,0:T(8,128)S(1)} all-to-all(f32[128,8,128]{2,1,0:T(8,128)S(1)} %broadcast_in_dim.68), channel_id=1, replica_groups=mesh['b8'=2,'b7'=2,'b6'=2,'b5'=2,'b4'=2,'b3'=2,'b2'=2,'b1'=2,'b0'=2] {'b..., dimensions={0} | all-to-all | bytes 1048576 | tf_op jit(solution)/shard_map/all_to_all | solution.py:170
  41.6 4.5 %collective-permute-start = (f32[2,2,2,2,2,2,2,8,128]{8,7,6,5,4,3,2,1,0:T(8,128)S(1)}, f32[2,2,2,2,2,2,2,8,128]{8,7,6,5,4,3,2,1,0:T(8,128)S(1)}, u32[]{:S(2)}, u32[]{:S(2)}) collective-permute-start(f32[2,2,2,2,2,2,2,8,128]{8,7,6,5,4,3,2,1,0:T(8,128)S(1)} %bitcast.52), channel_id=1, source_target_pairs={{0,2},{1,3},{2,0},{3,1},{4,6},{5,7},{6,4},{7,5},{8,10},{9,11},{10,... | collective-permute-start | bytes 1572872 | tf_op jit(solution)/shard_map/ppermute | solution.py:129
  46.1 10.7 %collective-permute-done = f32[2,2,2,2,2,2,2,8,128]{8,7,6,5,4,3,2,1,0:T(8,128)S(1)} collective-permute-done((f32[2,2,2,2,2,2,2,8,128]{8,7,6,5,4,3,2,1,0:T(8,128)S(1)}, f32[2,2,2,2,2,2,2,8,128]{8,7,6,5,4,3,2,1,0:T(8,128)S(1)}, u32[]{:S(2)}, u32[]{:S(2)}) %collective-permute-start) | collective-permute-done | bytes 524320 | tf_op jit(solution)/shard_map/ppermute | solution.py:129
  56.9 1.1 pad_maximum_fusion.1
  58.0 1.9 %collective-permute-start.1 = (f32[2,2,2,2,2,2,2,2,8,128]{9,8,7,6,5,4,3,2,1,0:T(8,128)}, f32[2,2,2,2,2,2,2,2,8,128]{9,8,7,6,5,4,3,2,1,0:T(8,128)S(1)}, u32[]{:S(2)}, u32[]{:S(2)}) collective-permute-start(f32[2,2,2,2,2,2,2,2,8,128]{9,8,7,6,5,4,3,2,1,0:T(8,128)} %pad_maximum_fusion.1), channel_id=1, source_target_pairs={{0,1},{1,0},{2,3},{3,2},{4,5},{5,4},{6,7},{7,6},{8,9},{9,8},{10,11... | collective-permute-start | bytes 3145736 | tf_op jit(solution)/shard_map/ppermute | solution.py:129
  60.2 2.6 %collective-permute-done.1 = f32[2,2,2,2,2,2,2,2,8,128]{9,8,7,6,5,4,3,2,1,0:T(8,128)S(1)} collective-permute-done((f32[2,2,2,2,2,2,2,2,8,128]{9,8,7,6,5,4,3,2,1,0:T(8,128)}, f32[2,2,2,2,2,2,2,2,8,128]{9,8,7,6,5,4,3,2,1,0:T(8,128)S(1)}, u32[]{:S(2)}, u32[]{:S(2)}) %collective-permute-start.1) | collective-permute-done | bytes 1048608 | tf_op jit(solution)/shard_map/ppermute | solution.py:129
  62.7 0.3 select_bitcast_fusion.1
  63.3 1.5 convolution_bitcast_fusion.1
  64.8 2.3 %collective-permute-start.2 = (f32[4,8,256]{2,1,0:T(8,128)S(1)}, f32[4,8,256]{2,1,0:T(8,128)S(1)}, u32[]{:S(2)}, u32[]{:S(2)}) collective-permute-start(f32[4,8,256]{2,1,0:T(8,128)S(1)} %get-tuple-element.8), channel_id=1, source_target_pairs={{0,16},{16,32},{32,48},{48,64},{64,80},{80,96},{96,112},{112,128},... | collective-permute-start | bytes 98312 | tf_op jit(solution)/shard_map/ppermute | solution.py:21
  67.1 1.3 collective-permute-start.3
  68.7 4.2 %collective-permute-done.3 = f32[4,8,256]{2,1,0:T(8,128)S(1)} collective-permute-done((f32[4,8,256]{2,1,0:T(8,128)S(1)}, f32[4,8,256]{2,1,0:T(8,128)S(1)}, u32[]{:S(2)}, u32[]{:S(2)}) %collective-permute-start.3) | collective-permute-done | bytes 32800 | tf_op jit(solution)/shard_map/ppermute | solution.py:24
  73.0 1.9 %collective-permute-start.4 = (f32[16,4,256]{2,1,0:T(4,128)S(1)}, f32[16,4,256]{2,1,0:T(4,128)S(1)}, u32[]{:S(2)}, u32[]{:S(2)}) collective-permute-start(f32[16,4,256]{2,1,0:T(4,128)S(1)} %get-tuple-element.6), channel_id=1, source_target_pairs={{0,1},{1,2},{2,3},{3,4},{4,5},{5,6},{6,7},{7,8},{8,9},{9,10},{10,1... | collective-permute-start | bytes 196616 | tf_op jit(solution)/shard_map/ppermute | solution.py:21
  74.9 3.6 %collective-permute-start.5 = (f32[16,4,256]{2,1,0:T(4,128)S(1)}, f32[16,4,256]{2,1,0:T(4,128)S(1)}, u32[]{:S(2)}, u32[]{:S(2)}) collective-permute-start(f32[16,4,256]{2,1,0:T(4,128)S(1)} %get-tuple-element.7), channel_id=1, source_target_pairs={{1,0},{2,1},{3,2},{4,3},{5,4},{6,5},{7,6},{8,7},{9,8},{10,9},{11,1... | collective-permute-start | bytes 196616 | tf_op jit(solution)/shard_map/ppermute | solution.py:24
  78.6 1.8 %collective-permute-done.5 = f32[16,4,256]{2,1,0:T(4,128)S(1)} collective-permute-done((f32[16,4,256]{2,1,0:T(4,128)S(1)}, f32[16,4,256]{2,1,0:T(4,128)S(1)}, u32[]{:S(2)}, u32[]{:S(2)}) %collective-permute-start.5) | collective-permute-done | bytes 65568 | tf_op jit(solution)/shard_map/ppermute | solution.py:24
  80.6 3.1 %select_convert_fusion.1 = bf16[14,14,32,128]{3,2,1,0:T(8,128)(2,1)S(1)} fusion(f32[32]{0:T(128)S(1)} %copy-done.6, pred[14,14]{1,0:T(8,128)(4,1)S(1)} %slice_bitcast_fusion.2, bf16[3,3,32,32]{3,2,1,0:T(8,128)(2,1)S(1)} %copy-done.4, f32[32]{0:T(128)S(1)} %copy-done.7, f32[32]{0:T(128)S(1)} %copy-done.10, f32[16,16,128]{2,1,0:T(8,128)S(1)} %slice.51, ...), kind=kOutput, calls=%fused_computation.2 | convolution fusion | flops 469024768 | bytes 1755972 | tf_op jit(solution)/shard_map/conv_general_dilated | solution.py:47
  83.7 3.5 %multiply_reduce_fusion = (f32[12,12,128]{2,1,0:T(8,128)S(1)}, f32[12,12,32,128]{3,2,1,0:T(8,128)}) fusion(f32[32]{0:T(128)S(1)} %copy-done.8, f32[32]{0:T(128)S(1)} %copy-done.9, bf16[14,14,32,128]{3,2,1,0:T(8,128)(2,1)S(1)} %select_convert_fusion.1, bf16[3,3,32,32]{3,2,1,0:T(8,128)(2,1)S(1)} %copy-done.5), kind=kOutput, calls=%fused_computation.4 | convolution fusion | flops 341489664 | bytes 4057344 | tf_op jit(solution)/shard_map/conv_general_dilated | solution.py:47
  87.3 4.2 %fusion.6 = f32[8,8,128]{2,1,0:T(8,128)S(1)} fusion(bf16[3,3,32,32]{3,2,1,0:T(8,128)(2,1)S(1)} %copy-done.4, bf16[3,3,32,32]{3,2,1,0:T(8,128)(2,1)S(1)} %copy-done.5, f32[12,12,32,128]{3,2,1,0:T(8,128)} %get-tuple-element.11, f32[12,12,128]{2,1,0:T(8,128)S(1)} %maximum_subtract_fusion, f32[32]{0:T(128)S(1)} %copy-done.8, f32[32]{0:T(128)S(1)} %copy-done.9, ...), kind=kOutput, calls=%fused_computation.15 | convolution fusion | flops 394027008 | bytes 3322484 | tf_op jit(solution)/shard_map/conv_general_dilated | solution.py:58
  91.6 3.2 %convolution_bitcast_fusion = f32[4096,128]{0,1:T(8,128)} fusion(f32[8,8,128]{2,1,0:T(8,128)S(1)} %fusion.6, f32[8,8,4096]{2,1,0:T(8,128)S(1)} %copy-done), kind=kOutput, calls=%fused_computation | convolution fusion | flops 402653184 | bytes 3178496 | tf_op jit(solution)/shard_map/dot_general | solution.py:203
  94.7 1.9 %copy.15 = f32[4096,128]{1,0:T(8,128)S(1)} copy(f32[4096,128]{0,1:T(8,128)} %convolution_bitcast_fusion) | data formatting | bytes 4194304 | tf_op jit(solution)/shard_map/dot_general | solution.py:203
  96.7 1.1 dynamic-slice_bitcast_fusion
  97.8 4.0 %collective-permute-start.6 = (f32[2,2,2,2,2,2,2,2,8,128]{9,8,7,6,5,4,3,2,1,0:T(8,128)}, f32[2,2,2,2,2,2,2,2,8,128]{9,8,7,6,5,4,3,2,1,0:T(8,128)}, u32[]{:S(2)}, u32[]{:S(2)}) collective-permute-start(f32[2,2,2,2,2,2,2,2,8,128]{9,8,7,6,5,4,3,2,1,0:T(8,128)} %dynamic-slice_bitcast_fusion), channel_id=1, source_target_pairs={{0,1},{1,0},{2,3},{3,2},{4,5},{5,4},{6,7},{7,6},{8,9},{9,8},{10,11... | collective-permute-start | bytes 3145736 | tf_op jit(solution)/shard_map/ppermute | solution.py:129
  101.8 2.6 %collective-permute-done.6 = f32[2,2,2,2,2,2,2,2,8,128]{9,8,7,6,5,4,3,2,1,0:T(8,128)} collective-permute-done((f32[2,2,2,2,2,2,2,2,8,128]{9,8,7,6,5,4,3,2,1,0:T(8,128)}, f32[2,2,2,2,2,2,2,2,8,128]{9,8,7,6,5,4,3,2,1,0:T(8,128)}, u32[]{:S(2)}, u32[]{:S(2)}) %collective-permute-start.6) | collective-permute-done | bytes 1048608 | tf_op jit(solution)/shard_map/ppermute | solution.py:129
  104.4 1.4 bitcast_add_fusion
  105.8 1.0 copy-done.1
  106.8 2.0 %collective-permute-start.7 = (f32[2,2,2,2,2,2,2,8,128]{8,7,6,5,4,3,2,1,0:T(8,128)S(1)}, f32[2,2,2,2,2,2,2,8,128]{8,7,6,5,4,3,2,1,0:T(8,128)S(1)}, u32[]{:S(2)}, u32[]{:S(2)}) collective-permute-start(f32[2,2,2,2,2,2,2,8,128]{8,7,6,5,4,3,2,1,0:T(8,128)S(1)} %dynamic-slice_bitcast_fusion.1), channel_id=1, source_target_pairs={{0,2},{1,3},{2,0},{3,1},{4,6},{5,7},{6,4},{7,5},{8,10},{9,11},{10,... | collective-permute-start | bytes 1572872 | tf_op jit(solution)/shard_map/ppermute | solution.py:129
  108.8 14.1 %collective-permute-done.7 = f32[2,2,2,2,2,2,2,8,128]{8,7,6,5,4,3,2,1,0:T(8,128)S(1)} collective-permute-done((f32[2,2,2,2,2,2,2,8,128]{8,7,6,5,4,3,2,1,0:T(8,128)S(1)}, f32[2,2,2,2,2,2,2,8,128]{8,7,6,5,4,3,2,1,0:T(8,128)S(1)}, u32[]{:S(2)}, u32[]{:S(2)}) %collective-permute-start.7) | collective-permute-done | bytes 524320 | tf_op jit(solution)/shard_map/ppermute | solution.py:129
  122.9 1.9 %bitcast_add_fusion.1 = f32[2,2,2,2,2,2,2,8,128]{8,7,6,5,4,3,2,1,0:T(8,128)} fusion(f32[2,2,2,2,2,2,2,8,128]{8,7,6,5,4,3,2,1,0:T(8,128)S(1)} %collective-permute-done.7, f32[2,2,2,2,2,2,2,2,8,128]{9,8,7,6,5,4,3,2,1,0:T(8,128)} %copy-done.1, s32[]{:T(128)S(6)} %select_n.66), kind=kLoop, calls=%fused_computation.28 | loop fusion | flops 131072 | bytes 1572868 | tf_op jit(solution)/shard_map/add | solution.py:152
  124.9 12.7 %all-to-all-start.1 = ((f32[128,8,128]{2,1,0:T(8,128)}), f32[128,8,128]{2,1,0:T(8,128)S(1)}, u32[]{:S(2)}, u32[]{:S(2)}) async-start(f32[128,8,128]{2,1,0:T(8,128)} %bitcast.21), calls=%async_computation.1 | async-start | bytes 1048576 | tf_op jit(solution)/shard_map/all_to_all | solution.py:156
  137.6 0.6 slice.52
  138.2 21.5 %all-to-all-done.1 = f32[128,8,128]{2,1,0:T(8,128)S(1)} async-done(((f32[128,8,128]{2,1,0:T(8,128)}), f32[128,8,128]{2,1,0:T(8,128)S(1)}, u32[]{:S(2)}, u32[]{:S(2)}) %all-to-all-start.1) | async-done | bytes 524320 | tf_op jit(solution)/shard_map/all_to_all | solution.py:156
  159.9 0.6 multiply_add_fusion
  (41 shorter events, 1.3 us)
Async XLA Ops:
  0.6 62.7 %copy-start = (f32[8,8,4096]{2,1,0:T(8,128)S(1)}, f32[8,8,4096]{2,1,0:T(8,128)}, u32[]{:S(2)}) copy-start(f32[8,8,4096]{2,1,0:T(8,128)} %param.11) | copy-start | bytes 3145732
  41.6 15.2 %collective-permute-start = (f32[2,2,2,2,2,2,2,8,128]{8,7,6,5,4,3,2,1,0:T(8,128)S(1)}, f32[2,2,2,2,2,2,2,8,128]{8,7,6,5,4,3,2,1,0:T(8,128)S(1)}, u32[]{:S(2)}, u32[]{:S(2)}) collective-permute-start(f32[2,2,2,2,2,2,2,8,128]{8,7,6,5,4,3,2,1,0:T(8,128)S(1)} %bitcast.52), channel_id=1, source_target_pairs={{0,2},{1,3},{2,0},{3,1},{4,6},{5,7},{6,4},{7,5},{8,10},{9,11},{10,... | collective-permute-start | bytes 1572872 | tf_op jit(solution)/shard_map/ppermute | solution.py:129
  58.0 4.8 %collective-permute-start.1 = (f32[2,2,2,2,2,2,2,2,8,128]{9,8,7,6,5,4,3,2,1,0:T(8,128)}, f32[2,2,2,2,2,2,2,2,8,128]{9,8,7,6,5,4,3,2,1,0:T(8,128)S(1)}, u32[]{:S(2)}, u32[]{:S(2)}) collective-permute-start(f32[2,2,2,2,2,2,2,2,8,128]{9,8,7,6,5,4,3,2,1,0:T(8,128)} %pad_maximum_fusion.1), channel_id=1, source_target_pairs={{0,1},{1,0},{2,3},{3,2},{4,5},{5,4},{6,7},{7,6},{8,9},{9,8},{10,11... | collective-permute-start | bytes 3145736 | tf_op jit(solution)/shard_map/ppermute | solution.py:129
  63.2 1.6 copy-start.2
  63.3 17.3 %copy-start.4 = (bf16[3,3,32,32]{3,2,1,0:T(8,128)(2,1)S(1)}, bf16[3,3,32,32]{3,2,1,0:T(8,128)(2,1)}, u32[]{:S(2)}) copy-start(bf16[3,3,32,32]{3,2,1,0:T(8,128)(2,1)} %param.15) | copy-start | bytes 55300
  63.3 17.3 %copy-start.6 = (f32[32]{0:T(128)S(1)}, f32[32]{0:T(128)}, u32[]{:S(2)}) copy-start(f32[32]{0:T(128)} %param.16) | copy-start | bytes 388
  63.3 17.3 %copy-start.7 = (f32[32]{0:T(128)S(1)}, f32[32]{0:T(128)}, u32[]{:S(2)}) copy-start(f32[32]{0:T(128)} %param.14) | copy-start | bytes 388
  63.3 17.3 %copy-start.10 = (f32[32]{0:T(128)S(1)}, f32[32]{0:T(128)}, u32[]{:S(2)}) copy-start(f32[32]{0:T(128)} %param.13) | copy-start | bytes 388
  64.8 3.9 %collective-permute-start.2 = (f32[4,8,256]{2,1,0:T(8,128)S(1)}, f32[4,8,256]{2,1,0:T(8,128)S(1)}, u32[]{:S(2)}, u32[]{:S(2)}) collective-permute-start(f32[4,8,256]{2,1,0:T(8,128)S(1)} %get-tuple-element.8), channel_id=1, source_target_pairs={{0,16},{16,32},{32,48},{48,64},{64,80},{80,96},{96,112},{112,128},... | collective-permute-start | bytes 98312 | tf_op jit(solution)/shard_map/ppermute | solution.py:21
  67.1 5.8 %collective-permute-start.3 = (f32[4,8,256]{2,1,0:T(8,128)S(1)}, f32[4,8,256]{2,1,0:T(8,128)S(1)}, u32[]{:S(2)}, u32[]{:S(2)}) collective-permute-start(f32[4,8,256]{2,1,0:T(8,128)S(1)} %get-tuple-element.9), channel_id=1, source_target_pairs={{16,0},{32,16},{48,32},{64,48},{80,64},{96,80},{112,96},{128,112},... | collective-permute-start | bytes 98312 | tf_op jit(solution)/shard_map/ppermute | solution.py:24
  73.0 5.7 %collective-permute-start.4 = (f32[16,4,256]{2,1,0:T(4,128)S(1)}, f32[16,4,256]{2,1,0:T(4,128)S(1)}, u32[]{:S(2)}, u32[]{:S(2)}) collective-permute-start(f32[16,4,256]{2,1,0:T(4,128)S(1)} %get-tuple-element.6), channel_id=1, source_target_pairs={{0,1},{1,2},{2,3},{3,4},{4,5},{5,6},{6,7},{7,8},{8,9},{9,10},{10,1... | collective-permute-start | bytes 196616 | tf_op jit(solution)/shard_map/ppermute | solution.py:21
  74.9 5.5 %collective-permute-start.5 = (f32[16,4,256]{2,1,0:T(4,128)S(1)}, f32[16,4,256]{2,1,0:T(4,128)S(1)}, u32[]{:S(2)}, u32[]{:S(2)}) collective-permute-start(f32[16,4,256]{2,1,0:T(4,128)S(1)} %get-tuple-element.7), channel_id=1, source_target_pairs={{1,0},{2,1},{3,2},{4,3},{5,4},{6,5},{7,6},{8,7},{9,8},{10,9},{11,1... | collective-permute-start | bytes 196616 | tf_op jit(solution)/shard_map/ppermute | solution.py:24
  80.6 3.2 %copy-start.5 = (bf16[3,3,32,32]{3,2,1,0:T(8,128)(2,1)S(1)}, bf16[3,3,32,32]{3,2,1,0:T(8,128)(2,1)}, u32[]{:S(2)}) copy-start(bf16[3,3,32,32]{3,2,1,0:T(8,128)(2,1)} %param.17) | copy-start | bytes 55300
  80.6 3.1 %copy-start.8 = (f32[32]{0:T(128)S(1)}, f32[32]{0:T(128)}, u32[]{:S(2)}) copy-start(f32[32]{0:T(128)} %param.19) | copy-start | bytes 388
  80.6 3.1 %copy-start.9 = (f32[32]{0:T(128)S(1)}, f32[32]{0:T(128)}, u32[]{:S(2)}) copy-start(f32[32]{0:T(128)} %param.18) | copy-start | bytes 388
  83.7 3.6 %copy-start.11 = (bf16[14,14,32,128]{3,2,1,0:T(8,128)(2,1)}, bf16[14,14,32,128]{3,2,1,0:T(8,128)(2,1)S(1)}, u32[]{:S(2)}) copy-start(bf16[14,14,32,128]{3,2,1,0:T(8,128)(2,1)S(1)} %select_convert_fusion.1) | copy-start | bytes 4816900
  97.8 6.6 %collective-permute-start.6 = (f32[2,2,2,2,2,2,2,2,8,128]{9,8,7,6,5,4,3,2,1,0:T(8,128)}, f32[2,2,2,2,2,2,2,2,8,128]{9,8,7,6,5,4,3,2,1,0:T(8,128)}, u32[]{:S(2)}, u32[]{:S(2)}) collective-permute-start(f32[2,2,2,2,2,2,2,2,8,128]{9,8,7,6,5,4,3,2,1,0:T(8,128)} %dynamic-slice_bitcast_fusion), channel_id=1, source_target_pairs={{0,1},{1,0},{2,3},{3,2},{4,5},{5,4},{6,7},{7,6},{8,9},{9,8},{10,11... | collective-permute-start | bytes 3145736 | tf_op jit(solution)/shard_map/ppermute | solution.py:129
  105.8 1.0 copy-start.1
  106.8 53.1 %copy-start.3 = (f32[8,128]{1,0:T(8,128)S(1)}, f32[8,128]{1,0:T(8,128)}, u32[]{:S(2)}) copy-start(f32[8,128]{1,0:T(8,128)} %param.10) | copy-start | bytes 12292
  106.8 16.1 %collective-permute-start.7 = (f32[2,2,2,2,2,2,2,8,128]{8,7,6,5,4,3,2,1,0:T(8,128)S(1)}, f32[2,2,2,2,2,2,2,8,128]{8,7,6,5,4,3,2,1,0:T(8,128)S(1)}, u32[]{:S(2)}, u32[]{:S(2)}) collective-permute-start(f32[2,2,2,2,2,2,2,8,128]{8,7,6,5,4,3,2,1,0:T(8,128)S(1)} %dynamic-slice_bitcast_fusion.1), channel_id=1, source_target_pairs={{0,2},{1,3},{2,0},{3,1},{4,6},{5,7},{6,4},{7,5},{8,10},{9,11},{10,... | collective-permute-start | bytes 1572872 | tf_op jit(solution)/shard_map/ppermute | solution.py:129
  124.9 34.8 %all-to-all-start.1 = ((f32[128,8,128]{2,1,0:T(8,128)}), f32[128,8,128]{2,1,0:T(8,128)S(1)}, u32[]{:S(2)}, u32[]{:S(2)}) async-start(f32[128,8,128]{2,1,0:T(8,128)} %bitcast.21), calls=%async_computation.1 | async-start | bytes 1048576 | tf_op jit(solution)/shard_map/all_to_all | solution.py:156

commit v12 on v9

--- a/solution.py
+++ b/solution.py
@@ -2,6 +2,7 @@
 import jax.numpy as jnp
 from jax import lax
 from jax.sharding import Mesh, PartitionSpec as P
+from jax.experimental.layout import Layout, with_layout_constraint
 import numpy as np
 
 prior_weight = 0.1
@@ -206,6 +207,7 @@
         precision=lax.Precision.HIGHEST,
         preferred_element_type=jnp.float32,
     )
+    projected = with_layout_constraint(projected, Layout(major_to_minor=(0, 1)))
     summed = scatter_sum(projected, coeffs.shape[0], sizes)
     grad_coeffs = summed + prior_weight * coeffs
     return (pressure, grad_coeffs)

time: 154 us -> 152 us (0.987)
  local copies, waits for them, and re-layouts: 4.88 us -> 3.19 us
    dot_general x1 -> x0, local copies, waits for them, and re-layouts: 1.91 us -> none  [shards(): lax.dot_general(flat_basis, grad_flat, (((0,), (0,)), ((), ())), precisio...]
where the time goes in v12:
time: 152 us; the launch traced here: 150 us
  waiting for transfers between devices  50.2 us (33%)
  starting transfers between devices  38.6 us (25%)
  blocking collectives  34 us (22%)
  matrix products  15.8 us (10%)
  other arithmetic  6.8 us (4%)
  local copies, waits for them, and re-layouts  3.19 us (2%)
    all_to_all x1, blocking collectives, gather_all(): data = lax.all_to_all(data, group, 0, 0, tiled=False)  34 us
    ppermute x6, waiting for transfers between devices, exchange(): return lax.ppermute(values, ALL_AXES, pairs)  29.6 us
    ppermute x6, starting transfers between devices, exchange(): return lax.ppermute(values, ALL_AXES, pairs)  19.9 us
    all_to_all x1, waiting for transfers between devices, scatter_sum(): data = lax.all_to_all(data, group, 0, 0, tiled=False)  13.9 us
    all_to_all x1, starting transfers between devices, scatter_sum(): data = lax.all_to_all(data, group, 0, 0, tiled=False)  9.46 us
    ppermute x2, waiting for transfers between devices, with_halo(): lax.ppermute(lax.slice_in_dim(block, 0, width, axis=dim), axis, backward)  6.68 us
    conv_general_dilated x2, matrix products, conv_valid(): lax.conv_general_dilated(values, weights, (1, 1), 'VALID', dimension_numb...  6.66 us
    ppermute x2, starting transfers between devices, with_halo(): lax.ppermute(lax.slice_in_dim(block, block.shape[dim] - width, None, axis...  5.8 us
  transfers between devices with their start and end apart: 11, of which 9 were waited for; matrix products, arithmetic and copies ran while one was open for 1% of the time, Pallas kernels for 0%

profile of v12, /device:TPU:1, one launch (start us, length us, event | category | flops | bytes accessed | tf_op | source)
XLA Modules:
  0.0 149.7 jit_solution(18236076625673917456)
XLA Ops:
  0.6 0.8 broadcast_in_dim.68
  1.4 34.0 %all_to_all.10 = f32[64,8,128]{2,1,0:T(8,128)S(1)} all-to-all(f32[64,8,128]{2,1,0:T(8,128)S(1)} %broadcast_in_dim.68), channel_id=1, replica_groups=mesh['b8'=2,'b7'=2,'b6'=2,'b5'=2,'b4'=2,'b3'=2,'b2'=2,'b1'=2,'b0'=2] {'b..., dimensions={0} | all-to-all | bytes 524288 | tf_op jit(solution)/shard_map/all_to_all | solution.py:170
  35.4 2.5 %collective-permute-start = (f32[2,2,2,2,2,2,8,128]{7,6,5,4,3,2,1,0:T(8,128)S(1)}, f32[2,2,2,2,2,2,8,128]{7,6,5,4,3,2,1,0:T(8,128)S(1)}, u32[]{:S(2)}, u32[]{:S(2)}) collective-permute-start(f32[2,2,2,2,2,2,8,128]{7,6,5,4,3,2,1,0:T(8,128)S(1)} %bitcast.86), channel_id=1, source_target_pairs={{0,16},{1,3},{2,18},{3,1},{4,20},{5,7},{6,22},{7,5},{8,24},{9,11},... | collective-permute-start | bytes 786440 | tf_op jit(solution)/shard_map/ppermute | solution.py:129
  38.0 4.6 %collective-permute-done = f32[2,2,2,2,2,2,8,128]{7,6,5,4,3,2,1,0:T(8,128)S(1)} collective-permute-done((f32[2,2,2,2,2,2,8,128]{7,6,5,4,3,2,1,0:T(8,128)S(1)}, f32[2,2,2,2,2,2,8,128]{7,6,5,4,3,2,1,0:T(8,128)S(1)}, u32[]{:S(2)}, u32[]{:S(2)}) %collective-permute-start) | collective-permute-done | bytes 262176 | tf_op jit(solution)/shard_map/ppermute | solution.py:129
  42.7 2.2 %collective-permute-start.1 = (f32[2,2,2,2,2,2,2,8,128]{8,7,6,5,4,3,2,1,0:T(8,128)S(1)}, f32[2,2,2,2,2,2,2,8,128]{8,7,6,5,4,3,2,1,0:T(8,128)S(1)}, u32[]{:S(2)}, u32[]{:S(2)}) collective-permute-start(f32[2,2,2,2,2,2,2,8,128]{8,7,6,5,4,3,2,1,0:T(8,128)S(1)} %maximum_select_fusion.1), channel_id=1, source_target_pairs={{0,2},{1,17},{2,0},{3,19},{4,6},{5,21},{6,4},{7,23},{8,10},{9,25},... | collective-permute-start | bytes 1572872 | tf_op jit(solution)/shard_map/ppermute | solution.py:129
  45.0 8.0 %collective-permute-done.1 = f32[2,2,2,2,2,2,2,8,128]{8,7,6,5,4,3,2,1,0:T(8,128)S(1)} collective-permute-done((f32[2,2,2,2,2,2,2,8,128]{8,7,6,5,4,3,2,1,0:T(8,128)S(1)}, f32[2,2,2,2,2,2,2,8,128]{8,7,6,5,4,3,2,1,0:T(8,128)S(1)}, u32[]{:S(2)}, u32[]{:S(2)}) %collective-permute-start.1) | collective-permute-done | bytes 524320 | tf_op jit(solution)/shard_map/ppermute | solution.py:129
  53.2 1.2 maximum_select_fusion
  54.4 6.9 %collective-permute-start.2 = (f32[2,2,2,2,2,2,2,2,8,128]{9,8,7,6,5,4,3,2,1,0:T(8,128)}, f32[2,2,2,2,2,2,2,2,8,128]{9,8,7,6,5,4,3,2,1,0:T(8,128)}, u32[]{:S(2)}, u32[]{:S(2)}) collective-permute-start(f32[2,2,2,2,2,2,2,2,8,128]{9,8,7,6,5,4,3,2,1,0:T(8,128)} %maximum_select_fusion), channel_id=1, source_target_pairs={{0,1},{1,0},{2,3},{3,2},{4,5},{5,4},{6,7},{7,6},{8,9},{9,8},{10,11... | collective-permute-start | bytes 3145736 | tf_op jit(solution)/shard_map/ppermute | solution.py:129
  61.6 2.3 %collective-permute-done.2 = f32[2,2,2,2,2,2,2,2,8,128]{9,8,7,6,5,4,3,2,1,0:T(8,128)} collective-permute-done((f32[2,2,2,2,2,2,2,2,8,128]{9,8,7,6,5,4,3,2,1,0:T(8,128)}, f32[2,2,2,2,2,2,2,2,8,128]{9,8,7,6,5,4,3,2,1,0:T(8,128)}, u32[]{:S(2)}, u32[]{:S(2)}) %collective-permute-start.2) | collective-permute-done | bytes 1048608 | tf_op jit(solution)/shard_map/ppermute | solution.py:129
  64.0 1.5 %select_bitcast_fusion.1 = (f32[2,2,2,2,2,2,2,2,1,8,128]{10,9,8,7,6,5,4,3,2,1,0:T(8,128)S(1)}, f32[2,2,2,2,2,2,2,2,1,8,128]{10,9,8,7,6,5,4,3,2,1,0:T(8,128)S(1)}) fusion(f32[2,2,2,2,2,2,2,2,8,128]{9,8,7,6,5,4,3,2,1,0:T(8,128)} %collective-permute-done.2, pred[]{:T(512)S(6)} %eq.8, f32[2,2,2,2,1,2,2,2,8,128]{9,8,7,6,5,4,3,2,1,0:T(8,128)S(1)} %get-tuple-element.5, ...), kind=kLoop, calls=%fused_computation.27 | loop fusion | flops 1310720 | bytes 5242882 | tf_op jit(solution)/shard_map/stack | solution.py:181
  65.8 1.5 convolution_bitcast_fusion
  67.3 2.2 %collective-permute-start.3 = (f32[4,8,256]{2,1,0:T(8,128)S(1)}, f32[4,8,256]{2,1,0:T(8,128)S(1)}, u32[]{:S(2)}, u32[]{:S(2)}) collective-permute-start(f32[4,8,256]{2,1,0:T(8,128)S(1)} %get-tuple-element.14), channel_id=1, source_target_pairs={{0,16},{16,32},{32,48},{48,64},{64,80},{80,96},{96,112},{112,128},... | collective-permute-start | bytes 98312 | tf_op jit(solution)/shard_map/ppermute | solution.py:22
  69.6 1.3 collective-permute-start.4
  70.9 3.3 %collective-permute-done.4 = f32[4,8,256]{2,1,0:T(8,128)S(1)} collective-permute-done((f32[4,8,256]{2,1,0:T(8,128)S(1)}, f32[4,8,256]{2,1,0:T(8,128)S(1)}, u32[]{:S(2)}, u32[]{:S(2)}) %collective-permute-start.4) | collective-permute-done | bytes 32800 | tf_op jit(solution)/shard_map/ppermute | solution.py:25
  74.3 3.6 %collective-permute-start.5 = (f32[16,4,256]{2,1,0:T(4,128)S(1)}, f32[16,4,256]{2,1,0:T(4,128)S(1)}, u32[]{:S(2)}, u32[]{:S(2)}) collective-permute-start(f32[16,4,256]{2,1,0:T(4,128)S(1)} %get-tuple-element.12), channel_id=1, source_target_pairs={{0,1},{1,2},{2,3},{3,4},{4,5},{5,6},{6,7},{7,8},{8,9},{9,10},{10,1... | collective-permute-start | bytes 196616 | tf_op jit(solution)/shard_map/ppermute | solution.py:22
  77.8 2.1 %collective-permute-start.6 = (f32[16,4,256]{2,1,0:T(4,128)S(1)}, f32[16,4,256]{2,1,0:T(4,128)S(1)}, u32[]{:S(2)}, u32[]{:S(2)}) collective-permute-start(f32[16,4,256]{2,1,0:T(4,128)S(1)} %get-tuple-element.13), channel_id=1, source_target_pairs={{1,0},{2,1},{3,2},{4,3},{5,4},{6,5},{7,6},{8,7},{9,8},{10,9},{11,1... | collective-permute-start | bytes 196616 | tf_op jit(solution)/shard_map/ppermute | solution.py:25
  80.0 3.4 %collective-permute-done.6 = f32[16,4,256]{2,1,0:T(4,128)S(1)} collective-permute-done((f32[16,4,256]{2,1,0:T(4,128)S(1)}, f32[16,4,256]{2,1,0:T(4,128)S(1)}, u32[]{:S(2)}, u32[]{:S(2)}) %collective-permute-start.6) | collective-permute-done | bytes 65568 | tf_op jit(solution)/shard_map/ppermute | solution.py:25
  83.6 3.1 %select_convert_fusion.1 = bf16[14,14,32,128]{3,2,1,0:T(8,128)(2,1)S(1)} fusion(f32[32]{0:T(128)S(1)} %copy-done.6, pred[14,14]{1,0:T(8,128)(4,1)S(1)} %slice_bitcast_fusion.2, bf16[3,3,32,32]{3,2,1,0:T(8,128)(2,1)S(1)} %copy-done.4, f32[32]{0:T(128)S(1)} %copy-done.7, f32[32]{0:T(128)S(1)} %copy-done.10, f32[16,16,128]{2,1,0:T(8,128)S(1)} %slice.51, ...), kind=kOutput, calls=%fused_computation.1 | convolution fusion | flops 469024768 | bytes 1755972 | tf_op jit(solution)/shard_map/conv_general_dilated | solution.py:48
  86.7 3.6 %multiply_reduce_fusion = (f32[12,12,128]{2,1,0:T(8,128)S(1)}, f32[12,12,32,128]{3,2,1,0:T(8,128)}) fusion(f32[32]{0:T(128)S(1)} %copy-done.8, f32[32]{0:T(128)S(1)} %copy-done.9, bf16[14,14,32,128]{3,2,1,0:T(8,128)(2,1)S(1)} %select_convert_fusion.1, bf16[3,3,32,32]{3,2,1,0:T(8,128)(2,1)S(1)} %copy-done.5), kind=kOutput, calls=%fused_computation.3 | convolution fusion | flops 341489664 | bytes 4057344 | tf_op jit(solution)/shard_map/conv_general_dilated | solution.py:48
  90.3 4.2 %fusion.6 = f32[8,8,128]{2,1,0:T(8,128)S(1)} fusion(bf16[3,3,32,32]{3,2,1,0:T(8,128)(2,1)S(1)} %copy-done.4, bf16[3,3,32,32]{3,2,1,0:T(8,128)(2,1)S(1)} %copy-done.5, f32[12,12,32,128]{3,2,1,0:T(8,128)} %get-tuple-element.17, f32[12,12,128]{2,1,0:T(8,128)S(1)} %maximum_subtract_fusion, f32[32]{0:T(128)S(1)} %copy-done.8, f32[32]{0:T(128)S(1)} %copy-done.9, ...), kind=kOutput, calls=%fused_computation.14 | convolution fusion | flops 394027008 | bytes 3322484 | tf_op jit(solution)/shard_map/conv_general_dilated | solution.py:59
  94.6 3.4 %fusion.22 = f32[128,4096,1]{0,1,2:T(8,128)S(1)} fusion(f32[8,8,128]{2,1,0:T(8,128)S(1)} %fusion.6, f32[8,8,4096]{2,1,0:T(8,128)S(1)} %copy-done), kind=kOutput, calls=%fused_computation.63 | convolution fusion | flops 402653184 | bytes 3178496 | tf_op jit(solution)/shard_map/dot_general | solution.py:203
  98.0 1.3 copy-done.1
  99.5 1.9 %collective-permute-start.7 = (f32[2,2,2,2,2,2,2,2,8,128]{9,8,7,6,5,4,3,2,1,0:T(8,128)S(1)}, f32[2,2,2,2,2,2,2,2,8,128]{9,8,7,6,5,4,3,2,1,0:T(8,128)S(1)}, u32[]{:S(2)}, u32[]{:S(2)}) collective-permute-start(f32[2,2,2,2,2,2,2,2,8,128]{9,8,7,6,5,4,3,2,1,0:T(8,128)S(1)} %dynamic-slice_bitcast_fusion), channel_id=1, source_target_pairs={{0,1},{1,0},{2,3},{3,2},{4,5},{5,4},{6,7},{7,6},{8,9},{9,8},{10,11... | collective-permute-start | bytes 3145736 | tf_op jit(solution)/shard_map/ppermute | solution.py:129
  101.4 2.6 %collective-permute-done.7 = f32[2,2,2,2,2,2,2,2,8,128]{9,8,7,6,5,4,3,2,1,0:T(8,128)S(1)} collective-permute-done((f32[2,2,2,2,2,2,2,2,8,128]{9,8,7,6,5,4,3,2,1,0:T(8,128)S(1)}, f32[2,2,2,2,2,2,2,2,8,128]{9,8,7,6,5,4,3,2,1,0:T(8,128)S(1)}, u32[]{:S(2)}, u32[]{:S(2)}) %collective-permute-start.7) | collective-permute-done | bytes 1048608 | tf_op jit(solution)/shard_map/ppermute | solution.py:129
  104.0 1.4 bitcast_add_fusion
  105.6 2.2 %collective-permute-start.8 = (f32[2,2,2,2,2,2,2,8,128]{8,7,6,5,4,3,2,1,0:T(8,128)S(1)}, f32[2,2,2,2,2,2,2,8,128]{8,7,6,5,4,3,2,1,0:T(8,128)S(1)}, u32[]{:S(2)}, u32[]{:S(2)}) collective-permute-start(f32[2,2,2,2,2,2,2,8,128]{8,7,6,5,4,3,2,1,0:T(8,128)S(1)} %bitcast_select_fusion), channel_id=1, source_target_pairs={{0,2},{1,17},{2,0},{3,19},{4,6},{5,21},{6,4},{7,23},{8,10},{9,25},... | collective-permute-start | bytes 1572872 | tf_op jit(solution)/shard_map/ppermute | solution.py:129
  107.8 8.0 %collective-permute-done.8 = f32[2,2,2,2,2,2,2,8,128]{8,7,6,5,4,3,2,1,0:T(8,128)S(1)} collective-permute-done((f32[2,2,2,2,2,2,2,8,128]{8,7,6,5,4,3,2,1,0:T(8,128)S(1)}, f32[2,2,2,2,2,2,2,8,128]{8,7,6,5,4,3,2,1,0:T(8,128)S(1)}, u32[]{:S(2)}, u32[]{:S(2)}) %collective-permute-start.8) | collective-permute-done | bytes 524320 | tf_op jit(solution)/shard_map/ppermute | solution.py:129
  116.0 4.2 %collective-permute-start.9 = (f32[2,2,2,2,2,2,8,128]{7,6,5,4,3,2,1,0:T(8,128)S(1)}, f32[2,2,2,2,2,2,8,128]{7,6,5,4,3,2,1,0:T(8,128)S(1)}, u32[]{:S(2)}, u32[]{:S(2)}) collective-permute-start(f32[2,2,2,2,2,2,8,128]{7,6,5,4,3,2,1,0:T(8,128)S(1)} %bitcast_select_fusion.2), channel_id=1, source_target_pairs={{0,16},{1,3},{2,18},{3,1},{4,20},{5,7},{6,22},{7,5},{8,24},{9,11},... | collective-permute-start | bytes 786440 | tf_op jit(solution)/shard_map/ppermute | solution.py:129
  120.2 4.0 %collective-permute-done.9 = f32[2,2,2,2,2,2,8,128]{7,6,5,4,3,2,1,0:T(8,128)S(1)} collective-permute-done((f32[2,2,2,2,2,2,8,128]{7,6,5,4,3,2,1,0:T(8,128)S(1)}, f32[2,2,2,2,2,2,8,128]{7,6,5,4,3,2,1,0:T(8,128)S(1)}, u32[]{:S(2)}, u32[]{:S(2)}) %collective-permute-start.9) | collective-permute-done | bytes 262176 | tf_op jit(solution)/shard_map/ppermute | solution.py:129
  124.2 0.8 fusion.14
  125.0 9.5 %all-to-all-start.1 = ((f32[64,8,128]{2,1,0:T(8,128)}), f32[64,8,128]{2,1,0:T(8,128)S(1)}, u32[]{:S(2)}, u32[]{:S(2)}) async-start(f32[64,8,128]{2,1,0:T(8,128)} %bitcast.36), calls=%async_computation.1 | async-start | bytes 524288 | tf_op jit(solution)/shard_map/all_to_all | solution.py:156
  135.1 13.9 %all-to-all-done.1 = f32[64,8,128]{2,1,0:T(8,128)S(1)} async-done(((f32[64,8,128]{2,1,0:T(8,128)}), f32[64,8,128]{2,1,0:T(8,128)S(1)}, u32[]{:S(2)}, u32[]{:S(2)}) %all-to-all-start.1) | async-done | bytes 262176 | tf_op jit(solution)/shard_map/all_to_all | solution.py:156
  (48 shorter events, 3.0 us)
Async XLA Ops:
  0.6 65.2 %copy-start = (f32[8,8,4096]{2,1,0:T(8,128)S(1)}, f32[8,8,4096]{2,1,0:T(8,128)}, u32[]{:S(2)}) copy-start(f32[8,8,4096]{2,1,0:T(8,128)} %param.11) | copy-start | bytes 3145732
  35.4 7.1 %collective-permute-start = (f32[2,2,2,2,2,2,8,128]{7,6,5,4,3,2,1,0:T(8,128)S(1)}, f32[2,2,2,2,2,2,8,128]{7,6,5,4,3,2,1,0:T(8,128)S(1)}, u32[]{:S(2)}, u32[]{:S(2)}) collective-permute-start(f32[2,2,2,2,2,2,8,128]{7,6,5,4,3,2,1,0:T(8,128)S(1)} %bitcast.86), channel_id=1, source_target_pairs={{0,16},{1,3},{2,18},{3,1},{4,20},{5,7},{6,22},{7,5},{8,24},{9,11},... | collective-permute-start | bytes 786440 | tf_op jit(solution)/shard_map/ppermute | solution.py:129
  42.7 10.2 %collective-permute-start.1 = (f32[2,2,2,2,2,2,2,8,128]{8,7,6,5,4,3,2,1,0:T(8,128)S(1)}, f32[2,2,2,2,2,2,2,8,128]{8,7,6,5,4,3,2,1,0:T(8,128)S(1)}, u32[]{:S(2)}, u32[]{:S(2)}) collective-permute-start(f32[2,2,2,2,2,2,2,8,128]{8,7,6,5,4,3,2,1,0:T(8,128)S(1)} %maximum_select_fusion.1), channel_id=1, source_target_pairs={{0,2},{1,17},{2,0},{3,19},{4,6},{5,21},{6,4},{7,23},{8,10},{9,25},... | collective-permute-start | bytes 1572872 | tf_op jit(solution)/shard_map/ppermute | solution.py:129
  54.4 9.6 %collective-permute-start.2 = (f32[2,2,2,2,2,2,2,2,8,128]{9,8,7,6,5,4,3,2,1,0:T(8,128)}, f32[2,2,2,2,2,2,2,2,8,128]{9,8,7,6,5,4,3,2,1,0:T(8,128)}, u32[]{:S(2)}, u32[]{:S(2)}) collective-permute-start(f32[2,2,2,2,2,2,2,2,8,128]{9,8,7,6,5,4,3,2,1,0:T(8,128)} %maximum_select_fusion), channel_id=1, source_target_pairs={{0,1},{1,0},{2,3},{3,2},{4,5},{5,4},{6,7},{7,6},{8,9},{9,8},{10,11... | collective-permute-start | bytes 3145736 | tf_op jit(solution)/shard_map/ppermute | solution.py:129
  65.7 1.6 %copy-start.2 = (f32[8,8,128]{2,1,0:T(8,128)S(1)}, f32[8,8,128]{2,1,0:T(8,128)}, u32[]{:S(2)}) copy-start(f32[8,8,128]{2,1,0:T(8,128)} %param.12) | copy-start | bytes 98308
  65.8 17.8 %copy-start.4 = (bf16[3,3,32,32]{3,2,1,0:T(8,128)(2,1)S(1)}, bf16[3,3,32,32]{3,2,1,0:T(8,128)(2,1)}, u32[]{:S(2)}) copy-start(bf16[3,3,32,32]{3,2,1,0:T(8,128)(2,1)} %param.15) | copy-start | bytes 55300
  65.8 17.8 %copy-start.6 = (f32[32]{0:T(128)S(1)}, f32[32]{0:T(128)}, u32[]{:S(2)}) copy-start(f32[32]{0:T(128)} %param.16) | copy-start | bytes 388
  65.8 17.8 %copy-start.7 = (f32[32]{0:T(128)S(1)}, f32[32]{0:T(128)}, u32[]{:S(2)}) copy-start(f32[32]{0:T(128)} %param.14) | copy-start | bytes 388
  65.8 17.7 %copy-start.10 = (f32[32]{0:T(128)S(1)}, f32[32]{0:T(128)}, u32[]{:S(2)}) copy-start(f32[32]{0:T(128)} %param.13) | copy-start | bytes 388
  67.3 3.6 %collective-permute-start.3 = (f32[4,8,256]{2,1,0:T(8,128)S(1)}, f32[4,8,256]{2,1,0:T(8,128)S(1)}, u32[]{:S(2)}, u32[]{:S(2)}) collective-permute-start(f32[4,8,256]{2,1,0:T(8,128)S(1)} %get-tuple-element.14), channel_id=1, source_target_pairs={{0,16},{16,32},{32,48},{48,64},{64,80},{80,96},{96,112},{112,128},... | collective-permute-start | bytes 98312 | tf_op jit(solution)/shard_map/ppermute | solution.py:22
  69.6 4.7 %collective-permute-start.4 = (f32[4,8,256]{2,1,0:T(8,128)S(1)}, f32[4,8,256]{2,1,0:T(8,128)S(1)}, u32[]{:S(2)}, u32[]{:S(2)}) collective-permute-start(f32[4,8,256]{2,1,0:T(8,128)S(1)} %get-tuple-element.15), channel_id=1, source_target_pairs={{16,0},{32,16},{48,32},{64,48},{80,64},{96,80},{112,96},{128,112},... | collective-permute-start | bytes 98312 | tf_op jit(solution)/shard_map/ppermute | solution.py:25
  74.3 5.8 %collective-permute-start.5 = (f32[16,4,256]{2,1,0:T(4,128)S(1)}, f32[16,4,256]{2,1,0:T(4,128)S(1)}, u32[]{:S(2)}, u32[]{:S(2)}) collective-permute-start(f32[16,4,256]{2,1,0:T(4,128)S(1)} %get-tuple-element.12), channel_id=1, source_target_pairs={{0,1},{1,2},{2,3},{3,4},{4,5},{5,6},{6,7},{7,8},{8,9},{9,10},{10,1... | collective-permute-start | bytes 196616 | tf_op jit(solution)/shard_map/ppermute | solution.py:22
  77.8 5.6 %collective-permute-start.6 = (f32[16,4,256]{2,1,0:T(4,128)S(1)}, f32[16,4,256]{2,1,0:T(4,128)S(1)}, u32[]{:S(2)}, u32[]{:S(2)}) collective-permute-start(f32[16,4,256]{2,1,0:T(4,128)S(1)} %get-tuple-element.13), channel_id=1, source_target_pairs={{1,0},{2,1},{3,2},{4,3},{5,4},{6,5},{7,6},{8,7},{9,8},{10,9},{11,1... | collective-permute-start | bytes 196616 | tf_op jit(solution)/shard_map/ppermute | solution.py:25
  83.5 3.1 %copy-start.5 = (bf16[3,3,32,32]{3,2,1,0:T(8,128)(2,1)S(1)}, bf16[3,3,32,32]{3,2,1,0:T(8,128)(2,1)}, u32[]{:S(2)}) copy-start(bf16[3,3,32,32]{3,2,1,0:T(8,128)(2,1)} %param.17) | copy-start | bytes 55300
  83.6 3.1 %copy-start.8 = (f32[32]{0:T(128)S(1)}, f32[32]{0:T(128)}, u32[]{:S(2)}) copy-start(f32[32]{0:T(128)} %param.19) | copy-start | bytes 388
  83.6 3.1 %copy-start.9 = (f32[32]{0:T(128)S(1)}, f32[32]{0:T(128)}, u32[]{:S(2)}) copy-start(f32[32]{0:T(128)} %param.18) | copy-start | bytes 388
  86.7 3.6 %copy-start.11 = (bf16[14,14,32,128]{3,2,1,0:T(8,128)(2,1)}, bf16[14,14,32,128]{3,2,1,0:T(8,128)(2,1)S(1)}, u32[]{:S(2)}) copy-start(bf16[14,14,32,128]{3,2,1,0:T(8,128)(2,1)S(1)} %select_convert_fusion.1) | copy-start | bytes 4816900
  98.0 1.3 copy-start.1
  99.5 4.6 %collective-permute-start.7 = (f32[2,2,2,2,2,2,2,2,8,128]{9,8,7,6,5,4,3,2,1,0:T(8,128)S(1)}, f32[2,2,2,2,2,2,2,2,8,128]{9,8,7,6,5,4,3,2,1,0:T(8,128)S(1)}, u32[]{:S(2)}, u32[]{:S(2)}) collective-permute-start(f32[2,2,2,2,2,2,2,2,8,128]{9,8,7,6,5,4,3,2,1,0:T(8,128)S(1)} %dynamic-slice_bitcast_fusion), channel_id=1, source_target_pairs={{0,1},{1,0},{2,3},{3,2},{4,5},{5,4},{6,7},{7,6},{8,9},{9,8},{10,11... | collective-permute-start | bytes 3145736 | tf_op jit(solution)/shard_map/ppermute | solution.py:129
  105.6 10.2 %collective-permute-start.8 = (f32[2,2,2,2,2,2,2,8,128]{8,7,6,5,4,3,2,1,0:T(8,128)S(1)}, f32[2,2,2,2,2,2,2,8,128]{8,7,6,5,4,3,2,1,0:T(8,128)S(1)}, u32[]{:S(2)}, u32[]{:S(2)}) collective-permute-start(f32[2,2,2,2,2,2,2,8,128]{8,7,6,5,4,3,2,1,0:T(8,128)S(1)} %bitcast_select_fusion), channel_id=1, source_target_pairs={{0,2},{1,17},{2,0},{3,19},{4,6},{5,21},{6,4},{7,23},{8,10},{9,25},... | collective-permute-start | bytes 1572872 | tf_op jit(solution)/shard_map/ppermute | solution.py:129
  107.7 41.3 %copy-start.3 = (f32[8,128]{1,0:T(8,128)S(1)}, f32[8,128]{1,0:T(8,128)}, u32[]{:S(2)}) copy-start(f32[8,128]{1,0:T(8,128)} %param.10) | copy-start | bytes 12292
  116.0 8.2 %collective-permute-start.9 = (f32[2,2,2,2,2,2,8,128]{7,6,5,4,3,2,1,0:T(8,128)S(1)}, f32[2,2,2,2,2,2,8,128]{7,6,5,4,3,2,1,0:T(8,128)S(1)}, u32[]{:S(2)}, u32[]{:S(2)}) collective-permute-start(f32[2,2,2,2,2,2,8,128]{7,6,5,4,3,2,1,0:T(8,128)S(1)} %bitcast_select_fusion.2), channel_id=1, source_target_pairs={{0,16},{1,3},{2,18},{3,1},{4,20},{5,7},{6,22},{7,5},{8,24},{9,11},... | collective-permute-start | bytes 786440 | tf_op jit(solution)/shard_map/ppermute | solution.py:129
  125.0 24.0 %all-to-all-start.1 = ((f32[64,8,128]{2,1,0:T(8,128)}), f32[64,8,128]{2,1,0:T(8,128)S(1)}, u32[]{:S(2)}, u32[]{:S(2)}) async-start(f32[64,8,128]{2,1,0:T(8,128)} %bitcast.36), calls=%async_computation.1 | async-start | bytes 524288 | tf_op jit(solution)/shard_map/all_to_all | solution.py:156

commit v13 on v12

--- a/solution.py
+++ b/solution.py
@@ -129,7 +129,7 @@
     return lax.ppermute(values, ALL_AXES, pairs)
 
 
-def scatter_sum(projected, mode_block, sizes):
+def scatter_sum(projected, mode_block, sizes, own):
     order, nbits = bit_order(sizes)
     count = 1 << nbits
     me = lax.axis_index(ALL_AXES)
@@ -153,6 +153,8 @@
     present = presents[0]
     group = tuple(f"b{bit}" for bit in present)
     data = data.reshape((1 << len(present), mode_block, projected.shape[1]))
+    to_self = jnp.arange(1 << len(present))[:, None, None] == lax.axis_index(group)
+    data = data + jnp.where(to_self, own[None], jnp.float32(0.0))
     data = lax.all_to_all(data, group, 0, 0, tiled=False)
     return jnp.sum(data, axis=0)
 
@@ -208,8 +210,7 @@
         preferred_element_type=jnp.float32,
     )
     projected = with_layout_constraint(projected, Layout(major_to_minor=(0, 1)))
-    summed = scatter_sum(projected, coeffs.shape[0], sizes)
-    grad_coeffs = summed + prior_weight * coeffs
+    grad_coeffs = scatter_sum(projected, coeffs.shape[0], sizes, prior_weight * coeffs)
     return (pressure, grad_coeffs)
 
 

time: 152 us -> 152 us (level)
  no operation moved by 1% of the time
where the time goes in v13:
time: 152 us; the launch traced here: 150 us
  waiting for transfers between devices  50.2 us (33%)
  starting transfers between devices  38.6 us (25%)
  blocking collectives  34 us (22%)
  matrix products  15.6 us (10%)
  other arithmetic  6.95 us (5%)
  local copies, waits for them, and re-layouts  3.19 us (2%)
    all_to_all x1, blocking collectives, gather_all(): data = lax.all_to_all(data, group, 0, 0, tiled=False)  34 us
    ppermute x6, waiting for transfers between devices, exchange(): return lax.ppermute(values, ALL_AXES, pairs)  29.5 us
    ppermute x6, starting transfers between devices, exchange(): return lax.ppermute(values, ALL_AXES, pairs)  19.9 us
    all_to_all x1, waiting for transfers between devices, scatter_sum(): data = lax.all_to_all(data, group, 0, 0, tiled=False)  14 us
    all_to_all x1, starting transfers between devices, scatter_sum(): data = lax.all_to_all(data, group, 0, 0, tiled=False)  9.46 us
    ppermute x2, waiting for transfers between devices, with_halo(): lax.ppermute(lax.slice_in_dim(block, 0, width, axis=dim), axis, backward)  6.68 us
    conv_general_dilated x2, matrix products, conv_valid(): lax.conv_general_dilated(values, weights, (1, 1), 'VALID', dimension_numb...  6.65 us
    ppermute x2, starting transfers between devices, with_halo(): lax.ppermute(lax.slice_in_dim(block, block.shape[dim] - width, None, axis...  5.8 us
  transfers between devices with their start and end apart: 11, of which 9 were waited for; matrix products, arithmetic and copies ran while one was open for 1% of the time, Pallas kernels for 0%

profile of v13, /device:TPU:1, one launch (start us, length us, event | category | flops | bytes accessed | tf_op | source)
XLA Modules:
  0.0 149.7 jit_solution(9013697174699751611)
XLA Ops:
  0.6 0.8 broadcast_in_dim.90
  1.4 34.0 %all_to_all.10 = f32[64,8,128]{2,1,0:T(8,128)S(1)} all-to-all(f32[64,8,128]{2,1,0:T(8,128)S(1)} %broadcast_in_dim.90), channel_id=1, replica_groups=mesh['b8'=2,'b7'=2,'b6'=2,'b5'=2,'b4'=2,'b3'=2,'b2'=2,'b1'=2,'b0'=2] {'b..., dimensions={0} | all-to-all | bytes 524288 | tf_op jit(solution)/shard_map/all_to_all | solution.py:172
  35.4 2.5 %collective-permute-start = (f32[2,2,2,2,2,2,8,128]{7,6,5,4,3,2,1,0:T(8,128)S(1)}, f32[2,2,2,2,2,2,8,128]{7,6,5,4,3,2,1,0:T(8,128)S(1)}, u32[]{:S(2)}, u32[]{:S(2)}) collective-permute-start(f32[2,2,2,2,2,2,8,128]{7,6,5,4,3,2,1,0:T(8,128)S(1)} %bitcast.87), channel_id=1, source_target_pairs={{0,16},{1,3},{2,18},{3,1},{4,20},{5,7},{6,22},{7,5},{8,24},{9,11},... | collective-permute-start | bytes 786440 | tf_op jit(solution)/shard_map/ppermute | solution.py:129
  38.0 4.6 %collective-permute-done = f32[2,2,2,2,2,2,8,128]{7,6,5,4,3,2,1,0:T(8,128)S(1)} collective-permute-done((f32[2,2,2,2,2,2,8,128]{7,6,5,4,3,2,1,0:T(8,128)S(1)}, f32[2,2,2,2,2,2,8,128]{7,6,5,4,3,2,1,0:T(8,128)S(1)}, u32[]{:S(2)}, u32[]{:S(2)}) %collective-permute-start) | collective-permute-done | bytes 262176 | tf_op jit(solution)/shard_map/ppermute | solution.py:129
  42.7 2.2 %collective-permute-start.1 = (f32[2,2,2,2,2,2,2,8,128]{8,7,6,5,4,3,2,1,0:T(8,128)S(1)}, f32[2,2,2,2,2,2,2,8,128]{8,7,6,5,4,3,2,1,0:T(8,128)S(1)}, u32[]{:S(2)}, u32[]{:S(2)}) collective-permute-start(f32[2,2,2,2,2,2,2,8,128]{8,7,6,5,4,3,2,1,0:T(8,128)S(1)} %maximum_select_fusion.1), channel_id=1, source_target_pairs={{0,2},{1,17},{2,0},{3,19},{4,6},{5,21},{6,4},{7,23},{8,10},{9,25},... | collective-permute-start | bytes 1572872 | tf_op jit(solution)/shard_map/ppermute | solution.py:129
  45.0 8.0 %collective-permute-done.1 = f32[2,2,2,2,2,2,2,8,128]{8,7,6,5,4,3,2,1,0:T(8,128)S(1)} collective-permute-done((f32[2,2,2,2,2,2,2,8,128]{8,7,6,5,4,3,2,1,0:T(8,128)S(1)}, f32[2,2,2,2,2,2,2,8,128]{8,7,6,5,4,3,2,1,0:T(8,128)S(1)}, u32[]{:S(2)}, u32[]{:S(2)}) %collective-permute-start.1) | collective-permute-done | bytes 524320 | tf_op jit(solution)/shard_map/ppermute | solution.py:129
  53.3 1.2 maximum_select_fusion
  54.4 6.9 %collective-permute-start.2 = (f32[2,2,2,2,2,2,2,2,8,128]{9,8,7,6,5,4,3,2,1,0:T(8,128)}, f32[2,2,2,2,2,2,2,2,8,128]{9,8,7,6,5,4,3,2,1,0:T(8,128)}, u32[]{:S(2)}, u32[]{:S(2)}) collective-permute-start(f32[2,2,2,2,2,2,2,2,8,128]{9,8,7,6,5,4,3,2,1,0:T(8,128)} %maximum_select_fusion), channel_id=1, source_target_pairs={{0,1},{1,0},{2,3},{3,2},{4,5},{5,4},{6,7},{7,6},{8,9},{9,8},{10,11... | collective-permute-start | bytes 3145736 | tf_op jit(solution)/shard_map/ppermute | solution.py:129
  61.6 2.3 %collective-permute-done.2 = f32[2,2,2,2,2,2,2,2,8,128]{9,8,7,6,5,4,3,2,1,0:T(8,128)} collective-permute-done((f32[2,2,2,2,2,2,2,2,8,128]{9,8,7,6,5,4,3,2,1,0:T(8,128)}, f32[2,2,2,2,2,2,2,2,8,128]{9,8,7,6,5,4,3,2,1,0:T(8,128)}, u32[]{:S(2)}, u32[]{:S(2)}) %collective-permute-start.2) | collective-permute-done | bytes 1048608 | tf_op jit(solution)/shard_map/ppermute | solution.py:129
  64.0 1.6 %select_bitcast_fusion.1 = (f32[2,2,2,2,2,2,2,2,1,8,128]{10,9,8,7,6,5,4,3,2,1,0:T(8,128)S(1)}, f32[2,2,2,2,2,2,2,2,1,8,128]{10,9,8,7,6,5,4,3,2,1,0:T(8,128)S(1)}) fusion(f32[2,2,2,2,2,2,2,2,8,128]{9,8,7,6,5,4,3,2,1,0:T(8,128)} %collective-permute-done.2, pred[]{:T(512)S(6)} %eq.31, f32[2,2,2,2,1,2,2,2,8,128]{9,8,7,6,5,4,3,2,1,0:T(8,128)S(1)} %get-tuple-element.5, ...), kind=kLoop, calls=%fused_computation.27 | loop fusion | flops 1310720 | bytes 5242882 | tf_op jit(solution)/shard_map/stack | solution.py:183
  65.8 1.5 convolution_bitcast_fusion
  67.3 2.2 %collective-permute-start.3 = (f32[4,8,256]{2,1,0:T(8,128)S(1)}, f32[4,8,256]{2,1,0:T(8,128)S(1)}, u32[]{:S(2)}, u32[]{:S(2)}) collective-permute-start(f32[4,8,256]{2,1,0:T(8,128)S(1)} %get-tuple-element.14), channel_id=1, source_target_pairs={{0,16},{16,32},{32,48},{48,64},{64,80},{80,96},{96,112},{112,128},... | collective-permute-start | bytes 98312 | tf_op jit(solution)/shard_map/ppermute | solution.py:22
  69.6 1.3 collective-permute-start.4
  71.0 3.3 %collective-permute-done.4 = f32[4,8,256]{2,1,0:T(8,128)S(1)} collective-permute-done((f32[4,8,256]{2,1,0:T(8,128)S(1)}, f32[4,8,256]{2,1,0:T(8,128)S(1)}, u32[]{:S(2)}, u32[]{:S(2)}) %collective-permute-start.4) | collective-permute-done | bytes 32800 | tf_op jit(solution)/shard_map/ppermute | solution.py:25
  74.3 3.6 %collective-permute-start.5 = (f32[16,4,256]{2,1,0:T(4,128)S(1)}, f32[16,4,256]{2,1,0:T(4,128)S(1)}, u32[]{:S(2)}, u32[]{:S(2)}) collective-permute-start(f32[16,4,256]{2,1,0:T(4,128)S(1)} %get-tuple-element.12), channel_id=1, source_target_pairs={{0,1},{1,2},{2,3},{3,4},{4,5},{5,6},{6,7},{7,8},{8,9},{9,10},{10,1... | collective-permute-start | bytes 196616 | tf_op jit(solution)/shard_map/ppermute | solution.py:22
  77.9 2.1 %collective-permute-start.6 = (f32[16,4,256]{2,1,0:T(4,128)S(1)}, f32[16,4,256]{2,1,0:T(4,128)S(1)}, u32[]{:S(2)}, u32[]{:S(2)}) collective-permute-start(f32[16,4,256]{2,1,0:T(4,128)S(1)} %get-tuple-element.13), channel_id=1, source_target_pairs={{1,0},{2,1},{3,2},{4,3},{5,4},{6,5},{7,6},{8,7},{9,8},{10,9},{11,1... | collective-permute-start | bytes 196616 | tf_op jit(solution)/shard_map/ppermute | solution.py:25
  80.1 3.4 %collective-permute-done.6 = f32[16,4,256]{2,1,0:T(4,128)S(1)} collective-permute-done((f32[16,4,256]{2,1,0:T(4,128)S(1)}, f32[16,4,256]{2,1,0:T(4,128)S(1)}, u32[]{:S(2)}, u32[]{:S(2)}) %collective-permute-start.6) | collective-permute-done | bytes 65568 | tf_op jit(solution)/shard_map/ppermute | solution.py:25
  83.6 3.1 %select_convert_fusion.1 = bf16[14,14,32,128]{3,2,1,0:T(8,128)(2,1)S(1)} fusion(f32[32]{0:T(128)S(1)} %copy-done.6, pred[14,14]{1,0:T(8,128)(4,1)S(1)} %slice_bitcast_fusion.2, bf16[3,3,32,32]{3,2,1,0:T(8,128)(2,1)S(1)} %copy-done.4, f32[32]{0:T(128)S(1)} %copy-done.7, f32[32]{0:T(128)S(1)} %copy-done.10, f32[16,16,128]{2,1,0:T(8,128)S(1)} %slice.51, ...), kind=kOutput, calls=%fused_computation.1 | convolution fusion | flops 469024768 | bytes 1755972 | tf_op jit(solution)/shard_map/conv_general_dilated | solution.py:48
  86.7 3.5 %multiply_reduce_fusion = (f32[12,12,128]{2,1,0:T(8,128)S(1)}, f32[12,12,32,128]{3,2,1,0:T(8,128)}) fusion(f32[32]{0:T(128)S(1)} %copy-done.8, f32[32]{0:T(128)S(1)} %copy-done.9, bf16[14,14,32,128]{3,2,1,0:T(8,128)(2,1)S(1)} %select_convert_fusion.1, bf16[3,3,32,32]{3,2,1,0:T(8,128)(2,1)S(1)} %copy-done.5), kind=kOutput, calls=%fused_computation.3 | convolution fusion | flops 341489664 | bytes 4057344 | tf_op jit(solution)/shard_map/conv_general_dilated | solution.py:48
  90.3 4.1 %fusion.6 = f32[8,8,128]{2,1,0:T(8,128)S(1)} fusion(bf16[3,3,32,32]{3,2,1,0:T(8,128)(2,1)S(1)} %copy-done.4, bf16[3,3,32,32]{3,2,1,0:T(8,128)(2,1)S(1)} %copy-done.5, f32[12,12,32,128]{3,2,1,0:T(8,128)} %get-tuple-element.17, f32[12,12,128]{2,1,0:T(8,128)S(1)} %maximum_subtract_fusion, f32[32]{0:T(128)S(1)} %copy-done.8, f32[32]{0:T(128)S(1)} %copy-done.9, ...), kind=kOutput, calls=%fused_computation.14 | convolution fusion | flops 394027008 | bytes 3462656 | tf_op jit(solution)/shard_map/conv_general_dilated | solution.py:59
  94.4 3.4 %fusion.22 = f32[128,4096,1]{0,1,2:T(8,128)S(1)} fusion(f32[8,8,128]{2,1,0:T(8,128)S(1)} %fusion.6, f32[8,8,4096]{2,1,0:T(8,128)S(1)} %copy-done), kind=kOutput, calls=%fused_computation.65 | convolution fusion | flops 402653184 | bytes 3178496 | tf_op jit(solution)/shard_map/dot_general | solution.py:205
  97.8 1.3 copy-done.1
  99.3 1.9 %collective-permute-start.7 = (f32[2,2,2,2,2,2,2,2,8,128]{9,8,7,6,5,4,3,2,1,0:T(8,128)S(1)}, f32[2,2,2,2,2,2,2,2,8,128]{9,8,7,6,5,4,3,2,1,0:T(8,128)S(1)}, u32[]{:S(2)}, u32[]{:S(2)}) collective-permute-start(f32[2,2,2,2,2,2,2,2,8,128]{9,8,7,6,5,4,3,2,1,0:T(8,128)S(1)} %dynamic-slice_bitcast_fusion), channel_id=1, source_target_pairs={{0,1},{1,0},{2,3},{3,2},{4,5},{5,4},{6,7},{7,6},{8,9},{9,8},{10,11... | collective-permute-start | bytes 3145736 | tf_op jit(solution)/shard_map/ppermute | solution.py:129
  101.2 2.6 %collective-permute-done.7 = f32[2,2,2,2,2,2,2,2,8,128]{9,8,7,6,5,4,3,2,1,0:T(8,128)S(1)} collective-permute-done((f32[2,2,2,2,2,2,2,2,8,128]{9,8,7,6,5,4,3,2,1,0:T(8,128)S(1)}, f32[2,2,2,2,2,2,2,2,8,128]{9,8,7,6,5,4,3,2,1,0:T(8,128)S(1)}, u32[]{:S(2)}, u32[]{:S(2)}) %collective-permute-start.7) | collective-permute-done | bytes 1048608 | tf_op jit(solution)/shard_map/ppermute | solution.py:129
  103.8 1.4 bitcast_add_fusion
  105.4 2.2 %collective-permute-start.8 = (f32[2,2,2,2,2,2,2,8,128]{8,7,6,5,4,3,2,1,0:T(8,128)S(1)}, f32[2,2,2,2,2,2,2,8,128]{8,7,6,5,4,3,2,1,0:T(8,128)S(1)}, u32[]{:S(2)}, u32[]{:S(2)}) collective-permute-start(f32[2,2,2,2,2,2,2,8,128]{8,7,6,5,4,3,2,1,0:T(8,128)S(1)} %bitcast_select_fusion), channel_id=1, source_target_pairs={{0,2},{1,17},{2,0},{3,19},{4,6},{5,21},{6,4},{7,23},{8,10},{9,25},... | collective-permute-start | bytes 1572872 | tf_op jit(solution)/shard_map/ppermute | solution.py:129
  107.6 8.0 %collective-permute-done.8 = f32[2,2,2,2,2,2,2,8,128]{8,7,6,5,4,3,2,1,0:T(8,128)S(1)} collective-permute-done((f32[2,2,2,2,2,2,2,8,128]{8,7,6,5,4,3,2,1,0:T(8,128)S(1)}, f32[2,2,2,2,2,2,2,8,128]{8,7,6,5,4,3,2,1,0:T(8,128)S(1)}, u32[]{:S(2)}, u32[]{:S(2)}) %collective-permute-start.8) | collective-permute-done | bytes 524320 | tf_op jit(solution)/shard_map/ppermute | solution.py:129
  115.8 4.2 %collective-permute-start.9 = (f32[2,2,2,2,2,2,8,128]{7,6,5,4,3,2,1,0:T(8,128)S(1)}, f32[2,2,2,2,2,2,8,128]{7,6,5,4,3,2,1,0:T(8,128)S(1)}, u32[]{:S(2)}, u32[]{:S(2)}) collective-permute-start(f32[2,2,2,2,2,2,8,128]{7,6,5,4,3,2,1,0:T(8,128)S(1)} %bitcast_select_fusion.2), channel_id=1, source_target_pairs={{0,16},{1,3},{2,18},{3,1},{4,20},{5,7},{6,22},{7,5},{8,24},{9,11},... | collective-permute-start | bytes 786440 | tf_op jit(solution)/shard_map/ppermute | solution.py:129
  120.0 4.0 %collective-permute-done.9 = f32[2,2,2,2,2,2,8,128]{7,6,5,4,3,2,1,0:T(8,128)S(1)} collective-permute-done((f32[2,2,2,2,2,2,8,128]{7,6,5,4,3,2,1,0:T(8,128)S(1)}, f32[2,2,2,2,2,2,8,128]{7,6,5,4,3,2,1,0:T(8,128)S(1)}, u32[]{:S(2)}, u32[]{:S(2)}) %collective-permute-start.9) | collective-permute-done | bytes 262176 | tf_op jit(solution)/shard_map/ppermute | solution.py:129
  124.1 0.8 bitcast_add_fusion.1
  124.9 9.5 %all-to-all-start.1 = ((f32[64,8,128]{2,1,0:T(8,128)}), f32[64,8,128]{2,1,0:T(8,128)S(1)}, u32[]{:S(2)}, u32[]{:S(2)}) async-start(f32[64,8,128]{2,1,0:T(8,128)} %bitcast_add_fusion.1), calls=%async_computation.1 | async-start | bytes 524288 | tf_op jit(solution)/shard_map/all_to_all | solution.py:158
  135.0 14.0 %all-to-all-done.1 = f32[64,8,128]{2,1,0:T(8,128)S(1)} async-done(((f32[64,8,128]{2,1,0:T(8,128)}), f32[64,8,128]{2,1,0:T(8,128)S(1)}, u32[]{:S(2)}, u32[]{:S(2)}) %all-to-all-start.1) | async-done | bytes 262176 | tf_op jit(solution)/shard_map/all_to_all | solution.py:158
  (48 shorter events, 3.0 us)
Async XLA Ops:
  0.6 65.2 %copy-start = (f32[8,8,4096]{2,1,0:T(8,128)S(1)}, f32[8,8,4096]{2,1,0:T(8,128)}, u32[]{:S(2)}) copy-start(f32[8,8,4096]{2,1,0:T(8,128)} %param.11) | copy-start | bytes 3145732
  35.4 7.1 %collective-permute-start = (f32[2,2,2,2,2,2,8,128]{7,6,5,4,3,2,1,0:T(8,128)S(1)}, f32[2,2,2,2,2,2,8,128]{7,6,5,4,3,2,1,0:T(8,128)S(1)}, u32[]{:S(2)}, u32[]{:S(2)}) collective-permute-start(f32[2,2,2,2,2,2,8,128]{7,6,5,4,3,2,1,0:T(8,128)S(1)} %bitcast.87), channel_id=1, source_target_pairs={{0,16},{1,3},{2,18},{3,1},{4,20},{5,7},{6,22},{7,5},{8,24},{9,11},... | collective-permute-start | bytes 786440 | tf_op jit(solution)/shard_map/ppermute | solution.py:129
  42.7 10.2 %collective-permute-start.1 = (f32[2,2,2,2,2,2,2,8,128]{8,7,6,5,4,3,2,1,0:T(8,128)S(1)}, f32[2,2,2,2,2,2,2,8,128]{8,7,6,5,4,3,2,1,0:T(8,128)S(1)}, u32[]{:S(2)}, u32[]{:S(2)}) collective-permute-start(f32[2,2,2,2,2,2,2,8,128]{8,7,6,5,4,3,2,1,0:T(8,128)S(1)} %maximum_select_fusion.1), channel_id=1, source_target_pairs={{0,2},{1,17},{2,0},{3,19},{4,6},{5,21},{6,4},{7,23},{8,10},{9,25},... | collective-permute-start | bytes 1572872 | tf_op jit(solution)/shard_map/ppermute | solution.py:129
  54.4 9.6 %collective-permute-start.2 = (f32[2,2,2,2,2,2,2,2,8,128]{9,8,7,6,5,4,3,2,1,0:T(8,128)}, f32[2,2,2,2,2,2,2,2,8,128]{9,8,7,6,5,4,3,2,1,0:T(8,128)}, u32[]{:S(2)}, u32[]{:S(2)}) collective-permute-start(f32[2,2,2,2,2,2,2,2,8,128]{9,8,7,6,5,4,3,2,1,0:T(8,128)} %maximum_select_fusion), channel_id=1, source_target_pairs={{0,1},{1,0},{2,3},{3,2},{4,5},{5,4},{6,7},{7,6},{8,9},{9,8},{10,11... | collective-permute-start | bytes 3145736 | tf_op jit(solution)/shard_map/ppermute | solution.py:129
  65.8 1.6 %copy-start.2 = (f32[8,8,128]{2,1,0:T(8,128)S(1)}, f32[8,8,128]{2,1,0:T(8,128)}, u32[]{:S(2)}) copy-start(f32[8,8,128]{2,1,0:T(8,128)} %param.12) | copy-start | bytes 98308
  65.8 17.8 %copy-start.4 = (bf16[3,3,32,32]{3,2,1,0:T(8,128)(2,1)S(1)}, bf16[3,3,32,32]{3,2,1,0:T(8,128)(2,1)}, u32[]{:S(2)}) copy-start(bf16[3,3,32,32]{3,2,1,0:T(8,128)(2,1)} %param.15) | copy-start | bytes 55300
  65.8 17.7 %copy-start.6 = (f32[32]{0:T(128)S(1)}, f32[32]{0:T(128)}, u32[]{:S(2)}) copy-start(f32[32]{0:T(128)} %param.16) | copy-start | bytes 388
  65.8 17.7 %copy-start.7 = (f32[32]{0:T(128)S(1)}, f32[32]{0:T(128)}, u32[]{:S(2)}) copy-start(f32[32]{0:T(128)} %param.14) | copy-start | bytes 388
  65.8 17.7 %copy-start.10 = (f32[32]{0:T(128)S(1)}, f32[32]{0:T(128)}, u32[]{:S(2)}) copy-start(f32[32]{0:T(128)} %param.13) | copy-start | bytes 388
  67.3 3.6 %collective-permute-start.3 = (f32[4,8,256]{2,1,0:T(8,128)S(1)}, f32[4,8,256]{2,1,0:T(8,128)S(1)}, u32[]{:S(2)}, u32[]{:S(2)}) collective-permute-start(f32[4,8,256]{2,1,0:T(8,128)S(1)} %get-tuple-element.14), channel_id=1, source_target_pairs={{0,16},{16,32},{32,48},{48,64},{64,80},{80,96},{96,112},{112,128},... | collective-permute-start | bytes 98312 | tf_op jit(solution)/shard_map/ppermute | solution.py:22
  69.6 4.7 %collective-permute-start.4 = (f32[4,8,256]{2,1,0:T(8,128)S(1)}, f32[4,8,256]{2,1,0:T(8,128)S(1)}, u32[]{:S(2)}, u32[]{:S(2)}) collective-permute-start(f32[4,8,256]{2,1,0:T(8,128)S(1)} %get-tuple-element.15), channel_id=1, source_target_pairs={{16,0},{32,16},{48,32},{64,48},{80,64},{96,80},{112,96},{128,112},... | collective-permute-start | bytes 98312 | tf_op jit(solution)/shard_map/ppermute | solution.py:25
  74.3 5.8 %collective-permute-start.5 = (f32[16,4,256]{2,1,0:T(4,128)S(1)}, f32[16,4,256]{2,1,0:T(4,128)S(1)}, u32[]{:S(2)}, u32[]{:S(2)}) collective-permute-start(f32[16,4,256]{2,1,0:T(4,128)S(1)} %get-tuple-element.12), channel_id=1, source_target_pairs={{0,1},{1,2},{2,3},{3,4},{4,5},{5,6},{6,7},{7,8},{8,9},{9,10},{10,1... | collective-permute-start | bytes 196616 | tf_op jit(solution)/shard_map/ppermute | solution.py:22
  77.9 5.6 %collective-permute-start.6 = (f32[16,4,256]{2,1,0:T(4,128)S(1)}, f32[16,4,256]{2,1,0:T(4,128)S(1)}, u32[]{:S(2)}, u32[]{:S(2)}) collective-permute-start(f32[16,4,256]{2,1,0:T(4,128)S(1)} %get-tuple-element.13), channel_id=1, source_target_pairs={{1,0},{2,1},{3,2},{4,3},{5,4},{6,5},{7,6},{8,7},{9,8},{10,9},{11,1... | collective-permute-start | bytes 196616 | tf_op jit(solution)/shard_map/ppermute | solution.py:25
  83.6 3.2 %copy-start.5 = (bf16[3,3,32,32]{3,2,1,0:T(8,128)(2,1)S(1)}, bf16[3,3,32,32]{3,2,1,0:T(8,128)(2,1)}, u32[]{:S(2)}) copy-start(bf16[3,3,32,32]{3,2,1,0:T(8,128)(2,1)} %param.17) | copy-start | bytes 55300
  83.6 3.2 %copy-start.8 = (f32[32]{0:T(128)S(1)}, f32[32]{0:T(128)}, u32[]{:S(2)}) copy-start(f32[32]{0:T(128)} %param.19) | copy-start | bytes 388
  83.6 3.2 %copy-start.9 = (f32[32]{0:T(128)S(1)}, f32[32]{0:T(128)}, u32[]{:S(2)}) copy-start(f32[32]{0:T(128)} %param.18) | copy-start | bytes 388
  97.8 1.3 copy-start.1
  99.3 4.6 %collective-permute-start.7 = (f32[2,2,2,2,2,2,2,2,8,128]{9,8,7,6,5,4,3,2,1,0:T(8,128)S(1)}, f32[2,2,2,2,2,2,2,2,8,128]{9,8,7,6,5,4,3,2,1,0:T(8,128)S(1)}, u32[]{:S(2)}, u32[]{:S(2)}) collective-permute-start(f32[2,2,2,2,2,2,2,2,8,128]{9,8,7,6,5,4,3,2,1,0:T(8,128)S(1)} %dynamic-slice_bitcast_fusion), channel_id=1, source_target_pairs={{0,1},{1,0},{2,3},{3,2},{4,5},{5,4},{6,7},{7,6},{8,9},{9,8},{10,11... | collective-permute-start | bytes 3145736 | tf_op jit(solution)/shard_map/ppermute | solution.py:129
  105.3 14.7 %copy-start.3 = (f32[8,128]{1,0:T(8,128)S(1)}, f32[8,128]{1,0:T(8,128)}, u32[]{:S(2)}) copy-start(f32[8,128]{1,0:T(8,128)} %param.10) | copy-start | bytes 12292
  105.4 10.2 %collective-permute-start.8 = (f32[2,2,2,2,2,2,2,8,128]{8,7,6,5,4,3,2,1,0:T(8,128)S(1)}, f32[2,2,2,2,2,2,2,8,128]{8,7,6,5,4,3,2,1,0:T(8,128)S(1)}, u32[]{:S(2)}, u32[]{:S(2)}) collective-permute-start(f32[2,2,2,2,2,2,2,8,128]{8,7,6,5,4,3,2,1,0:T(8,128)S(1)} %bitcast_select_fusion), channel_id=1, source_target_pairs={{0,2},{1,17},{2,0},{3,19},{4,6},{5,21},{6,4},{7,23},{8,10},{9,25},... | collective-permute-start | bytes 1572872 | tf_op jit(solution)/shard_map/ppermute | solution.py:129
  115.8 8.2 %collective-permute-start.9 = (f32[2,2,2,2,2,2,8,128]{7,6,5,4,3,2,1,0:T(8,128)S(1)}, f32[2,2,2,2,2,2,8,128]{7,6,5,4,3,2,1,0:T(8,128)S(1)}, u32[]{:S(2)}, u32[]{:S(2)}) collective-permute-start(f32[2,2,2,2,2,2,8,128]{7,6,5,4,3,2,1,0:T(8,128)S(1)} %bitcast_select_fusion.2), channel_id=1, source_target_pairs={{0,16},{1,3},{2,18},{3,1},{4,20},{5,7},{6,22},{7,5},{8,24},{9,11},... | collective-permute-start | bytes 786440 | tf_op jit(solution)/shard_map/ppermute | solution.py:129
  124.9 24.1 %all-to-all-start.1 = ((f32[64,8,128]{2,1,0:T(8,128)}), f32[64,8,128]{2,1,0:T(8,128)S(1)}, u32[]{:S(2)}, u32[]{:S(2)}) async-start(f32[64,8,128]{2,1,0:T(8,128)} %bitcast_add_fusion.1), calls=%async_computation.1 | async-start | bytes 524288 | tf_op jit(solution)/shard_map/all_to_all | solution.py:158
